TPU v7x, 32 devices: a whole 2x2x4 slice. The times are simulated.
32 devices in a mesh: scan: 16 (over z, y, core), row: 2 (over x).
Axes of the slice: x: 2, y: 2, z: 4, core: 2. Of those that a mesh axis runs over, the one named last changes fastest.
Arguments:
- estimate: float32 [128, 64, 512], P('scan', 'row'), may hold values from -6 to 6
- raw: float32 [128, 64, 512], P('scan', 'row'), may hold values from -6 to 6
- offsets: int32 [128], replicated, may hold values from 0 to 16, as said below
- depth_psf: float32 [64], replicated, may hold values from 0.03 to 0.2
- lateral_psf: float32 [17], replicated, may hold values from 0.05 to 0.4
- step_size: float32 [1], replicated, may hold values from 0.3 to 0.8
- threshold: float32 [1], replicated, may hold values from 0.3 to 1.5
Outputs:
- new_estimate: float32 [128, 64, 512], P('scan', 'row')
- misfit: float32 [128, 64, 512], P('scan', 'row')
Inputs may be any that keep to these rules, and one draw needn't show every extreme that they name: offsets[p] is how many planes beyond p the sheet of scan plane p begins; both 0 and 16 occur.
All inputs are finite; a program needn't handle non-finite values.
Results may differ from a plain program's by a relative error of at most 0.0003.
Values sent between devices are 32-bit elements; how exact they have to be, the bound alone decides.
No kernel may reach another device: no remote copies, remote signals or barrier semaphores. Data moves between devices by JAX's collectives and lax.ppermute only.
A program may use at most 64 MiB of HBM per device.

v0:
```python
import jax
import jax.numpy as jnp
from jax import lax
from jax.sharding import PartitionSpec as P

highest_mode = lax.Precision.HIGHEST


def with_halo(cells, sides, width):
    for axis, dim in sides:
        count = lax.axis_size(axis)
        ends = count - 1
        head = lax.slice_in_dim(cells, 0, width, axis=dim)
        tail = lax.slice_in_dim(cells, cells.shape[dim] - width, cells.shape[dim], axis=dim)
        cells = jnp.concatenate(
            [
                lax.ppermute(tail, axis, [(i, (i + 1) % count) for i in range(ends)]),
                cells,
                lax.ppermute(head, axis, [((i + 1) % count, i) for i in range(ends)]),
            ],
            axis=dim,
        )
    return cells


def lateral_blur(padded, kernel_taps, row_count):
    summed = jnp.zeros((padded.shape[0], row_count, padded.shape[2]), jnp.float32)
    for tap_index in range(kernel_taps.shape[0]):
        summed = summed + kernel_taps[tap_index] * padded[:, tap_index : tap_index + row_count, :]
    return summed


def sheet_matrix(own_offsets, depth_psf, column_count):
    plane_rows = jnp.arange(own_offsets.shape[0], dtype=jnp.int32)[:, None]
    plane_columns = jnp.arange(column_count, dtype=jnp.int32)[None, :]
    lag_planes = plane_columns - plane_rows - own_offsets[:, None]
    depth_count = depth_psf.shape[0]
    inside = (lag_planes >= 0) & (lag_planes < depth_count)
    looked = jnp.take(depth_psf, jnp.clip(lag_planes, 0, depth_count - 1))
    return jnp.where(inside, looked, 0.0)


def transpose_apply(sheet_psf, values):
    return lax.dot_general(sheet_psf, values, (((0,), (0,)), ((), ())), precision=highest_mode)


def body(estimate, raw, offsets, depth_psf, lateral_psf, step_size, threshold):
    plane_count, row_count, width_count = estimate.shape
    flat_count = row_count * width_count
    halo_rows = lateral_psf.shape[0] // 2
    padded = with_halo(estimate, (("row", 1),), halo_rows)
    blurred = lateral_blur(padded, lateral_psf, row_count).reshape(plane_count, flat_count)
    raw_flat = raw.reshape(plane_count, flat_count)
    sheet_psf = sheet_matrix(offsets, depth_psf, offsets.shape[0])
    pencil = lax.all_to_all(blurred, "scan", split_axis=1, concat_axis=0, tiled=True)
    predicted_pencil = jnp.dot(sheet_psf, pencil, precision=highest_mode)
    predicted = lax.all_to_all(predicted_pencil, "scan", split_axis=0, concat_axis=1, tiled=True)
    misfit = predicted - raw_flat
    misfit_pencil = lax.all_to_all(misfit, "scan", split_axis=1, concat_axis=0, tiled=True)
    back_pencil = transpose_apply(sheet_psf, misfit_pencil)
    back_flat = lax.all_to_all(back_pencil, "scan", split_axis=0, concat_axis=1, tiled=True)
    back_volume = back_flat.reshape(plane_count, row_count, width_count)
    padded_back = with_halo(back_volume, (("row", 1),), halo_rows)
    gradient = lateral_blur(padded_back, lateral_psf[::-1], row_count)
    stepped = estimate - step_size[0] * gradient
    shrink_level = step_size[0] * threshold[0]
    new_estimate = jnp.sign(stepped) * jnp.maximum(jnp.abs(stepped) - shrink_level, 0.0)
    return (new_estimate, misfit.reshape(plane_count, row_count, width_count))


def solution(mesh):
    placed = (P("scan", "row", None), P("scan", "row", None), P(), P(), P(), P(), P())
    return jax.shard_map(
        body,
        mesh=mesh,
        in_specs=placed,
        out_specs=(P("scan", "row", None), P("scan", "row", None)),
        check_vma=False,
    )
```

profile of v0, /device:TPU:0, one launch (start us, length us, event | category | flops | bytes accessed | tf_op | source)
XLA Modules:
  0.0 215.0 jit_solution(11334854748215008901)
XLA Ops:
  0.6 0.0 copy-start
  0.6 0.0 copy-start.1
  0.7 1.0 fusion.72
  1.7 0.0 copy-start.3
  1.7 4.8 %collective-permute-start = (f32[8,8,512]{2,1,0:T(8,128)S(1)}, f32[8,8,512]{2,1,0:T(8,128)S(1)}, u32[]{:S(2)}, u32[]{:S(2)}) collective-permute-start(f32[8,8,512]{2,1,0:T(8,128)S(1)} %get-tuple-element.8), channel_id=1, source_target_pairs={{0,1},{2,3},{4,5},{6,7},{8,9},{10,11},{12,13},{14,15},{16,17},{18,... | collective-permute-start | bytes 393224 | tf_op jit(solution)/shard_map/ppermute | solution.py:17
  6.6 1.3 collective-permute-start.1
  7.9 0.0 copy-done.3
  7.9 0.7 fusion.73
  8.6 0.7 collective-permute-done
  9.3 0.0 copy-done.1
  9.3 0.1 constant_dynamic-update-slice_fusion
  9.5 4.0 %collective-permute-done.1 = f32[8,8,512]{2,1,0:T(8,128)S(1)} collective-permute-done((f32[8,8,512]{2,1,0:T(8,128)S(1)}, f32[8,8,512]{2,1,0:T(8,128)S(1)}, u32[]{:S(2)}, u32[]{:S(2)}) %collective-permute-start.1) | collective-permute-done | bytes 131104 | tf_op jit(solution)/shard_map/ppermute | solution.py:19
  13.4 11.7 %fusion.18 = f32[8,32,512]{2,1,0:T(8,128)S(1)} fusion(f32[8,40,512]{2,1,0:T(8,128)S(1)} %constant_dynamic-update-slice_fusion.2, f32[8,40,512]{2,1,0:T(8,128)S(1)} %get-tuple-element.6, f32[8,32,512]{2,1,0:T(8,128)S(1)} %copy-done.1, f32[]{:T(128)} %bitcast.23, f32[]{:T(128)} %bitcast.22, f32[]{:T(128)} %bitcast.21, f32[]{:T(128)} %bitcast.20, f32[]{:T(128)} %bitcast.19, ...), kind=kLoop, calls=%fused_computation.36 | loop fusion | flops 4325376 | bytes 9437252 | tf_op jit(solution)/shard_map/add | solution.py:29
  25.1 0.2 all_to_all.48
  25.3 1.1 copy.16
  26.4 0.0 copy-start.4
  26.4 6.1 %all-to-all-start = ((f32[8,16,1024]{2,0,1:T(8,128)}), f32[8,16,1024]{2,0,1:T(8,128)S(1)}, u32[]{:S(2)}, u32[]{:S(2)}) async-start(f32[8,16,1024]{2,0,1:T(8,128)} %copy.16), calls=%async_computation | async-start | bytes 1048576 | tf_op jit(solution)/shard_map/all_to_all | solution.py:55
  32.5 0.0 copy-done.4
  32.5 0.1 sub.141
  32.6 0.1 fusion.39
  32.7 0.0 copy-done
  32.7 97.2 %gather_fusion = f32[16384]{0:T(1024)S(1)} fusion(f32[64]{0:T(128)S(1)} %copy-done, s32[16384]{0:T(1024)S(1)} %fusion.39), kind=kCustom, calls=%fused_computation | custom fusion | bytes 196608 | tf_op jit(solution)/shard_map/jit(_take)/gather | solution.py:39
  129.9 0.0 all-to-all-done
  130.0 1.4 fusion.36
  131.4 0.0 copy-start.2
  131.4 6.1 %all-to-all-start.1 = ((f32[16,8,1024]{2,1,0:T(8,128)}), f32[16,8,1024]{2,1,0:T(8,128)S(1)}, u32[]{:S(2)}, u32[]{:S(2)}) async-start(f32[16,8,1024]{2,1,0:T(8,128)} %fusion.36), calls=%async_computation.1 | async-start | bytes 1048576 | tf_op jit(solution)/shard_map/all_to_all | solution.py:57
  137.5 0.0 copy-done.2
  137.5 0.2 reshape.217
  137.7 14.3 %all-to-all-done.1 = f32[16,8,1024]{2,1,0:T(8,128)S(1)} async-done(((f32[16,8,1024]{2,1,0:T(8,128)}), f32[16,8,1024]{2,1,0:T(8,128)S(1)}, u32[]{:S(2)}, u32[]{:S(2)}) %all-to-all-start.1) | async-done | bytes 524320 | tf_op jit(solution)/shard_map/all_to_all | solution.py:57
  152.0 1.1 copy_subtract_fusion
  153.1 4.1 %all-to-all-start.2 = ((f32[8,16,1024]{2,0,1:T(8,128)}), f32[8,16,1024]{2,0,1:T(8,128)S(1)}, u32[]{:S(2)}, u32[]{:S(2)}) async-start(f32[8,16,1024]{2,0,1:T(8,128)} %copy_subtract_fusion), calls=%async_computation.2 | async-start | bytes 1048576 | tf_op jit(solution)/shard_map/all_to_all | solution.py:59
  157.2 0.1 fusion.40
  157.3 0.1 copy.15
  157.4 14.3 %all-to-all-done.2 = f32[8,16,1024]{2,0,1:T(8,128)S(1)} async-done(((f32[8,16,1024]{2,0,1:T(8,128)}), f32[8,16,1024]{2,0,1:T(8,128)S(1)}, u32[]{:S(2)}, u32[]{:S(2)}) %all-to-all-start.2) | async-done | bytes 524320 | tf_op jit(solution)/shard_map/all_to_all | solution.py:59
  171.7 0.6 fusion.34
  172.3 18.4 %all_to_all.64 = f32[16,8,1024]{2,1,0:T(8,128)S(1)} all-to-all(f32[16,8,1024]{2,1,0:T(8,128)S(1)} %fusion.34), channel_id=1, replica_groups=mesh['scan'=16,'row'=2] {'scan'}, dimensions={0} | all-to-all | bytes 1048576 | tf_op jit(solution)/shard_map/all_to_all | solution.py:61
  190.6 0.3 copy.18
  191.0 0.1 reshape.218
  191.1 1.5 collective-permute-start.2
  193.9 0.3 copy.19
  194.2 0.1 all_to_all.59
  194.3 0.9 sub.148
  195.1 1.3 collective-permute-start.3
  196.4 0.0 collective-permute-done.2
  196.5 0.1 constant_dynamic-update-slice_fusion.4
  196.6 5.7 %collective-permute-done.3 = f32[8,8,512]{2,1,0:T(8,128)S(1)} collective-permute-done((f32[8,8,512]{2,1,0:T(8,128)S(1)}, f32[8,8,512]{2,1,0:T(8,128)S(1)}, u32[]{:S(2)}, u32[]{:S(2)}) %collective-permute-start.3) | collective-permute-done | bytes 131104 | tf_op jit(solution)/shard_map/ppermute | solution.py:19
  202.3 12.7 %maximum_multiply_fusion = f32[8,32,512]{2,1,0:T(8,128)} fusion(f32[8,32,512]{2,1,0:T(8,128)S(1)} %copy-done.1, f32[8,40,512]{2,1,0:T(8,128)S(1)} %constant_dynamic-update-slice_fusion.6, f32[8,32,512]{2,1,0:T(8,128)S(1)} %reshape.218, f32[8,40,512]{2,1,0:T(8,128)S(1)} %get-tuple-element.2, f32[]{:T(128)S(6)} %mul.235, f32[]{:T(128)} %bitcast.23, ...), kind=kLoop, calls=%fused_computation.72 | loop fusion | flops 5242880 | bytes 9961548 | tf_op jit(solution)/shard_map/mul | solution.py:67
  (6 shorter events, 0.1 us)
Async XLA Ops:
  0.6 32.1 %copy-start = (f32[64]{0:T(128)S(1)}, f32[64]{0:T(128)}, u32[]{:S(2)}) copy-start(f32[64]{0:T(128)} %param.10) | copy-start | bytes 772
  0.6 8.7 %copy-start.1 = (f32[8,32,512]{2,1,0:T(8,128)S(1)}, f32[8,32,512]{2,1,0:T(8,128)}, u32[]{:S(2)}) copy-start(f32[8,32,512]{2,1,0:T(8,128)} %param.7) | copy-start | bytes 1572868
  1.7 6.2 %copy-start.3 = (f32[17]{0:T(128)S(1)}, f32[17]{0:T(128)}, u32[]{:S(2)}) copy-start(f32[17]{0:T(128)} %param.11) | copy-start | bytes 208
  1.7 7.6 %collective-permute-start = (f32[8,8,512]{2,1,0:T(8,128)S(1)}, f32[8,8,512]{2,1,0:T(8,128)S(1)}, u32[]{:S(2)}, u32[]{:S(2)}) collective-permute-start(f32[8,8,512]{2,1,0:T(8,128)S(1)} %get-tuple-element.8), channel_id=1, source_target_pairs={{0,1},{2,3},{4,5},{6,7},{8,9},{10,11},{12,13},{14,15},{16,17},{18,... | collective-permute-start | bytes 393224 | tf_op jit(solution)/shard_map/ppermute | solution.py:17
  6.6 6.9 %collective-permute-start.1 = (f32[8,8,512]{2,1,0:T(8,128)S(1)}, f32[8,8,512]{2,1,0:T(8,128)S(1)}, u32[]{:S(2)}, u32[]{:S(2)}) collective-permute-start(f32[8,8,512]{2,1,0:T(8,128)S(1)} %get-tuple-element.9), channel_id=1, source_target_pairs={{1,0},{3,2},{5,4},{7,6},{9,8},{11,10},{13,12},{15,14},{17,16},{19,... | collective-permute-start | bytes 393224 | tf_op jit(solution)/shard_map/ppermute | solution.py:19
  26.4 6.1 %copy-start.4 = (s32[128]{0:T(128)S(1)}, s32[128]{0:T(128)}, u32[]{:S(2)}) copy-start(s32[128]{0:T(128)} %param.9) | copy-start | bytes 1540
  26.4 103.5 %all-to-all-start = ((f32[8,16,1024]{2,0,1:T(8,128)}), f32[8,16,1024]{2,0,1:T(8,128)S(1)}, u32[]{:S(2)}, u32[]{:S(2)}) async-start(f32[8,16,1024]{2,0,1:T(8,128)} %copy.16), calls=%async_computation | async-start | bytes 1048576 | tf_op jit(solution)/shard_map/all_to_all | solution.py:55
  131.4 6.1 %copy-start.2 = (f32[8,32,512]{2,1,0:T(8,128)S(1)}, f32[8,32,512]{2,1,0:T(8,128)}, u32[]{:S(2)}) copy-start(f32[8,32,512]{2,1,0:T(8,128)} %param.8) | copy-start | bytes 1572868
  131.4 20.6 %all-to-all-start.1 = ((f32[16,8,1024]{2,1,0:T(8,128)}), f32[16,8,1024]{2,1,0:T(8,128)S(1)}, u32[]{:S(2)}, u32[]{:S(2)}) async-start(f32[16,8,1024]{2,1,0:T(8,128)} %fusion.36), calls=%async_computation.1 | async-start | bytes 1048576 | tf_op jit(solution)/shard_map/all_to_all | solution.py:57
  153.1 18.6 %all-to-all-start.2 = ((f32[8,16,1024]{2,0,1:T(8,128)}), f32[8,16,1024]{2,0,1:T(8,128)S(1)}, u32[]{:S(2)}, u32[]{:S(2)}) async-start(f32[8,16,1024]{2,0,1:T(8,128)} %copy_subtract_fusion), calls=%async_computation.2 | async-start | bytes 1048576 | tf_op jit(solution)/shard_map/all_to_all | solution.py:59
  191.1 5.4 %collective-permute-start.2 = (f32[8,8,512]{2,1,0:T(8,128)S(1)}, f32[8,8,512]{2,1,0:T(8,128)S(1)}, u32[]{:S(2)}, u32[]{:S(2)}) collective-permute-start(f32[8,8,512]{2,1,0:T(8,128)S(1)} %get-tuple-element.4), channel_id=1, source_target_pairs={{0,1},{2,3},{4,5},{6,7},{8,9},{10,11},{12,13},{14,15},{16,17},{18,... | collective-permute-start | bytes 393224 | tf_op jit(solution)/shard_map/ppermute | solution.py:17
  195.1 7.1 %collective-permute-start.3 = (f32[8,8,512]{2,1,0:T(8,128)S(1)}, f32[8,8,512]{2,1,0:T(8,128)S(1)}, u32[]{:S(2)}, u32[]{:S(2)}) collective-permute-start(f32[8,8,512]{2,1,0:T(8,128)S(1)} %get-tuple-element.5), channel_id=1, source_target_pairs={{1,0},{3,2},{5,4},{7,6},{9,8},{11,10},{13,12},{15,14},{17,16},{19,... | collective-permute-start | bytes 393224 | tf_op jit(solution)/shard_map/ppermute | solution.py:19
where the time goes:
time: 216 us; the launch traced here: 215 us
  local copies, waits for them, and re-layouts  102 us (47%)
  waiting for transfers between devices  38.9 us (18%)
  other arithmetic  26.6 us (12%)
  starting transfers between devices  25.2 us (12%)
  blocking collectives  18.4 us (9%)
  between operations  2.2 us (1%)
    gather x1, local copies, waits for them, and re-layouts, sheet_matrix(): looked = jnp.take(depth_psf, jnp.clip(lag_planes, 0, depth_count - 1))  97.2 us
    all_to_all x1, blocking collectives, body(): lax.all_to_all(back_pencil, 'scan', split_axis=0, concat_axis=1, tiled=True)  18.4 us
    all_to_all x1, waiting for transfers between devices, body(): lax.all_to_all(predicted_pencil, 'scan', split_axis=0, concat_axis=1, til...  14.3 us
    all_to_all x1, waiting for transfers between devices, body(): lax.all_to_all(misfit, 'scan', split_axis=1, concat_axis=0, tiled=True)  14.3 us
    mul x1, other arithmetic, body(): jnp.sign(stepped) * jnp.maximum(jnp.abs(stepped) - shrink_level, 0.0)  12.7 us
    add x1, other arithmetic, lateral_blur(): summed + kernel_taps[tap_index] * padded[:, tap_index:tap_index + row_cou...  11.7 us
    ppermute x2, waiting for transfers between devices, with_halo(): lax.ppermute(head, axis, [((i + 1) % count, i) for i in range(ends)])  9.63 us
    ppermute x2, starting transfers between devices, with_halo(): lax.ppermute(tail, axis, [(i, (i + 1) % count) for i in range(ends)])  6.34 us
  transfers between devices with their start and end apart: 7, of which 5 were waited for; matrix products, arithmetic and copies ran while one was open for 46% of the time, Pallas kernels for 0%

commit v1 on v0

--- a/solution.py
+++ b/solution.py
@@ -36,8 +36,9 @@
     lag_planes = plane_columns - plane_rows - own_offsets[:, None]
     depth_count = depth_psf.shape[0]
     inside = (lag_planes >= 0) & (lag_planes < depth_count)
-    looked = jnp.take(depth_psf, jnp.clip(lag_planes, 0, depth_count - 1))
-    return jnp.where(inside, looked, 0.0)
+    taps = jnp.arange(depth_count, dtype=jnp.int32)
+    picked = jnp.where(lag_planes[:, :, None] == taps, depth_psf, 0.0)
+    return jnp.where(inside, jnp.sum(picked, axis=-1), 0.0)
 
 
 def transpose_apply(sheet_psf, values):

time: 216 us -> 131 us (0.61)
  local copies, waits for them, and re-layouts: 102 us -> 5.76 us
  waiting for transfers between devices: 38.9 us -> 50.6 us
    gather x1 -> x0, local copies, waits for them, and re-layouts: 97.2 us -> none  [sheet_matrix(): looked = jnp.take(depth_psf, jnp.clip(lag_planes, 0, depth_count - 1))]
    all_to_all x1, waiting for transfers between devices: 0.01 us -> 12.9 us  [body(): lax.all_to_all(blurred, 'scan', split_axis=1, concat_axis=0, tiled=True)]
  transfers between devices with their start and end apart: 7 -> 7, of which waited for: 5 -> 5; matrix products, arithmetic and copies ran while one was open for 46% -> 4% of each run, Pallas kernels for 0% -> 0%
where the time goes in v1:
time: 131 us; the launch traced here: 130 us
  waiting for transfers between devices  50.6 us (39%)
  other arithmetic  28 us (21%)
  starting transfers between devices  23.3 us (18%)
  blocking collectives  18.4 us (14%)
  local copies, waits for them, and re-layouts  5.76 us (4%)
  between operations  2.17 us (2%)
  matrix products  2.01 us (2%)
    all_to_all x1, blocking collectives, body(): lax.all_to_all(back_pencil, 'scan', split_axis=0, concat_axis=1, tiled=True)  18.4 us
    all_to_all x1, waiting for transfers between devices, body(): lax.all_to_all(misfit, 'scan', split_axis=1, concat_axis=0, tiled=True)  14.4 us
    all_to_all x1, waiting for transfers between devices, body(): lax.all_to_all(predicted_pencil, 'scan', split_axis=0, concat_axis=1, til...  14.3 us
    all_to_all x1, waiting for transfers between devices, body(): lax.all_to_all(blurred, 'scan', split_axis=1, concat_axis=0, tiled=True)  12.9 us
    mul x1, other arithmetic, body(): jnp.sign(stepped) * jnp.maximum(jnp.abs(stepped) - shrink_level, 0.0)  12.8 us
    add x1, other arithmetic, lateral_blur(): summed + kernel_taps[tap_index] * padded[:, tap_index:tap_index + row_cou...  11.8 us
    ppermute x2, waiting for transfers between devices, with_halo(): lax.ppermute(head, axis, [((i + 1) % count, i) for i in range(ends)])  9.05 us
    ppermute x2, starting transfers between devices, with_halo(): lax.ppermute(tail, axis, [(i, (i + 1) % count) for i in range(ends)])  6.34 us
  transfers between devices with their start and end apart: 7, of which 5 were waited for; matrix products, arithmetic and copies ran while one was open for 4% of the time, Pallas kernels for 0%

profile of v1, /device:TPU:0, one launch (start us, length us, event | category | flops | bytes accessed | tf_op | source)
XLA Modules:
  0.0 130.2 jit_solution(17271320568263683405)
XLA Ops:
  0.6 0.0 copy-start
  0.6 1.0 fusion.65
  1.7 4.8 %collective-permute-start = (f32[8,8,512]{2,1,0:T(8,128)S(1)}, f32[8,8,512]{2,1,0:T(8,128)S(1)}, u32[]{:S(2)}, u32[]{:S(2)}) collective-permute-start(f32[8,8,512]{2,1,0:T(8,128)S(1)} %get-tuple-element.8), channel_id=1, source_target_pairs={{0,1},{2,3},{4,5},{6,7},{8,9},{10,11},{12,13},{14,15},{16,17},{18,... | collective-permute-start | bytes 393224 | tf_op jit(solution)/shard_map/ppermute | solution.py:17
  6.5 1.3 collective-permute-start.1
  7.8 2.0 %fusion.66 = (f32[1]{0:T(128)}, f32[1]{0:T(128)}, f32[1]{0:T(128)}, f32[1]{0:T(128)}, f32[1]{0:T(128)}, /*index=5*/f32[1]{0:T(128)}, f32[1]{0:T(128)}, f32[1]{0:...) fusion(f32[17]{0:T(128)} %param.11), kind=kLoop, calls=%fused_computation.113 | loop fusion | bytes 136 | tf_op jit(solution)/shard_map/slice | solution.py:29
  9.9 0.0 collective-permute-done
  9.9 0.0 copy-done
  9.9 0.1 constant_dynamic-update-slice_fusion
  10.0 3.4 %collective-permute-done.1 = f32[8,8,512]{2,1,0:T(8,128)S(1)} collective-permute-done((f32[8,8,512]{2,1,0:T(8,128)S(1)}, f32[8,8,512]{2,1,0:T(8,128)S(1)}, u32[]{:S(2)}, u32[]{:S(2)}) %collective-permute-start.1) | collective-permute-done | bytes 131104 | tf_op jit(solution)/shard_map/ppermute | solution.py:19
  13.4 11.8 %fusion.18 = f32[8,32,512]{2,1,0:T(8,128)S(1)} fusion(f32[8,40,512]{2,1,0:T(8,128)S(1)} %constant_dynamic-update-slice_fusion.2, f32[8,40,512]{2,1,0:T(8,128)S(1)} %get-tuple-element.6, f32[8,32,512]{2,1,0:T(8,128)S(1)} %copy-done, f32[]{:T(128)} %bitcast.20, f32[]{:T(128)} %bitcast.19, f32[]{:T(128)} %bitcast.18, f32[]{:T(128)} %bitcast.17, f32[]{:T(128)} %bitcast.16, ...), kind=kLoop, calls=%fused_computation.37 | loop fusion | flops 4325376 | bytes 9437252 | tf_op jit(solution)/shard_map/add | solution.py:29
  25.2 0.2 all_to_all.48
  25.4 1.1 copy.17
  26.5 0.0 copy-start.2
  26.5 0.0 copy-start.3
  26.5 6.1 %all-to-all-start = ((f32[8,16,1024]{2,0,1:T(8,128)}), f32[8,16,1024]{2,0,1:T(8,128)S(1)}, u32[]{:S(2)}, u32[]{:S(2)}) async-start(f32[8,16,1024]{2,0,1:T(8,128)} %copy.17), calls=%async_computation | async-start | bytes 1048576 | tf_op jit(solution)/shard_map/all_to_all | solution.py:56
  32.6 0.1 sub.103
  32.6 0.0 copy-done.2
  32.7 0.1 subtract_subtract_fusion.1
  32.7 0.0 copy-done.3
  32.7 1.4 %select_reduce_fusion = f32[128,128]{1,0:T(8,128)S(1)} fusion(f32[64]{0:T(128)S(1)} %copy-done.3, s32[128,128]{1,0:T(8,128)S(1)} %subtract_subtract_fusion.1), kind=kLoop, calls=%fused_computation | loop fusion | flops 3129344 | bytes 131328 | tf_op jit(solution)/shard_map/reduce_sum | solution.py:41
  34.1 12.9 %all-to-all-done = f32[8,16,1024]{2,0,1:T(8,128)S(1)} async-done(((f32[8,16,1024]{2,0,1:T(8,128)}), f32[8,16,1024]{2,0,1:T(8,128)S(1)}, u32[]{:S(2)}, u32[]{:S(2)}) %all-to-all-start) | async-done | bytes 524320 | tf_op jit(solution)/shard_map/all_to_all | solution.py:56
  47.0 1.4 %fusion.36 = f32[16,8,1024]{2,1,0:T(8,128)} fusion(f32[8,16,1024]{2,0,1:T(8,128)S(1)} %all-to-all-done, f32[128,128]{1,0:T(8,128)S(1)} %select_reduce_fusion, s32[128]{0:T(128)S(1)} %sub.103, s32[128]{0:T(128)S(1)} %copy-done.2), kind=kOutput, calls=%fused_computation.70 | convolution fusion | flops 201424896 | bytes 1115136 | tf_op jit(solution)/shard_map/dot_general | solution.py:57
  48.4 0.0 copy-start.1
  48.4 4.2 %all-to-all-start.1 = ((f32[16,8,1024]{2,1,0:T(8,128)}), f32[16,8,1024]{2,1,0:T(8,128)S(1)}, u32[]{:S(2)}, u32[]{:S(2)}) async-start(f32[16,8,1024]{2,1,0:T(8,128)} %fusion.36), calls=%async_computation.1 | async-start | bytes 1048576 | tf_op jit(solution)/shard_map/all_to_all | solution.py:58
  52.7 0.0 copy-done.1
  52.7 0.2 reshape.128
  52.9 14.3 %all-to-all-done.1 = f32[16,8,1024]{2,1,0:T(8,128)S(1)} async-done(((f32[16,8,1024]{2,1,0:T(8,128)}), f32[16,8,1024]{2,1,0:T(8,128)S(1)}, u32[]{:S(2)}, u32[]{:S(2)}) %all-to-all-start.1) | async-done | bytes 524320 | tf_op jit(solution)/shard_map/all_to_all | solution.py:58
  67.1 1.1 copy_subtract_fusion
  68.3 4.1 %all-to-all-start.2 = ((f32[8,16,1024]{2,0,1:T(8,128)}), f32[8,16,1024]{2,0,1:T(8,128)S(1)}, u32[]{:S(2)}, u32[]{:S(2)}) async-start(f32[8,16,1024]{2,0,1:T(8,128)} %copy_subtract_fusion), calls=%async_computation.2 | async-start | bytes 1048576 | tf_op jit(solution)/shard_map/all_to_all | solution.py:60
  72.4 0.1 copy.16
  72.5 14.4 %all-to-all-done.2 = f32[8,16,1024]{2,0,1:T(8,128)S(1)} async-done(((f32[8,16,1024]{2,0,1:T(8,128)}), f32[8,16,1024]{2,0,1:T(8,128)S(1)}, u32[]{:S(2)}, u32[]{:S(2)}) %all-to-all-start.2) | async-done | bytes 524320 | tf_op jit(solution)/shard_map/all_to_all | solution.py:60
  86.8 0.6 fusion.34
  87.4 18.4 %all_to_all.64 = f32[16,8,1024]{2,1,0:T(8,128)S(1)} all-to-all(f32[16,8,1024]{2,1,0:T(8,128)S(1)} %fusion.34), channel_id=1, replica_groups=mesh['scan'=16,'row'=2] {'scan'}, dimensions={0} | all-to-all | bytes 1048576 | tf_op jit(solution)/shard_map/all_to_all | solution.py:62
  105.8 0.3 copy.19
  106.1 0.1 reshape.129
  106.2 1.5 %collective-permute-start.2 = (f32[8,8,512]{2,1,0:T(8,128)S(1)}, f32[8,8,512]{2,1,0:T(8,128)S(1)}, u32[]{:S(2)}, u32[]{:S(2)}) collective-permute-start(f32[8,8,512]{2,1,0:T(8,128)S(1)} %get-tuple-element.4), channel_id=1, source_target_pairs={{0,1},{2,3},{4,5},{6,7},{8,9},{10,11},{12,13},{14,15},{16,17},{18,... | collective-permute-start | bytes 393224 | tf_op jit(solution)/shard_map/ppermute | solution.py:17
  109.0 0.3 copy.20
  109.3 0.1 all_to_all.59
  109.4 0.9 sub.111
  110.3 1.3 collective-permute-start.3
  111.6 0.0 collective-permute-done.2
  111.6 0.1 constant_dynamic-update-slice_fusion.4
  111.8 5.7 %collective-permute-done.3 = f32[8,8,512]{2,1,0:T(8,128)S(1)} collective-permute-done((f32[8,8,512]{2,1,0:T(8,128)S(1)}, f32[8,8,512]{2,1,0:T(8,128)S(1)}, u32[]{:S(2)}, u32[]{:S(2)}) %collective-permute-start.3) | collective-permute-done | bytes 131104 | tf_op jit(solution)/shard_map/ppermute | solution.py:19
  117.4 12.8 %maximum_multiply_fusion = f32[8,32,512]{2,1,0:T(8,128)} fusion(f32[8,32,512]{2,1,0:T(8,128)S(1)} %copy-done, f32[8,40,512]{2,1,0:T(8,128)S(1)} %constant_dynamic-update-slice_fusion.6, f32[8,32,512]{2,1,0:T(8,128)S(1)} %reshape.129, f32[8,40,512]{2,1,0:T(8,128)S(1)} %get-tuple-element.2, f32[]{:T(128)S(6)} %mul.235, f32[]{:T(128)} %bitcast.20, f32[]{:T(128)} %bitcast.19, ...), kind=kLoop, calls=%fused_computation.73 | loop fusion | flops 5242880 | bytes 9961548 | tf_op jit(solution)/shard_map/mul | solution.py:68
  (6 shorter events, 0.1 us)
Async XLA Ops:
  0.6 9.3 %copy-start = (f32[8,32,512]{2,1,0:T(8,128)S(1)}, f32[8,32,512]{2,1,0:T(8,128)}, u32[]{:S(2)}) copy-start(f32[8,32,512]{2,1,0:T(8,128)} %param.7) | copy-start | bytes 1572868
  1.7 8.2 %collective-permute-start = (f32[8,8,512]{2,1,0:T(8,128)S(1)}, f32[8,8,512]{2,1,0:T(8,128)S(1)}, u32[]{:S(2)}, u32[]{:S(2)}) collective-permute-start(f32[8,8,512]{2,1,0:T(8,128)S(1)} %get-tuple-element.8), channel_id=1, source_target_pairs={{0,1},{2,3},{4,5},{6,7},{8,9},{10,11},{12,13},{14,15},{16,17},{18,... | collective-permute-start | bytes 393224 | tf_op jit(solution)/shard_map/ppermute | solution.py:17
  6.5 6.9 %collective-permute-start.1 = (f32[8,8,512]{2,1,0:T(8,128)S(1)}, f32[8,8,512]{2,1,0:T(8,128)S(1)}, u32[]{:S(2)}, u32[]{:S(2)}) collective-permute-start(f32[8,8,512]{2,1,0:T(8,128)S(1)} %get-tuple-element.9), channel_id=1, source_target_pairs={{1,0},{3,2},{5,4},{7,6},{9,8},{11,10},{13,12},{15,14},{17,16},{19,... | collective-permute-start | bytes 393224 | tf_op jit(solution)/shard_map/ppermute | solution.py:19
  26.5 6.2 %copy-start.2 = (s32[128]{0:T(128)S(1)}, s32[128]{0:T(128)}, u32[]{:S(2)}) copy-start(s32[128]{0:T(128)} %param.9) | copy-start | bytes 1540
  26.5 6.3 %copy-start.3 = (f32[64]{0:T(128)S(1)}, f32[64]{0:T(128)}, u32[]{:S(2)}) copy-start(f32[64]{0:T(128)} %param.10) | copy-start | bytes 772
  26.5 20.5 %all-to-all-start = ((f32[8,16,1024]{2,0,1:T(8,128)}), f32[8,16,1024]{2,0,1:T(8,128)S(1)}, u32[]{:S(2)}, u32[]{:S(2)}) async-start(f32[8,16,1024]{2,0,1:T(8,128)} %copy.17), calls=%async_computation | async-start | bytes 1048576 | tf_op jit(solution)/shard_map/all_to_all | solution.py:56
  48.4 4.2 %copy-start.1 = (f32[8,32,512]{2,1,0:T(8,128)S(1)}, f32[8,32,512]{2,1,0:T(8,128)}, u32[]{:S(2)}) copy-start(f32[8,32,512]{2,1,0:T(8,128)} %param.8) | copy-start | bytes 1572868
  48.4 18.7 %all-to-all-start.1 = ((f32[16,8,1024]{2,1,0:T(8,128)}), f32[16,8,1024]{2,1,0:T(8,128)S(1)}, u32[]{:S(2)}, u32[]{:S(2)}) async-start(f32[16,8,1024]{2,1,0:T(8,128)} %fusion.36), calls=%async_computation.1 | async-start | bytes 1048576 | tf_op jit(solution)/shard_map/all_to_all | solution.py:58
  68.3 18.6 %all-to-all-start.2 = ((f32[8,16,1024]{2,0,1:T(8,128)}), f32[8,16,1024]{2,0,1:T(8,128)S(1)}, u32[]{:S(2)}, u32[]{:S(2)}) async-start(f32[8,16,1024]{2,0,1:T(8,128)} %copy_subtract_fusion), calls=%async_computation.2 | async-start | bytes 1048576 | tf_op jit(solution)/shard_map/all_to_all | solution.py:60
  106.2 5.4 %collective-permute-start.2 = (f32[8,8,512]{2,1,0:T(8,128)S(1)}, f32[8,8,512]{2,1,0:T(8,128)S(1)}, u32[]{:S(2)}, u32[]{:S(2)}) collective-permute-start(f32[8,8,512]{2,1,0:T(8,128)S(1)} %get-tuple-element.4), channel_id=1, source_target_pairs={{0,1},{2,3},{4,5},{6,7},{8,9},{10,11},{12,13},{14,15},{16,17},{18,... | collective-permute-start | bytes 393224 | tf_op jit(solution)/shard_map/ppermute | solution.py:17
  110.3 7.1 %collective-permute-start.3 = (f32[8,8,512]{2,1,0:T(8,128)S(1)}, f32[8,8,512]{2,1,0:T(8,128)S(1)}, u32[]{:S(2)}, u32[]{:S(2)}) collective-permute-start(f32[8,8,512]{2,1,0:T(8,128)S(1)} %get-tuple-element.5), channel_id=1, source_target_pairs={{1,0},{3,2},{5,4},{7,6},{9,8},{11,10},{13,12},{15,14},{17,16},{19,... | collective-permute-start | bytes 393224 | tf_op jit(solution)/shard_map/ppermute | solution.py:19

commit v2 on v1

--- a/solution.py
+++ b/solution.py
@@ -23,11 +23,17 @@
     return cells
 
 
-def lateral_blur(padded, kernel_taps, row_count):
-    summed = jnp.zeros((padded.shape[0], row_count, padded.shape[2]), jnp.float32)
-    for tap_index in range(kernel_taps.shape[0]):
-        summed = summed + kernel_taps[tap_index] * padded[:, tap_index : tap_index + row_count, :]
-    return summed
+def band_matrix(kernel_taps, row_count, shift):
+    tap_count = kernel_taps.shape[0]
+    out_rows = jnp.arange(row_count, dtype=jnp.int32)[:, None]
+    in_rows = jnp.arange(row_count + tap_count - 1, dtype=jnp.int32)[None, :]
+    lag = shift + in_rows - out_rows
+    taps = jnp.arange(tap_count, dtype=jnp.int32)
+    return jnp.sum(jnp.where(lag[:, :, None] == taps, kernel_taps, 0.0), axis=-1)
+
+
+def lateral_apply(band, padded):
+    return jnp.einsum("rk,pkc->prc", band, padded, precision=highest_mode)
 
 
 def sheet_matrix(own_offsets, depth_psf, column_count):
@@ -49,20 +55,22 @@
     plane_count, row_count, width_count = estimate.shape
     flat_count = row_count * width_count
     halo_rows = lateral_psf.shape[0] // 2
+    raw_pencil = lax.all_to_all(raw.reshape(plane_count, flat_count), "scan", split_axis=1, concat_axis=0, tiled=True)
+    sheet_psf = sheet_matrix(offsets, depth_psf, offsets.shape[0])
+    blur_band = band_matrix(lateral_psf, row_count, 0)
+    back_band = band_matrix(lateral_psf[::-1], row_count, 0)
     padded = with_halo(estimate, (("row", 1),), halo_rows)
-    blurred = lateral_blur(padded, lateral_psf, row_count).reshape(plane_count, flat_count)
-    raw_flat = raw.reshape(plane_count, flat_count)
-    sheet_psf = sheet_matrix(offsets, depth_psf, offsets.shape[0])
+    blurred = lateral_apply(blur_band, padded).reshape(plane_count, flat_count)
     pencil = lax.all_to_all(blurred, "scan", split_axis=1, concat_axis=0, tiled=True)
     predicted_pencil = jnp.dot(sheet_psf, pencil, precision=highest_mode)
-    predicted = lax.all_to_all(predicted_pencil, "scan", split_axis=0, concat_axis=1, tiled=True)
-    misfit = predicted - raw_flat
-    misfit_pencil = lax.all_to_all(misfit, "scan", split_axis=1, concat_axis=0, tiled=True)
+    misfit_pencil = predicted_pencil - raw_pencil
     back_pencil = transpose_apply(sheet_psf, misfit_pencil)
-    back_flat = lax.all_to_all(back_pencil, "scan", split_axis=0, concat_axis=1, tiled=True)
-    back_volume = back_flat.reshape(plane_count, row_count, width_count)
+    both_pencil = jnp.stack([misfit_pencil, back_pencil])
+    both = lax.all_to_all(both_pencil, "scan", split_axis=1, concat_axis=2, tiled=True)
+    misfit = both[0]
+    back_volume = both[1].reshape(plane_count, row_count, width_count)
     padded_back = with_halo(back_volume, (("row", 1),), halo_rows)
-    gradient = lateral_blur(padded_back, lateral_psf[::-1], row_count)
+    gradient = lateral_apply(back_band, padded_back)
     stepped = estimate - step_size[0] * gradient
     shrink_level = step_size[0] * threshold[0]
     new_estimate = jnp.sign(stepped) * jnp.maximum(jnp.abs(stepped) - shrink_level, 0.0)

time: 131 us -> 88.7 us (0.68)
  other arithmetic: 28 us -> 1.65 us
  waiting for transfers between devices: 50.6 us -> 24.8 us
  blocking collectives: 18.4 us -> 28.7 us
  starting transfers between devices: 23.3 us -> 21 us
  matrix products: 2.01 us -> 3.61 us
    all_to_all x2 -> x1, waiting for transfers between devices: 28.7 us -> 1.62 us  [body(): lax.all_to_all(raw.reshape(plane_count, flat_count), 'scan', split_axis=1...]
    mul x1 -> x0, other arithmetic: 12.8 us -> none  [body(): jnp.sign(stepped) * jnp.maximum(jnp.abs(stepped) - shrink_level, 0.0)]
    add x1 -> x0, other arithmetic: 11.8 us -> none  [lateral_blur(): summed + kernel_taps[tap_index] * padded[:, tap_index:tap_index + row_cou...]
    all_to_all x1, blocking collectives: 18.4 us -> 28.7 us  [body(): lax.all_to_all(both_pencil, 'scan', split_axis=1, concat_axis=2, tiled=True)]
    dot_general x0 -> x2, matrix products: none -> 2.28 us  [lateral_apply(): return jnp.einsum('rk,pkc->prc', band, padded, precision=highest_mode)]
    all_to_all x3, local copies, waits for them, and re-layouts: 0.7 us -> 2.92 us  [the longest x2 2.31 us: body(): lax.all_to_all(raw.reshape(plane_count, flat_count), 'scan', split_axis=1...]
    sub x2 -> x1, other arithmetic: 2.02 us -> 0.01 us  [band_matrix(): lag = shift + in_rows - out_rows]
    ppermute x2, waiting for transfers between devices: 0.01 us -> 1.96 us  [with_halo(): lax.ppermute(tail, axis, [(i, (i + 1) % count) for i in range(ends)])]
  transfers between devices with their start and end apart: 7 -> 6, of which waited for: 5 -> 6; matrix products, arithmetic and copies ran while one was open for 4% -> 5% of each run, Pallas kernels for 0% -> 0%
where the time goes in v2:
time: 88.7 us; the launch traced here: 88.2 us
  blocking collectives  28.7 us (32%)
  waiting for transfers between devices  24.8 us (28%)
  starting transfers between devices  21 us (24%)
  local copies, waits for them, and re-layouts  6.19 us (7%)
  matrix products  3.61 us (4%)
  between operations  2.14 us (2%)
  other arithmetic  1.65 us (2%)
    all_to_all x1, blocking collectives, body(): lax.all_to_all(both_pencil, 'scan', split_axis=1, concat_axis=2, tiled=True)  28.7 us
    all_to_all x1, waiting for transfers between devices, body(): lax.all_to_all(blurred, 'scan', split_axis=1, concat_axis=0, tiled=True)  13 us
    ppermute x2, waiting for transfers between devices, with_halo(): lax.ppermute(head, axis, [((i + 1) % count, i) for i in range(ends)])  8.24 us
    all_to_all x1, starting transfers between devices, body(): lax.all_to_all(raw.reshape(plane_count, flat_count), 'scan', split_axis=1...  7.52 us
    ppermute x2, starting transfers between devices, with_halo(): lax.ppermute(tail, axis, [(i, (i + 1) % count) for i in range(ends)])  6.79 us
    all_to_all x1, starting transfers between devices, body(): lax.all_to_all(blurred, 'scan', split_axis=1, concat_axis=0, tiled=True)  4.11 us
    ppermute x2, starting transfers between devices, with_halo(): lax.ppermute(head, axis, [((i + 1) % count, i) for i in range(ends)])  2.58 us
    all_to_all x2, local copies, waits for them, and re-layouts, body(): lax.all_to_all(raw.reshape(plane_count, flat_count), 'scan', split_axis=1...  2.31 us
  transfers between devices with their start and end apart: 6, of which 6 were waited for; matrix products, arithmetic and copies ran while one was open for 5% of the time, Pallas kernels for 0%

profile of v2, /device:TPU:0, one launch (start us, length us, event | category | flops | bytes accessed | tf_op | source)
XLA Modules:
  0.0 88.2 jit_solution(2663440975191117303)
XLA Ops:
  0.6 1.2 %all_to_all.43 = f32[8,16,1024]{2,1,0:T(8,128)S(1)} reshape(f32[8,32,512]{2,1,0:T(8,128)} %param.8) | data formatting | bytes 1048576 | tf_op jit(solution)/shard_map/all_to_all | solution.py:58
  1.8 0.0 copy-start
  1.9 1.1 %copy.21 = f32[8,16,1024]{2,0,1:T(8,128)} copy(f32[8,16,1024]{2,1,0:T(8,128)S(1)} %all_to_all.43) | data formatting | bytes 1048576 | tf_op jit(solution)/shard_map/all_to_all | solution.py:58
  3.0 0.0 copy-start.2
  3.0 7.5 %all-to-all-start.1 = ((f32[8,16,1024]{2,0,1:T(8,128)}), f32[8,16,1024]{2,0,1:T(8,128)S(1)}, u32[]{:S(2)}, u32[]{:S(2)}) async-start(f32[8,16,1024]{2,0,1:T(8,128)} %copy.21), calls=%async_computation.1 | async-start | bytes 1048576 | tf_op jit(solution)/shard_map/all_to_all | solution.py:58
  10.5 0.0 copy-done
  10.5 3.4 %collective-permute-start = (f32[8,8,512]{2,1,0:T(8,128)S(1)}, f32[8,8,512]{2,1,0:T(8,128)S(1)}, u32[]{:S(2)}, u32[]{:S(2)}) collective-permute-start(f32[8,8,512]{2,1,0:T(8,128)S(1)} %get-tuple-element.8), channel_id=1, source_target_pairs={{0,1},{2,3},{4,5},{6,7},{8,9},{10,11},{12,13},{14,15},{16,17},{18,... | collective-permute-start | bytes 393224 | tf_op jit(solution)/shard_map/ppermute | solution.py:17
  13.9 1.3 %collective-permute-start.1 = (f32[8,8,512]{2,1,0:T(8,128)S(1)}, f32[8,8,512]{2,1,0:T(8,128)S(1)}, u32[]{:S(2)}, u32[]{:S(2)}) collective-permute-start(f32[8,8,512]{2,1,0:T(8,128)S(1)} %get-tuple-element.9), channel_id=1, source_target_pairs={{1,0},{3,2},{5,4},{7,6},{9,8},{11,10},{13,12},{15,14},{17,16},{19,... | collective-permute-start | bytes 393224 | tf_op jit(solution)/shard_map/ppermute | solution.py:19
  15.2 0.0 copy-done.2
  15.3 0.1 rev.3
  15.4 0.1 select_reduce_fusion.1
  15.5 1.8 %collective-permute-done = f32[8,8,512]{2,1,0:T(8,128)S(1)} collective-permute-done((f32[8,8,512]{2,1,0:T(8,128)S(1)}, f32[8,8,512]{2,1,0:T(8,128)S(1)}, u32[]{:S(2)}, u32[]{:S(2)}) %collective-permute-start) | collective-permute-done | bytes 131104 | tf_op jit(solution)/shard_map/ppermute | solution.py:17
  17.3 4.1 %collective-permute-done.1 = f32[8,8,512]{2,1,0:T(8,128)S(1)} collective-permute-done((f32[8,8,512]{2,1,0:T(8,128)S(1)}, f32[8,8,512]{2,1,0:T(8,128)S(1)}, u32[]{:S(2)}, u32[]{:S(2)}) %collective-permute-start.1) | collective-permute-done | bytes 131104 | tf_op jit(solution)/shard_map/ppermute | solution.py:19
  21.4 0.6 convolution_bitcast_fusion.1
  22.0 0.2 all_to_all.39
  22.2 0.0 copy-start.1
  22.2 0.0 copy-start.3
  22.2 1.1 %copy.20 = f32[8,16,1024]{2,0,1:T(8,128)} copy(f32[8,16,1024]{2,1,0:T(8,128)S(1)} %all_to_all.39) | data formatting | bytes 1048576 | tf_op jit(solution)/shard_map/all_to_all | solution.py:64
  23.3 1.6 %all-to-all-done.1 = f32[8,16,1024]{2,0,1:T(8,128)S(1)} async-done(((f32[8,16,1024]{2,0,1:T(8,128)}), f32[8,16,1024]{2,0,1:T(8,128)S(1)}, u32[]{:S(2)}, u32[]{:S(2)}) %all-to-all-start.1) | async-done | bytes 524320 | tf_op jit(solution)/shard_map/all_to_all | solution.py:58
  25.0 4.1 %all-to-all-start = ((f32[8,16,1024]{2,0,1:T(8,128)}), f32[8,16,1024]{2,0,1:T(8,128)S(1)}, u32[]{:S(2)}, u32[]{:S(2)}) async-start(f32[8,16,1024]{2,0,1:T(8,128)} %copy.20), calls=%async_computation | async-start | bytes 1048576 | tf_op jit(solution)/shard_map/all_to_all | solution.py:64
  29.1 0.0 copy-done.1
  29.1 0.1 subtract_subtract_fusion
  29.2 0.0 copy-done.3
  29.2 1.4 %select_reduce_fusion = f32[128,128]{1,0:T(8,128)S(1)} fusion(f32[64]{0:T(128)S(1)} %copy-done.3, s32[128,128]{1,0:T(8,128)S(1)} %subtract_subtract_fusion), kind=kLoop, calls=%fused_computation | loop fusion | flops 3129344 | bytes 131328 | tf_op jit(solution)/shard_map/reduce_sum | solution.py:47
  30.5 13.0 %all-to-all-done = f32[8,16,1024]{2,0,1:T(8,128)S(1)} async-done(((f32[8,16,1024]{2,0,1:T(8,128)}), f32[8,16,1024]{2,0,1:T(8,128)S(1)}, u32[]{:S(2)}, u32[]{:S(2)}) %all-to-all-start) | async-done | bytes 524320 | tf_op jit(solution)/shard_map/all_to_all | solution.py:64
  43.5 0.6 convolution_subtract_fusion
  44.2 0.7 convolution_bitcast_fusion
  44.9 0.1 pad_maximum_fusion
  45.0 0.8 copy.22
  45.8 28.7 %all_to_all.53 = f32[2,128,1024]{2,0,1:T(2,128)S(1)} all-to-all(f32[2,128,1024]{2,0,1:T(2,128)S(1)} %copy.22), channel_id=1, replica_groups=mesh['scan'=16,'row'=2] {'scan'}, dimensions={1} | all-to-all | bytes 2097152 | tf_op jit(solution)/shard_map/all_to_all | solution.py:69
  74.5 0.6 copy.25
  75.1 0.1 fusion.25
  75.2 0.1 reshape_squeeze.6
  75.3 3.4 %collective-permute-start.2 = (f32[8,8,512]{2,1,0:T(8,128)S(1)}, f32[8,8,512]{2,1,0:T(8,128)S(1)}, u32[]{:S(2)}, u32[]{:S(2)}) collective-permute-start(f32[8,8,512]{2,1,0:T(8,128)S(1)} %get-tuple-element.6), channel_id=1, source_target_pairs={{0,1},{2,3},{4,5},{6,7},{8,9},{10,11},{12,13},{14,15},{16,17},{18,... | collective-permute-start | bytes 393224 | tf_op jit(solution)/shard_map/ppermute | solution.py:17
  78.7 1.3 %collective-permute-start.3 = (f32[8,8,512]{2,1,0:T(8,128)S(1)}, f32[8,8,512]{2,1,0:T(8,128)S(1)}, u32[]{:S(2)}, u32[]{:S(2)}) collective-permute-start(f32[8,8,512]{2,1,0:T(8,128)S(1)} %get-tuple-element.7), channel_id=1, source_target_pairs={{1,0},{3,2},{5,4},{7,6},{9,8},{11,10},{13,12},{15,14},{17,16},{19,... | collective-permute-start | bytes 393224 | tf_op jit(solution)/shard_map/ppermute | solution.py:19
  81.3 0.9 reshape_squeeze.7
  82.2 0.2 collective-permute-done.2
  82.4 4.1 %collective-permute-done.3 = f32[8,8,512]{2,1,0:T(8,128)S(1)} collective-permute-done((f32[8,8,512]{2,1,0:T(8,128)S(1)}, f32[8,8,512]{2,1,0:T(8,128)S(1)}, u32[]{:S(2)}, u32[]{:S(2)}) %collective-permute-start.3) | collective-permute-done | bytes 131104 | tf_op jit(solution)/shard_map/ppermute | solution.py:19
  86.5 1.6 %maximum_multiply_fusion = f32[8,32,512]{2,1,0:T(8,128)} fusion(f32[8,32,512]{2,1,0:T(8,128)S(1)} %copy-done, f32[8,8,512]{2,1,0:T(8,128)S(1)} %collective-permute-done.3, f32[8,32,512]{2,1,0:T(8,128)S(1)} %reshape_squeeze.6, f32[8,8,512]{2,1,0:T(8,128)S(1)} %collective-permute-done.2, f32[]{:T(128)S(6)} %mul.18, f32[]{:T(128)} %bitcast.37, ...), kind=kOutput, calls=%fused_computation.21 | convolution fusion | flops 76808192 | bytes 1841160 | tf_op jit(solution)/shard_map/rk,pkc->prc/dot_general | solution.py:36
  (3 shorter events, 0.0 us)
Async XLA Ops:
  1.8 8.6 %copy-start = (f32[8,32,512]{2,1,0:T(8,128)S(1)}, f32[8,32,512]{2,1,0:T(8,128)}, u32[]{:S(2)}) copy-start(f32[8,32,512]{2,1,0:T(8,128)} %param.7) | copy-start | bytes 1572868
  3.0 12.3 %copy-start.2 = (f32[17]{0:T(128)S(1)}, f32[17]{0:T(128)}, u32[]{:S(2)}) copy-start(f32[17]{0:T(128)} %param.11) | copy-start | bytes 208
  3.0 22.0 %all-to-all-start.1 = ((f32[8,16,1024]{2,0,1:T(8,128)}), f32[8,16,1024]{2,0,1:T(8,128)S(1)}, u32[]{:S(2)}, u32[]{:S(2)}) async-start(f32[8,16,1024]{2,0,1:T(8,128)} %copy.21), calls=%async_computation.1 | async-start | bytes 1048576 | tf_op jit(solution)/shard_map/all_to_all | solution.py:58
  10.5 6.7 %collective-permute-start = (f32[8,8,512]{2,1,0:T(8,128)S(1)}, f32[8,8,512]{2,1,0:T(8,128)S(1)}, u32[]{:S(2)}, u32[]{:S(2)}) collective-permute-start(f32[8,8,512]{2,1,0:T(8,128)S(1)} %get-tuple-element.8), channel_id=1, source_target_pairs={{0,1},{2,3},{4,5},{6,7},{8,9},{10,11},{12,13},{14,15},{16,17},{18,... | collective-permute-start | bytes 393224 | tf_op jit(solution)/shard_map/ppermute | solution.py:17
  13.9 7.4 %collective-permute-start.1 = (f32[8,8,512]{2,1,0:T(8,128)S(1)}, f32[8,8,512]{2,1,0:T(8,128)S(1)}, u32[]{:S(2)}, u32[]{:S(2)}) collective-permute-start(f32[8,8,512]{2,1,0:T(8,128)S(1)} %get-tuple-element.9), channel_id=1, source_target_pairs={{1,0},{3,2},{5,4},{7,6},{9,8},{11,10},{13,12},{15,14},{17,16},{19,... | collective-permute-start | bytes 393224 | tf_op jit(solution)/shard_map/ppermute | solution.py:19
  22.2 6.9 %copy-start.1 = (s32[128]{0:T(128)S(1)}, s32[128]{0:T(128)}, u32[]{:S(2)}) copy-start(s32[128]{0:T(128)} %param.9) | copy-start | bytes 1540
  22.2 6.9 %copy-start.3 = (f32[64]{0:T(128)S(1)}, f32[64]{0:T(128)}, u32[]{:S(2)}) copy-start(f32[64]{0:T(128)} %param.10) | copy-start | bytes 772
  25.0 18.6 %all-to-all-start = ((f32[8,16,1024]{2,0,1:T(8,128)}), f32[8,16,1024]{2,0,1:T(8,128)S(1)}, u32[]{:S(2)}, u32[]{:S(2)}) async-start(f32[8,16,1024]{2,0,1:T(8,128)} %copy.20), calls=%async_computation | async-start | bytes 1048576 | tf_op jit(solution)/shard_map/all_to_all | solution.py:64
  75.3 7.1 %collective-permute-start.2 = (f32[8,8,512]{2,1,0:T(8,128)S(1)}, f32[8,8,512]{2,1,0:T(8,128)S(1)}, u32[]{:S(2)}, u32[]{:S(2)}) collective-permute-start(f32[8,8,512]{2,1,0:T(8,128)S(1)} %get-tuple-element.6), channel_id=1, source_target_pairs={{0,1},{2,3},{4,5},{6,7},{8,9},{10,11},{12,13},{14,15},{16,17},{18,... | collective-permute-start | bytes 393224 | tf_op jit(solution)/shard_map/ppermute | solution.py:17
  78.7 7.8 %collective-permute-start.3 = (f32[8,8,512]{2,1,0:T(8,128)S(1)}, f32[8,8,512]{2,1,0:T(8,128)S(1)}, u32[]{:S(2)}, u32[]{:S(2)}) collective-permute-start(f32[8,8,512]{2,1,0:T(8,128)S(1)} %get-tuple-element.7), channel_id=1, source_target_pairs={{1,0},{3,2},{5,4},{7,6},{9,8},{11,10},{13,12},{15,14},{17,16},{19,... | collective-permute-start | bytes 393224 | tf_op jit(solution)/shard_map/ppermute | solution.py:19

commit v3 on v2

v3 whole, which is shorter than its diff:
```python
import jax
import jax.numpy as jnp
from jax import lax
from jax.sharding import PartitionSpec as P

highest_mode = lax.Precision.HIGHEST
both_axes = ("scan", "row")


def band_matrix(kernel_taps, row_count):
    tap_count = kernel_taps.shape[0]
    half = tap_count // 2
    out_rows = jnp.arange(row_count, dtype=jnp.int32)[:, None]
    in_rows = jnp.arange(row_count, dtype=jnp.int32)[None, :]
    lag = in_rows - out_rows + half
    taps = jnp.arange(tap_count, dtype=jnp.int32)
    return jnp.sum(jnp.where(lag[:, :, None] == taps, kernel_taps, 0.0), axis=-1)


def sheet_matrix(own_offsets, depth_psf, column_count):
    plane_rows = jnp.arange(own_offsets.shape[0], dtype=jnp.int32)[:, None]
    plane_columns = jnp.arange(column_count, dtype=jnp.int32)[None, :]
    lag_planes = plane_columns - plane_rows - own_offsets[:, None]
    depth_count = depth_psf.shape[0]
    inside = (lag_planes >= 0) & (lag_planes < depth_count)
    taps = jnp.arange(depth_count, dtype=jnp.int32)
    picked = jnp.where(lag_planes[:, :, None] == taps, depth_psf, 0.0)
    return jnp.where(inside, jnp.sum(picked, axis=-1), 0.0)


def body(estimate, raw, offsets, depth_psf, lateral_psf, step_size, threshold):
    plane_count, row_count, width_count = estimate.shape
    scan_count = lax.axis_size("scan")
    row_split = lax.axis_size("row")
    pencil_count = scan_count * row_split
    strip = width_count // pencil_count
    all_planes = scan_count * plane_count
    all_rows = row_split * row_count

    def chunked(volume):
        parts = volume.reshape(plane_count, row_count, pencil_count, strip)
        return parts.transpose(2, 0, 1, 3).reshape(pencil_count, plane_count, row_count * strip)

    outgoing = jnp.stack([chunked(estimate), chunked(raw)], axis=1)
    incoming = lax.all_to_all(outgoing, both_axes, split_axis=0, concat_axis=0, tiled=True)
    incoming = incoming.reshape(scan_count, row_split, 2, plane_count, row_count, strip)
    pencils = incoming.transpose(2, 1, 4, 5, 0, 3).reshape(2, all_rows, strip * all_planes)
    est_pencil = pencils[0]
    raw_pencil = pencils[1].reshape(all_rows * strip, all_planes)

    band = band_matrix(lateral_psf, all_rows)
    sheet_psf = sheet_matrix(offsets, depth_psf, offsets.shape[0])
    blurred = jnp.dot(band, est_pencil, precision=highest_mode).reshape(all_rows * strip, all_planes)
    predicted = lax.dot_general(blurred, sheet_psf, (((1,), (1,)), ((), ())), precision=highest_mode)
    misfit_pencil = predicted - raw_pencil
    back = jnp.dot(misfit_pencil, sheet_psf, precision=highest_mode).reshape(all_rows, strip * all_planes)
    gradient = lax.dot_general(band, back, (((0,), (0,)), ((), ())), precision=highest_mode)
    stepped = est_pencil - step_size[0] * gradient
    shrink_level = step_size[0] * threshold[0]
    new_pencil = jnp.sign(stepped) * jnp.maximum(jnp.abs(stepped) - shrink_level, 0.0)

    results = jnp.stack([new_pencil.reshape(all_rows * strip, all_planes), misfit_pencil])
    results = results.reshape(2, row_split, row_count, strip, scan_count, plane_count)
    results = results.transpose(4, 1, 0, 5, 2, 3).reshape(pencil_count, 2, plane_count, row_count * strip)
    homes = lax.all_to_all(results, both_axes, split_axis=0, concat_axis=0, tiled=True)
    homes = homes.reshape(pencil_count, 2, plane_count, row_count, strip)
    homes = homes.transpose(1, 2, 3, 0, 4).reshape(2, plane_count, row_count, width_count)
    return (homes[0], homes[1])


def solution(mesh):
    placed = (P("scan", "row", None), P("scan", "row", None), P(), P(), P(), P(), P())
    return jax.shard_map(
        body,
        mesh=mesh,
        in_specs=placed,
        out_specs=(P("scan", "row", None), P("scan", "row", None)),
        check_vma=False,
    )
```

time: 88.7 us -> 158 us (1.78)
  local copies, waits for them, and re-layouts: 6.19 us -> 83 us
  starting transfers between devices: 21 us -> 7.48 us
  other arithmetic: 1.65 us -> 8.83 us
  waiting for transfers between devices: 24.8 us -> 23.1 us
    slice x3 -> x6, local copies, waits for them, and re-layouts: 0.11 us -> 27.9 us  [the longest x2 13.3 us: body(): est_pencil = pencils[0]]
    another operation x3 -> x7, local copies, waits for them, and re-layouts: 1.76 us -> 16.3 us  [the longest x3 10.1 us: body(): jnp.stack([new_pencil.reshape(all_rows * strip, all_planes), misfit_pencil])]
    transpose x0 -> x3, local copies, waits for them, and re-layouts: none -> 13.7 us  [the longest x1 8.49 us: body(): results.transpose(4, 1, 0, 5, 2, 3)]
    reshape x0 -> x4, local copies, waits for them, and re-layouts: none -> 12.6 us  [the longest x1 7.6 us: body(): results.transpose(4, 1, 0, 5, 2, 3)]
    ppermute x4 -> x0, waiting for transfers between devices: 10.2 us -> none  [the longest x2 8.24 us: with_halo(): lax.ppermute(head, axis, [((i + 1) % count, i) for i in range(ends)])]
    ppermute x4 -> x0, starting transfers between devices: 9.38 us -> none  [the longest x2 6.79 us: with_halo(): lax.ppermute(tail, axis, [(i, (i + 1) % count) for i in range(ends)])]
    all_to_all x2 -> x1, waiting for transfers between devices: 14.6 us -> 23.1 us  [body(): lax.all_to_all(outgoing, both_axes, split_axis=0, concat_axis=0, tiled=True)]
    unnamed x8 -> x12, local copies, waits for them, and re-layouts: 0.02 us -> 7.76 us
  transfers between devices with their start and end apart: 6 -> 1, of which waited for: 6 -> 1; matrix products, arithmetic and copies ran while one was open for 5% -> 1% of each run, Pallas kernels for 0% -> 0%
where the time goes in v3:
time: 158 us
  local copies, waits for them, and re-layouts  83 us (53%)
  blocking collectives  29.7 us (19%)
  waiting for transfers between devices  23.1 us (15%)
  other arithmetic  8.83 us (6%)
  starting transfers between devices  7.48 us (5%)
  matrix products  3.29 us (2%)
  between operations  2.18 us (1%)
    all_to_all x1, blocking collectives, body(): lax.all_to_all(results, both_axes, split_axis=0, concat_axis=0, tiled=True)  29.7 us
    all_to_all x1, waiting for transfers between devices, body(): lax.all_to_all(outgoing, both_axes, split_axis=0, concat_axis=0, tiled=True)  23.1 us
    slice x2, local copies, waits for them, and re-layouts, body(): est_pencil = pencils[0]  13.3 us
    another operation x3, local copies, waits for them, and re-layouts, body(): jnp.stack([new_pencil.reshape(all_rows * strip, all_planes), misfit_pencil])  10.1 us
    slice x3, local copies, waits for them, and re-layouts, body(): return (homes[0], homes[1])  9.81 us
    transpose x1, local copies, waits for them, and re-layouts, body(): results.transpose(4, 1, 0, 5, 2, 3)  8.49 us
    unnamed x12, local copies, waits for them, and re-layouts  7.76 us
    reshape x1, local copies, waits for them, and re-layouts, body(): results.transpose(4, 1, 0, 5, 2, 3)  7.6 us
  transfers between devices with their start and end apart: 1, of which 1 were waited for; matrix products, arithmetic and copies ran while one was open for 1% of the time, Pallas kernels for 0%

profile of v3, /device:TPU:0, one launch (start us, length us, event | category | flops | bytes accessed | tf_op | source)
XLA Modules:
  0.0 157.5 jit_solution(1850641335402549929)
XLA Ops:
  0.6 0.0 copy-start
  0.6 3.0 %copy.46 = f32[8,32,512]{1,2,0:T(8,128)} copy(f32[8,32,512]{2,1,0:T(8,128)} %param.7) | data formatting | bytes 1048576 | tf_op args[0]
  3.7 2.6 %copy.47 = f32[32,8,32,16]{0,3,2,1:T(8,128)S(1)} copy(f32[32,8,32,16]{2,3,0,1:T(8,128)} %bitcast.47) | data formatting | bytes 1048576 | tf_op jit(solution)/shard_map/transpose | solution.py:42
  6.3 0.7 copy.50
  7.0 0.0 copy-done
  7.0 1.9 %copy.48 = f32[8,32,512]{1,2,0:T(8,128)} copy(f32[8,32,512]{2,1,0:T(8,128)S(1)} %copy-done) | data formatting | bytes 1048576 | tf_op args[1]
  9.0 2.6 %copy.49 = f32[32,8,32,16]{0,3,2,1:T(8,128)S(1)} copy(f32[32,8,32,16]{2,3,0,1:T(8,128)} %bitcast.48) | data formatting | bytes 1048576 | tf_op jit(solution)/shard_map/transpose | solution.py:42
  11.6 0.0 copy-start.2
  11.6 0.0 copy-start.1
  11.6 0.0 copy-start.3
  11.6 0.7 copy.51
  12.3 1.1 pad_maximum_fusion
  13.4 7.5 %all-to-all-start = ((f32[32,2,8,512]{3,2,1,0:T(8,128)}), f32[32,2,8,512]{3,2,1,0:T(8,128)S(1)}, u32[]{:S(2)}, u32[]{:S(2)}) async-start(f32[32,2,8,512]{3,2,1,0:T(8,128)} %pad_maximum_fusion), calls=%async_computation | async-start | bytes 2097152 | tf_op jit(solution)/shard_map/all_to_all | solution.py:45
  22.2 0.0 copy-done.2
  22.2 0.1 select_reduce_fusion.1
  22.3 0.0 copy-done.1
  22.3 0.1 subtract_subtract_fusion
  22.4 1.4 select_reduce_fusion
  23.8 23.1 %all-to-all-done = f32[32,2,8,512]{3,2,1,0:T(8,128)S(1)} async-done(((f32[32,2,8,512]{3,2,1,0:T(8,128)}), f32[32,2,8,512]{3,2,1,0:T(8,128)S(1)}, u32[]{:S(2)}, u32[]{:S(2)}) %all-to-all-start) | async-done | bytes 1048608 | tf_op jit(solution)/shard_map/all_to_all | solution.py:45
  46.9 4.8 %reshape.82 = f32[16,2,2,8,32,16]{5,4,3,2,1,0:T(8,128)} reshape(f32[32,2,8,512]{3,2,1,0:T(8,128)S(1)} %all-to-all-done) | data formatting | bytes 2097152 | tf_op jit(solution)/shard_map/reshape | solution.py:46
  51.8 8.5 %fusion.8 = (f32[1,2,32,16,16,8]{3,2,5,0,1,4:T(8,128)}, f32[1,2,32,16,16,8]{3,2,5,0,1,4:T(8,128)}) fusion(f32[2,2,32,16,16,8]{3,2,5,0,1,4:T(8,128)} %bitcast.41), kind=kLoop, calls=%fused_computation.20 | loop fusion | bytes 2097152 | tf_op jit(solution)/shard_map/slice | solution.py:48
  60.3 4.8 %copy.52 = f32[1,2,32,16,16,8]{2,1,5,4,3,0:T(2,128)S(1)} copy(f32[1,2,32,16,16,8]{3,2,5,0,1,4:T(8,128)} %get-tuple-element.8) | data formatting | bytes 1048576 | tf_op jit(solution)/shard_map/slice | solution.py:48
  65.1 1.1 squeeze.16
  66.3 0.3 copy.55
  66.6 1.2 fusion.10
  67.8 0.1 reshape.83
  67.9 4.8 %copy.53 = f32[1,2,32,16,16,8]{3,2,1,5,4,0:T(8,128)} copy(f32[1,2,32,16,16,8]{3,2,5,0,1,4:T(8,128)} %get-tuple-element.9) | data formatting | bytes 1048576 | tf_op jit(solution)/shard_map/slice | solution.py:49
  72.7 4.7 %reshape_squeeze.3 = f32[1024,128]{0,1:T(8,128)S(1)} reshape(f32[1,2,32,16,16,8]{3,2,1,5,4,0:T(8,128)} %copy.53) | data formatting | bytes 1048576 | tf_op jit(solution)/shard_map/reshape;squeeze | solution.py:49
  77.4 0.2 copy.54
  77.5 0.7 convolution_subtract_fusion
  78.2 0.6 fusion.1
  78.9 0.2 copy.57
  79.1 0.1 reshape.84
  79.2 0.8 maximum_multiply_fusion
  80.0 0.3 copy.56
  80.3 2.5 %stack.12 = f32[1,2,32,16,16,8]{2,1,5,4,3,0:T(2,128)} reshape(f32[64,2048]{0,1:T(8,128)S(1)} %copy.56) | data formatting | bytes 1048576 | tf_op jit(solution)/shard_map/stack | solution.py:62
  82.8 2.7 %stack.13 = f32[1,2,32,16,16,8]{3,2,1,5,4,0:T(8,128)} reshape(f32[1024,128]{0,1:T(8,128)S(1)} %copy.57) | data formatting | bytes 1048576 | tf_op jit(solution)/shard_map/stack | solution.py:62
  85.5 4.8 %copy.58 = f32[1,2,32,16,16,8]{2,1,5,4,3,0:T(2,128)S(1)} copy(f32[1,2,32,16,16,8]{3,2,1,5,4,0:T(8,128)} %stack.13) | data formatting | bytes 1048576 | tf_op jit(solution)/shard_map/stack | solution.py:62
  90.4 6.2 %maximum_bitcast_fusion = f32[16,2,2,8,32,16]{4,1,3,0,5,2:T(2,128)} fusion(f32[1,2,32,16,16,8]{2,1,5,4,3,0:T(2,128)S(1)} %copy.58, f32[1,2,32,16,16,8]{2,1,5,4,3,0:T(2,128)} %stack.12), kind=kLoop, calls=%fused_computation | loop fusion | flops 262144 | bytes 2097152 | tf_op jit(solution)/shard_map/transpose | solution.py:64
  96.6 8.5 %copy.59 = f32[16,2,2,8,32,16]{5,4,3,2,1,0:T(8,128)} copy(f32[16,2,2,8,32,16]{4,1,3,0,5,2:T(2,128)} %maximum_bitcast_fusion) | data formatting | bytes 2097152 | tf_op jit(solution)/shard_map/transpose | solution.py:64
  105.1 7.6 %reshape.85 = f32[32,2,8,512]{3,2,1,0:T(8,128)S(1)} reshape(f32[16,2,2,8,32,16]{5,4,3,2,1,0:T(8,128)} %copy.59) | data formatting | bytes 2097152 | tf_op jit(solution)/shard_map/reshape | solution.py:64
  112.7 29.7 %all_to_all.10 = f32[32,2,8,512]{3,2,1,0:T(8,128)S(1)} all-to-all(f32[32,2,8,512]{3,2,1,0:T(8,128)S(1)} %reshape.85), channel_id=1, replica_groups=mesh['scan'=16,'row'=2] {'scan','row'}, dimensions={0} | all-to-all | bytes 2097152 | tf_op jit(solution)/shard_map/all_to_all | solution.py:65
  142.3 2.6 %copy.60 = f32[32,2,8,512]{0,3,2,1:T(8,128)} copy(f32[32,2,8,512]{3,2,1,0:T(8,128)S(1)} %all_to_all.10) | data formatting | bytes 2097152 | tf_op jit(solution)/shard_map/all_to_all | solution.py:65
  145.0 4.6 %fusion.9 = (f32[1,8,32,32,16]{3,4,2,1,0:T(8,128)}, f32[1,8,32,32,16]{3,4,2,1,0:T(8,128)}) fusion(f32[2,8,32,32,16]{3,4,2,1,0:T(8,128)} %bitcast.42), kind=kLoop, calls=%fused_computation.21 | loop fusion | bytes 2097152 | tf_op jit(solution)/shard_map/slice | solution.py:68
  149.5 2.6 %copy.61 = f32[1,8,32,32,16]{2,4,3,1,0:T(8,128)S(1)} copy(f32[1,8,32,32,16]{3,4,2,1,0:T(8,128)} %get-tuple-element.11) | data formatting | bytes 1048576 | tf_op jit(solution)/shard_map/slice | solution.py:68
  152.2 1.4 copy.63
  153.5 2.6 %copy.62 = f32[1,8,32,32,16]{2,4,3,1,0:T(8,128)S(1)} copy(f32[1,8,32,32,16]{3,4,2,1,0:T(8,128)} %get-tuple-element.10) | data formatting | bytes 1048576 | tf_op jit(solution)/shard_map/slice | solution.py:68
  156.2 1.4 copy.64
  (2 shorter events, 0.0 us)
Async XLA Ops:
  0.6 6.4 %copy-start = (f32[8,32,512]{2,1,0:T(8,128)S(1)}, f32[8,32,512]{2,1,0:T(8,128)}, u32[]{:S(2)}) copy-start(f32[8,32,512]{2,1,0:T(8,128)} %param.8) | copy-start | bytes 1572868
  11.6 10.6 %copy-start.2 = (f32[17]{0:T(128)S(1)}, f32[17]{0:T(128)}, u32[]{:S(2)}) copy-start(f32[17]{0:T(128)} %param.11) | copy-start | bytes 208
  11.6 10.7 %copy-start.1 = (s32[128]{0:T(128)S(1)}, s32[128]{0:T(128)}, u32[]{:S(2)}) copy-start(s32[128]{0:T(128)} %param.9) | copy-start | bytes 1540
  11.6 10.8 %copy-start.3 = (f32[64]{0:T(128)S(1)}, f32[64]{0:T(128)}, u32[]{:S(2)}) copy-start(f32[64]{0:T(128)} %param.10) | copy-start | bytes 772
  13.4 33.5 %all-to-all-start = ((f32[32,2,8,512]{3,2,1,0:T(8,128)}), f32[32,2,8,512]{3,2,1,0:T(8,128)S(1)}, u32[]{:S(2)}, u32[]{:S(2)}) async-start(f32[32,2,8,512]{3,2,1,0:T(8,128)} %pad_maximum_fusion), calls=%async_computation | async-start | bytes 2097152 | tf_op jit(solution)/shard_map/all_to_all | solution.py:45

commit v4 on v2

--- a/solution.py
+++ b/solution.py
@@ -6,21 +6,21 @@
 highest_mode = lax.Precision.HIGHEST
 
 
-def with_halo(cells, sides, width):
-    for axis, dim in sides:
-        count = lax.axis_size(axis)
+def with_halo(cells, axis, width):
+    count = lax.axis_size(axis)
+    head = lax.slice_in_dim(cells, 0, width, axis=1)
+    tail = lax.slice_in_dim(cells, cells.shape[1] - width, cells.shape[1], axis=1)
+    zeros = jnp.zeros_like(head)
+    if count == 2:
+        first = lax.axis_index(axis) == 0
+        arrived = lax.ppermute(jnp.where(first, tail, head), axis, [(0, 1), (1, 0)])
+        above = jnp.where(first, zeros, arrived)
+        below = jnp.where(first, arrived, zeros)
+    else:
         ends = count - 1
-        head = lax.slice_in_dim(cells, 0, width, axis=dim)
-        tail = lax.slice_in_dim(cells, cells.shape[dim] - width, cells.shape[dim], axis=dim)
-        cells = jnp.concatenate(
-            [
-                lax.ppermute(tail, axis, [(i, (i + 1) % count) for i in range(ends)]),
-                cells,
-                lax.ppermute(head, axis, [((i + 1) % count, i) for i in range(ends)]),
-            ],
-            axis=dim,
-        )
-    return cells
+        above = lax.ppermute(tail, axis, [(i, (i + 1) % count) for i in range(ends)])
+        below = lax.ppermute(head, axis, [((i + 1) % count, i) for i in range(ends)])
+    return jnp.concatenate([above, cells, below], axis=1)
 
 
 def band_matrix(kernel_taps, row_count, shift):
@@ -59,17 +59,16 @@
     sheet_psf = sheet_matrix(offsets, depth_psf, offsets.shape[0])
     blur_band = band_matrix(lateral_psf, row_count, 0)
     back_band = band_matrix(lateral_psf[::-1], row_count, 0)
-    padded = with_halo(estimate, (("row", 1),), halo_rows)
+    padded = with_halo(estimate, "row", halo_rows)
     blurred = lateral_apply(blur_band, padded).reshape(plane_count, flat_count)
     pencil = lax.all_to_all(blurred, "scan", split_axis=1, concat_axis=0, tiled=True)
     predicted_pencil = jnp.dot(sheet_psf, pencil, precision=highest_mode)
     misfit_pencil = predicted_pencil - raw_pencil
     back_pencil = transpose_apply(sheet_psf, misfit_pencil)
-    both_pencil = jnp.stack([misfit_pencil, back_pencil])
-    both = lax.all_to_all(both_pencil, "scan", split_axis=1, concat_axis=2, tiled=True)
-    misfit = both[0]
-    back_volume = both[1].reshape(plane_count, row_count, width_count)
-    padded_back = with_halo(back_volume, (("row", 1),), halo_rows)
+    back_flat = lax.all_to_all(back_pencil, "scan", split_axis=0, concat_axis=1, tiled=True)
+    misfit = lax.all_to_all(misfit_pencil, "scan", split_axis=0, concat_axis=1, tiled=True)
+    back_volume = back_flat.reshape(plane_count, row_count, width_count)
+    padded_back = with_halo(back_volume, "row", halo_rows)
     gradient = lateral_apply(back_band, padded_back)
     stepped = estimate - step_size[0] * gradient
     shrink_level = step_size[0] * threshold[0]

time: 88.7 us -> 87.1 us (0.982)
  blocking collectives: 28.7 us -> 18.4 us
  waiting for transfers between devices: 24.8 us -> 34.8 us
  starting transfers between devices: 21 us -> 18.8 us
  matrix products: 3.61 us -> 5.46 us
  local copies, waits for them, and re-layouts: 6.19 us -> 5.26 us
    all_to_all x0 -> x1, waiting for transfers between devices: none -> 11.2 us  [body(): lax.all_to_all(misfit_pencil, 'scan', split_axis=0, concat_axis=1, tiled=...]
    all_to_all x1, blocking collectives: 28.7 us -> 18.4 us  [body(): lax.all_to_all(back_pencil, 'scan', split_axis=0, concat_axis=1, tiled=True)]
    ppermute x4 -> x2, starting transfers between devices: 9.38 us -> 3.11 us  [with_halo(): arrived = lax.ppermute(jnp.where(first, tail, head), axis, [(0, 1), (1, 0)])]
    ppermute x4 -> x2, waiting for transfers between devices: 10.2 us -> 4.1 us  [with_halo(): arrived = lax.ppermute(jnp.where(first, tail, head), axis, [(0, 1), (1, 0)])]
    all_to_all x1, waiting for transfers between devices: 1.62 us -> 6.56 us  [body(): lax.all_to_all(raw.reshape(plane_count, flat_count), 'scan', split_axis=1...]
    all_to_all x0 -> x1, starting transfers between devices: none -> 4.1 us  [body(): lax.all_to_all(misfit_pencil, 'scan', split_axis=0, concat_axis=1, tiled=...]
    another operation x3 -> x0, local copies, waits for them, and re-layouts: 1.76 us -> none  [the longest x1 0.87 us: body(): return (new_estimate, misfit.reshape(plane_count, row_count, width_count))]
    dot_general x1, matrix products: 0.7 us -> 1.74 us  [transpose_apply(): lax.dot_general(sheet_psf, values, (((0,), (0,)), ((), ())), precision=hi...]
  transfers between devices with their start and end apart: 6 -> 5, of which waited for: 6 -> 4; matrix products, arithmetic and copies ran while one was open for 5% -> 6% of each run, Pallas kernels for 0% -> 0%
where the time goes in v4:
time: 87.1 us; the launch traced here: 86.5 us
  waiting for transfers between devices  34.8 us (40%)
  starting transfers between devices  18.8 us (22%)
  blocking collectives  18.4 us (21%)
  matrix products  5.46 us (6%)
  local copies, waits for them, and re-layouts  5.26 us (6%)
  between operations  2.08 us (2%)
  other arithmetic  1.66 us (2%)
    all_to_all x1, blocking collectives, body(): lax.all_to_all(back_pencil, 'scan', split_axis=0, concat_axis=1, tiled=True)  18.4 us
    all_to_all x1, waiting for transfers between devices, body(): lax.all_to_all(blurred, 'scan', split_axis=1, concat_axis=0, tiled=True)  13 us
    all_to_all x1, waiting for transfers between devices, body(): lax.all_to_all(misfit_pencil, 'scan', split_axis=0, concat_axis=1, tiled=...  11.2 us
    all_to_all x1, starting transfers between devices, body(): lax.all_to_all(raw.reshape(plane_count, flat_count), 'scan', split_axis=1...  7.52 us
    all_to_all x1, waiting for transfers between devices, body(): lax.all_to_all(raw.reshape(plane_count, flat_count), 'scan', split_axis=1...  6.56 us
    ppermute x2, waiting for transfers between devices, with_halo(): arrived = lax.ppermute(jnp.where(first, tail, head), axis, [(0, 1), (1, 0)])  4.1 us
    all_to_all x1, starting transfers between devices, body(): lax.all_to_all(blurred, 'scan', split_axis=1, concat_axis=0, tiled=True)  4.1 us
    all_to_all x1, starting transfers between devices, body(): lax.all_to_all(misfit_pencil, 'scan', split_axis=0, concat_axis=1, tiled=...  4.1 us
  transfers between devices with their start and end apart: 5, of which 4 were waited for; matrix products, arithmetic and copies ran while one was open for 6% of the time, Pallas kernels for 0%

profile of v4, /device:TPU:0, one launch (start us, length us, event | category | flops | bytes accessed | tf_op | source)
XLA Modules:
  0.0 86.5 jit_solution(11151738883400588553)
XLA Ops:
  0.6 1.2 %all_to_all.56 = f32[8,16,1024]{2,1,0:T(8,128)S(1)} reshape(f32[8,32,512]{2,1,0:T(8,128)} %param.8) | data formatting | bytes 1048576 | tf_op jit(solution)/shard_map/all_to_all | solution.py:58
  1.8 1.1 %copy.21 = f32[8,16,1024]{2,0,1:T(8,128)} copy(f32[8,16,1024]{2,1,0:T(8,128)S(1)} %all_to_all.56) | data formatting | bytes 1048576 | tf_op jit(solution)/shard_map/all_to_all | solution.py:58
  2.9 0.0 copy-start
  2.9 0.0 copy-start.2
  2.9 7.5 %all-to-all-start.1 = ((f32[8,16,1024]{2,0,1:T(8,128)}), f32[8,16,1024]{2,0,1:T(8,128)S(1)}, u32[]{:S(2)}, u32[]{:S(2)}) async-start(f32[8,16,1024]{2,0,1:T(8,128)} %copy.21), calls=%async_computation.1 | async-start | bytes 1048576 | tf_op jit(solution)/shard_map/all_to_all | solution.py:58
  10.5 0.0 copy-done
  10.5 1.6 %collective-permute-start = (f32[8,8,512]{2,1,0:T(8,128)S(1)}, f32[8,8,512]{2,1,0:T(8,128)S(1)}, u32[]{:S(2)}, u32[]{:S(2)}) collective-permute-start(f32[8,8,512]{2,1,0:T(8,128)S(1)} %slice_select_fusion.1), channel_id=1, source_target_pairs={{0,1},{1,0},{2,3},{3,2},{4,5},{5,4},{6,7},{7,6},{8,9},{9,8},{10,11... | collective-permute-start | bytes 393224 | tf_op jit(solution)/shard_map/ppermute | solution.py:16
  12.1 0.0 copy-done.2
  12.1 0.1 rev.3
  12.2 0.1 select_reduce_fusion.1
  12.3 4.1 %collective-permute-done = f32[8,8,512]{2,1,0:T(8,128)S(1)} collective-permute-done((f32[8,8,512]{2,1,0:T(8,128)S(1)}, f32[8,8,512]{2,1,0:T(8,128)S(1)}, u32[]{:S(2)}, u32[]{:S(2)}) %collective-permute-start) | collective-permute-done | bytes 131104 | tf_op jit(solution)/shard_map/ppermute | solution.py:16
  16.4 0.6 convolution_bitcast_fusion.1
  17.1 0.2 all_to_all.52
  17.3 1.1 %copy.20 = f32[8,16,1024]{2,0,1:T(8,128)} copy(f32[8,16,1024]{2,1,0:T(8,128)S(1)} %all_to_all.52) | data formatting | bytes 1048576 | tf_op jit(solution)/shard_map/all_to_all | solution.py:64
  18.4 0.0 copy-start.1
  18.4 0.0 copy-start.3
  18.4 6.6 %all-to-all-done.1 = f32[8,16,1024]{2,0,1:T(8,128)S(1)} async-done(((f32[8,16,1024]{2,0,1:T(8,128)}), f32[8,16,1024]{2,0,1:T(8,128)S(1)}, u32[]{:S(2)}, u32[]{:S(2)}) %all-to-all-start.1) | async-done | bytes 524320 | tf_op jit(solution)/shard_map/all_to_all | solution.py:58
  24.9 4.1 %all-to-all-start = ((f32[8,16,1024]{2,0,1:T(8,128)}), f32[8,16,1024]{2,0,1:T(8,128)S(1)}, u32[]{:S(2)}, u32[]{:S(2)}) async-start(f32[8,16,1024]{2,0,1:T(8,128)} %copy.20), calls=%async_computation | async-start | bytes 1048576 | tf_op jit(solution)/shard_map/all_to_all | solution.py:64
  29.0 0.0 copy-done.1
  29.1 0.1 subtract_subtract_fusion
  29.1 0.0 copy-done.3
  29.2 1.4 %select_reduce_fusion = f32[128,128]{1,0:T(8,128)S(1)} fusion(f32[64]{0:T(128)S(1)} %copy-done.3, s32[128,128]{1,0:T(8,128)S(1)} %subtract_subtract_fusion), kind=kLoop, calls=%fused_computation | loop fusion | flops 3129344 | bytes 131328 | tf_op jit(solution)/shard_map/reduce_sum | solution.py:47
  30.5 13.0 %all-to-all-done = f32[8,16,1024]{2,0,1:T(8,128)S(1)} async-done(((f32[8,16,1024]{2,0,1:T(8,128)}), f32[8,16,1024]{2,0,1:T(8,128)S(1)}, u32[]{:S(2)}, u32[]{:S(2)}) %all-to-all-start) | async-done | bytes 524320 | tf_op jit(solution)/shard_map/all_to_all | solution.py:64
  43.5 1.4 %convolution_subtract_fusion = f32[128,1024]{1,0:T(8,128)} fusion(f32[8,16,1024]{2,0,1:T(8,128)S(1)} %all-to-all-done.1, f32[8,16,1024]{2,0,1:T(8,128)S(1)} %all-to-all-done, f32[128,128]{1,0:T(8,128)S(1)} %select_reduce_fusion, s32[128]{0:T(128)S(1)} %copy-done.1), kind=kOutput, calls=%fused_computation.4 | convolution fusion | flops 201555968 | bytes 1638912 | tf_op jit(solution)/shard_map/dot_general | solution.py:65
  44.9 1.7 %convolution_bitcast_fusion = f32[16,8,1024]{2,1,0:T(8,128)S(1)} fusion(f32[128,1024]{1,0:T(8,128)} %convolution_subtract_fusion, f32[128,128]{1,0:T(8,128)S(1)} %select_reduce_fusion, s32[128]{0:T(128)S(1)} %copy-done.1), kind=kOutput, calls=%fused_computation.2 | convolution fusion | flops 201424896 | bytes 1114624 | tf_op jit(solution)/shard_map/dot_general | solution.py:51
  46.7 18.4 %all_to_all.70 = f32[16,8,1024]{2,1,0:T(8,128)S(1)} all-to-all(f32[16,8,1024]{2,1,0:T(8,128)S(1)} %convolution_bitcast_fusion), channel_id=1, replica_groups=mesh['scan'=16,'row'=2] {'scan'}, dimensions={0} | all-to-all | bytes 1048576 | tf_op jit(solution)/shard_map/all_to_all | solution.py:68
  65.0 4.1 %all-to-all-start.3 = ((f32[16,8,1024]{2,1,0:T(8,128)}), f32[16,8,1024]{2,1,0:T(8,128)S(1)}, u32[]{:S(2)}, u32[]{:S(2)}) async-start(f32[16,8,1024]{2,1,0:T(8,128)} %bitcast.12), calls=%async_computation.3 | async-start | bytes 1048576 | tf_op jit(solution)/shard_map/all_to_all | solution.py:69
  69.2 0.3 copy.22
  69.5 0.1 reshape.67
  69.6 1.6 %collective-permute-start.1 = (f32[8,8,512]{2,1,0:T(8,128)S(1)}, f32[8,8,512]{2,1,0:T(8,128)S(1)}, u32[]{:S(2)}, u32[]{:S(2)}) collective-permute-start(f32[8,8,512]{2,1,0:T(8,128)S(1)} %slice_select_fusion), channel_id=1, source_target_pairs={{0,1},{1,0},{2,3},{3,2},{4,5},{5,4},{6,7},{7,6},{8,9},{9,8},{10,11... | collective-permute-start | bytes 393224 | tf_op jit(solution)/shard_map/ppermute | solution.py:16
  72.4 11.2 %all-to-all-done.3 = f32[16,8,1024]{2,1,0:T(8,128)S(1)} async-done(((f32[16,8,1024]{2,1,0:T(8,128)}), f32[16,8,1024]{2,1,0:T(8,128)S(1)}, u32[]{:S(2)}, u32[]{:S(2)}) %all-to-all-start.3) | async-done | bytes 524320 | tf_op jit(solution)/shard_map/all_to_all | solution.py:69
  83.6 0.3 copy.23
  83.9 0.9 %reshape.68 = f32[8,32,512]{2,1,0:T(8,128)} reshape(f32[8,16,1024]{2,1,0:T(8,128)S(1)} %copy.23) | data formatting | bytes 1048576 | tf_op jit(solution)/shard_map/reshape | solution.py:76
  84.8 0.0 collective-permute-done.1
  84.8 1.6 %maximum_multiply_fusion = f32[8,32,512]{2,1,0:T(8,128)} fusion(f32[8,32,512]{2,1,0:T(8,128)S(1)} %copy-done, f32[8,8,512]{2,1,0:T(8,128)S(1)} %get-tuple-element.5, f32[8,32,512]{2,1,0:T(8,128)S(1)} %reshape.67, f32[8,8,512]{2,1,0:T(8,128)S(1)} %get-tuple-element.4, f32[]{:T(128)S(6)} %mul.18, f32[]{:T(128)} %bitcast.31, f32[32,48]{1,0:T(8,128)S(1)} %get-tuple-element.2), kind=kOutput, calls=%fused_computation.19 | convolution fusion | flops 76808192 | bytes 1841160 | tf_op jit(solution)/shard_map/rk,pkc->prc/dot_general | solution.py:36
  (5 shorter events, 0.1 us)
Async XLA Ops:
  2.9 7.5 %copy-start = (f32[8,32,512]{2,1,0:T(8,128)S(1)}, f32[8,32,512]{2,1,0:T(8,128)}, u32[]{:S(2)}) copy-start(f32[8,32,512]{2,1,0:T(8,128)} %param.7) | copy-start | bytes 1572868
  2.9 9.1 %copy-start.2 = (f32[17]{0:T(128)S(1)}, f32[17]{0:T(128)}, u32[]{:S(2)}) copy-start(f32[17]{0:T(128)} %param.11) | copy-start | bytes 208
  2.9 22.0 %all-to-all-start.1 = ((f32[8,16,1024]{2,0,1:T(8,128)}), f32[8,16,1024]{2,0,1:T(8,128)S(1)}, u32[]{:S(2)}, u32[]{:S(2)}) async-start(f32[8,16,1024]{2,0,1:T(8,128)} %copy.21), calls=%async_computation.1 | async-start | bytes 1048576 | tf_op jit(solution)/shard_map/all_to_all | solution.py:58
  10.5 5.9 %collective-permute-start = (f32[8,8,512]{2,1,0:T(8,128)S(1)}, f32[8,8,512]{2,1,0:T(8,128)S(1)}, u32[]{:S(2)}, u32[]{:S(2)}) collective-permute-start(f32[8,8,512]{2,1,0:T(8,128)S(1)} %slice_select_fusion.1), channel_id=1, source_target_pairs={{0,1},{1,0},{2,3},{3,2},{4,5},{5,4},{6,7},{7,6},{8,9},{9,8},{10,11... | collective-permute-start | bytes 393224 | tf_op jit(solution)/shard_map/ppermute | solution.py:16
  18.4 10.7 %copy-start.1 = (s32[128]{0:T(128)S(1)}, s32[128]{0:T(128)}, u32[]{:S(2)}) copy-start(s32[128]{0:T(128)} %param.9) | copy-start | bytes 1540
  18.4 10.8 %copy-start.3 = (f32[64]{0:T(128)S(1)}, f32[64]{0:T(128)}, u32[]{:S(2)}) copy-start(f32[64]{0:T(128)} %param.10) | copy-start | bytes 772
  24.9 18.6 %all-to-all-start = ((f32[8,16,1024]{2,0,1:T(8,128)}), f32[8,16,1024]{2,0,1:T(8,128)S(1)}, u32[]{:S(2)}, u32[]{:S(2)}) async-start(f32[8,16,1024]{2,0,1:T(8,128)} %copy.20), calls=%async_computation | async-start | bytes 1048576 | tf_op jit(solution)/shard_map/all_to_all | solution.py:64
  65.0 18.6 %all-to-all-start.3 = ((f32[16,8,1024]{2,1,0:T(8,128)}), f32[16,8,1024]{2,1,0:T(8,128)S(1)}, u32[]{:S(2)}, u32[]{:S(2)}) async-start(f32[16,8,1024]{2,1,0:T(8,128)} %bitcast.12), calls=%async_computation.3 | async-start | bytes 1048576 | tf_op jit(solution)/shard_map/all_to_all | solution.py:69
  69.6 15.2 %collective-permute-start.1 = (f32[8,8,512]{2,1,0:T(8,128)S(1)}, f32[8,8,512]{2,1,0:T(8,128)S(1)}, u32[]{:S(2)}, u32[]{:S(2)}) collective-permute-start(f32[8,8,512]{2,1,0:T(8,128)S(1)} %slice_select_fusion), channel_id=1, source_target_pairs={{0,1},{1,0},{2,3},{3,2},{4,5},{5,4},{6,7},{7,6},{8,9},{9,8},{10,11... | collective-permute-start | bytes 393224 | tf_op jit(solution)/shard_map/ppermute | solution.py:16

commit v5 on v4

--- a/solution.py
+++ b/solution.py
@@ -55,19 +55,21 @@
     plane_count, row_count, width_count = estimate.shape
     flat_count = row_count * width_count
     halo_rows = lateral_psf.shape[0] // 2
-    raw_pencil = lax.all_to_all(raw.reshape(plane_count, flat_count), "scan", split_axis=1, concat_axis=0, tiled=True)
     sheet_psf = sheet_matrix(offsets, depth_psf, offsets.shape[0])
     blur_band = band_matrix(lateral_psf, row_count, 0)
     back_band = band_matrix(lateral_psf[::-1], row_count, 0)
     padded = with_halo(estimate, "row", halo_rows)
     blurred = lateral_apply(blur_band, padded).reshape(plane_count, flat_count)
-    pencil = lax.all_to_all(blurred, "scan", split_axis=1, concat_axis=0, tiled=True)
+    both_flat = jnp.stack([blurred, raw.reshape(plane_count, flat_count)])
+    both_in = lax.all_to_all(both_flat, "scan", split_axis=2, concat_axis=1, tiled=True)
+    pencil = both_in[0]
+    raw_pencil = both_in[1]
     predicted_pencil = jnp.dot(sheet_psf, pencil, precision=highest_mode)
     misfit_pencil = predicted_pencil - raw_pencil
     back_pencil = transpose_apply(sheet_psf, misfit_pencil)
-    back_flat = lax.all_to_all(back_pencil, "scan", split_axis=0, concat_axis=1, tiled=True)
-    misfit = lax.all_to_all(misfit_pencil, "scan", split_axis=0, concat_axis=1, tiled=True)
-    back_volume = back_flat.reshape(plane_count, row_count, width_count)
+    both_out = lax.all_to_all(jnp.stack([misfit_pencil, back_pencil]), "scan", split_axis=1, concat_axis=2, tiled=True)
+    misfit = both_out[0]
+    back_volume = both_out[1].reshape(plane_count, row_count, width_count)
     padded_back = with_halo(back_volume, "row", halo_rows)
     gradient = lateral_apply(back_band, padded_back)
     stepped = estimate - step_size[0] * gradient

time: 87.1 us -> 182 us (2.09)
  local copies, waits for them, and re-layouts: 5.26 us -> 101 us
  blocking collectives: 18.4 us -> 31.6 us
  waiting for transfers between devices: 34.8 us -> 24.8 us
  starting transfers between devices: 18.8 us -> 10.8 us
  other arithmetic: 1.66 us -> 6.57 us
    unnamed x8, local copies, waits for them, and re-layouts: 0.01 us -> 60.9 us
    another operation x0 -> x6, local copies, waits for them, and re-layouts: none -> 17.6 us  [the longest x3 15.8 us: body(): both_flat = jnp.stack([blurred, raw.reshape(plane_count, flat_count)])]
    all_to_all x6 -> x3, local copies, waits for them, and re-layouts: 4.2 us -> 21.4 us  [the longest x2 20.8 us: body(): lax.all_to_all(both_flat, 'scan', split_axis=2, concat_axis=1, tiled=True)]
    all_to_all x1, blocking collectives: 18.4 us -> 31.6 us  [body(): lax.all_to_all(jnp.stack([misfit_pencil, back_pencil]), 'scan', split_axi...]
    all_to_all x3 -> x1, starting transfers between devices: 15.7 us -> 6.2 us  [body(): lax.all_to_all(both_flat, 'scan', split_axis=2, concat_axis=1, tiled=True)]
    all_to_all x3 -> x1, waiting for transfers between devices: 30.7 us -> 21.5 us  [body(): lax.all_to_all(both_flat, 'scan', split_axis=2, concat_axis=1, tiled=True)]
    all_to_all x0 -> x1, other arithmetic: none -> 3.15 us  [body(): lax.all_to_all(both_flat, 'scan', split_axis=2, concat_axis=1, tiled=True)]
  transfers between devices with their start and end apart: 5 -> 3, of which waited for: 4 -> 3; matrix products, arithmetic and copies ran while one was open for 6% -> 3% of each run, Pallas kernels for 0% -> 0%
where the time goes in v5:
time: 182 us; the launch traced here: 181 us
  local copies, waits for them, and re-layouts  101 us (55%)
  blocking collectives  31.6 us (17%)
  waiting for transfers between devices  24.8 us (14%)
  starting transfers between devices  10.8 us (6%)
  other arithmetic  6.57 us (4%)
  matrix products  4.67 us (3%)
  between operations  2.12 us (1%)
    unnamed x8, local copies, waits for them, and re-layouts  60.9 us
    all_to_all x1, blocking collectives, body(): lax.all_to_all(jnp.stack([misfit_pencil, back_pencil]), 'scan', split_axi...  31.6 us
    all_to_all x1, waiting for transfers between devices, body(): lax.all_to_all(both_flat, 'scan', split_axis=2, concat_axis=1, tiled=True)  21.5 us
    all_to_all x2, local copies, waits for them, and re-layouts, body(): lax.all_to_all(both_flat, 'scan', split_axis=2, concat_axis=1, tiled=True)  20.8 us
    another operation x3, local copies, waits for them, and re-layouts, body(): both_flat = jnp.stack([blurred, raw.reshape(plane_count, flat_count)])  15.8 us
    all_to_all x1, starting transfers between devices, body(): lax.all_to_all(both_flat, 'scan', split_axis=2, concat_axis=1, tiled=True)  6.2 us
    ppermute x2, starting transfers between devices, with_halo(): arrived = lax.ppermute(jnp.where(first, tail, head), axis, [(0, 1), (1, 0)])  4.56 us
  transfers between devices with their start and end apart: 3, of which 3 were waited for; matrix products, arithmetic and copies ran while one was open for 3% of the time, Pallas kernels for 0%

profile of v5, /device:TPU:0, one launch (start us, length us, event | category | flops | bytes accessed | tf_op | source)
XLA Modules:
  0.0 181.3 jit_solution(13650661179167656259)
XLA Ops:
  0.6 1.0 slice_select_fusion.1
  1.6 3.0 %collective-permute-start = (f32[8,8,512]{2,1,0:T(8,128)S(1)}, f32[8,8,512]{2,1,0:T(8,128)S(1)}, u32[]{:S(2)}, u32[]{:S(2)}) collective-permute-start(f32[8,8,512]{2,1,0:T(8,128)S(1)} %slice_select_fusion.1), channel_id=1, source_target_pairs={{0,1},{1,0},{2,3},{3,2},{4,5},{5,4},{6,7},{7,6},{8,9},{9,8},{10,11... | collective-permute-start | bytes 393224 | tf_op jit(solution)/shard_map/ppermute | solution.py:16
  4.6 0.7 rev.3
  5.4 1.1 stack_reshape.7
  6.5 0.8 select_reduce_fusion.1
  7.3 0.8 collective-permute-done
  8.2 1.7 convolution_bitcast_fusion.1
  9.9 0.1 stack_reshape.6
  10.0 0.1 pad_maximum_fusion
  10.0 14.6 %copy.19 = f32[2,8,16384]{1,0,2:T(2,128)} copy(f32[2,8,16384]{2,1,0:T(8,128)S(1)} %pad_maximum_fusion) | data formatting | bytes 2097152 | tf_op jit(solution)/shard_map/stack | solution.py:63
  24.6 0.0 copy-start.1
  24.6 0.0 copy-start.2
  24.6 29.0 %reshape.53 = f32[16,1,16384]{2,1,0:T(1,128)} reshape(f32[16384,2,8]{2,1,0:T(2,128)} %bitcast.42) | data formatting | bytes 2097152
  53.6 6.2 %all-to-all-start = ((f32[16,1,16384]{2,1,0:T(1,128)}), f32[16,1,16384]{2,1,0:T(1,128)S(1)}, u32[]{:S(2)}, u32[]{:S(2)}) async-start(f32[16,1,16384]{2,1,0:T(1,128)} %reshape.53), calls=%async_computation | async-start | bytes 2097152 | tf_op jit(solution)/shard_map/all_to_all | solution.py:64
  59.8 0.0 copy-done.1
  59.8 0.1 subtract_subtract_fusion
  59.9 0.0 copy-done.2
  59.9 1.4 select_reduce_fusion
  61.3 21.5 %all-to-all-done = f32[16,1,16384]{2,1,0:T(1,128)S(1)} async-done(((f32[16,1,16384]{2,1,0:T(1,128)}), f32[16,1,16384]{2,1,0:T(1,128)S(1)}, u32[]{:S(2)}, u32[]{:S(2)}) %all-to-all-start) | async-done | bytes 1048608 | tf_op jit(solution)/shard_map/all_to_all | solution.py:64
  82.8 0.5 broadcast.33
  83.3 3.1 %reduce = f32[16,16384]{1,0:T(8,128)S(1)} reduce(f32[16,1,16384]{2,1,0:T(1,128)S(1)} %all-to-all-done, f32[]{:T(128)} %broadcast.33), dimensions={1}, to_apply=%all_to_all.22.reduce_sub_computation | reduce | bytes 2097156 | tf_op jit(solution)/shard_map/all_to_all | solution.py:64
  86.4 31.9 %reshape.54 = f32[16384,2,8]{2,1,0:T(2,128)} reshape(f32[16,16384]{1,0:T(8,128)S(1)} %reduce) | data formatting | bytes 2097152
  118.4 20.3 %copy.20 = f32[2,8,16,1024]{3,1,2,0:T(8,128)S(1)} copy(f32[2,8,16,1024]{1,0,3,2:T(2,128)} %bitcast.43) | data formatting | bytes 2097152 | tf_op jit(solution)/shard_map/all_to_all | solution.py:64
  138.7 0.6 convolution_subtract_fusion
  139.3 0.7 convolution_bitcast_fusion
  140.0 0.1 pad_maximum_fusion.1
  140.1 0.8 copy.21
  140.9 0.0 copy-start
  141.0 31.6 %all_to_all.30 = f32[2,128,1024]{2,0,1:T(2,128)S(1)} all-to-all(f32[2,128,1024]{2,0,1:T(2,128)S(1)} %copy.21), channel_id=1, replica_groups=mesh['scan'=16,'row'=2] {'scan'}, dimensions={1} | all-to-all | bytes 2097152 | tf_op jit(solution)/shard_map/all_to_all | solution.py:70
  172.6 0.6 copy.24
  173.2 0.1 fusion.24
  173.3 0.1 reshape_squeeze.6
  173.4 1.6 collective-permute-start.1
  176.3 0.9 reshape_squeeze.7
  177.1 2.5 %collective-permute-done.1 = f32[8,8,512]{2,1,0:T(8,128)S(1)} collective-permute-done((f32[8,8,512]{2,1,0:T(8,128)S(1)}, f32[8,8,512]{2,1,0:T(8,128)S(1)}, u32[]{:S(2)}, u32[]{:S(2)}) %collective-permute-start.1) | collective-permute-done | bytes 131104 | tf_op jit(solution)/shard_map/ppermute | solution.py:16
  179.7 0.0 copy-done
  179.7 1.6 maximum_multiply_fusion
  (4 shorter events, 0.1 us)
Async XLA Ops:
  1.6 6.5 %collective-permute-start = (f32[8,8,512]{2,1,0:T(8,128)S(1)}, f32[8,8,512]{2,1,0:T(8,128)S(1)}, u32[]{:S(2)}, u32[]{:S(2)}) collective-permute-start(f32[8,8,512]{2,1,0:T(8,128)S(1)} %slice_select_fusion.1), channel_id=1, source_target_pairs={{0,1},{1,0},{2,3},{3,2},{4,5},{5,4},{6,7},{7,6},{8,9},{9,8},{10,11... | collective-permute-start | bytes 393224 | tf_op jit(solution)/shard_map/ppermute | solution.py:16
  24.6 35.2 %copy-start.1 = (s32[128]{0:T(128)S(1)}, s32[128]{0:T(128)}, u32[]{:S(2)}) copy-start(s32[128]{0:T(128)} %param.9) | copy-start | bytes 1540
  24.6 35.3 %copy-start.2 = (f32[64]{0:T(128)S(1)}, f32[64]{0:T(128)}, u32[]{:S(2)}) copy-start(f32[64]{0:T(128)} %param.10) | copy-start | bytes 772
  53.6 29.1 %all-to-all-start = ((f32[16,1,16384]{2,1,0:T(1,128)}), f32[16,1,16384]{2,1,0:T(1,128)S(1)}, u32[]{:S(2)}, u32[]{:S(2)}) async-start(f32[16,1,16384]{2,1,0:T(1,128)} %reshape.53), calls=%async_computation | async-start | bytes 2097152 | tf_op jit(solution)/shard_map/all_to_all | solution.py:64
  140.9 38.7 %copy-start = (f32[8,32,512]{2,1,0:T(8,128)S(1)}, f32[8,32,512]{2,1,0:T(8,128)}, u32[]{:S(2)}) copy-start(f32[8,32,512]{2,1,0:T(8,128)} %param.7) | copy-start | bytes 1572868
  173.4 6.2 %collective-permute-start.1 = (f32[8,8,512]{2,1,0:T(8,128)S(1)}, f32[8,8,512]{2,1,0:T(8,128)S(1)}, u32[]{:S(2)}, u32[]{:S(2)}) collective-permute-start(f32[8,8,512]{2,1,0:T(8,128)S(1)} %slice_select_fusion), channel_id=1, source_target_pairs={{0,1},{1,0},{2,3},{3,2},{4,5},{5,4},{6,7},{7,6},{8,9},{9,8},{10,11... | collective-permute-start | bytes 393224 | tf_op jit(solution)/shard_map/ppermute | solution.py:16

commit v6 on v5

--- a/solution.py
+++ b/solution.py
@@ -60,10 +60,11 @@
     back_band = band_matrix(lateral_psf[::-1], row_count, 0)
     padded = with_halo(estimate, "row", halo_rows)
     blurred = lateral_apply(blur_band, padded).reshape(plane_count, flat_count)
-    both_flat = jnp.stack([blurred, raw.reshape(plane_count, flat_count)])
-    both_in = lax.all_to_all(both_flat, "scan", split_axis=2, concat_axis=1, tiled=True)
-    pencil = both_in[0]
-    raw_pencil = both_in[1]
+    both_flat = jnp.concatenate([blurred, raw.reshape(plane_count, flat_count)], axis=0)
+    both_in = lax.all_to_all(both_flat, "scan", split_axis=1, concat_axis=0, tiled=True)
+    both_in = both_in.reshape(lax.axis_size("scan"), 2, plane_count, -1)
+    pencil = both_in[:, 0].reshape(offsets.shape[0], -1)
+    raw_pencil = both_in[:, 1].reshape(offsets.shape[0], -1)
     predicted_pencil = jnp.dot(sheet_psf, pencil, precision=highest_mode)
     misfit_pencil = predicted_pencil - raw_pencil
     back_pencil = transpose_apply(sheet_psf, misfit_pencil)

time: 182 us -> 82.8 us (0.45)
  local copies, waits for them, and re-layouts: 101 us -> 6.17 us
  other arithmetic: 6.57 us -> 2.85 us
    unnamed x8, local copies, waits for them, and re-layouts: 60.9 us -> 0.02 us
    all_to_all x2 -> x0, local copies, waits for them, and re-layouts: 20.8 us -> none  [body(): lax.all_to_all(both_flat, 'scan', split_axis=2, concat_axis=1, tiled=True)]
    another operation x3 -> x0, local copies, waits for them, and re-layouts: 15.8 us -> none  [body(): both_flat = jnp.stack([blurred, raw.reshape(plane_count, flat_count)])]
    all_to_all x1 -> x0, other arithmetic: 3.15 us -> none  [body(): lax.all_to_all(both_flat, 'scan', split_axis=2, concat_axis=1, tiled=True)]
    concatenate x0 -> x3, local copies, waits for them, and re-layouts: none -> 2.97 us  [body(): jnp.concatenate([blurred, raw.reshape(plane_count, flat_count)], axis=0)]
  transfers between devices with their start and end apart: 3 -> 3, of which waited for: 3 -> 3; matrix products, arithmetic and copies ran while one was open for 3% -> 5% of each run, Pallas kernels for 0% -> 0%
where the time goes in v6:
time: 82.8 us; the launch traced here: 82.5 us
  blocking collectives  31.5 us (38%)
  waiting for transfers between devices  25.4 us (31%)
  starting transfers between devices  10.9 us (13%)
  local copies, waits for them, and re-layouts  6.17 us (7%)
  matrix products  3.62 us (4%)
  other arithmetic  2.85 us (3%)
  between operations  2.12 us (3%)
    all_to_all x1, blocking collectives, body(): lax.all_to_all(jnp.stack([misfit_pencil, back_pencil]), 'scan', split_axi...  31.5 us
    all_to_all x1, waiting for transfers between devices, body(): lax.all_to_all(both_flat, 'scan', split_axis=1, concat_axis=0, tiled=True)  21.5 us
    all_to_all x1, starting transfers between devices, body(): lax.all_to_all(both_flat, 'scan', split_axis=1, concat_axis=0, tiled=True)  6.32 us
    ppermute x2, starting transfers between devices, with_halo(): arrived = lax.ppermute(jnp.where(first, tail, head), axis, [(0, 1), (1, 0)])  4.57 us
    ppermute x2, waiting for transfers between devices, with_halo(): arrived = lax.ppermute(jnp.where(first, tail, head), axis, [(0, 1), (1, 0)])  3.89 us
    concatenate x3, local copies, waits for them, and re-layouts, body(): jnp.concatenate([blurred, raw.reshape(plane_count, flat_count)], axis=0)  2.97 us
    dot_general x2, matrix products, lateral_apply(): return jnp.einsum('rk,pkc->prc', band, padded, precision=highest_mode)  2.29 us
  transfers between devices with their start and end apart: 3, of which 3 were waited for; matrix products, arithmetic and copies ran while one was open for 5% of the time, Pallas kernels for 0%

profile of v6, /device:TPU:0, one launch (start us, length us, event | category | flops | bytes accessed | tf_op | source)
XLA Modules:
  0.0 82.5 jit_solution(1204283072880443003)
XLA Ops:
  0.6 0.0 copy-start
  0.6 0.0 copy-start.2
  0.7 1.0 %slice_select_fusion.1 = f32[8,8,512]{2,1,0:T(8,128)S(1)} fusion(f32[8,32,512]{2,1,0:T(8,128)} %param.7, pred[]{:T(512)S(6)} %eq.20), kind=kLoop, calls=%fused_computation.28 | loop fusion | flops 32768 | bytes 393217 | tf_op jit(solution)/shard_map/jit(_where)/select_n | solution.py:16
  1.7 3.0 %collective-permute-start = (f32[8,8,512]{2,1,0:T(8,128)S(1)}, f32[8,8,512]{2,1,0:T(8,128)S(1)}, u32[]{:S(2)}, u32[]{:S(2)}) collective-permute-start(f32[8,8,512]{2,1,0:T(8,128)S(1)} %slice_select_fusion.1), channel_id=1, source_target_pairs={{0,1},{1,0},{2,3},{3,2},{4,5},{5,4},{6,7},{7,6},{8,9},{9,8},{10,11... | collective-permute-start | bytes 393224 | tf_op jit(solution)/shard_map/ppermute | solution.py:16
  4.7 0.7 rev.3
  5.5 1.2 %concatenate.16 = f32[8,16,1024]{2,1,0:T(8,128)S(1)} reshape(f32[8,32,512]{2,1,0:T(8,128)} %param.8) | data formatting | bytes 1048576 | tf_op jit(solution)/shard_map/concatenate | solution.py:63
  6.7 0.0 copy-done.2
  6.7 0.1 select_reduce_fusion.1
  6.8 1.4 %collective-permute-done = f32[8,8,512]{2,1,0:T(8,128)S(1)} collective-permute-done((f32[8,8,512]{2,1,0:T(8,128)S(1)}, f32[8,8,512]{2,1,0:T(8,128)S(1)}, u32[]{:S(2)}, u32[]{:S(2)}) %collective-permute-start) | collective-permute-done | bytes 131104 | tf_op jit(solution)/shard_map/ppermute | solution.py:16
  8.2 0.0 copy-done
  8.2 0.6 convolution_bitcast_fusion.1
  8.9 0.2 concatenate.15
  9.1 0.1 pad_maximum_fusion
  9.2 1.6 %copy.19 = f32[16,16,1024]{2,0,1:T(8,128)} copy(f32[16,16,1024]{2,1,0:T(8,128)S(1)} %pad_maximum_fusion) | data formatting | bytes 2097152 | tf_op jit(solution)/shard_map/concatenate | solution.py:63
  10.8 0.0 copy-start.1
  10.8 0.0 copy-start.3
  10.8 6.3 %all-to-all-start = ((f32[16,16,1024]{2,0,1:T(8,128)}), f32[16,16,1024]{2,0,1:T(8,128)S(1)}, u32[]{:S(2)}, u32[]{:S(2)}) async-start(f32[16,16,1024]{2,0,1:T(8,128)} %copy.19), calls=%async_computation | async-start | bytes 2097152 | tf_op jit(solution)/shard_map/all_to_all | solution.py:64
  17.1 0.0 copy-done.1
  17.1 0.1 subtract_subtract_fusion
  17.2 0.0 copy-done.3
  17.2 1.4 %select_reduce_fusion = f32[128,128]{1,0:T(8,128)S(1)} fusion(f32[64]{0:T(128)S(1)} %copy-done.3, s32[128,128]{1,0:T(8,128)S(1)} %subtract_subtract_fusion), kind=kLoop, calls=%fused_computation | loop fusion | flops 3129344 | bytes 131328 | tf_op jit(solution)/shard_map/reduce_sum | solution.py:47
  18.6 21.5 %all-to-all-done = f32[16,16,1024]{2,0,1:T(8,128)S(1)} async-done(((f32[16,16,1024]{2,0,1:T(8,128)}), f32[16,16,1024]{2,0,1:T(8,128)S(1)}, u32[]{:S(2)}, u32[]{:S(2)}) %all-to-all-start) | async-done | bytes 1048608 | tf_op jit(solution)/shard_map/all_to_all | solution.py:64
  40.0 0.6 convolution_subtract_fusion
  40.7 0.7 convolution_bitcast_fusion
  41.4 0.1 pad_maximum_fusion.1
  41.5 0.8 copy.20
  42.3 31.5 %all_to_all.28 = f32[2,128,1024]{2,0,1:T(2,128)S(1)} all-to-all(f32[2,128,1024]{2,0,1:T(2,128)S(1)} %copy.20), channel_id=1, replica_groups=mesh['scan'=16,'row'=2] {'scan'}, dimensions={1} | all-to-all | bytes 2097152 | tf_op jit(solution)/shard_map/all_to_all | solution.py:71
  73.8 0.6 copy.23
  74.4 0.1 fusion.24
  74.5 0.1 reshape_squeeze.14
  74.6 1.6 %collective-permute-start.1 = (f32[8,8,512]{2,1,0:T(8,128)S(1)}, f32[8,8,512]{2,1,0:T(8,128)S(1)}, u32[]{:S(2)}, u32[]{:S(2)}) collective-permute-start(f32[8,8,512]{2,1,0:T(8,128)S(1)} %slice_select_fusion), channel_id=1, source_target_pairs={{0,1},{1,0},{2,3},{3,2},{4,5},{5,4},{6,7},{7,6},{8,9},{9,8},{10,11... | collective-permute-start | bytes 393224 | tf_op jit(solution)/shard_map/ppermute | solution.py:16
  77.5 0.9 %reshape_squeeze.15 = f32[8,32,512]{2,1,0:T(8,128)} reshape(f32[1,8,16,1024]{3,2,1,0:T(8,128)S(1)} %get-tuple-element.4) | data formatting | bytes 1048576 | tf_op jit(solution)/shard_map/reshape;squeeze | solution.py:79
  78.3 2.5 %collective-permute-done.1 = f32[8,8,512]{2,1,0:T(8,128)S(1)} collective-permute-done((f32[8,8,512]{2,1,0:T(8,128)S(1)}, f32[8,8,512]{2,1,0:T(8,128)S(1)}, u32[]{:S(2)}, u32[]{:S(2)}) %collective-permute-start.1) | collective-permute-done | bytes 131104 | tf_op jit(solution)/shard_map/ppermute | solution.py:16
  80.9 1.6 %maximum_multiply_fusion = f32[8,32,512]{2,1,0:T(8,128)} fusion(f32[8,32,512]{2,1,0:T(8,128)S(1)} %copy-done, f32[8,8,512]{2,1,0:T(8,128)S(1)} %get-tuple-element.7, f32[8,32,512]{2,1,0:T(8,128)S(1)} %reshape_squeeze.14, f32[8,8,512]{2,1,0:T(8,128)S(1)} %get-tuple-element.6, f32[]{:T(128)S(6)} %mul.18, f32[]{:T(128)} %bitcast.38, ...), kind=kOutput, calls=%fused_computation.23 | convolution fusion | flops 76808192 | bytes 1841160 | tf_op jit(solution)/shard_map/rk,pkc->prc/dot_general | solution.py:36
  (4 shorter events, 0.1 us)
Async XLA Ops:
  0.6 7.6 %copy-start = (f32[8,32,512]{2,1,0:T(8,128)S(1)}, f32[8,32,512]{2,1,0:T(8,128)}, u32[]{:S(2)}) copy-start(f32[8,32,512]{2,1,0:T(8,128)} %param.7) | copy-start | bytes 1572868
  0.6 6.0 %copy-start.2 = (f32[17]{0:T(128)S(1)}, f32[17]{0:T(128)}, u32[]{:S(2)}) copy-start(f32[17]{0:T(128)} %param.11) | copy-start | bytes 208
  1.7 6.5 %collective-permute-start = (f32[8,8,512]{2,1,0:T(8,128)S(1)}, f32[8,8,512]{2,1,0:T(8,128)S(1)}, u32[]{:S(2)}, u32[]{:S(2)}) collective-permute-start(f32[8,8,512]{2,1,0:T(8,128)S(1)} %slice_select_fusion.1), channel_id=1, source_target_pairs={{0,1},{1,0},{2,3},{3,2},{4,5},{5,4},{6,7},{7,6},{8,9},{9,8},{10,11... | collective-permute-start | bytes 393224 | tf_op jit(solution)/shard_map/ppermute | solution.py:16
  10.8 6.3 %copy-start.1 = (s32[128]{0:T(128)S(1)}, s32[128]{0:T(128)}, u32[]{:S(2)}) copy-start(s32[128]{0:T(128)} %param.9) | copy-start | bytes 1540
  10.8 6.4 %copy-start.3 = (f32[64]{0:T(128)S(1)}, f32[64]{0:T(128)}, u32[]{:S(2)}) copy-start(f32[64]{0:T(128)} %param.10) | copy-start | bytes 772
  10.8 29.3 %all-to-all-start = ((f32[16,16,1024]{2,0,1:T(8,128)}), f32[16,16,1024]{2,0,1:T(8,128)S(1)}, u32[]{:S(2)}, u32[]{:S(2)}) async-start(f32[16,16,1024]{2,0,1:T(8,128)} %copy.19), calls=%async_computation | async-start | bytes 2097152 | tf_op jit(solution)/shard_map/all_to_all | solution.py:64
  74.6 6.2 %collective-permute-start.1 = (f32[8,8,512]{2,1,0:T(8,128)S(1)}, f32[8,8,512]{2,1,0:T(8,128)S(1)}, u32[]{:S(2)}, u32[]{:S(2)}) collective-permute-start(f32[8,8,512]{2,1,0:T(8,128)S(1)} %slice_select_fusion), channel_id=1, source_target_pairs={{0,1},{1,0},{2,3},{3,2},{4,5},{5,4},{6,7},{7,6},{8,9},{9,8},{10,11... | collective-permute-start | bytes 393224 | tf_op jit(solution)/shard_map/ppermute | solution.py:16

commit v7 on v6

--- a/solution.py
+++ b/solution.py
@@ -21,6 +21,18 @@
         above = lax.ppermute(tail, axis, [(i, (i + 1) % count) for i in range(ends)])
         below = lax.ppermute(head, axis, [((i + 1) % count, i) for i in range(ends)])
     return jnp.concatenate([above, cells, below], axis=1)
+
+
+def ring_exchange(chunks, axis):
+    count = lax.axis_size(axis)
+    me = lax.axis_index(axis)
+    mine = lax.dynamic_index_in_dim(chunks, me, keepdims=False)
+    result = lax.dynamic_update_index_in_dim(jnp.zeros_like(chunks), mine, me, axis=0)
+    for shift in range(1, count):
+        piece = lax.dynamic_index_in_dim(chunks, (me + shift) % count, keepdims=False)
+        got = lax.ppermute(piece, axis, [(j, (j + shift) % count) for j in range(count)])
+        result = lax.dynamic_update_index_in_dim(result, got, (me + count - shift) % count, axis=0)
+    return result
 
 
 def band_matrix(kernel_taps, row_count, shift):
@@ -60,15 +72,17 @@
     back_band = band_matrix(lateral_psf[::-1], row_count, 0)
     padded = with_halo(estimate, "row", halo_rows)
     blurred = lateral_apply(blur_band, padded).reshape(plane_count, flat_count)
-    both_flat = jnp.concatenate([blurred, raw.reshape(plane_count, flat_count)], axis=0)
-    both_in = lax.all_to_all(both_flat, "scan", split_axis=1, concat_axis=0, tiled=True)
-    both_in = both_in.reshape(lax.axis_size("scan"), 2, plane_count, -1)
+    scan_count = lax.axis_size("scan")
+    both_flat = jnp.stack([blurred, raw.reshape(plane_count, flat_count)])
+    outgoing = both_flat.reshape(2, plane_count, scan_count, flat_count // scan_count).transpose(2, 0, 1, 3)
+    both_in = ring_exchange(outgoing, "scan")
     pencil = both_in[:, 0].reshape(offsets.shape[0], -1)
     raw_pencil = both_in[:, 1].reshape(offsets.shape[0], -1)
     predicted_pencil = jnp.dot(sheet_psf, pencil, precision=highest_mode)
     misfit_pencil = predicted_pencil - raw_pencil
     back_pencil = transpose_apply(sheet_psf, misfit_pencil)
-    both_out = lax.all_to_all(jnp.stack([misfit_pencil, back_pencil]), "scan", split_axis=1, concat_axis=2, tiled=True)
+    results = jnp.stack([misfit_pencil, back_pencil]).reshape(2, scan_count, plane_count, -1).transpose(1, 0, 2, 3)
+    both_out = ring_exchange(results, "scan").transpose(1, 2, 0, 3).reshape(2, plane_count, flat_count)
     misfit = both_out[0]
     back_volume = both_out[1].reshape(plane_count, row_count, width_count)
     padded_back = with_halo(back_volume, "row", halo_rows)

time: 82.8 us -> 84.9 us (1.025)
  starting transfers between devices: 10.9 us -> 44.2 us
  blocking collectives: 31.5 us -> 0 us
  local copies, waits for them, and re-layouts: 6.17 us -> 4.82 us
  other arithmetic: 2.85 us -> 4.14 us
    ppermute x0 -> x30, starting transfers between devices: none -> 39.9 us  [ring_exchange(): lax.ppermute(piece, axis, [(j, (j + shift) % count) for j in range(count)])]
    all_to_all x1 -> x0, blocking collectives: 31.5 us -> none  [body(): lax.all_to_all(jnp.stack([misfit_pencil, back_pencil]), 'scan', split_axi...]
    ppermute x0 -> x30, waiting for transfers between devices: none -> 22.8 us  [ring_exchange(): lax.ppermute(piece, axis, [(j, (j + shift) % count) for j in range(count)])]
    all_to_all x1 -> x0, waiting for transfers between devices: 21.5 us -> none  [body(): lax.all_to_all(both_flat, 'scan', split_axis=1, concat_axis=0, tiled=True)]
    all_to_all x1 -> x0, starting transfers between devices: 6.32 us -> none  [body(): lax.all_to_all(both_flat, 'scan', split_axis=1, concat_axis=0, tiled=True)]
    concatenate x3 -> x0, local copies, waits for them, and re-layouts: 2.97 us -> none  [body(): jnp.concatenate([blurred, raw.reshape(plane_count, flat_count)], axis=0)]
    ppermute x2, waiting for transfers between devices: 3.89 us -> 2.31 us  [with_halo(): arrived = lax.ppermute(jnp.where(first, tail, head), axis, [(0, 1), (1, 0)])]
    another operation x1 -> x6, local copies, waits for them, and re-layouts: 0.81 us -> 1.86 us  [body(): jnp.stack([misfit_pencil, back_pencil])]
  transfers between devices with their start and end apart: 3 -> 32, of which waited for: 3 -> 16; matrix products, arithmetic and copies ran while one was open for 5% -> 7% of each run, Pallas kernels for 0% -> 0%
where the time goes in v7:
time: 84.9 us; the launch traced here: 84.7 us
  starting transfers between devices  44.2 us (52%)
  waiting for transfers between devices  25.2 us (30%)
  local copies, waits for them, and re-layouts  4.82 us (6%)
  other arithmetic  4.14 us (5%)
  matrix products  3.62 us (4%)
  between operations  2.75 us (3%)
    ppermute x30, starting transfers between devices, ring_exchange(): lax.ppermute(piece, axis, [(j, (j + shift) % count) for j in range(count)])  39.9 us
    ppermute x30, waiting for transfers between devices, ring_exchange(): lax.ppermute(piece, axis, [(j, (j + shift) % count) for j in range(count)])  22.8 us
    ppermute x2, starting transfers between devices, with_halo(): arrived = lax.ppermute(jnp.where(first, tail, head), axis, [(0, 1), (1, 0)])  4.24 us
    ppermute x2, waiting for transfers between devices, with_halo(): arrived = lax.ppermute(jnp.where(first, tail, head), axis, [(0, 1), (1, 0)])  2.31 us
    dot_general x2, matrix products, lateral_apply(): return jnp.einsum('rk,pkc->prc', band, padded, precision=highest_mode)  2.29 us
    reduce_sum x1, other arithmetic, sheet_matrix(): return jnp.where(inside, jnp.sum(picked, axis=-1), 0.0)  1.99 us
  transfers between devices with their start and end apart: 32, of which 16 were waited for; matrix products, arithmetic and copies ran while one was open for 7% of the time, Pallas kernels for 0%

profile of v7, /device:TPU:0, one launch (start us, length us, event | category | flops | bytes accessed | tf_op | source)
XLA Modules:
  0.0 84.7 jit_solution(3468087343182784202)
XLA Ops:
  0.7 1.0 %slice_select_fusion.1 = f32[8,8,512]{2,1,0:T(8,128)S(1)} fusion(f32[8,32,512]{2,1,0:T(8,128)} %param.7, pred[]{:T(512)S(6)} %eq.104), kind=kLoop, calls=%fused_computation.57 | loop fusion | flops 32768 | bytes 393217 | tf_op jit(solution)/shard_map/jit(_where)/select_n | solution.py:16
  1.7 3.0 %collective-permute-start = (f32[8,8,512]{2,1,0:T(8,128)S(1)}, f32[8,8,512]{2,1,0:T(8,128)S(1)}, u32[]{:S(2)}, u32[]{:S(2)}) collective-permute-start(f32[8,8,512]{2,1,0:T(8,128)S(1)} %slice_select_fusion.1), channel_id=1, source_target_pairs={{0,1},{1,0},{2,3},{3,2},{4,5},{5,4},{6,7},{7,6},{8,9},{9,8},{10,11... | collective-permute-start | bytes 393224 | tf_op jit(solution)/shard_map/ppermute | solution.py:16
  4.7 0.8 subtract_subtract_fusion
  5.5 2.0 %select_reduce_fusion = f32[128,128]{1,0:T(8,128)S(1)} fusion(f32[64]{0:T(128)} %param.10, s32[128,128]{1,0:T(8,128)S(1)} %subtract_subtract_fusion), kind=kLoop, calls=%fused_computation | loop fusion | flops 3129344 | bytes 131328 | tf_op jit(solution)/shard_map/reduce_sum | solution.py:59
  7.6 0.7 rev.3
  8.8 0.6 convolution_bitcast_fusion.1
  9.7 1.3 %constant_dynamic-slice_fusion = (f32[2,8,1,1024]{3,2,1,0:T(1,128)S(1)}, f32[2,8,1,1024]{3,2,1,0:T(1,128)S(1)}, f32[2,8,1,1024]{3,2,1,0:T(1,128)S(1)}, f32[2,8,1...) fusion(f32[2,8,16,1024]{3,2,1,0:T(8,128)S(1)} %constant_dynamic, ...), kind=kLoop, calls=%fused_computation.143 | loop fusion | bytes 2097216 | tf_op jit(solution)/shard_map/dynamic-slice.15
  11.1 1.6 %collective-permute-start.2 = (f32[2,8,1024]{2,1,0:T(8,128)S(1)}, f32[2,8,1024]{2,1,0:T(8,128)S(1)}, u32[]{:S(2)}, u32[]{:S(2)}) collective-permute-start(f32[2,8,1024]{2,1,0:T(8,128)S(1)} %bitcast.192), channel_id=1, source_target_pairs={{0,4},{2,6},{4,8},{6,10},{8,12},{10,14},{12,16},{14,18},{16,20},{1... | collective-permute-start | bytes 196616 | tf_op jit(solution)/shard_map/ppermute | solution.py:33
  12.7 2.5 %collective-permute-start.3 = (f32[2,8,1024]{2,1,0:T(8,128)S(1)}, f32[2,8,1024]{2,1,0:T(8,128)S(1)}, u32[]{:S(2)}, u32[]{:S(2)}) collective-permute-start(f32[2,8,1024]{2,1,0:T(8,128)S(1)} %bitcast.191), channel_id=1, source_target_pairs={{0,6},{2,8},{4,10},{6,12},{8,14},{10,16},{12,18},{14,20},{16,22},{... | collective-permute-start | bytes 196616 | tf_op jit(solution)/shard_map/ppermute | solution.py:33
  15.2 1.6 %collective-permute-start.4 = (f32[2,8,1024]{2,1,0:T(8,128)S(1)}, f32[2,8,1024]{2,1,0:T(8,128)S(1)}, u32[]{:S(2)}, u32[]{:S(2)}) collective-permute-start(f32[2,8,1024]{2,1,0:T(8,128)S(1)} %bitcast.190), channel_id=1, source_target_pairs={{0,8},{2,10},{4,12},{6,14},{8,16},{10,18},{12,20},{14,22},{16,24},... | collective-permute-start | bytes 196616 | tf_op jit(solution)/shard_map/ppermute | solution.py:33
  17.6 1.1 %collective-permute-start.6 = (f32[2,8,1024]{2,1,0:T(8,128)S(1)}, f32[2,8,1024]{2,1,0:T(8,128)S(1)}, u32[]{:S(2)}, u32[]{:S(2)}) collective-permute-start(f32[2,8,1024]{2,1,0:T(8,128)S(1)} %bitcast.188), channel_id=1, source_target_pairs={{0,12},{2,14},{4,16},{6,18},{8,20},{10,22},{12,24},{14,26},{16,28}... | collective-permute-start | bytes 196616 | tf_op jit(solution)/shard_map/ppermute | solution.py:33
  18.7 4.4 %collective-permute-start.7 = (f32[2,8,1024]{2,1,0:T(8,128)S(1)}, f32[2,8,1024]{2,1,0:T(8,128)S(1)}, u32[]{:S(2)}, u32[]{:S(2)}) collective-permute-start(f32[2,8,1024]{2,1,0:T(8,128)S(1)} %bitcast.187), channel_id=1, source_target_pairs={{0,14},{2,16},{4,18},{6,20},{8,22},{10,24},{12,26},{14,28},{16,30}... | collective-permute-start | bytes 196616 | tf_op jit(solution)/shard_map/ppermute | solution.py:33
  23.2 0.4 collective-permute-start.8
  23.6 0.3 collective-permute-start.9
  23.9 6.1 %collective-permute-done.5 = f32[2,8,1024]{2,1,0:T(8,128)S(1)} collective-permute-done((f32[2,8,1024]{2,1,0:T(8,128)S(1)}, f32[2,8,1024]{2,1,0:T(8,128)S(1)}, u32[]{:S(2)}, u32[]{:S(2)}) %collective-permute-start.5) | collective-permute-done | bytes 65568 | tf_op jit(solution)/shard_map/ppermute | solution.py:33
  30.1 0.5 collective-permute-start.11
  30.6 0.7 collective-permute-done.7
  31.3 1.0 %collective-permute-start.12 = (f32[2,8,1024]{2,1,0:T(8,128)S(1)}, f32[2,8,1024]{2,1,0:T(8,128)S(1)}, u32[]{:S(2)}, u32[]{:S(2)}) collective-permute-start(f32[2,8,1024]{2,1,0:T(8,128)S(1)} %bitcast.182), channel_id=1, source_target_pairs={{0,24},{2,26},{4,28},{6,30},{8,0},{10,2},{12,4},{14,6},{16,8},{18,... | collective-permute-start | bytes 196616 | tf_op jit(solution)/shard_map/ppermute | solution.py:33
  32.3 0.3 collective-permute-done.8
  32.6 2.4 %collective-permute-start.13 = (f32[2,8,1024]{2,1,0:T(8,128)S(1)}, f32[2,8,1024]{2,1,0:T(8,128)S(1)}, u32[]{:S(2)}, u32[]{:S(2)}) collective-permute-start(f32[2,8,1024]{2,1,0:T(8,128)S(1)} %bitcast.181), channel_id=1, source_target_pairs={{0,26},{2,28},{4,30},{6,0},{8,2},{10,4},{12,6},{14,8},{16,10},{18,... | collective-permute-start | bytes 196616 | tf_op jit(solution)/shard_map/ppermute | solution.py:33
  35.0 2.7 %collective-permute-start.14 = (f32[2,8,1024]{2,1,0:T(8,128)S(1)}, f32[2,8,1024]{2,1,0:T(8,128)S(1)}, u32[]{:S(2)}, u32[]{:S(2)}) collective-permute-start(f32[2,8,1024]{2,1,0:T(8,128)S(1)} %bitcast.180), channel_id=1, source_target_pairs={{0,28},{2,30},{4,0},{6,2},{8,4},{10,6},{12,8},{14,10},{16,12},{18,... | collective-permute-start | bytes 196616 | tf_op jit(solution)/shard_map/ppermute | solution.py:33
  37.7 0.9 %collective-permute-start.15 = (f32[2,8,1024]{2,1,0:T(8,128)S(1)}, f32[2,8,1024]{2,1,0:T(8,128)S(1)}, u32[]{:S(2)}, u32[]{:S(2)}) collective-permute-start(f32[2,8,1024]{2,1,0:T(8,128)S(1)} %bitcast.179), channel_id=1, source_target_pairs={{0,30},{2,0},{4,2},{6,4},{8,6},{10,8},{12,10},{14,12},{16,14},{18,... | collective-permute-start | bytes 196616 | tf_op jit(solution)/shard_map/ppermute | solution.py:33
  38.7 3.1 %collective-permute-done.14 = f32[2,8,1024]{2,1,0:T(8,128)S(1)} collective-permute-done((f32[2,8,1024]{2,1,0:T(8,128)S(1)}, f32[2,8,1024]{2,1,0:T(8,128)S(1)}, u32[]{:S(2)}, u32[]{:S(2)}) %collective-permute-start.14) | collective-permute-done | bytes 65568 | tf_op jit(solution)/shard_map/ppermute | solution.py:33
  41.8 0.6 convolution_subtract_fusion
  42.5 0.7 convolution_bitcast_fusion
  43.3 3.0 %collective-permute-start.26 = (f32[2,8,1024]{2,1,0:T(8,128)S(1)}, f32[2,8,1024]{2,1,0:T(8,128)S(1)}, u32[]{:S(2)}, u32[]{:S(2)}) collective-permute-start(f32[2,8,1024]{2,1,0:T(8,128)S(1)} %get-tuple-element.19), channel_id=1, source_target_pairs={{0,22},{2,24},{4,26},{6,28},{8,30},{10,0},{12,2},{14,4},{16,6},{18... | collective-permute-start | bytes 196616 | tf_op jit(solution)/shard_map/ppermute | solution.py:33
  46.5 0.5 collective-permute-start.16
  47.1 2.7 %collective-permute-start.17 = (f32[2,8,1024]{2,1,0:T(8,128)S(1)}, f32[2,8,1024]{2,1,0:T(8,128)S(1)}, u32[]{:S(2)}, u32[]{:S(2)}) collective-permute-start(f32[2,8,1024]{2,1,0:T(8,128)S(1)} %get-tuple-element.8), channel_id=1, source_target_pairs={{0,4},{2,6},{4,8},{6,10},{8,12},{10,14},{12,16},{14,18},{16,20},{1... | collective-permute-start | bytes 196616 | tf_op jit(solution)/shard_map/ppermute | solution.py:33
  49.7 2.1 %collective-permute-start.18 = (f32[2,8,1024]{2,1,0:T(8,128)S(1)}, f32[2,8,1024]{2,1,0:T(8,128)S(1)}, u32[]{:S(2)}, u32[]{:S(2)}) collective-permute-start(f32[2,8,1024]{2,1,0:T(8,128)S(1)} %get-tuple-element.9), channel_id=1, source_target_pairs={{0,6},{2,8},{4,10},{6,12},{8,14},{10,16},{12,18},{14,20},{16,22},{... | collective-permute-start | bytes 196616 | tf_op jit(solution)/shard_map/ppermute | solution.py:33
  52.0 1.5 %collective-permute-done.16 = f32[2,8,1024]{2,1,0:T(8,128)S(1)} collective-permute-done((f32[2,8,1024]{2,1,0:T(8,128)S(1)}, f32[2,8,1024]{2,1,0:T(8,128)S(1)}, u32[]{:S(2)}, u32[]{:S(2)}) %collective-permute-start.16) | collective-permute-done | bytes 65568 | tf_op jit(solution)/shard_map/ppermute | solution.py:33
  53.5 0.9 %collective-permute-done.17 = f32[2,8,1024]{2,1,0:T(8,128)S(1)} collective-permute-done((f32[2,8,1024]{2,1,0:T(8,128)S(1)}, f32[2,8,1024]{2,1,0:T(8,128)S(1)}, u32[]{:S(2)}, u32[]{:S(2)}) %collective-permute-start.17) | collective-permute-done | bytes 65568 | tf_op jit(solution)/shard_map/ppermute | solution.py:33
  54.4 0.5 collective-permute-start.20
  55.2 3.4 %collective-permute-start.22 = (f32[2,8,1024]{2,1,0:T(8,128)S(1)}, f32[2,8,1024]{2,1,0:T(8,128)S(1)}, u32[]{:S(2)}, u32[]{:S(2)}) collective-permute-start(f32[2,8,1024]{2,1,0:T(8,128)S(1)} %get-tuple-element.14), channel_id=1, source_target_pairs={{0,14},{2,16},{4,18},{6,20},{8,22},{10,24},{12,26},{14,28},{16,30}... | collective-permute-start | bytes 196616 | tf_op jit(solution)/shard_map/ppermute | solution.py:33
  58.6 0.9 %collective-permute-done.19 = f32[2,8,1024]{2,1,0:T(8,128)S(1)} collective-permute-done((f32[2,8,1024]{2,1,0:T(8,128)S(1)}, f32[2,8,1024]{2,1,0:T(8,128)S(1)}, u32[]{:S(2)}, u32[]{:S(2)}) %collective-permute-start.19) | collective-permute-done | bytes 65568 | tf_op jit(solution)/shard_map/ppermute | solution.py:33
  59.5 3.4 %collective-permute-done.20 = f32[2,8,1024]{2,1,0:T(8,128)S(1)} collective-permute-done((f32[2,8,1024]{2,1,0:T(8,128)S(1)}, f32[2,8,1024]{2,1,0:T(8,128)S(1)}, u32[]{:S(2)}, u32[]{:S(2)}) %collective-permute-start.20) | collective-permute-done | bytes 65568 | tf_op jit(solution)/shard_map/ppermute | solution.py:33
  62.9 1.7 %collective-permute-start.25 = (f32[2,8,1024]{2,1,0:T(8,128)S(1)}, f32[2,8,1024]{2,1,0:T(8,128)S(1)}, u32[]{:S(2)}, u32[]{:S(2)}) collective-permute-start(f32[2,8,1024]{2,1,0:T(8,128)S(1)} %get-tuple-element.17), channel_id=1, source_target_pairs={{0,20},{2,22},{4,24},{6,26},{8,28},{10,30},{12,0},{14,2},{16,4},{1... | collective-permute-start | bytes 196616 | tf_op jit(solution)/shard_map/ppermute | solution.py:33
  64.6 0.8 collective-permute-start.27
  65.4 3.0 %collective-permute-done.23 = f32[2,8,1024]{2,1,0:T(8,128)S(1)} collective-permute-done((f32[2,8,1024]{2,1,0:T(8,128)S(1)}, f32[2,8,1024]{2,1,0:T(8,128)S(1)}, u32[]{:S(2)}, u32[]{:S(2)}) %collective-permute-start.23) | collective-permute-done | bytes 65568 | tf_op jit(solution)/shard_map/ppermute | solution.py:33
  68.4 0.9 %collective-permute-start.28 = (f32[2,8,1024]{2,1,0:T(8,128)S(1)}, f32[2,8,1024]{2,1,0:T(8,128)S(1)}, u32[]{:S(2)}, u32[]{:S(2)}) collective-permute-start(f32[2,8,1024]{2,1,0:T(8,128)S(1)} %get-tuple-element.18), channel_id=1, source_target_pairs={{0,26},{2,28},{4,30},{6,0},{8,2},{10,4},{12,6},{14,8},{16,10},{18,... | collective-permute-start | bytes 196616 | tf_op jit(solution)/shard_map/ppermute | solution.py:33
  69.3 0.6 collective-permute-done.24
  70.0 4.5 %collective-permute-start.30 = (f32[2,8,1024]{2,1,0:T(8,128)S(1)}, f32[2,8,1024]{2,1,0:T(8,128)S(1)}, u32[]{:S(2)}, u32[]{:S(2)}) collective-permute-start(f32[2,8,1024]{2,1,0:T(8,128)S(1)} %get-tuple-element.6), channel_id=1, source_target_pairs={{0,30},{2,0},{4,2},{6,4},{8,6},{10,8},{12,10},{14,12},{16,14},{18,... | collective-permute-start | bytes 196616 | tf_op jit(solution)/shard_map/ppermute | solution.py:33
  74.7 1.8 %collective-permute-done.30 = f32[2,8,1024]{2,1,0:T(8,128)S(1)} collective-permute-done((f32[2,8,1024]{2,1,0:T(8,128)S(1)}, f32[2,8,1024]{2,1,0:T(8,128)S(1)}, u32[]{:S(2)}, u32[]{:S(2)}) %collective-permute-start.30) | collective-permute-done | bytes 65568 | tf_op jit(solution)/shard_map/ppermute | solution.py:33
  76.5 0.3 copy.13
  77.0 1.2 %collective-permute-start.31 = (f32[8,8,512]{2,1,0:T(8,128)S(1)}, f32[8,8,512]{2,1,0:T(8,128)S(1)}, u32[]{:S(2)}, u32[]{:S(2)}) collective-permute-start(f32[8,8,512]{2,1,0:T(8,128)S(1)} %slice_select_fusion), channel_id=1, source_target_pairs={{0,1},{1,0},{2,3},{3,2},{4,5},{5,4},{6,7},{7,6},{8,9},{9,8},{10,11... | collective-permute-start | bytes 393224 | tf_op jit(solution)/shard_map/ppermute | solution.py:16
  79.5 0.3 copy.14
  79.8 0.9 %reshape_squeeze.15 = f32[8,32,512]{2,1,0:T(8,128)} reshape(f32[1,8,16,1024]{3,2,1,0:T(8,128)S(1)} %copy.14) | data formatting | bytes 1048576 | tf_op jit(solution)/shard_map/reshape;squeeze | solution.py:93
  80.7 2.3 %collective-permute-done.31 = f32[8,8,512]{2,1,0:T(8,128)S(1)} collective-permute-done((f32[8,8,512]{2,1,0:T(8,128)S(1)}, f32[8,8,512]{2,1,0:T(8,128)S(1)}, u32[]{:S(2)}, u32[]{:S(2)}) %collective-permute-start.31) | collective-permute-done | bytes 131104 | tf_op jit(solution)/shard_map/ppermute | solution.py:16
  83.0 1.6 %maximum_multiply_fusion = f32[8,32,512]{2,1,0:T(8,128)} fusion(f32[8,32,512]{2,1,0:T(8,128)S(1)} %copy-done, f32[8,8,512]{2,1,0:T(8,128)S(1)} %get-tuple-element.38, f32[8,32,512]{2,1,0:T(8,128)S(1)} %reshape_squeeze.14, f32[8,8,512]{2,1,0:T(8,128)S(1)} %get-tuple-element.37, f32[]{:T(128)S(6)} %mul.18, f32[]{:T(128)} %bitcast.171, ...), kind=kOutput, calls=%fused_computation.52 | convolution fusion | flops 76808192 | bytes 1841160 | tf_op jit(solution)/shard_map/rk,pkc->prc/dot_general | solution.py:48
  (99 shorter events, 2.8 us)
Async XLA Ops:
  0.6 7.7 %copy-start.1 = (f32[8,32,512]{2,1,0:T(8,128)S(1)}, f32[8,32,512]{2,1,0:T(8,128)}, u32[]{:S(2)}) copy-start(f32[8,32,512]{2,1,0:T(8,128)} %param.8) | copy-start | bytes 1572868
  0.6 8.0 %copy-start.3 = (f32[17]{0:T(128)S(1)}, f32[17]{0:T(128)}, u32[]{:S(2)}) copy-start(f32[17]{0:T(128)} %param.11) | copy-start | bytes 208
  1.7 7.1 %collective-permute-start = (f32[8,8,512]{2,1,0:T(8,128)S(1)}, f32[8,8,512]{2,1,0:T(8,128)S(1)}, u32[]{:S(2)}, u32[]{:S(2)}) collective-permute-start(f32[8,8,512]{2,1,0:T(8,128)S(1)} %slice_select_fusion.1), channel_id=1, source_target_pairs={{0,1},{1,0},{2,3},{3,2},{4,5},{5,4},{6,7},{7,6},{8,9},{9,8},{10,11... | collective-permute-start | bytes 393224 | tf_op jit(solution)/shard_map/ppermute | solution.py:16
  4.7 4.1 %copy-start = (f32[8,32,512]{2,1,0:T(8,128)S(1)}, f32[8,32,512]{2,1,0:T(8,128)}, u32[]{:S(2)}) copy-start(f32[8,32,512]{2,1,0:T(8,128)} %param.7) | copy-start | bytes 1572868
  11.0 6.5 %collective-permute-start.1 = (f32[2,8,1024]{2,1,0:T(8,128)S(1)}, f32[2,8,1024]{2,1,0:T(8,128)S(1)}, u32[]{:S(2)}, u32[]{:S(2)}) collective-permute-start(f32[2,8,1024]{2,1,0:T(8,128)S(1)} %bitcast.193), channel_id=1, source_target_pairs={{0,2},{2,4},{4,6},{6,8},{8,10},{10,12},{12,14},{14,16},{16,18},{18... | collective-permute-start | bytes 196616 | tf_op jit(solution)/shard_map/ppermute | solution.py:33
  11.1 7.6 %collective-permute-start.2 = (f32[2,8,1024]{2,1,0:T(8,128)S(1)}, f32[2,8,1024]{2,1,0:T(8,128)S(1)}, u32[]{:S(2)}, u32[]{:S(2)}) collective-permute-start(f32[2,8,1024]{2,1,0:T(8,128)S(1)} %bitcast.192), channel_id=1, source_target_pairs={{0,4},{2,6},{4,8},{6,10},{8,12},{10,14},{12,16},{14,18},{16,20},{1... | collective-permute-start | bytes 196616 | tf_op jit(solution)/shard_map/ppermute | solution.py:33
  12.7 10.4 %collective-permute-start.3 = (f32[2,8,1024]{2,1,0:T(8,128)S(1)}, f32[2,8,1024]{2,1,0:T(8,128)S(1)}, u32[]{:S(2)}, u32[]{:S(2)}) collective-permute-start(f32[2,8,1024]{2,1,0:T(8,128)S(1)} %bitcast.191), channel_id=1, source_target_pairs={{0,6},{2,8},{4,10},{6,12},{8,14},{10,16},{12,18},{14,20},{16,22},{... | collective-permute-start | bytes 196616 | tf_op jit(solution)/shard_map/ppermute | solution.py:33
  15.2 8.3 %collective-permute-start.4 = (f32[2,8,1024]{2,1,0:T(8,128)S(1)}, f32[2,8,1024]{2,1,0:T(8,128)S(1)}, u32[]{:S(2)}, u32[]{:S(2)}) collective-permute-start(f32[2,8,1024]{2,1,0:T(8,128)S(1)} %bitcast.190), channel_id=1, source_target_pairs={{0,8},{2,10},{4,12},{6,14},{8,16},{10,18},{12,20},{14,22},{16,24},... | collective-permute-start | bytes 196616 | tf_op jit(solution)/shard_map/ppermute | solution.py:33
  16.9 13.1 %collective-permute-start.5 = (f32[2,8,1024]{2,1,0:T(8,128)S(1)}, f32[2,8,1024]{2,1,0:T(8,128)S(1)}, u32[]{:S(2)}, u32[]{:S(2)}) collective-permute-start(f32[2,8,1024]{2,1,0:T(8,128)S(1)} %bitcast.189), channel_id=1, source_target_pairs={{0,10},{2,12},{4,14},{6,16},{8,18},{10,20},{12,22},{14,24},{16,26}... | collective-permute-start | bytes 196616 | tf_op jit(solution)/shard_map/ppermute | solution.py:33
  17.4 24.4 %copy-start.2 = (s32[128]{0:T(128)S(1)}, s32[128]{0:T(128)}, u32[]{:S(2)}) copy-start(s32[128]{0:T(128)} %param.9) | copy-start | bytes 1540
  17.6 12.6 %collective-permute-start.6 = (f32[2,8,1024]{2,1,0:T(8,128)S(1)}, f32[2,8,1024]{2,1,0:T(8,128)S(1)}, u32[]{:S(2)}, u32[]{:S(2)}) collective-permute-start(f32[2,8,1024]{2,1,0:T(8,128)S(1)} %bitcast.188), channel_id=1, source_target_pairs={{0,12},{2,14},{4,16},{6,18},{8,20},{10,22},{12,24},{14,26},{16,28}... | collective-permute-start | bytes 196616 | tf_op jit(solution)/shard_map/ppermute | solution.py:33
  18.7 12.6 %collective-permute-start.7 = (f32[2,8,1024]{2,1,0:T(8,128)S(1)}, f32[2,8,1024]{2,1,0:T(8,128)S(1)}, u32[]{:S(2)}, u32[]{:S(2)}) collective-permute-start(f32[2,8,1024]{2,1,0:T(8,128)S(1)} %bitcast.187), channel_id=1, source_target_pairs={{0,14},{2,16},{4,18},{6,20},{8,22},{10,24},{12,26},{14,28},{16,30}... | collective-permute-start | bytes 196616 | tf_op jit(solution)/shard_map/ppermute | solution.py:33
  23.2 9.4 %collective-permute-start.8 = (f32[2,8,1024]{2,1,0:T(8,128)S(1)}, f32[2,8,1024]{2,1,0:T(8,128)S(1)}, u32[]{:S(2)}, u32[]{:S(2)}) collective-permute-start(f32[2,8,1024]{2,1,0:T(8,128)S(1)} %bitcast.186), channel_id=1, source_target_pairs={{0,16},{2,18},{4,20},{6,22},{8,24},{10,26},{12,28},{14,30},{16,0},... | collective-permute-start | bytes 196616 | tf_op jit(solution)/shard_map/ppermute | solution.py:33
  23.6 11.4 %collective-permute-start.9 = (f32[2,8,1024]{2,1,0:T(8,128)S(1)}, f32[2,8,1024]{2,1,0:T(8,128)S(1)}, u32[]{:S(2)}, u32[]{:S(2)}) collective-permute-start(f32[2,8,1024]{2,1,0:T(8,128)S(1)} %bitcast.185), channel_id=1, source_target_pairs={{0,18},{2,20},{4,22},{6,24},{8,26},{10,28},{12,30},{14,0},{16,2},{... | collective-permute-start | bytes 196616 | tf_op jit(solution)/shard_map/ppermute | solution.py:33
  29.9 7.7 %collective-permute-start.10 = (f32[2,8,1024]{2,1,0:T(8,128)S(1)}, f32[2,8,1024]{2,1,0:T(8,128)S(1)}, u32[]{:S(2)}, u32[]{:S(2)}) collective-permute-start(f32[2,8,1024]{2,1,0:T(8,128)S(1)} %bitcast.184), channel_id=1, source_target_pairs={{0,20},{2,22},{4,24},{6,26},{8,28},{10,30},{12,0},{14,2},{16,4},{1... | collective-permute-start | bytes 196616 | tf_op jit(solution)/shard_map/ppermute | solution.py:33
  30.1 8.5 %collective-permute-start.11 = (f32[2,8,1024]{2,1,0:T(8,128)S(1)}, f32[2,8,1024]{2,1,0:T(8,128)S(1)}, u32[]{:S(2)}, u32[]{:S(2)}) collective-permute-start(f32[2,8,1024]{2,1,0:T(8,128)S(1)} %bitcast.183), channel_id=1, source_target_pairs={{0,22},{2,24},{4,26},{6,28},{8,30},{10,0},{12,2},{14,4},{16,6},{18... | collective-permute-start | bytes 196616 | tf_op jit(solution)/shard_map/ppermute | solution.py:33
  31.3 7.3 %collective-permute-start.12 = (f32[2,8,1024]{2,1,0:T(8,128)S(1)}, f32[2,8,1024]{2,1,0:T(8,128)S(1)}, u32[]{:S(2)}, u32[]{:S(2)}) collective-permute-start(f32[2,8,1024]{2,1,0:T(8,128)S(1)} %bitcast.182), channel_id=1, source_target_pairs={{0,24},{2,26},{4,28},{6,30},{8,0},{10,2},{12,4},{14,6},{16,8},{18,... | collective-permute-start | bytes 196616 | tf_op jit(solution)/shard_map/ppermute | solution.py:33
  32.6 6.1 %collective-permute-start.13 = (f32[2,8,1024]{2,1,0:T(8,128)S(1)}, f32[2,8,1024]{2,1,0:T(8,128)S(1)}, u32[]{:S(2)}, u32[]{:S(2)}) collective-permute-start(f32[2,8,1024]{2,1,0:T(8,128)S(1)} %bitcast.181), channel_id=1, source_target_pairs={{0,26},{2,28},{4,30},{6,0},{8,2},{10,4},{12,6},{14,8},{16,10},{18,... | collective-permute-start | bytes 196616 | tf_op jit(solution)/shard_map/ppermute | solution.py:33
  35.0 6.8 %collective-permute-start.14 = (f32[2,8,1024]{2,1,0:T(8,128)S(1)}, f32[2,8,1024]{2,1,0:T(8,128)S(1)}, u32[]{:S(2)}, u32[]{:S(2)}) collective-permute-start(f32[2,8,1024]{2,1,0:T(8,128)S(1)} %bitcast.180), channel_id=1, source_target_pairs={{0,28},{2,30},{4,0},{6,2},{8,4},{10,6},{12,8},{14,10},{16,12},{18,... | collective-permute-start | bytes 196616 | tf_op jit(solution)/shard_map/ppermute | solution.py:33
  37.7 4.1 %collective-permute-start.15 = (f32[2,8,1024]{2,1,0:T(8,128)S(1)}, f32[2,8,1024]{2,1,0:T(8,128)S(1)}, u32[]{:S(2)}, u32[]{:S(2)}) collective-permute-start(f32[2,8,1024]{2,1,0:T(8,128)S(1)} %bitcast.179), channel_id=1, source_target_pairs={{0,30},{2,0},{4,2},{6,4},{8,6},{10,8},{12,10},{14,12},{16,14},{18,... | collective-permute-start | bytes 196616 | tf_op jit(solution)/shard_map/ppermute | solution.py:33
  43.3 31.2 %collective-permute-start.26 = (f32[2,8,1024]{2,1,0:T(8,128)S(1)}, f32[2,8,1024]{2,1,0:T(8,128)S(1)}, u32[]{:S(2)}, u32[]{:S(2)}) collective-permute-start(f32[2,8,1024]{2,1,0:T(8,128)S(1)} %get-tuple-element.19), channel_id=1, source_target_pairs={{0,22},{2,24},{4,26},{6,28},{8,30},{10,0},{12,2},{14,4},{16,6},{18... | collective-permute-start | bytes 196616 | tf_op jit(solution)/shard_map/ppermute | solution.py:33
  46.3 16.6 %collective-permute-start.21 = (f32[2,8,1024]{2,1,0:T(8,128)S(1)}, f32[2,8,1024]{2,1,0:T(8,128)S(1)}, u32[]{:S(2)}, u32[]{:S(2)}) collective-permute-start(f32[2,8,1024]{2,1,0:T(8,128)S(1)} %get-tuple-element.13), channel_id=1, source_target_pairs={{0,12},{2,14},{4,16},{6,18},{8,20},{10,22},{12,24},{14,26},{16,28}... | collective-permute-start | bytes 196616 | tf_op jit(solution)/shard_map/ppermute | solution.py:33
  46.5 7.0 %collective-permute-start.16 = (f32[2,8,1024]{2,1,0:T(8,128)S(1)}, f32[2,8,1024]{2,1,0:T(8,128)S(1)}, u32[]{:S(2)}, u32[]{:S(2)}) collective-permute-start(f32[2,8,1024]{2,1,0:T(8,128)S(1)} %get-tuple-element.7), channel_id=1, source_target_pairs={{0,2},{2,4},{4,6},{6,8},{8,10},{10,12},{12,14},{14,16},{16,18},{18... | collective-permute-start | bytes 196616 | tf_op jit(solution)/shard_map/ppermute | solution.py:33
  47.1 7.3 %collective-permute-start.17 = (f32[2,8,1024]{2,1,0:T(8,128)S(1)}, f32[2,8,1024]{2,1,0:T(8,128)S(1)}, u32[]{:S(2)}, u32[]{:S(2)}) collective-permute-start(f32[2,8,1024]{2,1,0:T(8,128)S(1)} %get-tuple-element.8), channel_id=1, source_target_pairs={{0,4},{2,6},{4,8},{6,10},{8,12},{10,14},{12,16},{14,18},{16,20},{1... | collective-permute-start | bytes 196616 | tf_op jit(solution)/shard_map/ppermute | solution.py:33
  49.7 5.5 %collective-permute-start.18 = (f32[2,8,1024]{2,1,0:T(8,128)S(1)}, f32[2,8,1024]{2,1,0:T(8,128)S(1)}, u32[]{:S(2)}, u32[]{:S(2)}) collective-permute-start(f32[2,8,1024]{2,1,0:T(8,128)S(1)} %get-tuple-element.9), channel_id=1, source_target_pairs={{0,6},{2,8},{4,10},{6,12},{8,14},{10,16},{12,18},{14,20},{16,22},{... | collective-permute-start | bytes 196616 | tf_op jit(solution)/shard_map/ppermute | solution.py:33
  53.5 6.1 %collective-permute-start.19 = (f32[2,8,1024]{2,1,0:T(8,128)S(1)}, f32[2,8,1024]{2,1,0:T(8,128)S(1)}, u32[]{:S(2)}, u32[]{:S(2)}) collective-permute-start(f32[2,8,1024]{2,1,0:T(8,128)S(1)} %get-tuple-element.10), channel_id=1, source_target_pairs={{0,8},{2,10},{4,12},{6,14},{8,16},{10,18},{12,20},{14,22},{16,24},... | collective-permute-start | bytes 196616 | tf_op jit(solution)/shard_map/ppermute | solution.py:33
  54.4 8.5 %collective-permute-start.20 = (f32[2,8,1024]{2,1,0:T(8,128)S(1)}, f32[2,8,1024]{2,1,0:T(8,128)S(1)}, u32[]{:S(2)}, u32[]{:S(2)}) collective-permute-start(f32[2,8,1024]{2,1,0:T(8,128)S(1)} %get-tuple-element.11), channel_id=1, source_target_pairs={{0,10},{2,12},{4,14},{6,16},{8,18},{10,20},{12,22},{14,24},{16,26}... | collective-permute-start | bytes 196616 | tf_op jit(solution)/shard_map/ppermute | solution.py:33
  55.2 9.4 %collective-permute-start.22 = (f32[2,8,1024]{2,1,0:T(8,128)S(1)}, f32[2,8,1024]{2,1,0:T(8,128)S(1)}, u32[]{:S(2)}, u32[]{:S(2)}) collective-permute-start(f32[2,8,1024]{2,1,0:T(8,128)S(1)} %get-tuple-element.14), channel_id=1, source_target_pairs={{0,14},{2,16},{4,18},{6,20},{8,22},{10,24},{12,26},{14,28},{16,30}... | collective-permute-start | bytes 196616 | tf_op jit(solution)/shard_map/ppermute | solution.py:33
  59.5 8.9 %collective-permute-start.23 = (f32[2,8,1024]{2,1,0:T(8,128)S(1)}, f32[2,8,1024]{2,1,0:T(8,128)S(1)}, u32[]{:S(2)}, u32[]{:S(2)}) collective-permute-start(f32[2,8,1024]{2,1,0:T(8,128)S(1)} %get-tuple-element.15), channel_id=1, source_target_pairs={{0,16},{2,18},{4,20},{6,22},{8,24},{10,26},{12,28},{14,30},{16,0},... | collective-permute-start | bytes 196616 | tf_op jit(solution)/shard_map/ppermute | solution.py:33
  62.9 7.0 %collective-permute-start.24 = (f32[2,8,1024]{2,1,0:T(8,128)S(1)}, f32[2,8,1024]{2,1,0:T(8,128)S(1)}, u32[]{:S(2)}, u32[]{:S(2)}) collective-permute-start(f32[2,8,1024]{2,1,0:T(8,128)S(1)} %get-tuple-element.16), channel_id=1, source_target_pairs={{0,18},{2,20},{4,22},{6,24},{8,26},{10,28},{12,30},{14,0},{16,2},{... | collective-permute-start | bytes 196616 | tf_op jit(solution)/shard_map/ppermute | solution.py:33
  62.9 7.1 %collective-permute-start.25 = (f32[2,8,1024]{2,1,0:T(8,128)S(1)}, f32[2,8,1024]{2,1,0:T(8,128)S(1)}, u32[]{:S(2)}, u32[]{:S(2)}) collective-permute-start(f32[2,8,1024]{2,1,0:T(8,128)S(1)} %get-tuple-element.17), channel_id=1, source_target_pairs={{0,20},{2,22},{4,24},{6,26},{8,28},{10,30},{12,0},{14,2},{16,4},{1... | collective-permute-start | bytes 196616 | tf_op jit(solution)/shard_map/ppermute | solution.py:33
  64.6 9.9 %collective-permute-start.27 = (f32[2,8,1024]{2,1,0:T(8,128)S(1)}, f32[2,8,1024]{2,1,0:T(8,128)S(1)}, u32[]{:S(2)}, u32[]{:S(2)}) collective-permute-start(f32[2,8,1024]{2,1,0:T(8,128)S(1)} %get-tuple-element.20), channel_id=1, source_target_pairs={{0,24},{2,26},{4,28},{6,30},{8,0},{10,2},{12,4},{14,6},{16,8},{18,... | collective-permute-start | bytes 196616 | tf_op jit(solution)/shard_map/ppermute | solution.py:33
  68.4 6.2 %collective-permute-start.28 = (f32[2,8,1024]{2,1,0:T(8,128)S(1)}, f32[2,8,1024]{2,1,0:T(8,128)S(1)}, u32[]{:S(2)}, u32[]{:S(2)}) collective-permute-start(f32[2,8,1024]{2,1,0:T(8,128)S(1)} %get-tuple-element.18), channel_id=1, source_target_pairs={{0,26},{2,28},{4,30},{6,0},{8,2},{10,4},{12,6},{14,8},{16,10},{18,... | collective-permute-start | bytes 196616 | tf_op jit(solution)/shard_map/ppermute | solution.py:33
  69.9 4.7 %collective-permute-start.29 = (f32[2,8,1024]{2,1,0:T(8,128)S(1)}, f32[2,8,1024]{2,1,0:T(8,128)S(1)}, u32[]{:S(2)}, u32[]{:S(2)}) collective-permute-start(f32[2,8,1024]{2,1,0:T(8,128)S(1)} %get-tuple-element.12), channel_id=1, source_target_pairs={{0,28},{2,30},{4,0},{6,2},{8,4},{10,6},{12,8},{14,10},{16,12},{18,... | collective-permute-start | bytes 196616 | tf_op jit(solution)/shard_map/ppermute | solution.py:33
  70.0 6.4 %collective-permute-start.30 = (f32[2,8,1024]{2,1,0:T(8,128)S(1)}, f32[2,8,1024]{2,1,0:T(8,128)S(1)}, u32[]{:S(2)}, u32[]{:S(2)}) collective-permute-start(f32[2,8,1024]{2,1,0:T(8,128)S(1)} %get-tuple-element.6), channel_id=1, source_target_pairs={{0,30},{2,0},{4,2},{6,4},{8,6},{10,8},{12,10},{14,12},{16,14},{18,... | collective-permute-start | bytes 196616 | tf_op jit(solution)/shard_map/ppermute | solution.py:33
  77.0 6.0 %collective-permute-start.31 = (f32[8,8,512]{2,1,0:T(8,128)S(1)}, f32[8,8,512]{2,1,0:T(8,128)S(1)}, u32[]{:S(2)}, u32[]{:S(2)}) collective-permute-start(f32[8,8,512]{2,1,0:T(8,128)S(1)} %slice_select_fusion), channel_id=1, source_target_pairs={{0,1},{1,0},{2,3},{3,2},{4,5},{5,4},{6,7},{7,6},{8,9},{9,8},{10,11... | collective-permute-start | bytes 393224 | tf_op jit(solution)/shard_map/ppermute | solution.py:16

commit v8 on v7

--- a/solution.py
+++ b/solution.py
@@ -67,30 +67,36 @@
     plane_count, row_count, width_count = estimate.shape
     flat_count = row_count * width_count
     halo_rows = lateral_psf.shape[0] // 2
+    scan_count = lax.axis_size("scan")
+    piece = flat_count // scan_count
+
+    def to_pencil(volume):
+        parts = volume.reshape(plane_count, scan_count, piece).transpose(1, 0, 2)
+        return ring_exchange(parts, "scan").reshape(scan_count * plane_count, piece)
+
+    def to_home(pencil_values):
+        parts = pencil_values.reshape(scan_count, plane_count, piece)
+        return ring_exchange(parts, "scan").transpose(1, 0, 2).reshape(plane_count, row_count, width_count)
+
+    raw_pencil = to_pencil(raw)
     sheet_psf = sheet_matrix(offsets, depth_psf, offsets.shape[0])
     blur_band = band_matrix(lateral_psf, row_count, 0)
     back_band = band_matrix(lateral_psf[::-1], row_count, 0)
     padded = with_halo(estimate, "row", halo_rows)
-    blurred = lateral_apply(blur_band, padded).reshape(plane_count, flat_count)
-    scan_count = lax.axis_size("scan")
-    both_flat = jnp.stack([blurred, raw.reshape(plane_count, flat_count)])
-    outgoing = both_flat.reshape(2, plane_count, scan_count, flat_count // scan_count).transpose(2, 0, 1, 3)
-    both_in = ring_exchange(outgoing, "scan")
-    pencil = both_in[:, 0].reshape(offsets.shape[0], -1)
-    raw_pencil = both_in[:, 1].reshape(offsets.shape[0], -1)
+    blurred = lateral_apply(blur_band, padded)
+    pencil = to_pencil(blurred)
     predicted_pencil = jnp.dot(sheet_psf, pencil, precision=highest_mode)
     misfit_pencil = predicted_pencil - raw_pencil
     back_pencil = transpose_apply(sheet_psf, misfit_pencil)
-    results = jnp.stack([misfit_pencil, back_pencil]).reshape(2, scan_count, plane_count, -1).transpose(1, 0, 2, 3)
-    both_out = ring_exchange(results, "scan").transpose(1, 2, 0, 3).reshape(2, plane_count, flat_count)
-    misfit = both_out[0]
-    back_volume = both_out[1].reshape(plane_count, row_count, width_count)
+    back_volume = to_home(back_pencil)
+    back_volume, misfit_pencil = lax.optimization_barrier((back_volume, misfit_pencil))
+    misfit = to_home(misfit_pencil)
     padded_back = with_halo(back_volume, "row", halo_rows)
     gradient = lateral_apply(back_band, padded_back)
     stepped = estimate - step_size[0] * gradient
     shrink_level = step_size[0] * threshold[0]
     new_estimate = jnp.sign(stepped) * jnp.maximum(jnp.abs(stepped) - shrink_level, 0.0)
-    return (new_estimate, misfit.reshape(plane_count, row_count, width_count))
+    return (new_estimate, misfit)
 
 
 def solution(mesh):

time: 84.9 us -> 115 us (1.35)
  starting transfers between devices: 44.2 us -> 90.2 us
  waiting for transfers between devices: 25.2 us -> 10.7 us
  other arithmetic: 4.14 us -> 2.68 us
    ppermute x30 -> x60, starting transfers between devices: 39.9 us -> 85.6 us  [ring_exchange(): lax.ppermute(piece, axis, [(j, (j + shift) % count) for j in range(count)])]
    ppermute x30 -> x60, waiting for transfers between devices: 22.8 us -> 7.06 us  [ring_exchange(): lax.ppermute(piece, axis, [(j, (j + shift) % count) for j in range(count)])]
    ppermute x2, waiting for transfers between devices: 2.31 us -> 3.6 us  [with_halo(): arrived = lax.ppermute(jnp.where(first, tail, head), axis, [(0, 1), (1, 0)])]
    reshape x0 -> x4, local copies, waits for them, and re-layouts: none -> 1.29 us  [the longest x2 0.95 us: to_home(): ring_exchange(parts, 'scan').transpose(1, 0, 2)]
    another operation x8 -> x5, local copies, waits for them, and re-layouts: 2.81 us -> 1.86 us
  transfers between devices with their start and end apart: 32 -> 62, of which waited for: 16 -> 9; matrix products, arithmetic and copies ran while one was open for 7% -> 3% of each run, Pallas kernels for 0% -> 0%
where the time goes in v8:
time: 115 us
  starting transfers between devices  90.2 us (78%)
  waiting for transfers between devices  10.7 us (9%)
  local copies, waits for them, and re-layouts  4.69 us (4%)
  matrix products  3.63 us (3%)
  between operations  2.9 us (3%)
  other arithmetic  2.68 us (2%)
    ppermute x60, starting transfers between devices, ring_exchange(): lax.ppermute(piece, axis, [(j, (j + shift) % count) for j in range(count)])  85.6 us
    ppermute x60, waiting for transfers between devices, ring_exchange(): lax.ppermute(piece, axis, [(j, (j + shift) % count) for j in range(count)])  7.06 us
    ppermute x2, starting transfers between devices, with_halo(): arrived = lax.ppermute(jnp.where(first, tail, head), axis, [(0, 1), (1, 0)])  4.56 us
    ppermute x2, waiting for transfers between devices, with_halo(): arrived = lax.ppermute(jnp.where(first, tail, head), axis, [(0, 1), (1, 0)])  3.6 us
  transfers between devices with their start and end apart: 62, of which 9 were waited for; matrix products, arithmetic and copies ran while one was open for 3% of the time, Pallas kernels for 0%

profile of v8, /device:TPU:0, one launch (start us, length us, event | category | flops | bytes accessed | tf_op | source)
XLA Modules:
  0.0 114.8 jit_solution(14899679795944827918)
XLA Ops:
  0.7 1.0 slice_select_fusion.1
  1.7 3.0 %collective-permute-start = (f32[8,8,512]{2,1,0:T(8,128)S(1)}, f32[8,8,512]{2,1,0:T(8,128)S(1)}, u32[]{:S(2)}, u32[]{:S(2)}) collective-permute-start(f32[8,8,512]{2,1,0:T(8,128)S(1)} %slice_select_fusion.1), channel_id=1, source_target_pairs={{0,1},{1,0},{2,3},{3,2},{4,5},{5,4},{6,7},{7,6},{8,9},{9,8},{10,11... | collective-permute-start | bytes 393224 | tf_op jit(solution)/shard_map/ppermute | solution.py:16
  4.8 1.4 %select_reduce_fusion = f32[128,128]{1,0:T(8,128)S(1)} fusion(f32[64]{0:T(128)S(1)} %copy-done.3, s32[128,128]{1,0:T(8,128)S(1)} %subtract_subtract_fusion), kind=kLoop, calls=%fused_computation | loop fusion | flops 3129344 | bytes 131328 | tf_op jit(solution)/shard_map/reduce_sum | solution.py:59
  6.8 1.4 %collective-permute-done = f32[8,8,512]{2,1,0:T(8,128)S(1)} collective-permute-done((f32[8,8,512]{2,1,0:T(8,128)S(1)}, f32[8,8,512]{2,1,0:T(8,128)S(1)}, u32[]{:S(2)}, u32[]{:S(2)}) %collective-permute-start) | collective-permute-done | bytes 131104 | tf_op jit(solution)/shard_map/ppermute | solution.py:16
  9.1 1.7 %constant_dynamic-slice_fusion = (f32[8,1,1024]{2,1,0:T(1,128)S(1)}, f32[8,1,1024]{2,1,0:T(1,128)S(1)}, f32[8,1,1024]{2,1,0:T(1,128)S(1)}, f32[8,1,1024]{2,1,0:T...) fusion(f32[8,16,1024]{2,1,0:T(8,128)S(1)} %reshape.131, ...), kind=kLoop, calls=%fused_computation.156 | loop fusion | bytes 2097216 | tf_op jit(solution)/shard_map/dynamic-slice.31
  10.9 1.8 %collective-permute-start.2 = (f32[8,1024]{1,0:T(8,128)S(1)}, f32[8,1024]{1,0:T(8,128)S(1)}, u32[]{:S(2)}, u32[]{:S(2)}) collective-permute-start(f32[8,1024]{1,0:T(8,128)S(1)} %bitcast.337), channel_id=1, source_target_pairs={{0,4},{2,6},{4,8},{6,10},{8,12},{10,14},{12,16},{14,18},{16,20},{1... | collective-permute-start | bytes 98312 | tf_op jit(solution)/shard_map/ppermute | solution.py:33
  12.7 2.5 %collective-permute-start.3 = (f32[8,1024]{1,0:T(8,128)S(1)}, f32[8,1024]{1,0:T(8,128)S(1)}, u32[]{:S(2)}, u32[]{:S(2)}) collective-permute-start(f32[8,1024]{1,0:T(8,128)S(1)} %bitcast.336), channel_id=1, source_target_pairs={{0,6},{2,8},{4,10},{6,12},{8,14},{10,16},{12,18},{14,20},{16,22},{... | collective-permute-start | bytes 98312 | tf_op jit(solution)/shard_map/ppermute | solution.py:33
  15.2 1.6 %collective-permute-start.4 = (f32[8,1024]{1,0:T(8,128)S(1)}, f32[8,1024]{1,0:T(8,128)S(1)}, u32[]{:S(2)}, u32[]{:S(2)}) collective-permute-start(f32[8,1024]{1,0:T(8,128)S(1)} %bitcast.335), channel_id=1, source_target_pairs={{0,8},{2,10},{4,12},{6,14},{8,16},{10,18},{12,20},{14,22},{16,24},... | collective-permute-start | bytes 98312 | tf_op jit(solution)/shard_map/ppermute | solution.py:33
  17.7 1.2 %collective-permute-start.6 = (f32[8,1024]{1,0:T(8,128)S(1)}, f32[8,1024]{1,0:T(8,128)S(1)}, u32[]{:S(2)}, u32[]{:S(2)}) collective-permute-start(f32[8,1024]{1,0:T(8,128)S(1)} %bitcast.334), channel_id=1, source_target_pairs={{0,12},{2,14},{4,16},{6,18},{8,20},{10,22},{12,24},{14,26},{16,28}... | collective-permute-start | bytes 98312 | tf_op jit(solution)/shard_map/ppermute | solution.py:33
  18.9 4.4 %collective-permute-start.7 = (f32[8,1024]{1,0:T(8,128)S(1)}, f32[8,1024]{1,0:T(8,128)S(1)}, u32[]{:S(2)}, u32[]{:S(2)}) collective-permute-start(f32[8,1024]{1,0:T(8,128)S(1)} %bitcast.332), channel_id=1, source_target_pairs={{0,14},{2,16},{4,18},{6,20},{8,22},{10,24},{12,26},{14,28},{16,30}... | collective-permute-start | bytes 98312 | tf_op jit(solution)/shard_map/ppermute | solution.py:33
  24.0 2.5 %collective-permute-start.10 = (f32[8,1024]{1,0:T(8,128)S(1)}, f32[8,1024]{1,0:T(8,128)S(1)}, u32[]{:S(2)}, u32[]{:S(2)}) collective-permute-start(f32[8,1024]{1,0:T(8,128)S(1)} %bitcast.329), channel_id=1, source_target_pairs={{0,20},{2,22},{4,24},{6,26},{8,28},{10,30},{12,0},{14,2},{16,4},{1... | collective-permute-start | bytes 98312 | tf_op jit(solution)/shard_map/ppermute | solution.py:33
  26.5 2.9 %collective-permute-start.11 = (f32[8,1024]{1,0:T(8,128)S(1)}, f32[8,1024]{1,0:T(8,128)S(1)}, u32[]{:S(2)}, u32[]{:S(2)}) collective-permute-start(f32[8,1024]{1,0:T(8,128)S(1)} %bitcast.328), channel_id=1, source_target_pairs={{0,22},{2,24},{4,26},{6,28},{8,30},{10,0},{12,2},{14,4},{16,6},{18... | collective-permute-start | bytes 98312 | tf_op jit(solution)/shard_map/ppermute | solution.py:33
  29.4 1.9 %collective-permute-start.12 = (f32[8,1024]{1,0:T(8,128)S(1)}, f32[8,1024]{1,0:T(8,128)S(1)}, u32[]{:S(2)}, u32[]{:S(2)}) collective-permute-start(f32[8,1024]{1,0:T(8,128)S(1)} %bitcast.327), channel_id=1, source_target_pairs={{0,24},{2,26},{4,28},{6,30},{8,0},{10,2},{12,4},{14,6},{16,8},{18,... | collective-permute-start | bytes 98312 | tf_op jit(solution)/shard_map/ppermute | solution.py:33
  31.4 1.5 %collective-permute-start.14 = (f32[8,1024]{1,0:T(8,128)S(1)}, f32[8,1024]{1,0:T(8,128)S(1)}, u32[]{:S(2)}, u32[]{:S(2)}) collective-permute-start(f32[8,1024]{1,0:T(8,128)S(1)} %bitcast.325), channel_id=1, source_target_pairs={{0,28},{2,30},{4,0},{6,2},{8,4},{10,6},{12,8},{14,10},{16,12},{18,... | collective-permute-start | bytes 98312 | tf_op jit(solution)/shard_map/ppermute | solution.py:33
  32.8 2.3 %collective-permute-start.15 = (f32[8,1024]{1,0:T(8,128)S(1)}, f32[8,1024]{1,0:T(8,128)S(1)}, u32[]{:S(2)}, u32[]{:S(2)}) collective-permute-start(f32[8,1024]{1,0:T(8,128)S(1)} %bitcast.324), channel_id=1, source_target_pairs={{0,30},{2,0},{4,2},{6,4},{8,6},{10,8},{12,10},{14,12},{16,14},{18,... | collective-permute-start | bytes 98312 | tf_op jit(solution)/shard_map/ppermute | solution.py:33
  35.9 1.6 %collective-permute-start.18 = (f32[8,1024]{1,0:T(8,128)S(1)}, f32[8,1024]{1,0:T(8,128)S(1)}, u32[]{:S(2)}, u32[]{:S(2)}) collective-permute-start(f32[8,1024]{1,0:T(8,128)S(1)} %bitcast.321), channel_id=1, source_target_pairs={{0,6},{2,8},{4,10},{6,12},{8,14},{10,16},{12,18},{14,20},{16,22},{... | collective-permute-start | bytes 98312 | tf_op jit(solution)/shard_map/ppermute | solution.py:33
  38.5 2.7 %collective-permute-done.16 = f32[8,1024]{1,0:T(8,128)S(1)} collective-permute-done((f32[8,1024]{1,0:T(8,128)S(1)}, f32[8,1024]{1,0:T(8,128)S(1)}, u32[]{:S(2)}, u32[]{:S(2)}) %collective-permute-start.16) | collective-permute-done | bytes 32800 | tf_op jit(solution)/shard_map/ppermute | solution.py:33
  41.2 1.0 collective-permute-start.21
  42.2 1.4 %collective-permute-start.22 = (f32[8,1024]{1,0:T(8,128)S(1)}, f32[8,1024]{1,0:T(8,128)S(1)}, u32[]{:S(2)}, u32[]{:S(2)}) collective-permute-start(f32[8,1024]{1,0:T(8,128)S(1)} %bitcast.317), channel_id=1, source_target_pairs={{0,14},{2,16},{4,18},{6,20},{8,22},{10,24},{12,26},{14,28},{16,30}... | collective-permute-start | bytes 98312 | tf_op jit(solution)/shard_map/ppermute | solution.py:33
  43.6 2.6 %collective-permute-start.23 = (f32[8,1024]{1,0:T(8,128)S(1)}, f32[8,1024]{1,0:T(8,128)S(1)}, u32[]{:S(2)}, u32[]{:S(2)}) collective-permute-start(f32[8,1024]{1,0:T(8,128)S(1)} %bitcast.316), channel_id=1, source_target_pairs={{0,16},{2,18},{4,20},{6,22},{8,24},{10,26},{12,28},{14,30},{16,0},... | collective-permute-start | bytes 98312 | tf_op jit(solution)/shard_map/ppermute | solution.py:33
  46.3 2.0 %collective-permute-start.25 = (f32[8,1024]{1,0:T(8,128)S(1)}, f32[8,1024]{1,0:T(8,128)S(1)}, u32[]{:S(2)}, u32[]{:S(2)}) collective-permute-start(f32[8,1024]{1,0:T(8,128)S(1)} %bitcast.314), channel_id=1, source_target_pairs={{0,20},{2,22},{4,24},{6,26},{8,28},{10,30},{12,0},{14,2},{16,4},{1... | collective-permute-start | bytes 98312 | tf_op jit(solution)/shard_map/ppermute | solution.py:33
  48.5 3.5 %collective-permute-start.26 = (f32[8,1024]{1,0:T(8,128)S(1)}, f32[8,1024]{1,0:T(8,128)S(1)}, u32[]{:S(2)}, u32[]{:S(2)}) collective-permute-start(f32[8,1024]{1,0:T(8,128)S(1)} %bitcast.313), channel_id=1, source_target_pairs={{0,22},{2,24},{4,26},{6,28},{8,30},{10,0},{12,2},{14,4},{16,6},{18... | collective-permute-start | bytes 98312 | tf_op jit(solution)/shard_map/ppermute | solution.py:33
  52.1 1.2 %collective-permute-start.28 = (f32[8,1024]{1,0:T(8,128)S(1)}, f32[8,1024]{1,0:T(8,128)S(1)}, u32[]{:S(2)}, u32[]{:S(2)}) collective-permute-start(f32[8,1024]{1,0:T(8,128)S(1)} %bitcast.311), channel_id=1, source_target_pairs={{0,26},{2,28},{4,30},{6,0},{8,2},{10,4},{12,6},{14,8},{16,10},{18,... | collective-permute-start | bytes 98312 | tf_op jit(solution)/shard_map/ppermute | solution.py:33
  53.3 1.4 %collective-permute-start.29 = (f32[8,1024]{1,0:T(8,128)S(1)}, f32[8,1024]{1,0:T(8,128)S(1)}, u32[]{:S(2)}, u32[]{:S(2)}) collective-permute-start(f32[8,1024]{1,0:T(8,128)S(1)} %bitcast.310), channel_id=1, source_target_pairs={{0,28},{2,30},{4,0},{6,2},{8,4},{10,6},{12,8},{14,10},{16,12},{18,... | collective-permute-start | bytes 98312 | tf_op jit(solution)/shard_map/ppermute | solution.py:33
  54.7 2.3 %collective-permute-start.30 = (f32[8,1024]{1,0:T(8,128)S(1)}, f32[8,1024]{1,0:T(8,128)S(1)}, u32[]{:S(2)}, u32[]{:S(2)}) collective-permute-start(f32[8,1024]{1,0:T(8,128)S(1)} %bitcast.309), channel_id=1, source_target_pairs={{0,30},{2,0},{4,2},{6,4},{8,6},{10,8},{12,10},{14,12},{16,14},{18,... | collective-permute-start | bytes 98312 | tf_op jit(solution)/shard_map/ppermute | solution.py:33
  57.3 1.3 %collective-permute-done.30 = f32[8,1024]{1,0:T(8,128)S(1)} collective-permute-done((f32[8,1024]{1,0:T(8,128)S(1)}, f32[8,1024]{1,0:T(8,128)S(1)}, u32[]{:S(2)}, u32[]{:S(2)}) %collective-permute-start.30) | collective-permute-done | bytes 32800 | tf_op jit(solution)/shard_map/ppermute | solution.py:33
  62.1 1.5 %collective-permute-start.32 = (f32[8,1024]{1,0:T(8,128)S(1)}, f32[8,1024]{1,0:T(8,128)S(1)}, u32[]{:S(2)}, u32[]{:S(2)}) collective-permute-start(f32[8,1024]{1,0:T(8,128)S(1)} %get-tuple-element.37), channel_id=1, source_target_pairs={{0,4},{2,6},{4,8},{6,10},{8,12},{10,14},{12,16},{14,18},{16,20},{1... | collective-permute-start | bytes 98312 | tf_op jit(solution)/shard_map/ppermute | solution.py:33
  63.8 1.8 %collective-permute-start.34 = (f32[8,1024]{1,0:T(8,128)S(1)}, f32[8,1024]{1,0:T(8,128)S(1)}, u32[]{:S(2)}, u32[]{:S(2)}) collective-permute-start(f32[8,1024]{1,0:T(8,128)S(1)} %get-tuple-element.35), channel_id=1, source_target_pairs={{0,8},{2,10},{4,12},{6,14},{8,16},{10,18},{12,20},{14,22},{16,24},... | collective-permute-start | bytes 98312 | tf_op jit(solution)/shard_map/ppermute | solution.py:33
  65.6 1.8 %collective-permute-start.35 = (f32[8,1024]{1,0:T(8,128)S(1)}, f32[8,1024]{1,0:T(8,128)S(1)}, u32[]{:S(2)}, u32[]{:S(2)}) collective-permute-start(f32[8,1024]{1,0:T(8,128)S(1)} %get-tuple-element.34), channel_id=1, source_target_pairs={{0,10},{2,12},{4,14},{6,16},{8,18},{10,20},{12,22},{14,24},{16,26}... | collective-permute-start | bytes 98312 | tf_op jit(solution)/shard_map/ppermute | solution.py:33
  69.1 1.5 %collective-permute-start.37 = (f32[8,1024]{1,0:T(8,128)S(1)}, f32[8,1024]{1,0:T(8,128)S(1)}, u32[]{:S(2)}, u32[]{:S(2)}) collective-permute-start(f32[8,1024]{1,0:T(8,128)S(1)} %get-tuple-element.32), channel_id=1, source_target_pairs={{0,14},{2,16},{4,18},{6,20},{8,22},{10,24},{12,26},{14,28},{16,30}... | collective-permute-start | bytes 98312 | tf_op jit(solution)/shard_map/ppermute | solution.py:33
  70.6 1.6 %collective-permute-start.38 = (f32[8,1024]{1,0:T(8,128)S(1)}, f32[8,1024]{1,0:T(8,128)S(1)}, u32[]{:S(2)}, u32[]{:S(2)}) collective-permute-start(f32[8,1024]{1,0:T(8,128)S(1)} %get-tuple-element.31), channel_id=1, source_target_pairs={{0,16},{2,18},{4,20},{6,22},{8,24},{10,26},{12,28},{14,30},{16,0},... | collective-permute-start | bytes 98312 | tf_op jit(solution)/shard_map/ppermute | solution.py:33
  72.8 3.1 %collective-permute-start.40 = (f32[8,1024]{1,0:T(8,128)S(1)}, f32[8,1024]{1,0:T(8,128)S(1)}, u32[]{:S(2)}, u32[]{:S(2)}) collective-permute-start(f32[8,1024]{1,0:T(8,128)S(1)} %get-tuple-element.29), channel_id=1, source_target_pairs={{0,20},{2,22},{4,24},{6,26},{8,28},{10,30},{12,0},{14,2},{16,4},{1... | collective-permute-start | bytes 98312 | tf_op jit(solution)/shard_map/ppermute | solution.py:33
  75.8 3.0 %collective-permute-start.41 = (f32[8,1024]{1,0:T(8,128)S(1)}, f32[8,1024]{1,0:T(8,128)S(1)}, u32[]{:S(2)}, u32[]{:S(2)}) collective-permute-start(f32[8,1024]{1,0:T(8,128)S(1)} %get-tuple-element.28), channel_id=1, source_target_pairs={{0,22},{2,24},{4,26},{6,28},{8,30},{10,0},{12,2},{14,4},{16,6},{18... | collective-permute-start | bytes 98312 | tf_op jit(solution)/shard_map/ppermute | solution.py:33
  79.5 1.9 %collective-permute-start.44 = (f32[8,1024]{1,0:T(8,128)S(1)}, f32[8,1024]{1,0:T(8,128)S(1)}, u32[]{:S(2)}, u32[]{:S(2)}) collective-permute-start(f32[8,1024]{1,0:T(8,128)S(1)} %get-tuple-element.25), channel_id=1, source_target_pairs={{0,28},{2,30},{4,0},{6,2},{8,4},{10,6},{12,8},{14,10},{16,12},{18,... | collective-permute-start | bytes 98312 | tf_op jit(solution)/shard_map/ppermute | solution.py:33
  81.5 2.7 %collective-permute-start.45 = (f32[8,1024]{1,0:T(8,128)S(1)}, f32[8,1024]{1,0:T(8,128)S(1)}, u32[]{:S(2)}, u32[]{:S(2)}) collective-permute-start(f32[8,1024]{1,0:T(8,128)S(1)} %get-tuple-element.24), channel_id=1, source_target_pairs={{0,30},{2,0},{4,2},{6,4},{8,6},{10,8},{12,10},{14,12},{16,14},{18,... | collective-permute-start | bytes 98312 | tf_op jit(solution)/shard_map/ppermute | solution.py:33
  84.3 1.5 %collective-permute-done.45 = f32[8,1024]{1,0:T(8,128)S(1)} collective-permute-done((f32[8,1024]{1,0:T(8,128)S(1)}, f32[8,1024]{1,0:T(8,128)S(1)}, u32[]{:S(2)}, u32[]{:S(2)}) %collective-permute-start.45) | collective-permute-done | bytes 32800 | tf_op jit(solution)/shard_map/ppermute | solution.py:33
  87.8 1.8 %collective-permute-start.50 = (f32[8,1024]{1,0:T(8,128)S(1)}, f32[8,1024]{1,0:T(8,128)S(1)}, u32[]{:S(2)}, u32[]{:S(2)}) collective-permute-start(f32[8,1024]{1,0:T(8,128)S(1)} %get-tuple-element.19), channel_id=1, source_target_pairs={{0,8},{2,10},{4,12},{6,14},{8,16},{10,18},{12,20},{14,22},{16,24},... | collective-permute-start | bytes 98312 | tf_op jit(solution)/shard_map/ppermute | solution.py:33
  89.5 2.8 %collective-permute-start.51 = (f32[8,1024]{1,0:T(8,128)S(1)}, f32[8,1024]{1,0:T(8,128)S(1)}, u32[]{:S(2)}, u32[]{:S(2)}) collective-permute-start(f32[8,1024]{1,0:T(8,128)S(1)} %get-tuple-element.18), channel_id=1, source_target_pairs={{0,10},{2,12},{4,14},{6,16},{8,18},{10,20},{12,22},{14,24},{16,26}... | collective-permute-start | bytes 98312 | tf_op jit(solution)/shard_map/ppermute | solution.py:33
  93.5 1.2 %collective-permute-start.53 = (f32[8,1024]{1,0:T(8,128)S(1)}, f32[8,1024]{1,0:T(8,128)S(1)}, u32[]{:S(2)}, u32[]{:S(2)}) collective-permute-start(f32[8,1024]{1,0:T(8,128)S(1)} %get-tuple-element.16), channel_id=1, source_target_pairs={{0,14},{2,16},{4,18},{6,20},{8,22},{10,24},{12,26},{14,28},{16,30}... | collective-permute-start | bytes 98312 | tf_op jit(solution)/shard_map/ppermute | solution.py:33
  94.7 2.0 %collective-permute-start.54 = (f32[8,1024]{1,0:T(8,128)S(1)}, f32[8,1024]{1,0:T(8,128)S(1)}, u32[]{:S(2)}, u32[]{:S(2)}) collective-permute-start(f32[8,1024]{1,0:T(8,128)S(1)} %get-tuple-element.15), channel_id=1, source_target_pairs={{0,16},{2,18},{4,20},{6,22},{8,24},{10,26},{12,28},{14,30},{16,0},... | collective-permute-start | bytes 98312 | tf_op jit(solution)/shard_map/ppermute | solution.py:33
  96.8 3.0 %collective-permute-start.56 = (f32[8,1024]{1,0:T(8,128)S(1)}, f32[8,1024]{1,0:T(8,128)S(1)}, u32[]{:S(2)}, u32[]{:S(2)}) collective-permute-start(f32[8,1024]{1,0:T(8,128)S(1)} %get-tuple-element.13), channel_id=1, source_target_pairs={{0,20},{2,22},{4,24},{6,26},{8,28},{10,30},{12,0},{14,2},{16,4},{1... | collective-permute-start | bytes 98312 | tf_op jit(solution)/shard_map/ppermute | solution.py:33
  99.9 3.3 %collective-permute-start.57 = (f32[8,1024]{1,0:T(8,128)S(1)}, f32[8,1024]{1,0:T(8,128)S(1)}, u32[]{:S(2)}, u32[]{:S(2)}) collective-permute-start(f32[8,1024]{1,0:T(8,128)S(1)} %get-tuple-element.12), channel_id=1, source_target_pairs={{0,22},{2,24},{4,26},{6,28},{8,30},{10,0},{12,2},{14,4},{16,6},{18... | collective-permute-start | bytes 98312 | tf_op jit(solution)/shard_map/ppermute | solution.py:33
  104.4 1.4 %collective-permute-start.60 = (f32[8,1024]{1,0:T(8,128)S(1)}, f32[8,1024]{1,0:T(8,128)S(1)}, u32[]{:S(2)}, u32[]{:S(2)}) collective-permute-start(f32[8,1024]{1,0:T(8,128)S(1)} %get-tuple-element.9), channel_id=1, source_target_pairs={{0,28},{2,30},{4,0},{6,2},{8,4},{10,6},{12,8},{14,10},{16,12},{18,... | collective-permute-start | bytes 98312 | tf_op jit(solution)/shard_map/ppermute | solution.py:33
  105.8 2.3 %collective-permute-start.61 = (f32[8,1024]{1,0:T(8,128)S(1)}, f32[8,1024]{1,0:T(8,128)S(1)}, u32[]{:S(2)}, u32[]{:S(2)}) collective-permute-start(f32[8,1024]{1,0:T(8,128)S(1)} %get-tuple-element.8), channel_id=1, source_target_pairs={{0,30},{2,0},{4,2},{6,4},{8,6},{10,8},{12,10},{14,12},{16,14},{18,... | collective-permute-start | bytes 98312 | tf_op jit(solution)/shard_map/ppermute | solution.py:33
  108.1 1.6 %collective-permute-start.46 = (f32[8,8,512]{2,1,0:T(8,128)S(1)}, f32[8,8,512]{2,1,0:T(8,128)S(1)}, u32[]{:S(2)}, u32[]{:S(2)}) collective-permute-start(f32[8,8,512]{2,1,0:T(8,128)S(1)} %slice_select_fusion), channel_id=1, source_target_pairs={{0,1},{1,0},{2,3},{3,2},{4,5},{5,4},{6,7},{7,6},{8,9},{9,8},{10,11... | collective-permute-start | bytes 393224 | tf_op jit(solution)/shard_map/ppermute | solution.py:16
  110.0 0.9 reshape.136
  110.9 2.2 %collective-permute-done.46 = f32[8,8,512]{2,1,0:T(8,128)S(1)} collective-permute-done((f32[8,8,512]{2,1,0:T(8,128)S(1)}, f32[8,8,512]{2,1,0:T(8,128)S(1)}, u32[]{:S(2)}, u32[]{:S(2)}) %collective-permute-start.46) | collective-permute-done | bytes 131104 | tf_op jit(solution)/shard_map/ppermute | solution.py:16
  113.1 1.6 %maximum_multiply_fusion = f32[8,32,512]{2,1,0:T(8,128)} fusion(f32[8,32,512]{2,1,0:T(8,128)S(1)} %copy-done, f32[8,8,512]{2,1,0:T(8,128)S(1)} %get-tuple-element.73, f32[8,32,512]{2,1,0:T(8,128)S(1)} %reshape.134, f32[8,8,512]{2,1,0:T(8,128)S(1)} %get-tuple-element.72, f32[]{:T(128)S(6)} %mul.18, f32[]{:T(128)} %bitcast.303, f32[32,48]{1,0:T(8,128)S(1)} %get-tuple-element.6), kind=kOutput, calls=%fused_computation.19 | convolution fusion | flops 76808192 | bytes 1841160 | tf_op jit(solution)/shard_map/rk,pkc->prc/dot_general | solution.py:48
  (204 shorter events, 15.5 us)
Async XLA Ops:
  1.7 6.5 %collective-permute-start = (f32[8,8,512]{2,1,0:T(8,128)S(1)}, f32[8,8,512]{2,1,0:T(8,128)S(1)}, u32[]{:S(2)}, u32[]{:S(2)}) collective-permute-start(f32[8,8,512]{2,1,0:T(8,128)S(1)} %slice_select_fusion.1), channel_id=1, source_target_pairs={{0,1},{1,0},{2,3},{3,2},{4,5},{5,4},{6,7},{7,6},{8,9},{9,8},{10,11... | collective-permute-start | bytes 393224 | tf_op jit(solution)/shard_map/ppermute | solution.py:16
  10.8 6.8 %collective-permute-start.1 = (f32[8,1024]{1,0:T(8,128)S(1)}, f32[8,1024]{1,0:T(8,128)S(1)}, u32[]{:S(2)}, u32[]{:S(2)}) collective-permute-start(f32[8,1024]{1,0:T(8,128)S(1)} %bitcast.338), channel_id=1, source_target_pairs={{0,2},{2,4},{4,6},{6,8},{8,10},{10,12},{12,14},{14,16},{16,18},{18... | collective-permute-start | bytes 98312 | tf_op jit(solution)/shard_map/ppermute | solution.py:33
  10.9 8.0 %collective-permute-start.2 = (f32[8,1024]{1,0:T(8,128)S(1)}, f32[8,1024]{1,0:T(8,128)S(1)}, u32[]{:S(2)}, u32[]{:S(2)}) collective-permute-start(f32[8,1024]{1,0:T(8,128)S(1)} %bitcast.337), channel_id=1, source_target_pairs={{0,4},{2,6},{4,8},{6,10},{8,12},{10,14},{12,16},{14,18},{16,20},{1... | collective-permute-start | bytes 98312 | tf_op jit(solution)/shard_map/ppermute | solution.py:33
  12.7 10.6 %collective-permute-start.3 = (f32[8,1024]{1,0:T(8,128)S(1)}, f32[8,1024]{1,0:T(8,128)S(1)}, u32[]{:S(2)}, u32[]{:S(2)}) collective-permute-start(f32[8,1024]{1,0:T(8,128)S(1)} %bitcast.336), channel_id=1, source_target_pairs={{0,6},{2,8},{4,10},{6,12},{8,14},{10,16},{12,18},{14,20},{16,22},{... | collective-permute-start | bytes 98312 | tf_op jit(solution)/shard_map/ppermute | solution.py:33
  15.2 8.4 %collective-permute-start.4 = (f32[8,1024]{1,0:T(8,128)S(1)}, f32[8,1024]{1,0:T(8,128)S(1)}, u32[]{:S(2)}, u32[]{:S(2)}) collective-permute-start(f32[8,1024]{1,0:T(8,128)S(1)} %bitcast.335), channel_id=1, source_target_pairs={{0,8},{2,10},{4,12},{6,14},{8,16},{10,18},{12,20},{14,22},{16,24},... | collective-permute-start | bytes 98312 | tf_op jit(solution)/shard_map/ppermute | solution.py:33
  16.9 7.1 %collective-permute-start.5 = (f32[8,1024]{1,0:T(8,128)S(1)}, f32[8,1024]{1,0:T(8,128)S(1)}, u32[]{:S(2)}, u32[]{:S(2)}) collective-permute-start(f32[8,1024]{1,0:T(8,128)S(1)} %bitcast.333), channel_id=1, source_target_pairs={{0,10},{2,12},{4,14},{6,16},{8,18},{10,20},{12,22},{14,24},{16,26}... | collective-permute-start | bytes 98312 | tf_op jit(solution)/shard_map/ppermute | solution.py:33
  17.7 8.8 %collective-permute-start.6 = (f32[8,1024]{1,0:T(8,128)S(1)}, f32[8,1024]{1,0:T(8,128)S(1)}, u32[]{:S(2)}, u32[]{:S(2)}) collective-permute-start(f32[8,1024]{1,0:T(8,128)S(1)} %bitcast.334), channel_id=1, source_target_pairs={{0,12},{2,14},{4,16},{6,18},{8,20},{10,22},{12,24},{14,26},{16,28}... | collective-permute-start | bytes 98312 | tf_op jit(solution)/shard_map/ppermute | solution.py:33
  18.9 10.5 %collective-permute-start.7 = (f32[8,1024]{1,0:T(8,128)S(1)}, f32[8,1024]{1,0:T(8,128)S(1)}, u32[]{:S(2)}, u32[]{:S(2)}) collective-permute-start(f32[8,1024]{1,0:T(8,128)S(1)} %bitcast.332), channel_id=1, source_target_pairs={{0,14},{2,16},{4,18},{6,20},{8,22},{10,24},{12,26},{14,28},{16,30}... | collective-permute-start | bytes 98312 | tf_op jit(solution)/shard_map/ppermute | solution.py:33
  23.3 8.0 %collective-permute-start.8 = (f32[8,1024]{1,0:T(8,128)S(1)}, f32[8,1024]{1,0:T(8,128)S(1)}, u32[]{:S(2)}, u32[]{:S(2)}) collective-permute-start(f32[8,1024]{1,0:T(8,128)S(1)} %bitcast.331), channel_id=1, source_target_pairs={{0,16},{2,18},{4,20},{6,22},{8,24},{10,26},{12,28},{14,30},{16,0},... | collective-permute-start | bytes 98312 | tf_op jit(solution)/shard_map/ppermute | solution.py:33
  23.7 7.7 %collective-permute-start.9 = (f32[8,1024]{1,0:T(8,128)S(1)}, f32[8,1024]{1,0:T(8,128)S(1)}, u32[]{:S(2)}, u32[]{:S(2)}) collective-permute-start(f32[8,1024]{1,0:T(8,128)S(1)} %bitcast.330), channel_id=1, source_target_pairs={{0,18},{2,20},{4,22},{6,24},{8,26},{10,28},{12,30},{14,0},{16,2},{... | collective-permute-start | bytes 98312 | tf_op jit(solution)/shard_map/ppermute | solution.py:33
  24.0 8.8 %collective-permute-start.10 = (f32[8,1024]{1,0:T(8,128)S(1)}, f32[8,1024]{1,0:T(8,128)S(1)}, u32[]{:S(2)}, u32[]{:S(2)}) collective-permute-start(f32[8,1024]{1,0:T(8,128)S(1)} %bitcast.329), channel_id=1, source_target_pairs={{0,20},{2,22},{4,24},{6,26},{8,28},{10,30},{12,0},{14,2},{16,4},{1... | collective-permute-start | bytes 98312 | tf_op jit(solution)/shard_map/ppermute | solution.py:33
  26.5 8.6 %collective-permute-start.11 = (f32[8,1024]{1,0:T(8,128)S(1)}, f32[8,1024]{1,0:T(8,128)S(1)}, u32[]{:S(2)}, u32[]{:S(2)}) collective-permute-start(f32[8,1024]{1,0:T(8,128)S(1)} %bitcast.328), channel_id=1, source_target_pairs={{0,22},{2,24},{4,26},{6,28},{8,30},{10,0},{12,2},{14,4},{16,6},{18... | collective-permute-start | bytes 98312 | tf_op jit(solution)/shard_map/ppermute | solution.py:33
  31.4 6.1 %collective-permute-start.14 = (f32[8,1024]{1,0:T(8,128)S(1)}, f32[8,1024]{1,0:T(8,128)S(1)}, u32[]{:S(2)}, u32[]{:S(2)}) collective-permute-start(f32[8,1024]{1,0:T(8,128)S(1)} %bitcast.325), channel_id=1, source_target_pairs={{0,28},{2,30},{4,0},{6,2},{8,4},{10,6},{12,8},{14,10},{16,12},{18,... | collective-permute-start | bytes 98312 | tf_op jit(solution)/shard_map/ppermute | solution.py:33
  35.1 6.1 %collective-permute-start.16 = (f32[8,1024]{1,0:T(8,128)S(1)}, f32[8,1024]{1,0:T(8,128)S(1)}, u32[]{:S(2)}, u32[]{:S(2)}) collective-permute-start(f32[8,1024]{1,0:T(8,128)S(1)} %bitcast.323), channel_id=1, source_target_pairs={{0,2},{2,4},{4,6},{6,8},{8,10},{10,12},{12,14},{14,16},{16,18},{18... | collective-permute-start | bytes 98312 | tf_op jit(solution)/shard_map/ppermute | solution.py:33
  35.2 7.0 %collective-permute-start.17 = (f32[8,1024]{1,0:T(8,128)S(1)}, f32[8,1024]{1,0:T(8,128)S(1)}, u32[]{:S(2)}, u32[]{:S(2)}) collective-permute-start(f32[8,1024]{1,0:T(8,128)S(1)} %bitcast.322), channel_id=1, source_target_pairs={{0,4},{2,6},{4,8},{6,10},{8,12},{10,14},{12,16},{14,18},{16,20},{1... | collective-permute-start | bytes 98312 | tf_op jit(solution)/shard_map/ppermute | solution.py:33
  35.9 7.7 %collective-permute-start.18 = (f32[8,1024]{1,0:T(8,128)S(1)}, f32[8,1024]{1,0:T(8,128)S(1)}, u32[]{:S(2)}, u32[]{:S(2)}) collective-permute-start(f32[8,1024]{1,0:T(8,128)S(1)} %bitcast.321), channel_id=1, source_target_pairs={{0,6},{2,8},{4,10},{6,12},{8,14},{10,16},{12,18},{14,20},{16,22},{... | collective-permute-start | bytes 98312 | tf_op jit(solution)/shard_map/ppermute | solution.py:33
  37.5 8.8 %collective-permute-start.19 = (f32[8,1024]{1,0:T(8,128)S(1)}, f32[8,1024]{1,0:T(8,128)S(1)}, u32[]{:S(2)}, u32[]{:S(2)}) collective-permute-start(f32[8,1024]{1,0:T(8,128)S(1)} %bitcast.320), channel_id=1, source_target_pairs={{0,8},{2,10},{4,12},{6,14},{8,16},{10,18},{12,20},{14,22},{16,24},... | collective-permute-start | bytes 98312 | tf_op jit(solution)/shard_map/ppermute | solution.py:33
  38.1 8.3 %collective-permute-start.20 = (f32[8,1024]{1,0:T(8,128)S(1)}, f32[8,1024]{1,0:T(8,128)S(1)}, u32[]{:S(2)}, u32[]{:S(2)}) collective-permute-start(f32[8,1024]{1,0:T(8,128)S(1)} %bitcast.319), channel_id=1, source_target_pairs={{0,10},{2,12},{4,14},{6,16},{8,18},{10,20},{12,22},{14,24},{16,26}... | collective-permute-start | bytes 98312 | tf_op jit(solution)/shard_map/ppermute | solution.py:33
  41.2 7.3 %collective-permute-start.21 = (f32[8,1024]{1,0:T(8,128)S(1)}, f32[8,1024]{1,0:T(8,128)S(1)}, u32[]{:S(2)}, u32[]{:S(2)}) collective-permute-start(f32[8,1024]{1,0:T(8,128)S(1)} %bitcast.318), channel_id=1, source_target_pairs={{0,12},{2,14},{4,16},{6,18},{8,20},{10,22},{12,24},{14,26},{16,28}... | collective-permute-start | bytes 98312 | tf_op jit(solution)/shard_map/ppermute | solution.py:33
  42.2 9.8 %collective-permute-start.22 = (f32[8,1024]{1,0:T(8,128)S(1)}, f32[8,1024]{1,0:T(8,128)S(1)}, u32[]{:S(2)}, u32[]{:S(2)}) collective-permute-start(f32[8,1024]{1,0:T(8,128)S(1)} %bitcast.317), channel_id=1, source_target_pairs={{0,14},{2,16},{4,18},{6,20},{8,22},{10,24},{12,26},{14,28},{16,30}... | collective-permute-start | bytes 98312 | tf_op jit(solution)/shard_map/ppermute | solution.py:33
  43.6 8.5 %collective-permute-start.23 = (f32[8,1024]{1,0:T(8,128)S(1)}, f32[8,1024]{1,0:T(8,128)S(1)}, u32[]{:S(2)}, u32[]{:S(2)}) collective-permute-start(f32[8,1024]{1,0:T(8,128)S(1)} %bitcast.316), channel_id=1, source_target_pairs={{0,16},{2,18},{4,20},{6,22},{8,24},{10,26},{12,28},{14,30},{16,0},... | collective-permute-start | bytes 98312 | tf_op jit(solution)/shard_map/ppermute | solution.py:33
  46.3 7.0 %collective-permute-start.24 = (f32[8,1024]{1,0:T(8,128)S(1)}, f32[8,1024]{1,0:T(8,128)S(1)}, u32[]{:S(2)}, u32[]{:S(2)}) collective-permute-start(f32[8,1024]{1,0:T(8,128)S(1)} %bitcast.315), channel_id=1, source_target_pairs={{0,18},{2,20},{4,22},{6,24},{8,26},{10,28},{12,30},{14,0},{16,2},{... | collective-permute-start | bytes 98312 | tf_op jit(solution)/shard_map/ppermute | solution.py:33
  46.3 8.3 %collective-permute-start.25 = (f32[8,1024]{1,0:T(8,128)S(1)}, f32[8,1024]{1,0:T(8,128)S(1)}, u32[]{:S(2)}, u32[]{:S(2)}) collective-permute-start(f32[8,1024]{1,0:T(8,128)S(1)} %bitcast.314), channel_id=1, source_target_pairs={{0,20},{2,22},{4,24},{6,26},{8,28},{10,30},{12,0},{14,2},{16,4},{1... | collective-permute-start | bytes 98312 | tf_op jit(solution)/shard_map/ppermute | solution.py:33
  48.5 8.4 %collective-permute-start.26 = (f32[8,1024]{1,0:T(8,128)S(1)}, f32[8,1024]{1,0:T(8,128)S(1)}, u32[]{:S(2)}, u32[]{:S(2)}) collective-permute-start(f32[8,1024]{1,0:T(8,128)S(1)} %bitcast.313), channel_id=1, source_target_pairs={{0,22},{2,24},{4,26},{6,28},{8,30},{10,0},{12,2},{14,4},{16,6},{18... | collective-permute-start | bytes 98312 | tf_op jit(solution)/shard_map/ppermute | solution.py:33
  60.1 7.4 %collective-permute-start.31 = (f32[8,1024]{1,0:T(8,128)S(1)}, f32[8,1024]{1,0:T(8,128)S(1)}, u32[]{:S(2)}, u32[]{:S(2)}) collective-permute-start(f32[8,1024]{1,0:T(8,128)S(1)} %get-tuple-element.38), channel_id=1, source_target_pairs={{0,2},{2,4},{4,6},{6,8},{8,10},{10,12},{12,14},{14,16},{16,18},{18... | collective-permute-start | bytes 98312 | tf_op jit(solution)/shard_map/ppermute | solution.py:33
  62.1 7.0 %collective-permute-start.32 = (f32[8,1024]{1,0:T(8,128)S(1)}, f32[8,1024]{1,0:T(8,128)S(1)}, u32[]{:S(2)}, u32[]{:S(2)}) collective-permute-start(f32[8,1024]{1,0:T(8,128)S(1)} %get-tuple-element.37), channel_id=1, source_target_pairs={{0,4},{2,6},{4,8},{6,10},{8,12},{10,14},{12,16},{14,18},{16,20},{1... | collective-permute-start | bytes 98312 | tf_op jit(solution)/shard_map/ppermute | solution.py:33
  63.6 7.0 %collective-permute-start.33 = (f32[8,1024]{1,0:T(8,128)S(1)}, f32[8,1024]{1,0:T(8,128)S(1)}, u32[]{:S(2)}, u32[]{:S(2)}) collective-permute-start(f32[8,1024]{1,0:T(8,128)S(1)} %get-tuple-element.36), channel_id=1, source_target_pairs={{0,6},{2,8},{4,10},{6,12},{8,14},{10,16},{12,18},{14,20},{16,22},{... | collective-permute-start | bytes 98312 | tf_op jit(solution)/shard_map/ppermute | solution.py:33
  63.8 8.4 %collective-permute-start.34 = (f32[8,1024]{1,0:T(8,128)S(1)}, f32[8,1024]{1,0:T(8,128)S(1)}, u32[]{:S(2)}, u32[]{:S(2)}) collective-permute-start(f32[8,1024]{1,0:T(8,128)S(1)} %get-tuple-element.35), channel_id=1, source_target_pairs={{0,8},{2,10},{4,12},{6,14},{8,16},{10,18},{12,20},{14,22},{16,24},... | collective-permute-start | bytes 98312 | tf_op jit(solution)/shard_map/ppermute | solution.py:33
  65.6 7.2 %collective-permute-start.35 = (f32[8,1024]{1,0:T(8,128)S(1)}, f32[8,1024]{1,0:T(8,128)S(1)}, u32[]{:S(2)}, u32[]{:S(2)}) collective-permute-start(f32[8,1024]{1,0:T(8,128)S(1)} %get-tuple-element.34), channel_id=1, source_target_pairs={{0,10},{2,12},{4,14},{6,16},{8,18},{10,20},{12,22},{14,24},{16,26}... | collective-permute-start | bytes 98312 | tf_op jit(solution)/shard_map/ppermute | solution.py:33
  67.5 8.4 %collective-permute-start.36 = (f32[8,1024]{1,0:T(8,128)S(1)}, f32[8,1024]{1,0:T(8,128)S(1)}, u32[]{:S(2)}, u32[]{:S(2)}) collective-permute-start(f32[8,1024]{1,0:T(8,128)S(1)} %get-tuple-element.33), channel_id=1, source_target_pairs={{0,12},{2,14},{4,16},{6,18},{8,20},{10,22},{12,24},{14,26},{16,28}... | collective-permute-start | bytes 98312 | tf_op jit(solution)/shard_map/ppermute | solution.py:33
  69.1 9.7 %collective-permute-start.37 = (f32[8,1024]{1,0:T(8,128)S(1)}, f32[8,1024]{1,0:T(8,128)S(1)}, u32[]{:S(2)}, u32[]{:S(2)}) collective-permute-start(f32[8,1024]{1,0:T(8,128)S(1)} %get-tuple-element.32), channel_id=1, source_target_pairs={{0,14},{2,16},{4,18},{6,20},{8,22},{10,24},{12,26},{14,28},{16,30}... | collective-permute-start | bytes 98312 | tf_op jit(solution)/shard_map/ppermute | solution.py:33
  70.6 8.4 %collective-permute-start.38 = (f32[8,1024]{1,0:T(8,128)S(1)}, f32[8,1024]{1,0:T(8,128)S(1)}, u32[]{:S(2)}, u32[]{:S(2)}) collective-permute-start(f32[8,1024]{1,0:T(8,128)S(1)} %get-tuple-element.31), channel_id=1, source_target_pairs={{0,16},{2,18},{4,20},{6,22},{8,24},{10,26},{12,28},{14,30},{16,0},... | collective-permute-start | bytes 98312 | tf_op jit(solution)/shard_map/ppermute | solution.py:33
  72.2 7.4 %collective-permute-start.39 = (f32[8,1024]{1,0:T(8,128)S(1)}, f32[8,1024]{1,0:T(8,128)S(1)}, u32[]{:S(2)}, u32[]{:S(2)}) collective-permute-start(f32[8,1024]{1,0:T(8,128)S(1)} %get-tuple-element.30), channel_id=1, source_target_pairs={{0,18},{2,20},{4,22},{6,24},{8,26},{10,28},{12,30},{14,0},{16,2},{... | collective-permute-start | bytes 98312 | tf_op jit(solution)/shard_map/ppermute | solution.py:33
  72.8 8.7 %collective-permute-start.40 = (f32[8,1024]{1,0:T(8,128)S(1)}, f32[8,1024]{1,0:T(8,128)S(1)}, u32[]{:S(2)}, u32[]{:S(2)}) collective-permute-start(f32[8,1024]{1,0:T(8,128)S(1)} %get-tuple-element.29), channel_id=1, source_target_pairs={{0,20},{2,22},{4,24},{6,26},{8,28},{10,30},{12,0},{14,2},{16,4},{1... | collective-permute-start | bytes 98312 | tf_op jit(solution)/shard_map/ppermute | solution.py:33
  75.8 8.3 %collective-permute-start.41 = (f32[8,1024]{1,0:T(8,128)S(1)}, f32[8,1024]{1,0:T(8,128)S(1)}, u32[]{:S(2)}, u32[]{:S(2)}) collective-permute-start(f32[8,1024]{1,0:T(8,128)S(1)} %get-tuple-element.28), channel_id=1, source_target_pairs={{0,22},{2,24},{4,26},{6,28},{8,30},{10,0},{12,2},{14,4},{16,6},{18... | collective-permute-start | bytes 98312 | tf_op jit(solution)/shard_map/ppermute | solution.py:33
  86.3 6.1 %collective-permute-start.47 = (f32[8,1024]{1,0:T(8,128)S(1)}, f32[8,1024]{1,0:T(8,128)S(1)}, u32[]{:S(2)}, u32[]{:S(2)}) collective-permute-start(f32[8,1024]{1,0:T(8,128)S(1)} %get-tuple-element.22), channel_id=1, source_target_pairs={{0,2},{2,4},{4,6},{6,8},{8,10},{10,12},{12,14},{14,16},{16,18},{18... | collective-permute-start | bytes 98312 | tf_op jit(solution)/shard_map/ppermute | solution.py:33
  86.9 6.6 %collective-permute-start.48 = (f32[8,1024]{1,0:T(8,128)S(1)}, f32[8,1024]{1,0:T(8,128)S(1)}, u32[]{:S(2)}, u32[]{:S(2)}) collective-permute-start(f32[8,1024]{1,0:T(8,128)S(1)} %get-tuple-element.21), channel_id=1, source_target_pairs={{0,4},{2,6},{4,8},{6,10},{8,12},{10,14},{12,16},{14,18},{16,20},{1... | collective-permute-start | bytes 98312 | tf_op jit(solution)/shard_map/ppermute | solution.py:33
  87.7 7.0 %collective-permute-start.49 = (f32[8,1024]{1,0:T(8,128)S(1)}, f32[8,1024]{1,0:T(8,128)S(1)}, u32[]{:S(2)}, u32[]{:S(2)}) collective-permute-start(f32[8,1024]{1,0:T(8,128)S(1)} %get-tuple-element.20), channel_id=1, source_target_pairs={{0,6},{2,8},{4,10},{6,12},{8,14},{10,16},{12,18},{14,20},{16,22},{... | collective-permute-start | bytes 98312 | tf_op jit(solution)/shard_map/ppermute | solution.py:33
  87.8 8.9 %collective-permute-start.50 = (f32[8,1024]{1,0:T(8,128)S(1)}, f32[8,1024]{1,0:T(8,128)S(1)}, u32[]{:S(2)}, u32[]{:S(2)}) collective-permute-start(f32[8,1024]{1,0:T(8,128)S(1)} %get-tuple-element.19), channel_id=1, source_target_pairs={{0,8},{2,10},{4,12},{6,14},{8,16},{10,18},{12,20},{14,22},{16,24},... | collective-permute-start | bytes 98312 | tf_op jit(solution)/shard_map/ppermute | solution.py:33
  89.5 7.3 %collective-permute-start.51 = (f32[8,1024]{1,0:T(8,128)S(1)}, f32[8,1024]{1,0:T(8,128)S(1)}, u32[]{:S(2)}, u32[]{:S(2)}) collective-permute-start(f32[8,1024]{1,0:T(8,128)S(1)} %get-tuple-element.18), channel_id=1, source_target_pairs={{0,10},{2,12},{4,14},{6,16},{8,18},{10,20},{12,22},{14,24},{16,26}... | collective-permute-start | bytes 98312 | tf_op jit(solution)/shard_map/ppermute | solution.py:33
  92.4 7.4 %collective-permute-start.52 = (f32[8,1024]{1,0:T(8,128)S(1)}, f32[8,1024]{1,0:T(8,128)S(1)}, u32[]{:S(2)}, u32[]{:S(2)}) collective-permute-start(f32[8,1024]{1,0:T(8,128)S(1)} %get-tuple-element.17), channel_id=1, source_target_pairs={{0,12},{2,14},{4,16},{6,18},{8,20},{10,22},{12,24},{14,26},{16,28}... | collective-permute-start | bytes 98312 | tf_op jit(solution)/shard_map/ppermute | solution.py:33
  93.5 9.6 %collective-permute-start.53 = (f32[8,1024]{1,0:T(8,128)S(1)}, f32[8,1024]{1,0:T(8,128)S(1)}, u32[]{:S(2)}, u32[]{:S(2)}) collective-permute-start(f32[8,1024]{1,0:T(8,128)S(1)} %get-tuple-element.16), channel_id=1, source_target_pairs={{0,14},{2,16},{4,18},{6,20},{8,22},{10,24},{12,26},{14,28},{16,30}... | collective-permute-start | bytes 98312 | tf_op jit(solution)/shard_map/ppermute | solution.py:33
  94.7 8.9 %collective-permute-start.54 = (f32[8,1024]{1,0:T(8,128)S(1)}, f32[8,1024]{1,0:T(8,128)S(1)}, u32[]{:S(2)}, u32[]{:S(2)}) collective-permute-start(f32[8,1024]{1,0:T(8,128)S(1)} %get-tuple-element.15), channel_id=1, source_target_pairs={{0,16},{2,18},{4,20},{6,22},{8,24},{10,26},{12,28},{14,30},{16,0},... | collective-permute-start | bytes 98312 | tf_op jit(solution)/shard_map/ppermute | solution.py:33
  96.7 7.7 %collective-permute-start.55 = (f32[8,1024]{1,0:T(8,128)S(1)}, f32[8,1024]{1,0:T(8,128)S(1)}, u32[]{:S(2)}, u32[]{:S(2)}) collective-permute-start(f32[8,1024]{1,0:T(8,128)S(1)} %get-tuple-element.14), channel_id=1, source_target_pairs={{0,18},{2,20},{4,22},{6,24},{8,26},{10,28},{12,30},{14,0},{16,2},{... | collective-permute-start | bytes 98312 | tf_op jit(solution)/shard_map/ppermute | solution.py:33
  96.8 9.0 %collective-permute-start.56 = (f32[8,1024]{1,0:T(8,128)S(1)}, f32[8,1024]{1,0:T(8,128)S(1)}, u32[]{:S(2)}, u32[]{:S(2)}) collective-permute-start(f32[8,1024]{1,0:T(8,128)S(1)} %get-tuple-element.13), channel_id=1, source_target_pairs={{0,20},{2,22},{4,24},{6,26},{8,28},{10,30},{12,0},{14,2},{16,4},{1... | collective-permute-start | bytes 98312 | tf_op jit(solution)/shard_map/ppermute | solution.py:33
  99.9 8.2 %collective-permute-start.57 = (f32[8,1024]{1,0:T(8,128)S(1)}, f32[8,1024]{1,0:T(8,128)S(1)}, u32[]{:S(2)}, u32[]{:S(2)}) collective-permute-start(f32[8,1024]{1,0:T(8,128)S(1)} %get-tuple-element.12), channel_id=1, source_target_pairs={{0,22},{2,24},{4,26},{6,28},{8,30},{10,0},{12,2},{14,4},{16,6},{18... | collective-permute-start | bytes 98312 | tf_op jit(solution)/shard_map/ppermute | solution.py:33
  103.1 6.5 %collective-permute-start.58 = (f32[8,1024]{1,0:T(8,128)S(1)}, f32[8,1024]{1,0:T(8,128)S(1)}, u32[]{:S(2)}, u32[]{:S(2)}) collective-permute-start(f32[8,1024]{1,0:T(8,128)S(1)} %get-tuple-element.11), channel_id=1, source_target_pairs={{0,24},{2,26},{4,28},{6,30},{8,0},{10,2},{12,4},{14,6},{16,8},{18,... | collective-permute-start | bytes 98312 | tf_op jit(solution)/shard_map/ppermute | solution.py:33
  103.6 6.1 %collective-permute-start.59 = (f32[8,1024]{1,0:T(8,128)S(1)}, f32[8,1024]{1,0:T(8,128)S(1)}, u32[]{:S(2)}, u32[]{:S(2)}) collective-permute-start(f32[8,1024]{1,0:T(8,128)S(1)} %get-tuple-element.10), channel_id=1, source_target_pairs={{0,26},{2,28},{4,30},{6,0},{8,2},{10,4},{12,6},{14,8},{16,10},{18,... | collective-permute-start | bytes 98312 | tf_op jit(solution)/shard_map/ppermute | solution.py:33
  (19 other events, 88.8 us)

commit v9 on v6

--- a/solution.py
+++ b/solution.py
@@ -6,21 +6,23 @@
 highest_mode = lax.Precision.HIGHEST
 
 
-def with_halo(cells, axis, width):
+def blur_rows(band, cells, axis, width):
     count = lax.axis_size(axis)
-    head = lax.slice_in_dim(cells, 0, width, axis=1)
-    tail = lax.slice_in_dim(cells, cells.shape[1] - width, cells.shape[1], axis=1)
-    zeros = jnp.zeros_like(head)
+    rows = cells.shape[1]
+    summed = lateral_apply(band[:, width : width + rows], cells)
     if count == 2:
         first = lax.axis_index(axis) == 0
-        arrived = lax.ppermute(jnp.where(first, tail, head), axis, [(0, 1), (1, 0)])
-        above = jnp.where(first, zeros, arrived)
-        below = jnp.where(first, arrived, zeros)
-    else:
-        ends = count - 1
-        above = lax.ppermute(tail, axis, [(i, (i + 1) % count) for i in range(ends)])
-        below = lax.ppermute(head, axis, [((i + 1) % count, i) for i in range(ends)])
-    return jnp.concatenate([above, cells, below], axis=1)
+        sent = lax.dynamic_slice_in_dim(cells, jnp.where(first, rows - width, 0), width, axis=1)
+        arrived = lax.ppermute(sent, axis, [(0, 1), (1, 0)])
+        edge = jnp.where(first, band[:, width + rows :], band[:, :width])
+        return summed + lateral_apply(edge, arrived)
+    ends = count - 1
+    head = lax.slice_in_dim(cells, 0, width, axis=1)
+    tail = lax.slice_in_dim(cells, rows - width, rows, axis=1)
+    above = lax.ppermute(tail, axis, [(i, (i + 1) % count) for i in range(ends)])
+    below = lax.ppermute(head, axis, [((i + 1) % count, i) for i in range(ends)])
+    summed = summed + lateral_apply(band[:, :width], above)
+    return summed + lateral_apply(band[:, width + rows :], below)
 
 
 def band_matrix(kernel_taps, row_count, shift):
@@ -58,8 +60,7 @@
     sheet_psf = sheet_matrix(offsets, depth_psf, offsets.shape[0])
     blur_band = band_matrix(lateral_psf, row_count, 0)
     back_band = band_matrix(lateral_psf[::-1], row_count, 0)
-    padded = with_halo(estimate, "row", halo_rows)
-    blurred = lateral_apply(blur_band, padded).reshape(plane_count, flat_count)
+    blurred = blur_rows(blur_band, estimate, "row", halo_rows).reshape(plane_count, flat_count)
     both_flat = jnp.concatenate([blurred, raw.reshape(plane_count, flat_count)], axis=0)
     both_in = lax.all_to_all(both_flat, "scan", split_axis=1, concat_axis=0, tiled=True)
     both_in = both_in.reshape(lax.axis_size("scan"), 2, plane_count, -1)
@@ -71,8 +72,7 @@
     both_out = lax.all_to_all(jnp.stack([misfit_pencil, back_pencil]), "scan", split_axis=1, concat_axis=2, tiled=True)
     misfit = both_out[0]
     back_volume = both_out[1].reshape(plane_count, row_count, width_count)
-    padded_back = with_halo(back_volume, "row", halo_rows)
-    gradient = lateral_apply(back_band, padded_back)
+    gradient = blur_rows(back_band, back_volume, "row", halo_rows)
     stepped = estimate - step_size[0] * gradient
     shrink_level = step_size[0] * threshold[0]
     new_estimate = jnp.sign(stepped) * jnp.maximum(jnp.abs(stepped) - shrink_level, 0.0)

time: 82.8 us -> 82.3 us (level)
  blocking collectives: 31.5 us -> 0 us
  waiting for transfers between devices: 25.4 us -> 46.9 us
  starting transfers between devices: 10.9 us -> 17.8 us
  local copies, waits for them, and re-layouts: 6.17 us -> 8.13 us
  matrix products: 3.62 us -> 4.86 us
  other arithmetic: 2.85 us -> 1.75 us
    all_to_all x1 -> x0, blocking collectives: 31.5 us -> none  [body(): lax.all_to_all(jnp.stack([misfit_pencil, back_pencil]), 'scan', split_axi...]
    all_to_all x0 -> x1, waiting for transfers between devices: none -> 21.6 us  [body(): lax.all_to_all(jnp.stack([misfit_pencil, back_pencil]), 'scan', split_axi...]
    all_to_all x0 -> x1, starting transfers between devices: none -> 6.87 us  [body(): lax.all_to_all(jnp.stack([misfit_pencil, back_pencil]), 'scan', split_axi...]
    dot_general x2 -> x4, matrix products: 2.29 us -> 3.53 us  [lateral_apply(): return jnp.einsum('rk,pkc->prc', band, padded, precision=highest_mode)]
    select_n x4 -> x0, other arithmetic: 1.1 us -> none  [the longest x2 1.06 us: with_halo(): arrived = lax.ppermute(jnp.where(first, tail, head), axis, [(0, 1), (1, 0)])]
    dynamic_slice x0 -> x2, local copies, waits for them, and re-layouts: none -> 0.99 us  [blur_rows(): lax.dynamic_slice_in_dim(cells, jnp.where(first, rows - width, 0), width,...]
    another operation x1, local copies, waits for them, and re-layouts: 0.81 us -> 1.78 us  [body(): jnp.stack([misfit_pencil, back_pencil])]
  transfers between devices with their start and end apart: 3 -> 4, of which waited for: 3 -> 4; matrix products, arithmetic and copies ran while one was open for 5% -> 7% of each run, Pallas kernels for 0% -> 0%
where the time goes in v9:
time: 82.3 us; the launch traced here: 81.5 us
  waiting for transfers between devices  46.9 us (57%)
  starting transfers between devices  17.8 us (22%)
  local copies, waits for them, and re-layouts  8.13 us (10%)
  matrix products  4.86 us (6%)
  between operations  2.12 us (3%)
  other arithmetic  1.75 us (2%)
    all_to_all x1, waiting for transfers between devices, body(): lax.all_to_all(jnp.stack([misfit_pencil, back_pencil]), 'scan', split_axi...  21.6 us
    all_to_all x1, waiting for transfers between devices, body(): lax.all_to_all(both_flat, 'scan', split_axis=1, concat_axis=0, tiled=True)  21.5 us
    all_to_all x1, starting transfers between devices, body(): lax.all_to_all(jnp.stack([misfit_pencil, back_pencil]), 'scan', split_axi...  6.87 us
    all_to_all x1, starting transfers between devices, body(): lax.all_to_all(both_flat, 'scan', split_axis=1, concat_axis=0, tiled=True)  6.34 us
    ppermute x2, starting transfers between devices, blur_rows(): arrived = lax.ppermute(sent, axis, [(0, 1), (1, 0)])  4.56 us
    ppermute x2, waiting for transfers between devices, blur_rows(): arrived = lax.ppermute(sent, axis, [(0, 1), (1, 0)])  3.74 us
    dot_general x4, matrix products, lateral_apply(): return jnp.einsum('rk,pkc->prc', band, padded, precision=highest_mode)  3.53 us
    concatenate x3, local copies, waits for them, and re-layouts, body(): jnp.concatenate([blurred, raw.reshape(plane_count, flat_count)], axis=0)  2.97 us
  transfers between devices with their start and end apart: 4, of which 4 were waited for; matrix products, arithmetic and copies ran while one was open for 7% of the time, Pallas kernels for 0%

profile of v9, /device:TPU:0, one launch (start us, length us, event | category | flops | bytes accessed | tf_op | source)
XLA Modules:
  0.0 81.5 jit_solution(4290266452393810198)
XLA Ops:
  0.6 0.0 copy-start
  0.6 0.0 copy-start.2
  0.7 1.0 %constant_dynamic-slice_fusion.1 = f32[8,8,512]{2,1,0:T(8,128)S(1)} fusion(f32[8,32,512]{2,1,0:T(8,128)} %param.7, s32[]{:T(128)S(6)} %select_n.37), kind=kLoop, calls=%fused_computation.36 | loop fusion | bytes 262148 | tf_op jit(solution)/shard_map/dynamic_slice | solution.py:15
  1.6 3.0 %collective-permute-start = (f32[8,8,512]{2,1,0:T(8,128)S(1)}, f32[8,8,512]{2,1,0:T(8,128)S(1)}, u32[]{:S(2)}, u32[]{:S(2)}) collective-permute-start(f32[8,8,512]{2,1,0:T(8,128)S(1)} %constant_dynamic-slice_fusion.1), channel_id=1, source_target_pairs={{0,1},{1,0},{2,3},{3,2},{4,5},{5,4},{6,7},{7,6},{8,9},{9,8},{10,11... | collective-permute-start | bytes 393224 | tf_op jit(solution)/shard_map/ppermute | solution.py:16
  4.6 0.7 rev.3
  5.4 1.2 %concatenate.9 = f32[8,16,1024]{2,1,0:T(8,128)S(1)} reshape(f32[8,32,512]{2,1,0:T(8,128)} %param.8) | data formatting | bytes 1048576 | tf_op jit(solution)/shard_map/concatenate | solution.py:64
  6.6 0.0 copy-done.2
  6.6 0.1 select_reduce_fusion.1
  6.7 0.0 copy-done
  6.8 0.6 convolution_bitcast_fusion.2
  7.4 0.7 collective-permute-done
  8.1 0.6 fusion
  8.8 0.2 concatenate.8
  9.0 0.1 pad_maximum_fusion
  9.1 1.6 %copy.34 = f32[16,16,1024]{2,0,1:T(8,128)} copy(f32[16,16,1024]{2,1,0:T(8,128)S(1)} %pad_maximum_fusion) | data formatting | bytes 2097152 | tf_op jit(solution)/shard_map/concatenate | solution.py:64
  10.6 0.0 copy-start.1
  10.7 0.0 copy-start.3
  10.7 6.3 %all-to-all-start = ((f32[16,16,1024]{2,0,1:T(8,128)}), f32[16,16,1024]{2,0,1:T(8,128)S(1)}, u32[]{:S(2)}, u32[]{:S(2)}) async-start(f32[16,16,1024]{2,0,1:T(8,128)} %copy.34), calls=%async_computation | async-start | bytes 2097152 | tf_op jit(solution)/shard_map/all_to_all | solution.py:65
  17.0 0.0 copy-done.1
  17.0 0.1 subtract_subtract_fusion
  17.1 0.0 copy-done.3
  17.1 1.4 %select_reduce_fusion = f32[128,128]{1,0:T(8,128)S(1)} fusion(f32[64]{0:T(128)S(1)} %copy-done.3, s32[128,128]{1,0:T(8,128)S(1)} %subtract_subtract_fusion), kind=kLoop, calls=%fused_computation | loop fusion | flops 3129344 | bytes 131328 | tf_op jit(solution)/shard_map/reduce_sum | solution.py:49
  18.5 21.5 %all-to-all-done = f32[16,16,1024]{2,0,1:T(8,128)S(1)} async-done(((f32[16,16,1024]{2,0,1:T(8,128)}), f32[16,16,1024]{2,0,1:T(8,128)S(1)}, u32[]{:S(2)}, u32[]{:S(2)}) %all-to-all-start) | async-done | bytes 1048608 | tf_op jit(solution)/shard_map/all_to_all | solution.py:65
  39.9 0.6 convolution_subtract_fusion
  40.6 0.7 convolution_bitcast_fusion
  41.3 0.1 pad_maximum_fusion.1
  41.4 1.8 %copy.35 = f32[2,128,1024]{2,0,1:T(2,128)} copy(f32[2,128,1024]{2,1,0:T(8,128)S(1)} %pad_maximum_fusion.1) | data formatting | bytes 2097152 | tf_op jit(solution)/shard_map/stack | solution.py:72
  43.1 6.9 %all-to-all-start.1 = ((f32[2,128,1024]{2,0,1:T(2,128)}), f32[2,128,1024]{2,0,1:T(2,128)S(1)}, u32[]{:S(2)}, u32[]{:S(2)}) async-start(f32[2,128,1024]{2,0,1:T(2,128)} %copy.35), calls=%async_computation.1 | async-start | bytes 2097152 | tf_op jit(solution)/shard_map/all_to_all | solution.py:72
  51.3 21.6 %all-to-all-done.1 = f32[2,128,1024]{2,0,1:T(2,128)S(1)} async-done(((f32[2,128,1024]{2,0,1:T(2,128)}), f32[2,128,1024]{2,0,1:T(2,128)S(1)}, u32[]{:S(2)}, u32[]{:S(2)}) %all-to-all-start.1) | async-done | bytes 1048608 | tf_op jit(solution)/shard_map/all_to_all | solution.py:72
  73.0 0.6 copy.43
  73.6 0.1 fusion.19
  73.6 0.1 reshape_squeeze.14
  73.8 1.6 %collective-permute-start.1 = (f32[8,8,512]{2,1,0:T(8,128)S(1)}, f32[8,8,512]{2,1,0:T(8,128)S(1)}, u32[]{:S(2)}, u32[]{:S(2)}) collective-permute-start(f32[8,8,512]{2,1,0:T(8,128)S(1)} %constant_dynamic-slice_fusion), channel_id=1, source_target_pairs={{0,1},{1,0},{2,3},{3,2},{4,5},{5,4},{6,7},{7,6},{8,9},{9,8},{10,11... | collective-permute-start | bytes 393224 | tf_op jit(solution)/shard_map/ppermute | solution.py:16
  75.3 0.9 %reshape_squeeze.15 = f32[8,32,512]{2,1,0:T(8,128)} reshape(f32[1,8,16,1024]{3,2,1,0:T(8,128)S(1)} %get-tuple-element.4) | data formatting | bytes 1048576 | tf_op jit(solution)/shard_map/reshape;squeeze | solution.py:79
  76.2 0.6 fusion.7
  76.8 3.0 %collective-permute-done.1 = f32[8,8,512]{2,1,0:T(8,128)S(1)} collective-permute-done((f32[8,8,512]{2,1,0:T(8,128)S(1)}, f32[8,8,512]{2,1,0:T(8,128)S(1)}, u32[]{:S(2)}, u32[]{:S(2)}) %collective-permute-start.1) | collective-permute-done | bytes 131104 | tf_op jit(solution)/shard_map/ppermute | solution.py:16
  79.8 1.6 %maximum_multiply_fusion = f32[8,32,512]{2,1,0:T(8,128)} fusion(f32[8,32,512]{2,1,0:T(8,128)S(1)} %copy-done, f32[8,512,32]{1,2,0:T(8,128)S(1)} %fusion.7, f32[8,8,512]{2,1,0:T(8,128)S(1)} %collective-permute-done.1, f32[]{:T(128)S(6)} %mul.18, f32[]{:T(128)} %bitcast.52, f32[32,48]{1,0:T(8,128)S(1)} %get-tuple-element.2, pred[]{:T(512)S(6)} %eq.49), kind=kOutput, calls=%fused_computation.16 | convolution fusion | flops 13631744 | bytes 1736713 | tf_op jit(solution)/shard_map/rk,pkc->prc/dot_general | solution.py:38
  (2 shorter events, 0.0 us)
Async XLA Ops:
  0.6 6.1 %copy-start = (f32[8,32,512]{2,1,0:T(8,128)S(1)}, f32[8,32,512]{2,1,0:T(8,128)}, u32[]{:S(2)}) copy-start(f32[8,32,512]{2,1,0:T(8,128)} %param.7) | copy-start | bytes 1572868
  0.6 6.0 %copy-start.2 = (f32[17]{0:T(128)S(1)}, f32[17]{0:T(128)}, u32[]{:S(2)}) copy-start(f32[17]{0:T(128)} %param.11) | copy-start | bytes 208
  1.6 6.5 %collective-permute-start = (f32[8,8,512]{2,1,0:T(8,128)S(1)}, f32[8,8,512]{2,1,0:T(8,128)S(1)}, u32[]{:S(2)}, u32[]{:S(2)}) collective-permute-start(f32[8,8,512]{2,1,0:T(8,128)S(1)} %constant_dynamic-slice_fusion.1), channel_id=1, source_target_pairs={{0,1},{1,0},{2,3},{3,2},{4,5},{5,4},{6,7},{7,6},{8,9},{9,8},{10,11... | collective-permute-start | bytes 393224 | tf_op jit(solution)/shard_map/ppermute | solution.py:16
  10.6 6.3 %copy-start.1 = (s32[128]{0:T(128)S(1)}, s32[128]{0:T(128)}, u32[]{:S(2)}) copy-start(s32[128]{0:T(128)} %param.9) | copy-start | bytes 1540
  10.7 6.4 %copy-start.3 = (f32[64]{0:T(128)S(1)}, f32[64]{0:T(128)}, u32[]{:S(2)}) copy-start(f32[64]{0:T(128)} %param.10) | copy-start | bytes 772
  10.7 29.3 %all-to-all-start = ((f32[16,16,1024]{2,0,1:T(8,128)}), f32[16,16,1024]{2,0,1:T(8,128)S(1)}, u32[]{:S(2)}, u32[]{:S(2)}) async-start(f32[16,16,1024]{2,0,1:T(8,128)} %copy.34), calls=%async_computation | async-start | bytes 2097152 | tf_op jit(solution)/shard_map/all_to_all | solution.py:65
  43.1 29.8 %all-to-all-start.1 = ((f32[2,128,1024]{2,0,1:T(2,128)}), f32[2,128,1024]{2,0,1:T(2,128)S(1)}, u32[]{:S(2)}, u32[]{:S(2)}) async-start(f32[2,128,1024]{2,0,1:T(2,128)} %copy.35), calls=%async_computation.1 | async-start | bytes 2097152 | tf_op jit(solution)/shard_map/all_to_all | solution.py:72
  73.8 6.1 %collective-permute-start.1 = (f32[8,8,512]{2,1,0:T(8,128)S(1)}, f32[8,8,512]{2,1,0:T(8,128)S(1)}, u32[]{:S(2)}, u32[]{:S(2)}) collective-permute-start(f32[8,8,512]{2,1,0:T(8,128)S(1)} %constant_dynamic-slice_fusion), channel_id=1, source_target_pairs={{0,1},{1,0},{2,3},{3,2},{4,5},{5,4},{6,7},{7,6},{8,9},{9,8},{10,11... | collective-permute-start | bytes 393224 | tf_op jit(solution)/shard_map/ppermute | solution.py:16

commit v10 on v9

--- a/solution.py
+++ b/solution.py
@@ -58,20 +58,18 @@
     flat_count = row_count * width_count
     halo_rows = lateral_psf.shape[0] // 2
     sheet_psf = sheet_matrix(offsets, depth_psf, offsets.shape[0])
+    raw_pencil = lax.all_to_all(raw.reshape(plane_count, flat_count), "scan", split_axis=1, concat_axis=0, tiled=True)
     blur_band = band_matrix(lateral_psf, row_count, 0)
     back_band = band_matrix(lateral_psf[::-1], row_count, 0)
     blurred = blur_rows(blur_band, estimate, "row", halo_rows).reshape(plane_count, flat_count)
-    both_flat = jnp.concatenate([blurred, raw.reshape(plane_count, flat_count)], axis=0)
-    both_in = lax.all_to_all(both_flat, "scan", split_axis=1, concat_axis=0, tiled=True)
-    both_in = both_in.reshape(lax.axis_size("scan"), 2, plane_count, -1)
-    pencil = both_in[:, 0].reshape(offsets.shape[0], -1)
-    raw_pencil = both_in[:, 1].reshape(offsets.shape[0], -1)
+    pencil = lax.all_to_all(blurred, "scan", split_axis=1, concat_axis=0, tiled=True)
     predicted_pencil = jnp.dot(sheet_psf, pencil, precision=highest_mode)
     misfit_pencil = predicted_pencil - raw_pencil
     back_pencil = transpose_apply(sheet_psf, misfit_pencil)
-    both_out = lax.all_to_all(jnp.stack([misfit_pencil, back_pencil]), "scan", split_axis=1, concat_axis=2, tiled=True)
-    misfit = both_out[0]
-    back_volume = both_out[1].reshape(plane_count, row_count, width_count)
+    back_flat = lax.all_to_all(back_pencil, "scan", split_axis=0, concat_axis=1, tiled=True)
+    back_flat, misfit_pencil = lax.optimization_barrier((back_flat, misfit_pencil))
+    misfit = lax.all_to_all(misfit_pencil, "scan", split_axis=0, concat_axis=1, tiled=True)
+    back_volume = back_flat.reshape(plane_count, row_count, width_count)
     gradient = blur_rows(back_band, back_volume, "row", halo_rows)
     stepped = estimate - step_size[0] * gradient
     shrink_level = step_size[0] * threshold[0]

time: 82.3 us -> 85.4 us (1.038)
  blocking collectives: 0 us -> 18.4 us
  waiting for transfers between devices: 46.9 us -> 31.8 us
  local copies, waits for them, and re-layouts: 8.13 us -> 5.22 us
  matrix products: 4.86 us -> 6.97 us
  starting transfers between devices: 17.8 us -> 18.8 us
    all_to_all x0 -> x1, blocking collectives: none -> 18.4 us  [body(): lax.all_to_all(back_pencil, 'scan', split_axis=0, concat_axis=1, tiled=True)]
    all_to_all x2 -> x3, waiting for transfers between devices: 43.1 us -> 24.9 us  [the longest x1 13 us: body(): lax.all_to_all(blurred, 'scan', split_axis=1, concat_axis=0, tiled=True)]
    all_to_all x1 -> x5, local copies, waits for them, and re-layouts: 0.61 us -> 3.89 us  [the longest x2 2.31 us: body(): lax.all_to_all(raw.reshape(plane_count, flat_count), 'scan', split_axis=1...]
    ppermute x2, waiting for transfers between devices: 3.74 us -> 6.88 us  [blur_rows(): arrived = lax.ppermute(sent, axis, [(0, 1), (1, 0)])]
    concatenate x3 -> x0, local copies, waits for them, and re-layouts: 2.97 us -> none  [body(): jnp.concatenate([blurred, raw.reshape(plane_count, flat_count)], axis=0)]
    another operation x3 -> x0, local copies, waits for them, and re-layouts: 2.73 us -> none  [the longest x1 1.78 us: body(): jnp.stack([misfit_pencil, back_pencil])]
    all_to_all x2 -> x3, starting transfers between devices: 13.2 us -> 15.7 us  [the longest x1 7.52 us: body(): lax.all_to_all(raw.reshape(plane_count, flat_count), 'scan', split_axis=1...]
    ppermute x2, starting transfers between devices: 4.56 us -> 3.11 us  [blur_rows(): arrived = lax.ppermute(sent, axis, [(0, 1), (1, 0)])]
  transfers between devices with their start and end apart: 4 -> 5, of which waited for: 4 -> 5; matrix products, arithmetic and copies ran while one was open for 7% -> 8% of each run, Pallas kernels for 0% -> 0%
where the time goes in v10:
time: 85.4 us; the launch traced here: 84.8 us
  waiting for transfers between devices  31.8 us (37%)
  starting transfers between devices  18.8 us (22%)
  blocking collectives  18.4 us (22%)
  matrix products  6.97 us (8%)
  local copies, waits for them, and re-layouts  5.22 us (6%)
  between operations  2.07 us (2%)
  other arithmetic  1.58 us (2%)
    all_to_all x1, blocking collectives, body(): lax.all_to_all(back_pencil, 'scan', split_axis=0, concat_axis=1, tiled=True)  18.4 us
    all_to_all x1, waiting for transfers between devices, body(): lax.all_to_all(blurred, 'scan', split_axis=1, concat_axis=0, tiled=True)  13 us
    all_to_all x1, starting transfers between devices, body(): lax.all_to_all(raw.reshape(plane_count, flat_count), 'scan', split_axis=1...  7.52 us
    ppermute x2, waiting for transfers between devices, blur_rows(): arrived = lax.ppermute(sent, axis, [(0, 1), (1, 0)])  6.88 us
    all_to_all x1, waiting for transfers between devices, body(): lax.all_to_all(raw.reshape(plane_count, flat_count), 'scan', split_axis=1...  6.58 us
    all_to_all x1, waiting for transfers between devices, body(): lax.all_to_all(misfit_pencil, 'scan', split_axis=0, concat_axis=1, tiled=...  5.31 us
    all_to_all x1, starting transfers between devices, body(): lax.all_to_all(blurred, 'scan', split_axis=1, concat_axis=0, tiled=True)  4.1 us
    all_to_all x1, starting transfers between devices, body(): lax.all_to_all(misfit_pencil, 'scan', split_axis=0, concat_axis=1, tiled=...  4.1 us
  transfers between devices with their start and end apart: 5, of which 5 were waited for; matrix products, arithmetic and copies ran while one was open for 8% of the time, Pallas kernels for 0%

profile of v10, /device:TPU:0, one launch (start us, length us, event | category | flops | bytes accessed | tf_op | source)
XLA Modules:
  0.0 84.8 jit_solution(8935472928152048701)
XLA Ops:
  0.6 1.2 %all_to_all.58 = f32[8,16,1024]{2,1,0:T(8,128)S(1)} reshape(f32[8,32,512]{2,1,0:T(8,128)} %param.8) | data formatting | bytes 1048576 | tf_op jit(solution)/shard_map/all_to_all | solution.py:61
  1.8 1.1 %copy.20 = f32[8,16,1024]{2,0,1:T(8,128)} copy(f32[8,16,1024]{2,1,0:T(8,128)S(1)} %all_to_all.58) | data formatting | bytes 1048576 | tf_op jit(solution)/shard_map/all_to_all | solution.py:61
  2.9 0.0 copy-start
  2.9 0.0 copy-start.2
  2.9 7.5 %all-to-all-start.1 = ((f32[8,16,1024]{2,0,1:T(8,128)}), f32[8,16,1024]{2,0,1:T(8,128)S(1)}, u32[]{:S(2)}, u32[]{:S(2)}) async-start(f32[8,16,1024]{2,0,1:T(8,128)} %copy.20), calls=%async_computation.1 | async-start | bytes 1048576 | tf_op jit(solution)/shard_map/all_to_all | solution.py:61
  10.5 0.0 copy-done
  10.5 1.6 %collective-permute-start = (f32[8,8,512]{2,1,0:T(8,128)S(1)}, f32[8,8,512]{2,1,0:T(8,128)S(1)}, u32[]{:S(2)}, u32[]{:S(2)}) collective-permute-start(f32[8,8,512]{2,1,0:T(8,128)S(1)} %constant_dynamic-slice_fusion.1), channel_id=1, source_target_pairs={{0,1},{1,0},{2,3},{3,2},{4,5},{5,4},{6,7},{7,6},{8,9},{9,8},{10,11... | collective-permute-start | bytes 393224 | tf_op jit(solution)/shard_map/ppermute | solution.py:16
  12.1 0.0 copy-done.2
  12.1 0.1 rev.3
  12.2 0.1 select_reduce_fusion.2
  12.3 0.6 convolution_bitcast_fusion.2
  13.0 3.5 %collective-permute-done = f32[8,8,512]{2,1,0:T(8,128)S(1)} collective-permute-done((f32[8,8,512]{2,1,0:T(8,128)S(1)}, f32[8,8,512]{2,1,0:T(8,128)S(1)}, u32[]{:S(2)}, u32[]{:S(2)}) %collective-permute-start) | collective-permute-done | bytes 131104 | tf_op jit(solution)/shard_map/ppermute | solution.py:16
  16.4 0.6 fusion
  17.1 0.2 all_to_all.54
  17.3 1.1 %copy.19 = f32[8,16,1024]{2,0,1:T(8,128)} copy(f32[8,16,1024]{2,1,0:T(8,128)S(1)} %all_to_all.54) | data formatting | bytes 1048576 | tf_op jit(solution)/shard_map/all_to_all | solution.py:65
  18.4 0.0 copy-start.1
  18.4 0.0 copy-start.3
  18.4 6.6 %all-to-all-done.1 = f32[8,16,1024]{2,0,1:T(8,128)S(1)} async-done(((f32[8,16,1024]{2,0,1:T(8,128)}), f32[8,16,1024]{2,0,1:T(8,128)S(1)}, u32[]{:S(2)}, u32[]{:S(2)}) %all-to-all-start.1) | async-done | bytes 524320 | tf_op jit(solution)/shard_map/all_to_all | solution.py:61
  24.9 4.1 %all-to-all-start = ((f32[8,16,1024]{2,0,1:T(8,128)}), f32[8,16,1024]{2,0,1:T(8,128)S(1)}, u32[]{:S(2)}, u32[]{:S(2)}) async-start(f32[8,16,1024]{2,0,1:T(8,128)} %copy.19), calls=%async_computation | async-start | bytes 1048576 | tf_op jit(solution)/shard_map/all_to_all | solution.py:65
  29.0 0.0 copy-done.1
  29.1 0.1 subtract_subtract_fusion
  29.1 0.0 copy-done.3
  29.2 1.4 %select_reduce_fusion = f32[128,128]{1,0:T(8,128)S(1)} fusion(f32[64]{0:T(128)S(1)} %copy-done.3, s32[128,128]{1,0:T(8,128)S(1)} %subtract_subtract_fusion), kind=kLoop, calls=%fused_computation | loop fusion | flops 3129344 | bytes 131328 | tf_op jit(solution)/shard_map/reduce_sum | solution.py:49
  30.5 13.0 %all-to-all-done = f32[8,16,1024]{2,0,1:T(8,128)S(1)} async-done(((f32[8,16,1024]{2,0,1:T(8,128)}), f32[8,16,1024]{2,0,1:T(8,128)S(1)}, u32[]{:S(2)}, u32[]{:S(2)}) %all-to-all-start) | async-done | bytes 524320 | tf_op jit(solution)/shard_map/all_to_all | solution.py:65
  43.5 1.4 %convolution_subtract_fusion = f32[128,1024]{1,0:T(8,128)} fusion(f32[8,16,1024]{2,0,1:T(8,128)S(1)} %all-to-all-done.1, f32[8,16,1024]{2,0,1:T(8,128)S(1)} %all-to-all-done, f32[128,128]{1,0:T(8,128)S(1)} %select_reduce_fusion, s32[128]{0:T(128)S(1)} %copy-done.1), kind=kOutput, calls=%fused_computation.7 | convolution fusion | flops 201555968 | bytes 1638912 | tf_op jit(solution)/shard_map/dot_general | solution.py:66
  44.9 1.7 %convolution_bitcast_fusion = f32[16,8,1024]{2,1,0:T(8,128)S(1)} fusion(f32[128,1024]{1,0:T(8,128)} %convolution_subtract_fusion, f32[128,128]{1,0:T(8,128)S(1)} %select_reduce_fusion, s32[128]{0:T(128)S(1)} %copy-done.1), kind=kOutput, calls=%fused_computation.3 | convolution fusion | flops 201424896 | bytes 1114624 | tf_op jit(solution)/shard_map/dot_general | solution.py:53
  46.7 18.4 %all_to_all.73 = f32[16,8,1024]{2,1,0:T(8,128)S(1)} all-to-all(f32[16,8,1024]{2,1,0:T(8,128)S(1)} %convolution_bitcast_fusion), channel_id=1, replica_groups=mesh['scan'=16,'row'=2] {'scan'}, dimensions={0} | all-to-all | bytes 1048576 | tf_op jit(solution)/shard_map/all_to_all | solution.py:69
  65.0 4.1 %all-to-all-start.3 = ((f32[16,8,1024]{2,1,0:T(8,128)}), f32[16,8,1024]{2,1,0:T(8,128)S(1)}, u32[]{:S(2)}, u32[]{:S(2)}) async-start(f32[16,8,1024]{2,1,0:T(8,128)} %bitcast.16), calls=%async_computation.3 | async-start | bytes 1048576 | tf_op jit(solution)/shard_map/all_to_all | solution.py:71
  70.4 0.3 copy.30
  70.8 1.6 %collective-permute-start.1 = (f32[8,8,512]{2,1,0:T(8,128)S(1)}, f32[8,8,512]{2,1,0:T(8,128)S(1)}, u32[]{:S(2)}, u32[]{:S(2)}) collective-permute-start(f32[8,8,512]{2,1,0:T(8,128)S(1)} %constant_dynamic-slice_fusion), channel_id=1, source_target_pairs={{0,1},{1,0},{2,3},{3,2},{4,5},{5,4},{6,7},{7,6},{8,9},{9,8},{10,11... | collective-permute-start | bytes 393224 | tf_op jit(solution)/shard_map/ppermute | solution.py:16
  72.3 0.9 %fusion.8 = f32[8,512,32]{1,2,0:T(8,128)S(1)} fusion(f32[32,48]{1,0:T(8,128)S(1)} %get-tuple-element.7, f32[1,8,32,512]{3,1,2,0:T(8,128)S(1)} %bitcast.55), kind=kOutput, calls=%fused_computation.23 | convolution fusion | flops 50331648 | bytes 1054720 | tf_op jit(solution)/shard_map/rk,pkc->prc/dot_general | solution.py:38
  73.3 3.4 %collective-permute-done.1 = f32[8,8,512]{2,1,0:T(8,128)S(1)} collective-permute-done((f32[8,8,512]{2,1,0:T(8,128)S(1)}, f32[8,8,512]{2,1,0:T(8,128)S(1)}, u32[]{:S(2)}, u32[]{:S(2)}) %collective-permute-start.1) | collective-permute-done | bytes 131104 | tf_op jit(solution)/shard_map/ppermute | solution.py:16
  76.7 1.6 %maximum_multiply_fusion = f32[8,32,512]{2,1,0:T(8,128)} fusion(f32[8,32,512]{2,1,0:T(8,128)S(1)} %copy-done, f32[8,512,32]{1,2,0:T(8,128)S(1)} %fusion.8, f32[8,8,512]{2,1,0:T(8,128)S(1)} %collective-permute-done.1, f32[]{:T(128)S(6)} %mul.18, f32[]{:T(128)} %bitcast.51, f32[32,48]{1,0:T(8,128)S(1)} %get-tuple-element.7, pred[]{:T(512)S(6)} %eq.49), kind=kOutput, calls=%fused_computation.13 | convolution fusion | flops 13631744 | bytes 1736713 | tf_op jit(solution)/shard_map/rk,pkc->prc/dot_general | solution.py:38
  78.3 5.3 %all-to-all-done.3 = f32[16,8,1024]{2,1,0:T(8,128)S(1)} async-done(((f32[16,8,1024]{2,1,0:T(8,128)}), f32[16,8,1024]{2,1,0:T(8,128)S(1)}, u32[]{:S(2)}, u32[]{:S(2)}) %all-to-all-start.3) | async-done | bytes 524320 | tf_op jit(solution)/shard_map/all_to_all | solution.py:71
  83.6 0.3 copy.22
  83.9 0.9 %reshape.67 = f32[8,32,512]{2,1,0:T(8,128)} reshape(f32[8,16,1024]{2,1,0:T(8,128)S(1)} %copy.22) | data formatting | bytes 1048576 | tf_op jit(solution)/shard_map/reshape | solution.py:77
  (3 shorter events, 0.0 us)
Async XLA Ops:
  2.9 7.5 %copy-start = (f32[8,32,512]{2,1,0:T(8,128)S(1)}, f32[8,32,512]{2,1,0:T(8,128)}, u32[]{:S(2)}) copy-start(f32[8,32,512]{2,1,0:T(8,128)} %param.7) | copy-start | bytes 1572868
  2.9 9.1 %copy-start.2 = (f32[17]{0:T(128)S(1)}, f32[17]{0:T(128)}, u32[]{:S(2)}) copy-start(f32[17]{0:T(128)} %param.11) | copy-start | bytes 208
  2.9 22.0 %all-to-all-start.1 = ((f32[8,16,1024]{2,0,1:T(8,128)}), f32[8,16,1024]{2,0,1:T(8,128)S(1)}, u32[]{:S(2)}, u32[]{:S(2)}) async-start(f32[8,16,1024]{2,0,1:T(8,128)} %copy.20), calls=%async_computation.1 | async-start | bytes 1048576 | tf_op jit(solution)/shard_map/all_to_all | solution.py:61
  10.5 5.9 %collective-permute-start = (f32[8,8,512]{2,1,0:T(8,128)S(1)}, f32[8,8,512]{2,1,0:T(8,128)S(1)}, u32[]{:S(2)}, u32[]{:S(2)}) collective-permute-start(f32[8,8,512]{2,1,0:T(8,128)S(1)} %constant_dynamic-slice_fusion.1), channel_id=1, source_target_pairs={{0,1},{1,0},{2,3},{3,2},{4,5},{5,4},{6,7},{7,6},{8,9},{9,8},{10,11... | collective-permute-start | bytes 393224 | tf_op jit(solution)/shard_map/ppermute | solution.py:16
  18.4 10.7 %copy-start.1 = (s32[128]{0:T(128)S(1)}, s32[128]{0:T(128)}, u32[]{:S(2)}) copy-start(s32[128]{0:T(128)} %param.9) | copy-start | bytes 1540
  18.4 10.8 %copy-start.3 = (f32[64]{0:T(128)S(1)}, f32[64]{0:T(128)}, u32[]{:S(2)}) copy-start(f32[64]{0:T(128)} %param.10) | copy-start | bytes 772
  24.9 18.6 %all-to-all-start = ((f32[8,16,1024]{2,0,1:T(8,128)}), f32[8,16,1024]{2,0,1:T(8,128)S(1)}, u32[]{:S(2)}, u32[]{:S(2)}) async-start(f32[8,16,1024]{2,0,1:T(8,128)} %copy.19), calls=%async_computation | async-start | bytes 1048576 | tf_op jit(solution)/shard_map/all_to_all | solution.py:65
  65.0 18.6 %all-to-all-start.3 = ((f32[16,8,1024]{2,1,0:T(8,128)}), f32[16,8,1024]{2,1,0:T(8,128)S(1)}, u32[]{:S(2)}, u32[]{:S(2)}) async-start(f32[16,8,1024]{2,1,0:T(8,128)} %bitcast.16), calls=%async_computation.3 | async-start | bytes 1048576 | tf_op jit(solution)/shard_map/all_to_all | solution.py:71
  70.8 5.9 %collective-permute-start.1 = (f32[8,8,512]{2,1,0:T(8,128)S(1)}, f32[8,8,512]{2,1,0:T(8,128)S(1)}, u32[]{:S(2)}, u32[]{:S(2)}) collective-permute-start(f32[8,8,512]{2,1,0:T(8,128)S(1)} %constant_dynamic-slice_fusion), channel_id=1, source_target_pairs={{0,1},{1,0},{2,3},{3,2},{4,5},{5,4},{6,7},{7,6},{8,9},{9,8},{10,11... | collective-permute-start | bytes 393224 | tf_op jit(solution)/shard_map/ppermute | solution.py:16

commit v11 on v10

--- a/solution.py
+++ b/solution.py
@@ -58,11 +58,14 @@
     flat_count = row_count * width_count
     halo_rows = lateral_psf.shape[0] // 2
     sheet_psf = sheet_matrix(offsets, depth_psf, offsets.shape[0])
-    raw_pencil = lax.all_to_all(raw.reshape(plane_count, flat_count), "scan", split_axis=1, concat_axis=0, tiled=True)
     blur_band = band_matrix(lateral_psf, row_count, 0)
     back_band = band_matrix(lateral_psf[::-1], row_count, 0)
     blurred = blur_rows(blur_band, estimate, "row", halo_rows).reshape(plane_count, flat_count)
-    pencil = lax.all_to_all(blurred, "scan", split_axis=1, concat_axis=0, tiled=True)
+    both_flat = jnp.concatenate([blurred, raw.reshape(plane_count, flat_count)], axis=0)
+    both_in = lax.all_to_all(both_flat, "scan", split_axis=1, concat_axis=0, tiled=True)
+    both_in = both_in.reshape(lax.axis_size("scan"), 2, plane_count, -1)
+    pencil = both_in[:, 0].reshape(offsets.shape[0], -1)
+    raw_pencil = both_in[:, 1].reshape(offsets.shape[0], -1)
     predicted_pencil = jnp.dot(sheet_psf, pencil, precision=highest_mode)
     misfit_pencil = predicted_pencil - raw_pencil
     back_pencil = transpose_apply(sheet_psf, misfit_pencil)

time: 85.4 us -> 84.5 us (0.989)
  starting transfers between devices: 18.8 us -> 15 us
  blocking collectives: 18.4 us -> 21.1 us
  local copies, waits for them, and re-layouts: 5.22 us -> 6.21 us
  waiting for transfers between devices: 31.8 us -> 30.9 us
    all_to_all x2 -> x1, starting transfers between devices: 11.6 us -> 6.34 us  [body(): lax.all_to_all(both_flat, 'scan', split_axis=1, concat_axis=0, tiled=True)]
    all_to_all x4 -> x0, local copies, waits for them, and re-layouts: 3.58 us -> none  [the longest x2 2.31 us: body(): lax.all_to_all(raw.reshape(plane_count, flat_count), 'scan', split_axis=1...]
    concatenate x0 -> x3, local copies, waits for them, and re-layouts: none -> 2.97 us  [body(): jnp.concatenate([blurred, raw.reshape(plane_count, flat_count)], axis=0)]
    all_to_all x1, blocking collectives: 18.4 us -> 21.1 us  [body(): lax.all_to_all(back_pencil, 'scan', split_axis=0, concat_axis=1, tiled=True)]
    ppermute x2, waiting for transfers between devices: 6.88 us -> 4.15 us  [blur_rows(): arrived = lax.ppermute(sent, axis, [(0, 1), (1, 0)])]
    all_to_all x2 -> x1, waiting for transfers between devices: 19.6 us -> 21.5 us  [body(): lax.all_to_all(both_flat, 'scan', split_axis=1, concat_axis=0, tiled=True)]
    ppermute x2, starting transfers between devices: 3.11 us -> 4.56 us  [blur_rows(): arrived = lax.ppermute(sent, axis, [(0, 1), (1, 0)])]
    dynamic_slice x2, local copies, waits for them, and re-layouts: 0.04 us -> 0.99 us  [blur_rows(): lax.dynamic_slice_in_dim(cells, jnp.where(first, rows - width, 0), width,...]
  transfers between devices with their start and end apart: 5 -> 4, of which waited for: 5 -> 4; matrix products, arithmetic and copies ran while one was open for 8% -> 8% of each run, Pallas kernels for 0% -> 0%
where the time goes in v11:
time: 84.5 us; the launch traced here: 84 us
  waiting for transfers between devices  30.9 us (37%)
  blocking collectives  21.1 us (25%)
  starting transfers between devices  15 us (18%)
  matrix products  6.96 us (8%)
  local copies, waits for them, and re-layouts  6.21 us (7%)
  between operations  2.09 us (2%)
  other arithmetic  1.68 us (2%)
    all_to_all x1, waiting for transfers between devices, body(): lax.all_to_all(both_flat, 'scan', split_axis=1, concat_axis=0, tiled=True)  21.5 us
    all_to_all x1, blocking collectives, body(): lax.all_to_all(back_pencil, 'scan', split_axis=0, concat_axis=1, tiled=True)  21.1 us
    all_to_all x1, starting transfers between devices, body(): lax.all_to_all(both_flat, 'scan', split_axis=1, concat_axis=0, tiled=True)  6.34 us
    all_to_all x1, waiting for transfers between devices, body(): lax.all_to_all(misfit_pencil, 'scan', split_axis=0, concat_axis=1, tiled=...  5.31 us
    ppermute x2, starting transfers between devices, blur_rows(): arrived = lax.ppermute(sent, axis, [(0, 1), (1, 0)])  4.56 us
    ppermute x2, waiting for transfers between devices, blur_rows(): arrived = lax.ppermute(sent, axis, [(0, 1), (1, 0)])  4.15 us
    all_to_all x1, starting transfers between devices, body(): lax.all_to_all(misfit_pencil, 'scan', split_axis=0, concat_axis=1, tiled=...  4.1 us
    dot_general x4, matrix products, lateral_apply(): return jnp.einsum('rk,pkc->prc', band, padded, precision=highest_mode)  3.8 us
  transfers between devices with their start and end apart: 4, of which 4 were waited for; matrix products, arithmetic and copies ran while one was open for 8% of the time, Pallas kernels for 0%

profile of v11, /device:TPU:0, one launch (start us, length us, event | category | flops | bytes accessed | tf_op | source)
XLA Modules:
  0.0 84.0 jit_solution(14876159002783412787)
XLA Ops:
  0.6 0.0 copy-start
  0.6 0.0 copy-start.2
  0.7 1.0 %constant_dynamic-slice_fusion.1 = f32[8,8,512]{2,1,0:T(8,128)S(1)} fusion(f32[8,32,512]{2,1,0:T(8,128)} %param.7, s32[]{:T(128)S(6)} %select_n.37), kind=kLoop, calls=%fused_computation.35 | loop fusion | bytes 262148 | tf_op jit(solution)/shard_map/dynamic_slice | solution.py:15
  1.6 3.0 %collective-permute-start = (f32[8,8,512]{2,1,0:T(8,128)S(1)}, f32[8,8,512]{2,1,0:T(8,128)S(1)}, u32[]{:S(2)}, u32[]{:S(2)}) collective-permute-start(f32[8,8,512]{2,1,0:T(8,128)S(1)} %constant_dynamic-slice_fusion.1), channel_id=1, source_target_pairs={{0,1},{1,0},{2,3},{3,2},{4,5},{5,4},{6,7},{7,6},{8,9},{9,8},{10,11... | collective-permute-start | bytes 393224 | tf_op jit(solution)/shard_map/ppermute | solution.py:16
  4.6 0.7 rev.3
  5.4 1.2 %concatenate.9 = f32[8,16,1024]{2,1,0:T(8,128)S(1)} reshape(f32[8,32,512]{2,1,0:T(8,128)} %param.8) | data formatting | bytes 1048576 | tf_op jit(solution)/shard_map/concatenate | solution.py:64
  6.6 0.0 copy-done.2
  6.6 0.1 select_reduce_fusion.2
  6.7 0.0 copy-done
  6.8 0.6 convolution_bitcast_fusion.2
  7.4 0.7 collective-permute-done
  8.1 0.6 fusion
  8.8 0.2 concatenate.8
  9.0 0.1 pad_maximum_fusion
  9.1 1.6 %copy.29 = f32[16,16,1024]{2,0,1:T(8,128)} copy(f32[16,16,1024]{2,1,0:T(8,128)S(1)} %pad_maximum_fusion) | data formatting | bytes 2097152 | tf_op jit(solution)/shard_map/concatenate | solution.py:64
  10.7 0.0 copy-start.1
  10.7 0.0 copy-start.3
  10.7 6.3 %all-to-all-start = ((f32[16,16,1024]{2,0,1:T(8,128)}), f32[16,16,1024]{2,0,1:T(8,128)S(1)}, u32[]{:S(2)}, u32[]{:S(2)}) async-start(f32[16,16,1024]{2,0,1:T(8,128)} %copy.29), calls=%async_computation | async-start | bytes 2097152 | tf_op jit(solution)/shard_map/all_to_all | solution.py:65
  17.0 0.0 copy-done.1
  17.0 0.1 subtract_subtract_fusion
  17.1 0.0 copy-done.3
  17.1 1.4 %select_reduce_fusion = f32[128,128]{1,0:T(8,128)S(1)} fusion(f32[64]{0:T(128)S(1)} %copy-done.3, s32[128,128]{1,0:T(8,128)S(1)} %subtract_subtract_fusion), kind=kLoop, calls=%fused_computation | loop fusion | flops 3129344 | bytes 131328 | tf_op jit(solution)/shard_map/reduce_sum | solution.py:49
  18.5 21.5 %all-to-all-done = f32[16,16,1024]{2,0,1:T(8,128)S(1)} async-done(((f32[16,16,1024]{2,0,1:T(8,128)}), f32[16,16,1024]{2,0,1:T(8,128)S(1)}, u32[]{:S(2)}, u32[]{:S(2)}) %all-to-all-start) | async-done | bytes 1048608 | tf_op jit(solution)/shard_map/all_to_all | solution.py:65
  39.9 1.4 %convolution_subtract_fusion = f32[128,1024]{1,0:T(8,128)} fusion(f32[16,2,8,1024]{3,2,1,0:T(8,128)S(1)} %bitcast.57, f32[128,128]{1,0:T(8,128)S(1)} %select_reduce_fusion, s32[128]{0:T(128)S(1)} %copy-done.1), kind=kOutput, calls=%fused_computation.7 | convolution fusion | flops 201555968 | bytes 1638912 | tf_op jit(solution)/shard_map/dot_general | solution.py:69
  41.4 1.7 %convolution_bitcast_fusion = f32[16,8,1024]{2,1,0:T(8,128)S(1)} fusion(f32[128,1024]{1,0:T(8,128)} %convolution_subtract_fusion, f32[128,128]{1,0:T(8,128)S(1)} %select_reduce_fusion, s32[128]{0:T(128)S(1)} %copy-done.1), kind=kOutput, calls=%fused_computation.3 | convolution fusion | flops 201424896 | bytes 1114624 | tf_op jit(solution)/shard_map/dot_general | solution.py:53
  43.1 21.1 %all_to_all.48 = f32[16,8,1024]{2,1,0:T(8,128)S(1)} all-to-all(f32[16,8,1024]{2,1,0:T(8,128)S(1)} %convolution_bitcast_fusion), channel_id=1, replica_groups=mesh['scan'=16,'row'=2] {'scan'}, dimensions={0} | all-to-all | bytes 1048576 | tf_op jit(solution)/shard_map/all_to_all | solution.py:72
  64.2 4.1 %all-to-all-start.2 = ((f32[16,8,1024]{2,1,0:T(8,128)}), f32[16,8,1024]{2,1,0:T(8,128)S(1)}, u32[]{:S(2)}, u32[]{:S(2)}) async-start(f32[16,8,1024]{2,1,0:T(8,128)} %bitcast.17), calls=%async_computation.2 | async-start | bytes 1048576 | tf_op jit(solution)/shard_map/all_to_all | solution.py:74
  69.6 0.3 copy.39
  70.0 1.6 %collective-permute-start.1 = (f32[8,8,512]{2,1,0:T(8,128)S(1)}, f32[8,8,512]{2,1,0:T(8,128)S(1)}, u32[]{:S(2)}, u32[]{:S(2)}) collective-permute-start(f32[8,8,512]{2,1,0:T(8,128)S(1)} %constant_dynamic-slice_fusion), channel_id=1, source_target_pairs={{0,1},{1,0},{2,3},{3,2},{4,5},{5,4},{6,7},{7,6},{8,9},{9,8},{10,11... | collective-permute-start | bytes 393224 | tf_op jit(solution)/shard_map/ppermute | solution.py:16
  71.5 0.9 %fusion.7 = f32[8,512,32]{1,2,0:T(8,128)S(1)} fusion(f32[32,48]{1,0:T(8,128)S(1)} %get-tuple-element.7, f32[1,8,32,512]{3,1,2,0:T(8,128)S(1)} %bitcast.56), kind=kOutput, calls=%fused_computation.25 | convolution fusion | flops 50331648 | bytes 1054720 | tf_op jit(solution)/shard_map/rk,pkc->prc/dot_general | solution.py:38
  72.5 3.4 %collective-permute-done.1 = f32[8,8,512]{2,1,0:T(8,128)S(1)} collective-permute-done((f32[8,8,512]{2,1,0:T(8,128)S(1)}, f32[8,8,512]{2,1,0:T(8,128)S(1)}, u32[]{:S(2)}, u32[]{:S(2)}) %collective-permute-start.1) | collective-permute-done | bytes 131104 | tf_op jit(solution)/shard_map/ppermute | solution.py:16
  75.9 1.6 %maximum_multiply_fusion = f32[8,32,512]{2,1,0:T(8,128)} fusion(f32[8,32,512]{2,1,0:T(8,128)S(1)} %copy-done, f32[8,512,32]{1,2,0:T(8,128)S(1)} %fusion.7, f32[8,8,512]{2,1,0:T(8,128)S(1)} %collective-permute-done.1, f32[]{:T(128)S(6)} %mul.18, f32[]{:T(128)} %bitcast.52, f32[32,48]{1,0:T(8,128)S(1)} %get-tuple-element.7, pred[]{:T(512)S(6)} %eq.49), kind=kOutput, calls=%fused_computation.15 | convolution fusion | flops 13631744 | bytes 1736713 | tf_op jit(solution)/shard_map/rk,pkc->prc/dot_general | solution.py:38
  77.5 5.3 %all-to-all-done.2 = f32[16,8,1024]{2,1,0:T(8,128)S(1)} async-done(((f32[16,8,1024]{2,1,0:T(8,128)}), f32[16,8,1024]{2,1,0:T(8,128)S(1)}, u32[]{:S(2)}, u32[]{:S(2)}) %all-to-all-start.2) | async-done | bytes 524320 | tf_op jit(solution)/shard_map/all_to_all | solution.py:74
  82.8 0.3 copy.31
  83.1 0.9 %reshape.71 = f32[8,32,512]{2,1,0:T(8,128)} reshape(f32[8,16,1024]{2,1,0:T(8,128)S(1)} %copy.31) | data formatting | bytes 1048576 | tf_op jit(solution)/shard_map/reshape | solution.py:80
  (2 shorter events, 0.0 us)
Async XLA Ops:
  0.6 6.1 %copy-start = (f32[8,32,512]{2,1,0:T(8,128)S(1)}, f32[8,32,512]{2,1,0:T(8,128)}, u32[]{:S(2)}) copy-start(f32[8,32,512]{2,1,0:T(8,128)} %param.7) | copy-start | bytes 1572868
  0.6 6.0 %copy-start.2 = (f32[17]{0:T(128)S(1)}, f32[17]{0:T(128)}, u32[]{:S(2)}) copy-start(f32[17]{0:T(128)} %param.11) | copy-start | bytes 208
  1.6 6.5 %collective-permute-start = (f32[8,8,512]{2,1,0:T(8,128)S(1)}, f32[8,8,512]{2,1,0:T(8,128)S(1)}, u32[]{:S(2)}, u32[]{:S(2)}) collective-permute-start(f32[8,8,512]{2,1,0:T(8,128)S(1)} %constant_dynamic-slice_fusion.1), channel_id=1, source_target_pairs={{0,1},{1,0},{2,3},{3,2},{4,5},{5,4},{6,7},{7,6},{8,9},{9,8},{10,11... | collective-permute-start | bytes 393224 | tf_op jit(solution)/shard_map/ppermute | solution.py:16
  10.7 6.3 %copy-start.1 = (s32[128]{0:T(128)S(1)}, s32[128]{0:T(128)}, u32[]{:S(2)}) copy-start(s32[128]{0:T(128)} %param.9) | copy-start | bytes 1540
  10.7 6.4 %copy-start.3 = (f32[64]{0:T(128)S(1)}, f32[64]{0:T(128)}, u32[]{:S(2)}) copy-start(f32[64]{0:T(128)} %param.10) | copy-start | bytes 772
  10.7 29.3 %all-to-all-start = ((f32[16,16,1024]{2,0,1:T(8,128)}), f32[16,16,1024]{2,0,1:T(8,128)S(1)}, u32[]{:S(2)}, u32[]{:S(2)}) async-start(f32[16,16,1024]{2,0,1:T(8,128)} %copy.29), calls=%async_computation | async-start | bytes 2097152 | tf_op jit(solution)/shard_map/all_to_all | solution.py:65
  64.2 18.6 %all-to-all-start.2 = ((f32[16,8,1024]{2,1,0:T(8,128)}), f32[16,8,1024]{2,1,0:T(8,128)S(1)}, u32[]{:S(2)}, u32[]{:S(2)}) async-start(f32[16,8,1024]{2,1,0:T(8,128)} %bitcast.17), calls=%async_computation.2 | async-start | bytes 1048576 | tf_op jit(solution)/shard_map/all_to_all | solution.py:74
  70.0 5.9 %collective-permute-start.1 = (f32[8,8,512]{2,1,0:T(8,128)S(1)}, f32[8,8,512]{2,1,0:T(8,128)S(1)}, u32[]{:S(2)}, u32[]{:S(2)}) collective-permute-start(f32[8,8,512]{2,1,0:T(8,128)S(1)} %constant_dynamic-slice_fusion), channel_id=1, source_target_pairs={{0,1},{1,0},{2,3},{3,2},{4,5},{5,4},{6,7},{7,6},{8,9},{9,8},{10,11... | collective-permute-start | bytes 393224 | tf_op jit(solution)/shard_map/ppermute | solution.py:16

commit v12 on v9

--- a/solution.py
+++ b/solution.py
@@ -25,11 +25,13 @@
     return summed + lateral_apply(band[:, width + rows :], below)
 
 
-def band_matrix(kernel_taps, row_count, shift):
+def band_matrix(kernel_taps, row_count, flip):
     tap_count = kernel_taps.shape[0]
     out_rows = jnp.arange(row_count, dtype=jnp.int32)[:, None]
     in_rows = jnp.arange(row_count + tap_count - 1, dtype=jnp.int32)[None, :]
-    lag = shift + in_rows - out_rows
+    lag = in_rows - out_rows
+    if flip:
+        lag = (tap_count - 1) - lag
     taps = jnp.arange(tap_count, dtype=jnp.int32)
     return jnp.sum(jnp.where(lag[:, :, None] == taps, kernel_taps, 0.0), axis=-1)
 
@@ -58,8 +60,8 @@
     flat_count = row_count * width_count
     halo_rows = lateral_psf.shape[0] // 2
     sheet_psf = sheet_matrix(offsets, depth_psf, offsets.shape[0])
-    blur_band = band_matrix(lateral_psf, row_count, 0)
-    back_band = band_matrix(lateral_psf[::-1], row_count, 0)
+    blur_band = band_matrix(lateral_psf, row_count, False)
+    back_band = band_matrix(lateral_psf, row_count, True)
     blurred = blur_rows(blur_band, estimate, "row", halo_rows).reshape(plane_count, flat_count)
     both_flat = jnp.concatenate([blurred, raw.reshape(plane_count, flat_count)], axis=0)
     both_in = lax.all_to_all(both_flat, "scan", split_axis=1, concat_axis=0, tiled=True)
@@ -69,9 +71,9 @@
     predicted_pencil = jnp.dot(sheet_psf, pencil, precision=highest_mode)
     misfit_pencil = predicted_pencil - raw_pencil
     back_pencil = transpose_apply(sheet_psf, misfit_pencil)
-    both_out = lax.all_to_all(jnp.stack([misfit_pencil, back_pencil]), "scan", split_axis=1, concat_axis=2, tiled=True)
-    misfit = both_out[0]
-    back_volume = both_out[1].reshape(plane_count, row_count, width_count)
+    both_out = lax.all_to_all(jnp.stack([misfit_pencil, back_pencil], axis=1), "scan", split_axis=0, concat_axis=2, tiled=True)
+    misfit = both_out[:, 0]
+    back_volume = both_out[:, 1].reshape(plane_count, row_count, width_count)
     gradient = blur_rows(back_band, back_volume, "row", halo_rows)
     stepped = estimate - step_size[0] * gradient
     shrink_level = step_size[0] * threshold[0]

time: 82.3 us -> 82.2 us (level)
    unnamed x8 -> x10, local copies, waits for them, and re-layouts: 0.02 us -> 1.42 us
    another operation x3 -> x1, local copies, waits for them, and re-layouts: 2.73 us -> 1.78 us  [body(): jnp.stack([misfit_pencil, back_pencil], axis=1)]
where the time goes in v12:
time: 82.2 us; the launch traced here: 81.4 us
  waiting for transfers between devices  47.1 us (57%)
  starting transfers between devices  17.8 us (22%)
  local copies, waits for them, and re-layouts  7.56 us (9%)
  matrix products  5.14 us (6%)
  between operations  2.12 us (3%)
  other arithmetic  1.76 us (2%)
    all_to_all x1, waiting for transfers between devices, body(): lax.all_to_all(jnp.stack([misfit_pencil, back_pencil], axis=1), 'scan', s...  21.6 us
    all_to_all x1, waiting for transfers between devices, body(): lax.all_to_all(both_flat, 'scan', split_axis=1, concat_axis=0, tiled=True)  21.5 us
    all_to_all x1, starting transfers between devices, body(): lax.all_to_all(jnp.stack([misfit_pencil, back_pencil], axis=1), 'scan', s...  6.86 us
    all_to_all x1, starting transfers between devices, body(): lax.all_to_all(both_flat, 'scan', split_axis=1, concat_axis=0, tiled=True)  6.33 us
    ppermute x2, starting transfers between devices, blur_rows(): arrived = lax.ppermute(sent, axis, [(0, 1), (1, 0)])  4.56 us
    ppermute x2, waiting for transfers between devices, blur_rows(): arrived = lax.ppermute(sent, axis, [(0, 1), (1, 0)])  3.97 us
    dot_general x4, matrix products, lateral_apply(): return jnp.einsum('rk,pkc->prc', band, padded, precision=highest_mode)  3.81 us
    concatenate x3, local copies, waits for them, and re-layouts, body(): jnp.concatenate([blurred, raw.reshape(plane_count, flat_count)], axis=0)  2.96 us
  transfers between devices with their start and end apart: 4, of which 4 were waited for; matrix products, arithmetic and copies ran while one was open for 7% of the time, Pallas kernels for 0%

profile of v12, /device:TPU:0, one launch (start us, length us, event | category | flops | bytes accessed | tf_op | source)
XLA Modules:
  0.0 81.4 jit_solution(3228266658101645648)
XLA Ops:
  0.6 0.0 copy-start
  0.6 0.0 copy-start.2
  0.7 1.0 %constant_dynamic-slice_fusion.1 = f32[8,8,512]{2,1,0:T(8,128)S(1)} fusion(f32[8,32,512]{2,1,0:T(8,128)} %param.7, s32[]{:T(128)S(6)} %select_n.37), kind=kLoop, calls=%fused_computation.39 | loop fusion | bytes 262148 | tf_op jit(solution)/shard_map/dynamic_slice | solution.py:15
  1.6 3.0 %collective-permute-start = (f32[8,8,512]{2,1,0:T(8,128)S(1)}, f32[8,8,512]{2,1,0:T(8,128)S(1)}, u32[]{:S(2)}, u32[]{:S(2)}) collective-permute-start(f32[8,8,512]{2,1,0:T(8,128)S(1)} %constant_dynamic-slice_fusion.1), channel_id=1, source_target_pairs={{0,1},{1,0},{2,3},{3,2},{4,5},{5,4},{6,7},{7,6},{8,9},{9,8},{10,11... | collective-permute-start | bytes 393224 | tf_op jit(solution)/shard_map/ppermute | solution.py:16
  4.6 1.2 %concatenate.9 = f32[8,16,1024]{2,1,0:T(8,128)S(1)} reshape(f32[8,32,512]{2,1,0:T(8,128)} %param.8) | data formatting | bytes 1048576 | tf_op jit(solution)/shard_map/concatenate | solution.py:66
  5.9 0.0 copy-done.2
  5.9 0.1 select_reduce_fusion.2
  6.0 0.0 copy-done
  6.0 0.6 convolution_bitcast_fusion.2
  6.7 1.5 %collective-permute-done = f32[8,8,512]{2,1,0:T(8,128)S(1)} collective-permute-done((f32[8,8,512]{2,1,0:T(8,128)S(1)}, f32[8,8,512]{2,1,0:T(8,128)S(1)}, u32[]{:S(2)}, u32[]{:S(2)}) %collective-permute-start) | collective-permute-done | bytes 131104 | tf_op jit(solution)/shard_map/ppermute | solution.py:16
  8.1 0.6 fusion
  8.8 0.2 concatenate.8
  9.0 0.1 pad_maximum_fusion
  9.1 1.6 %copy.26 = f32[16,16,1024]{2,0,1:T(8,128)} copy(f32[16,16,1024]{2,1,0:T(8,128)S(1)} %pad_maximum_fusion) | data formatting | bytes 2097152 | tf_op jit(solution)/shard_map/concatenate | solution.py:66
  10.6 0.0 copy-start.1
  10.6 0.0 copy-start.3
  10.6 6.3 %all-to-all-start = ((f32[16,16,1024]{2,0,1:T(8,128)}), f32[16,16,1024]{2,0,1:T(8,128)S(1)}, u32[]{:S(2)}, u32[]{:S(2)}) async-start(f32[16,16,1024]{2,0,1:T(8,128)} %copy.26), calls=%async_computation | async-start | bytes 2097152 | tf_op jit(solution)/shard_map/all_to_all | solution.py:67
  17.0 0.0 copy-done.1
  17.0 0.1 subtract_subtract_fusion
  17.1 0.0 copy-done.3
  17.1 1.4 %select_reduce_fusion = f32[128,128]{1,0:T(8,128)S(1)} fusion(f32[64]{0:T(128)S(1)} %copy-done.3, s32[128,128]{1,0:T(8,128)S(1)} %subtract_subtract_fusion), kind=kLoop, calls=%fused_computation | loop fusion | flops 3129344 | bytes 131328 | tf_op jit(solution)/shard_map/reduce_sum | solution.py:51
  18.5 21.5 %all-to-all-done = f32[16,16,1024]{2,0,1:T(8,128)S(1)} async-done(((f32[16,16,1024]{2,0,1:T(8,128)}), f32[16,16,1024]{2,0,1:T(8,128)S(1)}, u32[]{:S(2)}, u32[]{:S(2)}) %all-to-all-start) | async-done | bytes 1048608 | tf_op jit(solution)/shard_map/all_to_all | solution.py:67
  39.9 0.6 convolution_subtract_fusion
  40.6 0.7 convolution_bitcast_fusion
  41.3 0.1 pad_maximum_fusion.1
  41.4 1.8 %copy.27 = f32[128,2,1024]{2,1,0:T(2,128)} copy(f32[128,2,1024]{2,0,1:T(8,128)S(1)} %pad_maximum_fusion.1) | data formatting | bytes 2097152 | tf_op jit(solution)/shard_map/stack | solution.py:74
  43.1 6.9 %all-to-all-start.1 = ((f32[128,2,1024]{2,1,0:T(2,128)}), f32[128,2,1024]{2,1,0:T(2,128)S(1)}, u32[]{:S(2)}, u32[]{:S(2)}) async-start(f32[128,2,1024]{2,1,0:T(2,128)} %copy.27), calls=%async_computation.1 | async-start | bytes 2097152 | tf_op jit(solution)/shard_map/all_to_all | solution.py:74
  51.3 21.6 %all-to-all-done.1 = f32[128,2,1024]{2,1,0:T(2,128)S(1)} async-done(((f32[128,2,1024]{2,1,0:T(2,128)}), f32[128,2,1024]{2,1,0:T(2,128)S(1)}, u32[]{:S(2)}, u32[]{:S(2)}) %all-to-all-start.1) | async-done | bytes 1048608 | tf_op jit(solution)/shard_map/all_to_all | solution.py:74
  72.9 0.3 copy.28
  73.3 0.1 fusion.19
  73.4 0.3 copy.40
  73.7 1.6 %collective-permute-start.1 = (f32[8,8,512]{2,1,0:T(8,128)S(1)}, f32[8,8,512]{2,1,0:T(8,128)S(1)}, u32[]{:S(2)}, u32[]{:S(2)}) collective-permute-start(f32[8,8,512]{2,1,0:T(8,128)S(1)} %constant_dynamic-slice_fusion), channel_id=1, source_target_pairs={{0,1},{1,0},{2,3},{3,2},{4,5},{5,4},{6,7},{7,6},{8,9},{9,8},{10,11... | collective-permute-start | bytes 393224 | tf_op jit(solution)/shard_map/ppermute | solution.py:16
  75.3 1.1 %copy.39 = f32[1,8,32,512]{3,2,1,0:T(8,128)} copy(f32[1,8,32,512]{3,1,2,0:T(8,128)S(1)} %bitcast.69) | data formatting | bytes 1048576
  76.4 0.9 %fusion.7 = f32[8,512,32]{1,2,0:T(8,128)S(1)} fusion(f32[32,48]{1,0:T(8,128)S(1)} %get-tuple-element.3, f32[1,8,32,512]{3,1,2,0:T(8,128)S(1)} %bitcast.64), kind=kOutput, calls=%fused_computation.28 | convolution fusion | flops 50331648 | bytes 1054720 | tf_op jit(solution)/shard_map/rk,pkc->prc/dot_general | solution.py:40
  77.3 2.5 %collective-permute-done.1 = f32[8,8,512]{2,1,0:T(8,128)S(1)} collective-permute-done((f32[8,8,512]{2,1,0:T(8,128)S(1)}, f32[8,8,512]{2,1,0:T(8,128)S(1)}, u32[]{:S(2)}, u32[]{:S(2)}) %collective-permute-start.1) | collective-permute-done | bytes 131104 | tf_op jit(solution)/shard_map/ppermute | solution.py:16
  79.8 1.6 %maximum_multiply_fusion = f32[8,32,512]{2,1,0:T(8,128)} fusion(f32[8,32,512]{2,1,0:T(8,128)S(1)} %copy-done, f32[8,512,32]{1,2,0:T(8,128)S(1)} %fusion.7, f32[8,8,512]{2,1,0:T(8,128)S(1)} %collective-permute-done.1, f32[]{:T(128)S(6)} %mul.18, f32[]{:T(128)} %bitcast.60, f32[32,48]{1,0:T(8,128)S(1)} %get-tuple-element.3, pred[]{:T(512)S(6)} %eq.49), kind=kOutput, calls=%fused_computation.17 | convolution fusion | flops 13631744 | bytes 1736713 | tf_op jit(solution)/shard_map/rk,pkc->prc/dot_general | solution.py:40
  (2 shorter events, 0.0 us)
Async XLA Ops:
  0.6 5.4 %copy-start = (f32[8,32,512]{2,1,0:T(8,128)S(1)}, f32[8,32,512]{2,1,0:T(8,128)}, u32[]{:S(2)}) copy-start(f32[8,32,512]{2,1,0:T(8,128)} %param.7) | copy-start | bytes 1572868
  0.6 5.2 %copy-start.2 = (f32[17]{0:T(128)S(1)}, f32[17]{0:T(128)}, u32[]{:S(2)}) copy-start(f32[17]{0:T(128)} %param.11) | copy-start | bytes 208
  1.6 6.5 %collective-permute-start = (f32[8,8,512]{2,1,0:T(8,128)S(1)}, f32[8,8,512]{2,1,0:T(8,128)S(1)}, u32[]{:S(2)}, u32[]{:S(2)}) collective-permute-start(f32[8,8,512]{2,1,0:T(8,128)S(1)} %constant_dynamic-slice_fusion.1), channel_id=1, source_target_pairs={{0,1},{1,0},{2,3},{3,2},{4,5},{5,4},{6,7},{7,6},{8,9},{9,8},{10,11... | collective-permute-start | bytes 393224 | tf_op jit(solution)/shard_map/ppermute | solution.py:16
  10.6 6.3 %copy-start.1 = (s32[128]{0:T(128)S(1)}, s32[128]{0:T(128)}, u32[]{:S(2)}) copy-start(s32[128]{0:T(128)} %param.9) | copy-start | bytes 1540
  10.6 6.4 %copy-start.3 = (f32[64]{0:T(128)S(1)}, f32[64]{0:T(128)}, u32[]{:S(2)}) copy-start(f32[64]{0:T(128)} %param.10) | copy-start | bytes 772
  10.6 29.3 %all-to-all-start = ((f32[16,16,1024]{2,0,1:T(8,128)}), f32[16,16,1024]{2,0,1:T(8,128)S(1)}, u32[]{:S(2)}, u32[]{:S(2)}) async-start(f32[16,16,1024]{2,0,1:T(8,128)} %copy.26), calls=%async_computation | async-start | bytes 2097152 | tf_op jit(solution)/shard_map/all_to_all | solution.py:67
  43.1 29.8 %all-to-all-start.1 = ((f32[128,2,1024]{2,1,0:T(2,128)}), f32[128,2,1024]{2,1,0:T(2,128)S(1)}, u32[]{:S(2)}, u32[]{:S(2)}) async-start(f32[128,2,1024]{2,1,0:T(2,128)} %copy.27), calls=%async_computation.1 | async-start | bytes 2097152 | tf_op jit(solution)/shard_map/all_to_all | solution.py:74
  73.7 6.1 %collective-permute-start.1 = (f32[8,8,512]{2,1,0:T(8,128)S(1)}, f32[8,8,512]{2,1,0:T(8,128)S(1)}, u32[]{:S(2)}, u32[]{:S(2)}) collective-permute-start(f32[8,8,512]{2,1,0:T(8,128)S(1)} %constant_dynamic-slice_fusion), channel_id=1, source_target_pairs={{0,1},{1,0},{2,3},{3,2},{4,5},{5,4},{6,7},{7,6},{8,9},{9,8},{10,11... | collective-permute-start | bytes 393224 | tf_op jit(solution)/shard_map/ppermute | solution.py:16

commit v13 on v12

--- a/solution.py
+++ b/solution.py
@@ -70,10 +70,15 @@
     raw_pencil = both_in[:, 1].reshape(offsets.shape[0], -1)
     predicted_pencil = jnp.dot(sheet_psf, pencil, precision=highest_mode)
     misfit_pencil = predicted_pencil - raw_pencil
-    back_pencil = transpose_apply(sheet_psf, misfit_pencil)
-    both_out = lax.all_to_all(jnp.stack([misfit_pencil, back_pencil], axis=1), "scan", split_axis=0, concat_axis=2, tiled=True)
-    misfit = both_out[:, 0]
-    back_volume = both_out[:, 1].reshape(plane_count, row_count, width_count)
+    scan_count = lax.axis_size("scan")
+    all_planes = offsets.shape[0]
+    keep = jnp.eye(all_planes, dtype=jnp.float32).reshape(scan_count, 1, plane_count, all_planes)
+    spread = sheet_psf.T.reshape(scan_count, 1, plane_count, all_planes)
+    joint = jnp.concatenate([keep, spread], axis=1).reshape(2 * all_planes, all_planes)
+    both_pencil = jnp.dot(joint, misfit_pencil, precision=highest_mode)
+    both_out = lax.all_to_all(both_pencil, "scan", split_axis=0, concat_axis=1, tiled=True)
+    misfit = both_out[:plane_count]
+    back_volume = both_out[plane_count:].reshape(plane_count, row_count, width_count)
     gradient = blur_rows(back_band, back_volume, "row", halo_rows)
     stepped = estimate - step_size[0] * gradient
     shrink_level = step_size[0] * threshold[0]

time: 82.2 us -> 81.4 us (level)
  local copies, waits for them, and re-layouts: 7.56 us -> 5.71 us
  matrix products: 5.14 us -> 6.11 us
    another operation x1 -> x0, local copies, waits for them, and re-layouts: 1.78 us -> none  [body(): jnp.stack([misfit_pencil, back_pencil], axis=1)]
    unnamed x10 -> x8, local copies, waits for them, and re-layouts: 1.42 us -> 0.02 us
    dot_general x1, matrix products: 0.7 us -> 1.95 us  [body(): both_pencil = jnp.dot(joint, misfit_pencil, precision=highest_mode)]
    reshape x0 -> x2, local copies, waits for them, and re-layouts: none -> 0.95 us  [the longest x1 0.87 us: body(): return (new_estimate, misfit.reshape(plane_count, row_count, width_count))]
where the time goes in v13:
time: 81.4 us; the launch traced here: 80.6 us
  waiting for transfers between devices  47.1 us (58%)
  starting transfers between devices  17.8 us (22%)
  matrix products  6.11 us (8%)
  local copies, waits for them, and re-layouts  5.71 us (7%)
  between operations  2.13 us (3%)
  other arithmetic  1.8 us (2%)
    all_to_all x1, waiting for transfers between devices, body(): lax.all_to_all(both_pencil, 'scan', split_axis=0, concat_axis=1, tiled=True)  21.6 us
    all_to_all x1, waiting for transfers between devices, body(): lax.all_to_all(both_flat, 'scan', split_axis=1, concat_axis=0, tiled=True)  21.2 us
    all_to_all x1, starting transfers between devices, body(): lax.all_to_all(both_pencil, 'scan', split_axis=0, concat_axis=1, tiled=True)  6.86 us
    all_to_all x1, starting transfers between devices, body(): lax.all_to_all(both_flat, 'scan', split_axis=1, concat_axis=0, tiled=True)  6.33 us
    ppermute x2, starting transfers between devices, blur_rows(): arrived = lax.ppermute(sent, axis, [(0, 1), (1, 0)])  4.56 us
    ppermute x2, waiting for transfers between devices, blur_rows(): arrived = lax.ppermute(sent, axis, [(0, 1), (1, 0)])  4.17 us
    dot_general x4, matrix products, lateral_apply(): return jnp.einsum('rk,pkc->prc', band, padded, precision=highest_mode)  3.53 us
    concatenate x3, local copies, waits for them, and re-layouts, body(): jnp.concatenate([blurred, raw.reshape(plane_count, flat_count)], axis=0)  2.96 us
  transfers between devices with their start and end apart: 4, of which 4 were waited for; matrix products, arithmetic and copies ran while one was open for 7% of the time, Pallas kernels for 0%

profile of v13, /device:TPU:0, one launch (start us, length us, event | category | flops | bytes accessed | tf_op | source)
XLA Modules:
  0.0 80.6 jit_solution(12860772970138471814)
XLA Ops:
  0.6 0.0 copy-start
  0.6 0.0 copy-start.2
  0.7 1.0 %constant_dynamic-slice_fusion.1 = f32[8,8,512]{2,1,0:T(8,128)S(1)} fusion(f32[8,32,512]{2,1,0:T(8,128)} %param.7, s32[]{:T(128)S(6)} %select_n.41), kind=kLoop, calls=%fused_computation.55 | loop fusion | bytes 262148 | tf_op jit(solution)/shard_map/dynamic_slice | solution.py:15
  1.6 3.0 %collective-permute-start = (f32[8,8,512]{2,1,0:T(8,128)S(1)}, f32[8,8,512]{2,1,0:T(8,128)S(1)}, u32[]{:S(2)}, u32[]{:S(2)}) collective-permute-start(f32[8,8,512]{2,1,0:T(8,128)S(1)} %constant_dynamic-slice_fusion.1), channel_id=1, source_target_pairs={{0,1},{1,0},{2,3},{3,2},{4,5},{5,4},{6,7},{7,6},{8,9},{9,8},{10,11... | collective-permute-start | bytes 393224 | tf_op jit(solution)/shard_map/ppermute | solution.py:16
  4.6 1.2 %concatenate.13 = f32[8,16,1024]{2,1,0:T(8,128)S(1)} reshape(f32[8,32,512]{2,1,0:T(8,128)} %param.8) | data formatting | bytes 1048576 | tf_op jit(solution)/shard_map/concatenate | solution.py:66
  5.9 0.0 copy-done.2
  5.9 0.1 select_reduce_fusion.1
  6.0 0.0 copy-done
  6.0 0.6 convolution_bitcast_fusion.1
  6.7 1.5 %collective-permute-done = f32[8,8,512]{2,1,0:T(8,128)S(1)} collective-permute-done((f32[8,8,512]{2,1,0:T(8,128)S(1)}, f32[8,8,512]{2,1,0:T(8,128)S(1)}, u32[]{:S(2)}, u32[]{:S(2)}) %collective-permute-start) | collective-permute-done | bytes 131104 | tf_op jit(solution)/shard_map/ppermute | solution.py:16
  8.1 0.6 fusion
  8.8 0.2 concatenate.12
  9.0 0.1 pad_maximum_fusion
  9.1 1.6 %copy.39 = f32[16,16,1024]{2,0,1:T(8,128)} copy(f32[16,16,1024]{2,1,0:T(8,128)S(1)} %pad_maximum_fusion) | data formatting | bytes 2097152 | tf_op jit(solution)/shard_map/concatenate | solution.py:66
  10.6 0.0 copy-start.1
  10.6 0.0 copy-start.3
  10.6 6.3 %all-to-all-start = ((f32[16,16,1024]{2,0,1:T(8,128)}), f32[16,16,1024]{2,0,1:T(8,128)S(1)}, u32[]{:S(2)}, u32[]{:S(2)}) async-start(f32[16,16,1024]{2,0,1:T(8,128)} %copy.39), calls=%async_computation | async-start | bytes 2097152 | tf_op jit(solution)/shard_map/all_to_all | solution.py:67
  17.0 0.0 copy-done.1
  17.0 0.1 subtract_subtract_fusion
  17.1 0.0 copy-done.3
  17.1 1.4 %select_reduce_fusion = f32[128,128]{1,0:T(8,128)S(1)} fusion(f32[64]{0:T(128)S(1)} %copy-done.3, s32[128,128]{1,0:T(8,128)S(1)} %subtract_subtract_fusion), kind=kLoop, calls=%fused_computation | loop fusion | flops 3129344 | bytes 131328 | tf_op jit(solution)/shard_map/reduce_sum | solution.py:51
  18.5 0.1 copy.36
  18.6 0.1 fusion.13
  18.7 21.2 %all-to-all-done = f32[16,16,1024]{2,0,1:T(8,128)S(1)} async-done(((f32[16,16,1024]{2,0,1:T(8,128)}), f32[16,16,1024]{2,0,1:T(8,128)S(1)}, u32[]{:S(2)}, u32[]{:S(2)}) %all-to-all-start) | async-done | bytes 1048608 | tf_op jit(solution)/shard_map/all_to_all | solution.py:67
  39.9 0.6 fusion.1
  40.6 1.9 %fusion.5 = f32[16,16,1024]{2,1,0:T(8,128)} fusion(f32[128,1024,1]{1,0,2:T(8,128)S(1)} %fusion.1, f32[16,1,8,128]{3,2,1,0:T(8,128)S(1)} %fusion.8, f32[16,1,8,128]{3,2,1,0:T(8,128)S(1)} %fusion.13), kind=kOutput, calls=%fused_computation.20 | convolution fusion | flops 402685952 | bytes 1703936 | tf_op jit(solution)/shard_map/dot_general | solution.py:78
  42.5 6.9 %all-to-all-start.1 = ((f32[16,16,1024]{2,1,0:T(8,128)}), f32[16,16,1024]{2,1,0:T(8,128)S(1)}, u32[]{:S(2)}, u32[]{:S(2)}) async-start(f32[16,16,1024]{2,1,0:T(8,128)} %fusion.5), calls=%async_computation.1 | async-start | bytes 2097152 | tf_op jit(solution)/shard_map/all_to_all | solution.py:79
  50.7 21.6 %all-to-all-done.1 = f32[16,16,1024]{2,1,0:T(8,128)S(1)} async-done(((f32[16,16,1024]{2,1,0:T(8,128)}), f32[16,16,1024]{2,1,0:T(8,128)S(1)}, u32[]{:S(2)}, u32[]{:S(2)}) %all-to-all-start.1) | async-done | bytes 1048608 | tf_op jit(solution)/shard_map/all_to_all | solution.py:79
  72.3 0.1 fusion.33
  72.4 0.3 copy.40
  72.7 0.1 reshape.109
  72.9 1.6 %collective-permute-start.1 = (f32[8,8,512]{2,1,0:T(8,128)S(1)}, f32[8,8,512]{2,1,0:T(8,128)S(1)}, u32[]{:S(2)}, u32[]{:S(2)}) collective-permute-start(f32[8,8,512]{2,1,0:T(8,128)S(1)} %constant_dynamic-slice_fusion), channel_id=1, source_target_pairs={{0,1},{1,0},{2,3},{3,2},{4,5},{5,4},{6,7},{7,6},{8,9},{9,8},{10,11... | collective-permute-start | bytes 393224 | tf_op jit(solution)/shard_map/ppermute | solution.py:16
  74.4 0.3 copy.42
  74.7 0.9 %reshape.110 = f32[8,32,512]{2,1,0:T(8,128)} reshape(f32[8,16,1024]{2,1,0:T(8,128)S(1)} %copy.42) | data formatting | bytes 1048576 | tf_op jit(solution)/shard_map/reshape | solution.py:86
  75.6 0.6 fusion.23
  76.2 2.7 %collective-permute-done.1 = f32[8,8,512]{2,1,0:T(8,128)S(1)} collective-permute-done((f32[8,8,512]{2,1,0:T(8,128)S(1)}, f32[8,8,512]{2,1,0:T(8,128)S(1)}, u32[]{:S(2)}, u32[]{:S(2)}) %collective-permute-start.1) | collective-permute-done | bytes 131104 | tf_op jit(solution)/shard_map/ppermute | solution.py:16
  78.9 1.6 %maximum_multiply_fusion = f32[8,32,512]{2,1,0:T(8,128)} fusion(f32[8,32,512]{2,1,0:T(8,128)S(1)} %copy-done, f32[8,512,32]{1,2,0:T(8,128)S(1)} %fusion.23, f32[8,8,512]{2,1,0:T(8,128)S(1)} %collective-permute-done.1, f32[]{:T(128)S(6)} %mul.18, f32[]{:T(128)} %bitcast.55, f32[32,48]{1,0:T(8,128)S(1)} %get-tuple-element.2, pred[]{:T(512)S(6)} %eq.60), kind=kOutput, calls=%fused_computation.14 | convolution fusion | flops 13631744 | bytes 1736713 | tf_op jit(solution)/shard_map/rk,pkc->prc/dot_general | solution.py:40
  (4 shorter events, 0.1 us)
Async XLA Ops:
  0.6 5.4 %copy-start = (f32[8,32,512]{2,1,0:T(8,128)S(1)}, f32[8,32,512]{2,1,0:T(8,128)}, u32[]{:S(2)}) copy-start(f32[8,32,512]{2,1,0:T(8,128)} %param.7) | copy-start | bytes 1572868
  0.6 5.2 %copy-start.2 = (f32[17]{0:T(128)S(1)}, f32[17]{0:T(128)}, u32[]{:S(2)}) copy-start(f32[17]{0:T(128)} %param.11) | copy-start | bytes 208
  1.6 6.5 %collective-permute-start = (f32[8,8,512]{2,1,0:T(8,128)S(1)}, f32[8,8,512]{2,1,0:T(8,128)S(1)}, u32[]{:S(2)}, u32[]{:S(2)}) collective-permute-start(f32[8,8,512]{2,1,0:T(8,128)S(1)} %constant_dynamic-slice_fusion.1), channel_id=1, source_target_pairs={{0,1},{1,0},{2,3},{3,2},{4,5},{5,4},{6,7},{7,6},{8,9},{9,8},{10,11... | collective-permute-start | bytes 393224 | tf_op jit(solution)/shard_map/ppermute | solution.py:16
  10.6 6.3 %copy-start.1 = (s32[128]{0:T(128)S(1)}, s32[128]{0:T(128)}, u32[]{:S(2)}) copy-start(s32[128]{0:T(128)} %param.9) | copy-start | bytes 1540
  10.6 6.4 %copy-start.3 = (f32[64]{0:T(128)S(1)}, f32[64]{0:T(128)}, u32[]{:S(2)}) copy-start(f32[64]{0:T(128)} %param.10) | copy-start | bytes 772
  10.6 29.3 %all-to-all-start = ((f32[16,16,1024]{2,0,1:T(8,128)}), f32[16,16,1024]{2,0,1:T(8,128)S(1)}, u32[]{:S(2)}, u32[]{:S(2)}) async-start(f32[16,16,1024]{2,0,1:T(8,128)} %copy.39), calls=%async_computation | async-start | bytes 2097152 | tf_op jit(solution)/shard_map/all_to_all | solution.py:67
  42.5 29.8 %all-to-all-start.1 = ((f32[16,16,1024]{2,1,0:T(8,128)}), f32[16,16,1024]{2,1,0:T(8,128)S(1)}, u32[]{:S(2)}, u32[]{:S(2)}) async-start(f32[16,16,1024]{2,1,0:T(8,128)} %fusion.5), calls=%async_computation.1 | async-start | bytes 2097152 | tf_op jit(solution)/shard_map/all_to_all | solution.py:79
  72.9 6.1 %collective-permute-start.1 = (f32[8,8,512]{2,1,0:T(8,128)S(1)}, f32[8,8,512]{2,1,0:T(8,128)S(1)}, u32[]{:S(2)}, u32[]{:S(2)}) collective-permute-start(f32[8,8,512]{2,1,0:T(8,128)S(1)} %constant_dynamic-slice_fusion), channel_id=1, source_target_pairs={{0,1},{1,0},{2,3},{3,2},{4,5},{5,4},{6,7},{7,6},{8,9},{9,8},{10,11... | collective-permute-start | bytes 393224 | tf_op jit(solution)/shard_map/ppermute | solution.py:16

commit v14 on v13

--- a/solution.py
+++ b/solution.py
@@ -62,12 +62,14 @@
     sheet_psf = sheet_matrix(offsets, depth_psf, offsets.shape[0])
     blur_band = band_matrix(lateral_psf, row_count, False)
     back_band = band_matrix(lateral_psf, row_count, True)
-    blurred = blur_rows(blur_band, estimate, "row", halo_rows).reshape(plane_count, flat_count)
-    both_flat = jnp.concatenate([blurred, raw.reshape(plane_count, flat_count)], axis=0)
-    both_in = lax.all_to_all(both_flat, "scan", split_axis=1, concat_axis=0, tiled=True)
-    both_in = both_in.reshape(lax.axis_size("scan"), 2, plane_count, -1)
-    pencil = both_in[:, 0].reshape(offsets.shape[0], -1)
-    raw_pencil = both_in[:, 1].reshape(offsets.shape[0], -1)
+    chunk_count = lax.axis_size("scan")
+    raw_chunks = raw.reshape(plane_count, chunk_count, flat_count // chunk_count).transpose(1, 0, 2)
+    blurred = blur_rows(blur_band, estimate, "row", halo_rows)
+    blurred_chunks = blurred.reshape(plane_count, chunk_count, flat_count // chunk_count).transpose(1, 0, 2)
+    both_chunks = jnp.concatenate([blurred_chunks, raw_chunks], axis=1)
+    both_in = lax.all_to_all(both_chunks, "scan", split_axis=0, concat_axis=0, tiled=True)
+    pencil = both_in[:, :plane_count].reshape(offsets.shape[0], -1)
+    raw_pencil = both_in[:, plane_count:].reshape(offsets.shape[0], -1)
     predicted_pencil = jnp.dot(sheet_psf, pencil, precision=highest_mode)
     misfit_pencil = predicted_pencil - raw_pencil
     scan_count = lax.axis_size("scan")

time: 81.4 us -> 81.4 us (level)
    concatenate x3 -> x1, local copies, waits for them, and re-layouts: 2.96 us -> 1.58 us  [body(): both_chunks = jnp.concatenate([blurred_chunks, raw_chunks], axis=1)]
    reshape x0 -> x2, local copies, waits for them, and re-layouts: none -> 1.38 us  [the longest x1 1.21 us: body(): raw.reshape(plane_count, chunk_count, flat_count // chunk_count)]
where the time goes in v14:
time: 81.4 us; the launch traced here: 80.6 us
  waiting for transfers between devices  47.1 us (58%)
  starting transfers between devices  17.8 us (22%)
  matrix products  6.11 us (8%)
  local copies, waits for them, and re-layouts  5.71 us (7%)
  between operations  2.13 us (3%)
  other arithmetic  1.8 us (2%)
    all_to_all x1, waiting for transfers between devices, body(): lax.all_to_all(both_pencil, 'scan', split_axis=0, concat_axis=1, tiled=True)  21.6 us
    all_to_all x1, waiting for transfers between devices, body(): lax.all_to_all(both_chunks, 'scan', split_axis=0, concat_axis=0, tiled=True)  21.2 us
    all_to_all x1, starting transfers between devices, body(): lax.all_to_all(both_pencil, 'scan', split_axis=0, concat_axis=1, tiled=True)  6.86 us
    all_to_all x1, starting transfers between devices, body(): lax.all_to_all(both_chunks, 'scan', split_axis=0, concat_axis=0, tiled=True)  6.33 us
    ppermute x2, starting transfers between devices, blur_rows(): arrived = lax.ppermute(sent, axis, [(0, 1), (1, 0)])  4.56 us
    ppermute x2, waiting for transfers between devices, blur_rows(): arrived = lax.ppermute(sent, axis, [(0, 1), (1, 0)])  4.17 us
    dot_general x4, matrix products, lateral_apply(): return jnp.einsum('rk,pkc->prc', band, padded, precision=highest_mode)  3.53 us
    dot_general x1, matrix products, body(): both_pencil = jnp.dot(joint, misfit_pencil, precision=highest_mode)  1.95 us
  transfers between devices with their start and end apart: 4, of which 4 were waited for; matrix products, arithmetic and copies ran while one was open for 7% of the time, Pallas kernels for 0%

profile of v14, /device:TPU:0, one launch (start us, length us, event | category | flops | bytes accessed | tf_op | source)
XLA Modules:
  0.0 80.6 jit_solution(101984110688082097)
XLA Ops:
  0.6 0.0 copy-start
  0.6 0.0 copy-start.2
  0.7 1.0 %constant_dynamic-slice_fusion.1 = f32[8,8,512]{2,1,0:T(8,128)S(1)} fusion(f32[8,32,512]{2,1,0:T(8,128)} %param.7, s32[]{:T(128)S(6)} %select_n.41), kind=kLoop, calls=%fused_computation.55 | loop fusion | bytes 262148 | tf_op jit(solution)/shard_map/dynamic_slice | solution.py:15
  1.6 3.0 %collective-permute-start = (f32[8,8,512]{2,1,0:T(8,128)S(1)}, f32[8,8,512]{2,1,0:T(8,128)S(1)}, u32[]{:S(2)}, u32[]{:S(2)}) collective-permute-start(f32[8,8,512]{2,1,0:T(8,128)S(1)} %constant_dynamic-slice_fusion.1), channel_id=1, source_target_pairs={{0,1},{1,0},{2,3},{3,2},{4,5},{5,4},{6,7},{7,6},{8,9},{9,8},{10,11... | collective-permute-start | bytes 393224 | tf_op jit(solution)/shard_map/ppermute | solution.py:16
  4.6 1.2 %reshape.108 = f32[8,16,1024]{2,1,0:T(8,128)S(1)} reshape(f32[8,32,512]{2,1,0:T(8,128)} %param.8) | data formatting | bytes 1048576 | tf_op jit(solution)/shard_map/reshape | solution.py:66
  5.9 0.0 copy-done.2
  5.9 0.1 select_reduce_fusion.1
  6.0 0.0 copy-done
  6.0 0.6 convolution_bitcast_fusion.1
  6.7 1.5 %collective-permute-done = f32[8,8,512]{2,1,0:T(8,128)S(1)} collective-permute-done((f32[8,8,512]{2,1,0:T(8,128)S(1)}, f32[8,8,512]{2,1,0:T(8,128)S(1)}, u32[]{:S(2)}, u32[]{:S(2)}) %collective-permute-start) | collective-permute-done | bytes 131104 | tf_op jit(solution)/shard_map/ppermute | solution.py:16
  8.1 0.6 fusion
  8.8 0.2 reshape.107
  9.0 0.1 pad_maximum_fusion
  9.1 1.6 %copy.35 = f32[16,16,1024]{2,1,0:T(8,128)} copy(f32[16,16,1024]{2,0,1:T(8,128)S(1)} %pad_maximum_fusion) | data formatting | bytes 2097152 | tf_op jit(solution)/shard_map/concatenate | solution.py:69
  10.6 0.0 copy-start.1
  10.6 0.0 copy-start.3
  10.6 6.3 %all-to-all-start = ((f32[16,16,1024]{2,1,0:T(8,128)}), f32[16,16,1024]{2,1,0:T(8,128)S(1)}, u32[]{:S(2)}, u32[]{:S(2)}) async-start(f32[16,16,1024]{2,1,0:T(8,128)} %copy.35), calls=%async_computation | async-start | bytes 2097152 | tf_op jit(solution)/shard_map/all_to_all | solution.py:70
  17.0 0.0 copy-done.1
  17.0 0.1 subtract_subtract_fusion
  17.1 0.0 copy-done.3
  17.1 1.4 %select_reduce_fusion = f32[128,128]{1,0:T(8,128)S(1)} fusion(f32[64]{0:T(128)S(1)} %copy-done.3, s32[128,128]{1,0:T(8,128)S(1)} %subtract_subtract_fusion), kind=kLoop, calls=%fused_computation | loop fusion | flops 3129344 | bytes 131328 | tf_op jit(solution)/shard_map/reduce_sum | solution.py:51
  18.5 0.1 copy.32
  18.6 0.1 fusion.13
  18.7 21.2 %all-to-all-done = f32[16,16,1024]{2,1,0:T(8,128)S(1)} async-done(((f32[16,16,1024]{2,1,0:T(8,128)}), f32[16,16,1024]{2,1,0:T(8,128)S(1)}, u32[]{:S(2)}, u32[]{:S(2)}) %all-to-all-start) | async-done | bytes 1048608 | tf_op jit(solution)/shard_map/all_to_all | solution.py:70
  39.9 0.6 fusion.1
  40.6 1.9 %fusion.5 = f32[16,16,1024]{2,1,0:T(8,128)} fusion(f32[128,1024,1]{1,0,2:T(8,128)S(1)} %fusion.1, f32[16,1,8,128]{3,2,1,0:T(8,128)S(1)} %fusion.8, f32[16,1,8,128]{3,2,1,0:T(8,128)S(1)} %fusion.13), kind=kOutput, calls=%fused_computation.20 | convolution fusion | flops 402685952 | bytes 1703936 | tf_op jit(solution)/shard_map/dot_general | solution.py:80
  42.5 6.9 %all-to-all-start.1 = ((f32[16,16,1024]{2,1,0:T(8,128)}), f32[16,16,1024]{2,1,0:T(8,128)S(1)}, u32[]{:S(2)}, u32[]{:S(2)}) async-start(f32[16,16,1024]{2,1,0:T(8,128)} %fusion.5), calls=%async_computation.1 | async-start | bytes 2097152 | tf_op jit(solution)/shard_map/all_to_all | solution.py:81
  50.7 21.6 %all-to-all-done.1 = f32[16,16,1024]{2,1,0:T(8,128)S(1)} async-done(((f32[16,16,1024]{2,1,0:T(8,128)}), f32[16,16,1024]{2,1,0:T(8,128)S(1)}, u32[]{:S(2)}, u32[]{:S(2)}) %all-to-all-start.1) | async-done | bytes 1048608 | tf_op jit(solution)/shard_map/all_to_all | solution.py:81
  72.3 0.1 fusion.33
  72.4 0.3 copy.36
  72.7 0.1 reshape.111
  72.9 1.6 %collective-permute-start.1 = (f32[8,8,512]{2,1,0:T(8,128)S(1)}, f32[8,8,512]{2,1,0:T(8,128)S(1)}, u32[]{:S(2)}, u32[]{:S(2)}) collective-permute-start(f32[8,8,512]{2,1,0:T(8,128)S(1)} %constant_dynamic-slice_fusion), channel_id=1, source_target_pairs={{0,1},{1,0},{2,3},{3,2},{4,5},{5,4},{6,7},{7,6},{8,9},{9,8},{10,11... | collective-permute-start | bytes 393224 | tf_op jit(solution)/shard_map/ppermute | solution.py:16
  74.4 0.3 copy.38
  74.7 0.9 %reshape.112 = f32[8,32,512]{2,1,0:T(8,128)} reshape(f32[8,16,1024]{2,1,0:T(8,128)S(1)} %copy.38) | data formatting | bytes 1048576 | tf_op jit(solution)/shard_map/reshape | solution.py:88
  75.6 0.6 fusion.23
  76.2 2.7 %collective-permute-done.1 = f32[8,8,512]{2,1,0:T(8,128)S(1)} collective-permute-done((f32[8,8,512]{2,1,0:T(8,128)S(1)}, f32[8,8,512]{2,1,0:T(8,128)S(1)}, u32[]{:S(2)}, u32[]{:S(2)}) %collective-permute-start.1) | collective-permute-done | bytes 131104 | tf_op jit(solution)/shard_map/ppermute | solution.py:16
  78.9 1.6 %maximum_multiply_fusion = f32[8,32,512]{2,1,0:T(8,128)} fusion(f32[8,32,512]{2,1,0:T(8,128)S(1)} %copy-done, f32[8,512,32]{1,2,0:T(8,128)S(1)} %fusion.23, f32[8,8,512]{2,1,0:T(8,128)S(1)} %collective-permute-done.1, f32[]{:T(128)S(6)} %mul.18, f32[]{:T(128)} %bitcast.54, f32[32,48]{1,0:T(8,128)S(1)} %get-tuple-element.2, pred[]{:T(512)S(6)} %eq.60), kind=kOutput, calls=%fused_computation.14 | convolution fusion | flops 13631744 | bytes 1736713 | tf_op jit(solution)/shard_map/rk,pkc->prc/dot_general | solution.py:40
  (4 shorter events, 0.1 us)
Async XLA Ops:
  0.6 5.4 %copy-start = (f32[8,32,512]{2,1,0:T(8,128)S(1)}, f32[8,32,512]{2,1,0:T(8,128)}, u32[]{:S(2)}) copy-start(f32[8,32,512]{2,1,0:T(8,128)} %param.7) | copy-start | bytes 1572868
  0.6 5.2 %copy-start.2 = (f32[17]{0:T(128)S(1)}, f32[17]{0:T(128)}, u32[]{:S(2)}) copy-start(f32[17]{0:T(128)} %param.11) | copy-start | bytes 208
  1.6 6.5 %collective-permute-start = (f32[8,8,512]{2,1,0:T(8,128)S(1)}, f32[8,8,512]{2,1,0:T(8,128)S(1)}, u32[]{:S(2)}, u32[]{:S(2)}) collective-permute-start(f32[8,8,512]{2,1,0:T(8,128)S(1)} %constant_dynamic-slice_fusion.1), channel_id=1, source_target_pairs={{0,1},{1,0},{2,3},{3,2},{4,5},{5,4},{6,7},{7,6},{8,9},{9,8},{10,11... | collective-permute-start | bytes 393224 | tf_op jit(solution)/shard_map/ppermute | solution.py:16
  10.6 6.3 %copy-start.1 = (s32[128]{0:T(128)S(1)}, s32[128]{0:T(128)}, u32[]{:S(2)}) copy-start(s32[128]{0:T(128)} %param.9) | copy-start | bytes 1540
  10.6 6.4 %copy-start.3 = (f32[64]{0:T(128)S(1)}, f32[64]{0:T(128)}, u32[]{:S(2)}) copy-start(f32[64]{0:T(128)} %param.10) | copy-start | bytes 772
  10.6 29.3 %all-to-all-start = ((f32[16,16,1024]{2,1,0:T(8,128)}), f32[16,16,1024]{2,1,0:T(8,128)S(1)}, u32[]{:S(2)}, u32[]{:S(2)}) async-start(f32[16,16,1024]{2,1,0:T(8,128)} %copy.35), calls=%async_computation | async-start | bytes 2097152 | tf_op jit(solution)/shard_map/all_to_all | solution.py:70
  42.5 29.8 %all-to-all-start.1 = ((f32[16,16,1024]{2,1,0:T(8,128)}), f32[16,16,1024]{2,1,0:T(8,128)S(1)}, u32[]{:S(2)}, u32[]{:S(2)}) async-start(f32[16,16,1024]{2,1,0:T(8,128)} %fusion.5), calls=%async_computation.1 | async-start | bytes 2097152 | tf_op jit(solution)/shard_map/all_to_all | solution.py:81
  72.9 6.1 %collective-permute-start.1 = (f32[8,8,512]{2,1,0:T(8,128)S(1)}, f32[8,8,512]{2,1,0:T(8,128)S(1)}, u32[]{:S(2)}, u32[]{:S(2)}) collective-permute-start(f32[8,8,512]{2,1,0:T(8,128)S(1)} %constant_dynamic-slice_fusion), channel_id=1, source_target_pairs={{0,1},{1,0},{2,3},{3,2},{4,5},{5,4},{6,7},{7,6},{8,9},{9,8},{10,11... | collective-permute-start | bytes 393224 | tf_op jit(solution)/shard_map/ppermute | solution.py:16

commit v15 on v13

--- a/solution.py
+++ b/solution.py
@@ -3,7 +3,7 @@
 from jax import lax
 from jax.sharding import PartitionSpec as P
 
-highest_mode = lax.Precision.HIGHEST
+matmul_mode = lax.Precision.HIGH
 
 
 def blur_rows(band, cells, axis, width):
@@ -37,7 +37,7 @@
 
 
 def lateral_apply(band, padded):
-    return jnp.einsum("rk,pkc->prc", band, padded, precision=highest_mode)
+    return jnp.einsum("rk,pkc->prc", band, padded, precision=matmul_mode)
 
 
 def sheet_matrix(own_offsets, depth_psf, column_count):
@@ -52,7 +52,7 @@
 
 
 def transpose_apply(sheet_psf, values):
-    return lax.dot_general(sheet_psf, values, (((0,), (0,)), ((), ())), precision=highest_mode)
+    return lax.dot_general(sheet_psf, values, (((0,), (0,)), ((), ())), precision=matmul_mode)
 
 
 def body(estimate, raw, offsets, depth_psf, lateral_psf, step_size, threshold):
@@ -68,14 +68,14 @@
     both_in = both_in.reshape(lax.axis_size("scan"), 2, plane_count, -1)
     pencil = both_in[:, 0].reshape(offsets.shape[0], -1)
     raw_pencil = both_in[:, 1].reshape(offsets.shape[0], -1)
-    predicted_pencil = jnp.dot(sheet_psf, pencil, precision=highest_mode)
+    predicted_pencil = jnp.dot(sheet_psf, pencil, precision=matmul_mode)
     misfit_pencil = predicted_pencil - raw_pencil
     scan_count = lax.axis_size("scan")
     all_planes = offsets.shape[0]
     keep = jnp.eye(all_planes, dtype=jnp.float32).reshape(scan_count, 1, plane_count, all_planes)
     spread = sheet_psf.T.reshape(scan_count, 1, plane_count, all_planes)
     joint = jnp.concatenate([keep, spread], axis=1).reshape(2 * all_planes, all_planes)
-    both_pencil = jnp.dot(joint, misfit_pencil, precision=highest_mode)
+    both_pencil = jnp.dot(joint, misfit_pencil, precision=matmul_mode)
     both_out = lax.all_to_all(both_pencil, "scan", split_axis=0, concat_axis=1, tiled=True)
     misfit = both_out[:plane_count]
     back_volume = both_out[plane_count:].reshape(plane_count, row_count, width_count)

time: 81.4 us -> 80.3 us (0.986)
  matrix products: 6.11 us -> 4.66 us
    dot_general x6, matrix products: 6.11 us -> 4.66 us  [the longest x4 2.69 us: lateral_apply(): return jnp.einsum('rk,pkc->prc', band, padded, precision=matmul_mode)]
  transfers between devices with their start and end apart: 4 -> 4, of which waited for: 4 -> 4; matrix products, arithmetic and copies ran while one was open for 7% -> 6% of each run, Pallas kernels for 0% -> 0%
where the time goes in v15:
time: 80.3 us; the launch traced here: 79.5 us
  waiting for transfers between devices  47.5 us (59%)
  starting transfers between devices  17.7 us (22%)
  local copies, waits for them, and re-layouts  5.71 us (7%)
  matrix products  4.66 us (6%)
  between operations  2.13 us (3%)
  other arithmetic  1.8 us (2%)
    all_to_all x1, waiting for transfers between devices, body(): lax.all_to_all(both_pencil, 'scan', split_axis=0, concat_axis=1, tiled=True)  21.6 us
    all_to_all x1, waiting for transfers between devices, body(): lax.all_to_all(both_flat, 'scan', split_axis=1, concat_axis=0, tiled=True)  21.2 us
    all_to_all x1, starting transfers between devices, body(): lax.all_to_all(both_pencil, 'scan', split_axis=0, concat_axis=1, tiled=True)  6.86 us
    all_to_all x1, starting transfers between devices, body(): lax.all_to_all(both_flat, 'scan', split_axis=1, concat_axis=0, tiled=True)  6.32 us
    ppermute x2, waiting for transfers between devices, blur_rows(): arrived = lax.ppermute(sent, axis, [(0, 1), (1, 0)])  4.59 us
    ppermute x2, starting transfers between devices, blur_rows(): arrived = lax.ppermute(sent, axis, [(0, 1), (1, 0)])  4.56 us
    concatenate x3, local copies, waits for them, and re-layouts, body(): jnp.concatenate([blurred, raw.reshape(plane_count, flat_count)], axis=0)  2.96 us
    dot_general x4, matrix products, lateral_apply(): return jnp.einsum('rk,pkc->prc', band, padded, precision=matmul_mode)  2.69 us
  transfers between devices with their start and end apart: 4, of which 4 were waited for; matrix products, arithmetic and copies ran while one was open for 6% of the time, Pallas kernels for 0%

profile of v15, /device:TPU:0, one launch (start us, length us, event | category | flops | bytes accessed | tf_op | source)
XLA Modules:
  0.0 79.5 jit_solution(4175543560962624139)
XLA Ops:
  0.6 0.0 copy-start
  0.6 0.0 copy-start.2
  0.7 1.0 %constant_dynamic-slice_fusion.1 = f32[8,8,512]{2,1,0:T(8,128)S(1)} fusion(f32[8,32,512]{2,1,0:T(8,128)} %param.7, s32[]{:T(128)S(6)} %select_n.41), kind=kLoop, calls=%fused_computation.55 | loop fusion | bytes 262148 | tf_op jit(solution)/shard_map/dynamic_slice | solution.py:15
  1.6 3.0 %collective-permute-start = (f32[8,8,512]{2,1,0:T(8,128)S(1)}, f32[8,8,512]{2,1,0:T(8,128)S(1)}, u32[]{:S(2)}, u32[]{:S(2)}) collective-permute-start(f32[8,8,512]{2,1,0:T(8,128)S(1)} %constant_dynamic-slice_fusion.1), channel_id=1, source_target_pairs={{0,1},{1,0},{2,3},{3,2},{4,5},{5,4},{6,7},{7,6},{8,9},{9,8},{10,11... | collective-permute-start | bytes 393224 | tf_op jit(solution)/shard_map/ppermute | solution.py:16
  4.6 1.2 %concatenate.13 = f32[8,16,1024]{2,1,0:T(8,128)S(1)} reshape(f32[8,32,512]{2,1,0:T(8,128)} %param.8) | data formatting | bytes 1048576 | tf_op jit(solution)/shard_map/concatenate | solution.py:66
  5.9 0.0 copy-done.2
  5.9 0.1 select_reduce_fusion.1
  6.0 0.0 copy-done
  6.0 0.4 convolution_bitcast_fusion.1
  6.4 1.7 %collective-permute-done = f32[8,8,512]{2,1,0:T(8,128)S(1)} collective-permute-done((f32[8,8,512]{2,1,0:T(8,128)S(1)}, f32[8,8,512]{2,1,0:T(8,128)S(1)}, u32[]{:S(2)}, u32[]{:S(2)}) %collective-permute-start) | collective-permute-done | bytes 131104 | tf_op jit(solution)/shard_map/ppermute | solution.py:16
  8.1 0.4 fusion
  8.6 0.2 concatenate.12
  8.8 0.1 pad_maximum_fusion
  8.9 1.6 %copy.39 = f32[16,16,1024]{2,0,1:T(8,128)} copy(f32[16,16,1024]{2,1,0:T(8,128)S(1)} %pad_maximum_fusion) | data formatting | bytes 2097152 | tf_op jit(solution)/shard_map/concatenate | solution.py:66
  10.4 0.0 copy-start.1
  10.4 0.0 copy-start.3
  10.4 6.3 %all-to-all-start = ((f32[16,16,1024]{2,0,1:T(8,128)}), f32[16,16,1024]{2,0,1:T(8,128)S(1)}, u32[]{:S(2)}, u32[]{:S(2)}) async-start(f32[16,16,1024]{2,0,1:T(8,128)} %copy.39), calls=%async_computation | async-start | bytes 2097152 | tf_op jit(solution)/shard_map/all_to_all | solution.py:67
  16.8 0.0 copy-done.1
  16.8 0.1 subtract_subtract_fusion
  16.9 0.0 copy-done.3
  16.9 1.4 %select_reduce_fusion = f32[128,128]{1,0:T(8,128)S(1)} fusion(f32[64]{0:T(128)S(1)} %copy-done.3, s32[128,128]{1,0:T(8,128)S(1)} %subtract_subtract_fusion), kind=kLoop, calls=%fused_computation | loop fusion | flops 3129344 | bytes 131328 | tf_op jit(solution)/shard_map/reduce_sum | solution.py:51
  18.2 0.1 copy.36
  18.4 0.1 fusion.13
  18.5 21.2 %all-to-all-done = f32[16,16,1024]{2,0,1:T(8,128)S(1)} async-done(((f32[16,16,1024]{2,0,1:T(8,128)}), f32[16,16,1024]{2,0,1:T(8,128)S(1)}, u32[]{:S(2)}, u32[]{:S(2)}) %all-to-all-start) | async-done | bytes 1048608 | tf_op jit(solution)/shard_map/all_to_all | solution.py:67
  39.7 0.4 fusion.1
  40.1 1.6 %fusion.5 = f32[16,16,1024]{2,1,0:T(8,128)} fusion(f32[128,1024,1]{1,0,2:T(8,128)S(1)} %fusion.1, f32[16,1,8,128]{3,2,1,0:T(8,128)S(1)} %fusion.8, f32[16,1,8,128]{3,2,1,0:T(8,128)S(1)} %fusion.13), kind=kOutput, calls=%fused_computation.20 | convolution fusion | flops 201359360 | bytes 1703936 | tf_op jit(solution)/shard_map/dot_general | solution.py:78
  41.7 6.9 %all-to-all-start.1 = ((f32[16,16,1024]{2,1,0:T(8,128)}), f32[16,16,1024]{2,1,0:T(8,128)S(1)}, u32[]{:S(2)}, u32[]{:S(2)}) async-start(f32[16,16,1024]{2,1,0:T(8,128)} %fusion.5), calls=%async_computation.1 | async-start | bytes 2097152 | tf_op jit(solution)/shard_map/all_to_all | solution.py:79
  49.9 21.6 %all-to-all-done.1 = f32[16,16,1024]{2,1,0:T(8,128)S(1)} async-done(((f32[16,16,1024]{2,1,0:T(8,128)}), f32[16,16,1024]{2,1,0:T(8,128)S(1)}, u32[]{:S(2)}, u32[]{:S(2)}) %all-to-all-start.1) | async-done | bytes 1048608 | tf_op jit(solution)/shard_map/all_to_all | solution.py:79
  71.5 0.1 fusion.33
  71.6 0.3 copy.40
  71.9 0.1 reshape.109
  72.0 1.6 %collective-permute-start.1 = (f32[8,8,512]{2,1,0:T(8,128)S(1)}, f32[8,8,512]{2,1,0:T(8,128)S(1)}, u32[]{:S(2)}, u32[]{:S(2)}) collective-permute-start(f32[8,8,512]{2,1,0:T(8,128)S(1)} %constant_dynamic-slice_fusion), channel_id=1, source_target_pairs={{0,1},{1,0},{2,3},{3,2},{4,5},{5,4},{6,7},{7,6},{8,9},{9,8},{10,11... | collective-permute-start | bytes 393224 | tf_op jit(solution)/shard_map/ppermute | solution.py:16
  73.6 0.3 copy.42
  73.9 0.9 %reshape.110 = f32[8,32,512]{2,1,0:T(8,128)} reshape(f32[8,16,1024]{2,1,0:T(8,128)S(1)} %copy.42) | data formatting | bytes 1048576 | tf_op jit(solution)/shard_map/reshape | solution.py:86
  74.8 0.4 fusion.23
  75.2 2.9 %collective-permute-done.1 = f32[8,8,512]{2,1,0:T(8,128)S(1)} collective-permute-done((f32[8,8,512]{2,1,0:T(8,128)S(1)}, f32[8,8,512]{2,1,0:T(8,128)S(1)}, u32[]{:S(2)}, u32[]{:S(2)}) %collective-permute-start.1) | collective-permute-done | bytes 131104 | tf_op jit(solution)/shard_map/ppermute | solution.py:16
  78.1 1.4 %maximum_multiply_fusion = f32[8,32,512]{2,1,0:T(8,128)} fusion(f32[8,32,512]{2,1,0:T(8,128)S(1)} %copy-done, f32[8,512,32]{1,2,0:T(8,128)S(1)} %fusion.23, f32[8,8,512]{2,1,0:T(8,128)S(1)} %collective-permute-done.1, f32[]{:T(128)S(6)} %mul.18, f32[]{:T(128)} %bitcast.55, f32[32,48]{1,0:T(8,128)S(1)} %get-tuple-element.2, pred[]{:T(512)S(6)} %eq.60), kind=kOutput, calls=%fused_computation.14 | convolution fusion | flops 7340288 | bytes 1736713 | tf_op jit(solution)/shard_map/rk,pkc->prc/dot_general | solution.py:40
  (4 shorter events, 0.1 us)
Async XLA Ops:
  0.6 5.4 %copy-start = (f32[8,32,512]{2,1,0:T(8,128)S(1)}, f32[8,32,512]{2,1,0:T(8,128)}, u32[]{:S(2)}) copy-start(f32[8,32,512]{2,1,0:T(8,128)} %param.7) | copy-start | bytes 1572868
  0.6 5.2 %copy-start.2 = (f32[17]{0:T(128)S(1)}, f32[17]{0:T(128)}, u32[]{:S(2)}) copy-start(f32[17]{0:T(128)} %param.11) | copy-start | bytes 208
  1.6 6.5 %collective-permute-start = (f32[8,8,512]{2,1,0:T(8,128)S(1)}, f32[8,8,512]{2,1,0:T(8,128)S(1)}, u32[]{:S(2)}, u32[]{:S(2)}) collective-permute-start(f32[8,8,512]{2,1,0:T(8,128)S(1)} %constant_dynamic-slice_fusion.1), channel_id=1, source_target_pairs={{0,1},{1,0},{2,3},{3,2},{4,5},{5,4},{6,7},{7,6},{8,9},{9,8},{10,11... | collective-permute-start | bytes 393224 | tf_op jit(solution)/shard_map/ppermute | solution.py:16
  10.4 6.3 %copy-start.1 = (s32[128]{0:T(128)S(1)}, s32[128]{0:T(128)}, u32[]{:S(2)}) copy-start(s32[128]{0:T(128)} %param.9) | copy-start | bytes 1540
  10.4 6.4 %copy-start.3 = (f32[64]{0:T(128)S(1)}, f32[64]{0:T(128)}, u32[]{:S(2)}) copy-start(f32[64]{0:T(128)} %param.10) | copy-start | bytes 772
  10.4 29.3 %all-to-all-start = ((f32[16,16,1024]{2,0,1:T(8,128)}), f32[16,16,1024]{2,0,1:T(8,128)S(1)}, u32[]{:S(2)}, u32[]{:S(2)}) async-start(f32[16,16,1024]{2,0,1:T(8,128)} %copy.39), calls=%async_computation | async-start | bytes 2097152 | tf_op jit(solution)/shard_map/all_to_all | solution.py:67
  41.7 29.8 %all-to-all-start.1 = ((f32[16,16,1024]{2,1,0:T(8,128)}), f32[16,16,1024]{2,1,0:T(8,128)S(1)}, u32[]{:S(2)}, u32[]{:S(2)}) async-start(f32[16,16,1024]{2,1,0:T(8,128)} %fusion.5), calls=%async_computation.1 | async-start | bytes 2097152 | tf_op jit(solution)/shard_map/all_to_all | solution.py:79
  72.0 6.1 %collective-permute-start.1 = (f32[8,8,512]{2,1,0:T(8,128)S(1)}, f32[8,8,512]{2,1,0:T(8,128)S(1)}, u32[]{:S(2)}, u32[]{:S(2)}) collective-permute-start(f32[8,8,512]{2,1,0:T(8,128)S(1)} %constant_dynamic-slice_fusion), channel_id=1, source_target_pairs={{0,1},{1,0},{2,3},{3,2},{4,5},{5,4},{6,7},{7,6},{8,9},{9,8},{10,11... | collective-permute-start | bytes 393224 | tf_op jit(solution)/shard_map/ppermute | solution.py:16

commit v16 on v13

--- a/solution.py
+++ b/solution.py
@@ -4,25 +4,26 @@
 from jax.sharding import PartitionSpec as P
 
 highest_mode = lax.Precision.HIGHEST
+high_mode = lax.Precision.HIGH
 
 
-def blur_rows(band, cells, axis, width):
+def blur_rows(band, cells, axis, width, precision=highest_mode):
     count = lax.axis_size(axis)
     rows = cells.shape[1]
-    summed = lateral_apply(band[:, width : width + rows], cells)
+    summed = lateral_apply(band[:, width : width + rows], cells, precision)
     if count == 2:
         first = lax.axis_index(axis) == 0
         sent = lax.dynamic_slice_in_dim(cells, jnp.where(first, rows - width, 0), width, axis=1)
         arrived = lax.ppermute(sent, axis, [(0, 1), (1, 0)])
         edge = jnp.where(first, band[:, width + rows :], band[:, :width])
-        return summed + lateral_apply(edge, arrived)
+        return summed + lateral_apply(edge, arrived, precision)
     ends = count - 1
     head = lax.slice_in_dim(cells, 0, width, axis=1)
     tail = lax.slice_in_dim(cells, rows - width, rows, axis=1)
     above = lax.ppermute(tail, axis, [(i, (i + 1) % count) for i in range(ends)])
     below = lax.ppermute(head, axis, [((i + 1) % count, i) for i in range(ends)])
-    summed = summed + lateral_apply(band[:, :width], above)
-    return summed + lateral_apply(band[:, width + rows :], below)
+    summed = summed + lateral_apply(band[:, :width], above, precision)
+    return summed + lateral_apply(band[:, width + rows :], below, precision)
 
 
 def band_matrix(kernel_taps, row_count, flip):
@@ -36,8 +37,8 @@
     return jnp.sum(jnp.where(lag[:, :, None] == taps, kernel_taps, 0.0), axis=-1)
 
 
-def lateral_apply(band, padded):
-    return jnp.einsum("rk,pkc->prc", band, padded, precision=highest_mode)
+def lateral_apply(band, padded, precision=highest_mode):
+    return jnp.einsum("rk,pkc->prc", band, padded, precision=precision)
 
 
 def sheet_matrix(own_offsets, depth_psf, column_count):
@@ -75,11 +76,11 @@
     keep = jnp.eye(all_planes, dtype=jnp.float32).reshape(scan_count, 1, plane_count, all_planes)
     spread = sheet_psf.T.reshape(scan_count, 1, plane_count, all_planes)
     joint = jnp.concatenate([keep, spread], axis=1).reshape(2 * all_planes, all_planes)
-    both_pencil = jnp.dot(joint, misfit_pencil, precision=highest_mode)
+    both_pencil = jnp.dot(joint, misfit_pencil, precision=high_mode)
     both_out = lax.all_to_all(both_pencil, "scan", split_axis=0, concat_axis=1, tiled=True)
     misfit = both_out[:plane_count]
     back_volume = both_out[plane_count:].reshape(plane_count, row_count, width_count)
-    gradient = blur_rows(back_band, back_volume, "row", halo_rows)
+    gradient = blur_rows(back_band, back_volume, "row", halo_rows, high_mode)
     stepped = estimate - step_size[0] * gradient
     shrink_level = step_size[0] * threshold[0]
     new_estimate = jnp.sign(stepped) * jnp.maximum(jnp.abs(stepped) - shrink_level, 0.0)

time: 81.4 us -> 80.8 us (level)
  matrix products: 6.11 us -> 5.29 us
    dot_general x5, matrix products: 5.48 us -> 4.65 us  [the longest x4 3.1 us: lateral_apply(): return jnp.einsum('rk,pkc->prc', band, padded, precision=precision)]
where the time goes in v16:
time: 80.8 us; the launch traced here: 80 us
  waiting for transfers between devices  47.3 us (59%)
  starting transfers between devices  17.8 us (22%)
  local copies, waits for them, and re-layouts  5.71 us (7%)
  matrix products  5.29 us (7%)
  between operations  2.13 us (3%)
  other arithmetic  1.8 us (2%)
    all_to_all x1, waiting for transfers between devices, body(): lax.all_to_all(both_pencil, 'scan', split_axis=0, concat_axis=1, tiled=True)  21.6 us
    all_to_all x1, waiting for transfers between devices, body(): lax.all_to_all(both_flat, 'scan', split_axis=1, concat_axis=0, tiled=True)  21.2 us
    all_to_all x1, starting transfers between devices, body(): lax.all_to_all(both_pencil, 'scan', split_axis=0, concat_axis=1, tiled=True)  6.86 us
    all_to_all x1, starting transfers between devices, body(): lax.all_to_all(both_flat, 'scan', split_axis=1, concat_axis=0, tiled=True)  6.33 us
    ppermute x2, starting transfers between devices, blur_rows(): arrived = lax.ppermute(sent, axis, [(0, 1), (1, 0)])  4.56 us
    ppermute x2, waiting for transfers between devices, blur_rows(): arrived = lax.ppermute(sent, axis, [(0, 1), (1, 0)])  4.38 us
    dot_general x4, matrix products, lateral_apply(): return jnp.einsum('rk,pkc->prc', band, padded, precision=precision)  3.1 us
    concatenate x3, local copies, waits for them, and re-layouts, body(): jnp.concatenate([blurred, raw.reshape(plane_count, flat_count)], axis=0)  2.96 us
  transfers between devices with their start and end apart: 4, of which 4 were waited for; matrix products, arithmetic and copies ran while one was open for 7% of the time, Pallas kernels for 0%

profile of v16, /device:TPU:0, one launch (start us, length us, event | category | flops | bytes accessed | tf_op | source)
XLA Modules:
  0.0 80.0 jit_solution(2319969064565095970)
XLA Ops:
  0.6 0.0 copy-start
  0.6 0.0 copy-start.2
  0.7 1.0 %constant_dynamic-slice_fusion.1 = f32[8,8,512]{2,1,0:T(8,128)S(1)} fusion(f32[8,32,512]{2,1,0:T(8,128)} %param.7, s32[]{:T(128)S(6)} %select_n.41), kind=kLoop, calls=%fused_computation.55 | loop fusion | bytes 262148 | tf_op jit(solution)/shard_map/dynamic_slice | solution.py:16
  1.6 3.0 %collective-permute-start = (f32[8,8,512]{2,1,0:T(8,128)S(1)}, f32[8,8,512]{2,1,0:T(8,128)S(1)}, u32[]{:S(2)}, u32[]{:S(2)}) collective-permute-start(f32[8,8,512]{2,1,0:T(8,128)S(1)} %constant_dynamic-slice_fusion.1), channel_id=1, source_target_pairs={{0,1},{1,0},{2,3},{3,2},{4,5},{5,4},{6,7},{7,6},{8,9},{9,8},{10,11... | collective-permute-start | bytes 393224 | tf_op jit(solution)/shard_map/ppermute | solution.py:17
  4.6 1.2 %concatenate.13 = f32[8,16,1024]{2,1,0:T(8,128)S(1)} reshape(f32[8,32,512]{2,1,0:T(8,128)} %param.8) | data formatting | bytes 1048576 | tf_op jit(solution)/shard_map/concatenate | solution.py:67
  5.9 0.0 copy-done.2
  5.9 0.1 select_reduce_fusion.1
  6.0 0.0 copy-done
  6.0 0.6 convolution_bitcast_fusion.1
  6.7 1.5 %collective-permute-done = f32[8,8,512]{2,1,0:T(8,128)S(1)} collective-permute-done((f32[8,8,512]{2,1,0:T(8,128)S(1)}, f32[8,8,512]{2,1,0:T(8,128)S(1)}, u32[]{:S(2)}, u32[]{:S(2)}) %collective-permute-start) | collective-permute-done | bytes 131104 | tf_op jit(solution)/shard_map/ppermute | solution.py:17
  8.1 0.6 fusion
  8.8 0.2 concatenate.12
  9.0 0.1 pad_maximum_fusion
  9.1 1.6 %copy.39 = f32[16,16,1024]{2,0,1:T(8,128)} copy(f32[16,16,1024]{2,1,0:T(8,128)S(1)} %pad_maximum_fusion) | data formatting | bytes 2097152 | tf_op jit(solution)/shard_map/concatenate | solution.py:67
  10.6 0.0 copy-start.1
  10.6 0.0 copy-start.3
  10.6 6.3 %all-to-all-start = ((f32[16,16,1024]{2,0,1:T(8,128)}), f32[16,16,1024]{2,0,1:T(8,128)S(1)}, u32[]{:S(2)}, u32[]{:S(2)}) async-start(f32[16,16,1024]{2,0,1:T(8,128)} %copy.39), calls=%async_computation | async-start | bytes 2097152 | tf_op jit(solution)/shard_map/all_to_all | solution.py:68
  17.0 0.0 copy-done.1
  17.0 0.1 subtract_subtract_fusion
  17.1 0.0 copy-done.3
  17.1 1.4 %select_reduce_fusion = f32[128,128]{1,0:T(8,128)S(1)} fusion(f32[64]{0:T(128)S(1)} %copy-done.3, s32[128,128]{1,0:T(8,128)S(1)} %subtract_subtract_fusion), kind=kLoop, calls=%fused_computation | loop fusion | flops 3129344 | bytes 131328 | tf_op jit(solution)/shard_map/reduce_sum | solution.py:52
  18.5 0.1 copy.36
  18.6 0.1 fusion.13
  18.7 21.2 %all-to-all-done = f32[16,16,1024]{2,0,1:T(8,128)S(1)} async-done(((f32[16,16,1024]{2,0,1:T(8,128)}), f32[16,16,1024]{2,0,1:T(8,128)S(1)}, u32[]{:S(2)}, u32[]{:S(2)}) %all-to-all-start) | async-done | bytes 1048608 | tf_op jit(solution)/shard_map/all_to_all | solution.py:68
  39.9 0.6 fusion.1
  40.6 1.6 %fusion.5 = f32[16,16,1024]{2,1,0:T(8,128)} fusion(f32[128,1024,1]{1,0,2:T(8,128)S(1)} %fusion.1, f32[16,1,8,128]{3,2,1,0:T(8,128)S(1)} %fusion.8, f32[16,1,8,128]{3,2,1,0:T(8,128)S(1)} %fusion.13), kind=kOutput, calls=%fused_computation.20 | convolution fusion | flops 201359360 | bytes 1703936 | tf_op jit(solution)/shard_map/dot_general | solution.py:79
  42.1 6.9 %all-to-all-start.1 = ((f32[16,16,1024]{2,1,0:T(8,128)}), f32[16,16,1024]{2,1,0:T(8,128)S(1)}, u32[]{:S(2)}, u32[]{:S(2)}) async-start(f32[16,16,1024]{2,1,0:T(8,128)} %fusion.5), calls=%async_computation.1 | async-start | bytes 2097152 | tf_op jit(solution)/shard_map/all_to_all | solution.py:80
  50.3 21.6 %all-to-all-done.1 = f32[16,16,1024]{2,1,0:T(8,128)S(1)} async-done(((f32[16,16,1024]{2,1,0:T(8,128)}), f32[16,16,1024]{2,1,0:T(8,128)S(1)}, u32[]{:S(2)}, u32[]{:S(2)}) %all-to-all-start.1) | async-done | bytes 1048608 | tf_op jit(solution)/shard_map/all_to_all | solution.py:80
  71.9 0.1 fusion.33
  72.0 0.3 copy.40
  72.4 0.1 reshape.109
  72.5 1.6 %collective-permute-start.1 = (f32[8,8,512]{2,1,0:T(8,128)S(1)}, f32[8,8,512]{2,1,0:T(8,128)S(1)}, u32[]{:S(2)}, u32[]{:S(2)}) collective-permute-start(f32[8,8,512]{2,1,0:T(8,128)S(1)} %constant_dynamic-slice_fusion), channel_id=1, source_target_pairs={{0,1},{1,0},{2,3},{3,2},{4,5},{5,4},{6,7},{7,6},{8,9},{9,8},{10,11... | collective-permute-start | bytes 393224 | tf_op jit(solution)/shard_map/ppermute | solution.py:17
  74.0 0.3 copy.42
  74.3 0.9 %reshape.110 = f32[8,32,512]{2,1,0:T(8,128)} reshape(f32[8,16,1024]{2,1,0:T(8,128)S(1)} %copy.42) | data formatting | bytes 1048576 | tf_op jit(solution)/shard_map/reshape | solution.py:87
  75.2 0.4 fusion.23
  75.6 2.9 %collective-permute-done.1 = f32[8,8,512]{2,1,0:T(8,128)S(1)} collective-permute-done((f32[8,8,512]{2,1,0:T(8,128)S(1)}, f32[8,8,512]{2,1,0:T(8,128)S(1)}, u32[]{:S(2)}, u32[]{:S(2)}) %collective-permute-start.1) | collective-permute-done | bytes 131104 | tf_op jit(solution)/shard_map/ppermute | solution.py:17
  78.5 1.4 %maximum_multiply_fusion = f32[8,32,512]{2,1,0:T(8,128)} fusion(f32[8,32,512]{2,1,0:T(8,128)S(1)} %copy-done, f32[8,512,32]{1,2,0:T(8,128)S(1)} %fusion.23, f32[8,8,512]{2,1,0:T(8,128)S(1)} %collective-permute-done.1, f32[]{:T(128)S(6)} %mul.18, f32[]{:T(128)} %bitcast.55, f32[32,48]{1,0:T(8,128)S(1)} %get-tuple-element.2, pred[]{:T(512)S(6)} %eq.60), kind=kOutput, calls=%fused_computation.14 | convolution fusion | flops 7340288 | bytes 1736713 | tf_op jit(solution)/shard_map/rk,pkc->prc/dot_general | solution.py:41
  (4 shorter events, 0.1 us)
Async XLA Ops:
  0.6 5.4 %copy-start = (f32[8,32,512]{2,1,0:T(8,128)S(1)}, f32[8,32,512]{2,1,0:T(8,128)}, u32[]{:S(2)}) copy-start(f32[8,32,512]{2,1,0:T(8,128)} %param.7) | copy-start | bytes 1572868
  0.6 5.2 %copy-start.2 = (f32[17]{0:T(128)S(1)}, f32[17]{0:T(128)}, u32[]{:S(2)}) copy-start(f32[17]{0:T(128)} %param.11) | copy-start | bytes 208
  1.6 6.5 %collective-permute-start = (f32[8,8,512]{2,1,0:T(8,128)S(1)}, f32[8,8,512]{2,1,0:T(8,128)S(1)}, u32[]{:S(2)}, u32[]{:S(2)}) collective-permute-start(f32[8,8,512]{2,1,0:T(8,128)S(1)} %constant_dynamic-slice_fusion.1), channel_id=1, source_target_pairs={{0,1},{1,0},{2,3},{3,2},{4,5},{5,4},{6,7},{7,6},{8,9},{9,8},{10,11... | collective-permute-start | bytes 393224 | tf_op jit(solution)/shard_map/ppermute | solution.py:17
  10.6 6.3 %copy-start.1 = (s32[128]{0:T(128)S(1)}, s32[128]{0:T(128)}, u32[]{:S(2)}) copy-start(s32[128]{0:T(128)} %param.9) | copy-start | bytes 1540
  10.6 6.4 %copy-start.3 = (f32[64]{0:T(128)S(1)}, f32[64]{0:T(128)}, u32[]{:S(2)}) copy-start(f32[64]{0:T(128)} %param.10) | copy-start | bytes 772
  10.6 29.3 %all-to-all-start = ((f32[16,16,1024]{2,0,1:T(8,128)}), f32[16,16,1024]{2,0,1:T(8,128)S(1)}, u32[]{:S(2)}, u32[]{:S(2)}) async-start(f32[16,16,1024]{2,0,1:T(8,128)} %copy.39), calls=%async_computation | async-start | bytes 2097152 | tf_op jit(solution)/shard_map/all_to_all | solution.py:68
  42.1 29.8 %all-to-all-start.1 = ((f32[16,16,1024]{2,1,0:T(8,128)}), f32[16,16,1024]{2,1,0:T(8,128)S(1)}, u32[]{:S(2)}, u32[]{:S(2)}) async-start(f32[16,16,1024]{2,1,0:T(8,128)} %fusion.5), calls=%async_computation.1 | async-start | bytes 2097152 | tf_op jit(solution)/shard_map/all_to_all | solution.py:80
  72.5 6.1 %collective-permute-start.1 = (f32[8,8,512]{2,1,0:T(8,128)S(1)}, f32[8,8,512]{2,1,0:T(8,128)S(1)}, u32[]{:S(2)}, u32[]{:S(2)}) collective-permute-start(f32[8,8,512]{2,1,0:T(8,128)S(1)} %constant_dynamic-slice_fusion), channel_id=1, source_target_pairs={{0,1},{1,0},{2,3},{3,2},{4,5},{5,4},{6,7},{7,6},{8,9},{9,8},{10,11... | collective-permute-start | bytes 393224 | tf_op jit(solution)/shard_map/ppermute | solution.py:17

commit v17 on v13

--- a/solution.py
+++ b/solution.py
@@ -23,6 +23,30 @@
     below = lax.ppermute(head, axis, [((i + 1) % count, i) for i in range(ends)])
     summed = summed + lateral_apply(band[:, :width], above)
     return summed + lateral_apply(band[:, width + rows :], below)
+
+
+def chunked_forward(estimate, raw, band, sheet_psf, width, chunk_count):
+    plane_count, rows, columns = estimate.shape
+    per_chunk = rows // chunk_count
+    first = lax.axis_index("row") == 0
+    sent = lax.dynamic_slice_in_dim(estimate, jnp.where(first, rows - width, 0), width, axis=1)
+    arrived = lax.ppermute(sent, "row", [(0, 1), (1, 0)])
+    stacked = jnp.concatenate([estimate, raw], axis=1)
+    own = band[:, width : width + rows]
+    keep = jnp.eye(rows, dtype=own.dtype)
+    zero = jnp.zeros_like(own)
+    joint = jnp.stack([jnp.concatenate([own, zero], axis=1), jnp.concatenate([zero, keep], axis=1)])
+    joint = joint.reshape(2, chunk_count, per_chunk, 2 * rows).transpose(1, 0, 2, 3)
+    edge = jnp.where(first, band[:, width + rows :], band[:, :width])
+    edge = jnp.stack([edge, jnp.zeros_like(edge)]).reshape(2, chunk_count, per_chunk, width).transpose(1, 0, 2, 3)
+    outgoing = jnp.einsum("karj,pjc->karpc", joint, stacked, precision=highest_mode)
+    outgoing = outgoing + jnp.einsum("karj,pjc->karpc", edge, arrived, precision=highest_mode)
+    incoming = lax.all_to_all(outgoing, "scan", split_axis=0, concat_axis=0, tiled=True)
+    all_planes = sheet_psf.shape[0]
+    sheet_parts = sheet_psf.reshape(all_planes, chunk_count, plane_count)
+    predicted = jnp.einsum("qsp,srpc->qrc", sheet_parts, incoming[:, 0], precision=highest_mode)
+    raw_pencil = incoming[:, 1].transpose(0, 2, 1, 3).reshape(all_planes, per_chunk, columns)
+    return (predicted - raw_pencil).reshape(all_planes, per_chunk * columns)
 
 
 def band_matrix(kernel_taps, row_count, flip):
@@ -62,14 +86,18 @@
     sheet_psf = sheet_matrix(offsets, depth_psf, offsets.shape[0])
     blur_band = band_matrix(lateral_psf, row_count, False)
     back_band = band_matrix(lateral_psf, row_count, True)
-    blurred = blur_rows(blur_band, estimate, "row", halo_rows).reshape(plane_count, flat_count)
-    both_flat = jnp.concatenate([blurred, raw.reshape(plane_count, flat_count)], axis=0)
-    both_in = lax.all_to_all(both_flat, "scan", split_axis=1, concat_axis=0, tiled=True)
-    both_in = both_in.reshape(lax.axis_size("scan"), 2, plane_count, -1)
-    pencil = both_in[:, 0].reshape(offsets.shape[0], -1)
-    raw_pencil = both_in[:, 1].reshape(offsets.shape[0], -1)
-    predicted_pencil = jnp.dot(sheet_psf, pencil, precision=highest_mode)
-    misfit_pencil = predicted_pencil - raw_pencil
+    scan_count = lax.axis_size("scan")
+    if row_count % scan_count == 0 and lax.axis_size("row") == 2:
+        misfit_pencil = chunked_forward(estimate, raw, blur_band, sheet_psf, halo_rows, scan_count)
+    else:
+        blurred = blur_rows(blur_band, estimate, "row", halo_rows).reshape(plane_count, flat_count)
+        both_flat = jnp.concatenate([blurred, raw.reshape(plane_count, flat_count)], axis=0)
+        both_in = lax.all_to_all(both_flat, "scan", split_axis=1, concat_axis=0, tiled=True)
+        both_in = both_in.reshape(scan_count, 2, plane_count, -1)
+        pencil = both_in[:, 0].reshape(offsets.shape[0], -1)
+        raw_pencil = both_in[:, 1].reshape(offsets.shape[0], -1)
+        predicted_pencil = jnp.dot(sheet_psf, pencil, precision=highest_mode)
+        misfit_pencil = predicted_pencil - raw_pencil
     scan_count = lax.axis_size("scan")
     all_planes = offsets.shape[0]
     keep = jnp.eye(all_planes, dtype=jnp.float32).reshape(scan_count, 1, plane_count, all_planes)

time: 81.4 us -> 81.7 us (level)
  matrix products: 6.11 us -> 8.16 us
  waiting for transfers between devices: 47.1 us -> 45.5 us
  local copies, waits for them, and re-layouts: 5.71 us -> 4.81 us
    dot_general x1 -> x3, matrix products: 0.64 us -> 3.93 us  [the longest x1 2.21 us: chunked_forward(): jnp.einsum('karj,pjc->karpc', joint, stacked, precision=highest_mode)]
    ppermute x0 -> x1, starting transfers between devices: none -> 3 us  [chunked_forward(): arrived = lax.ppermute(sent, 'row', [(0, 1), (1, 0)])]
    ppermute x2 -> x1, starting transfers between devices: 4.56 us -> 1.56 us  [blur_rows(): arrived = lax.ppermute(sent, axis, [(0, 1), (1, 0)])]
    concatenate x3 -> x1, local copies, waits for them, and re-layouts: 2.96 us -> 0.01 us  [chunked_forward(): jnp.concatenate([own, zero], axis=1)]
    add x0 -> x1, local copies, waits for them, and re-layouts: none -> 1.58 us  [chunked_forward(): outgoing + jnp.einsum('karj,pjc->karpc', edge, arrived, precision=highest...]
    ppermute x2 -> x1, waiting for transfers between devices: 4.17 us -> 2.67 us  [blur_rows(): arrived = lax.ppermute(sent, axis, [(0, 1), (1, 0)])]
    dot_general x4 -> x2, matrix products: 3.53 us -> 2.28 us  [lateral_apply(): return jnp.einsum('rk,pkc->prc', band, padded, precision=highest_mode)]
    dynamic_slice x2 -> x1, local copies, waits for them, and re-layouts: 0.99 us -> 0.02 us  [blur_rows(): lax.dynamic_slice_in_dim(cells, jnp.where(first, rows - width, 0), width,...]
  transfers between devices with their start and end apart: 4 -> 4, of which waited for: 4 -> 4; matrix products, arithmetic and copies ran while one was open for 7% -> 9% of each run, Pallas kernels for 0% -> 0%
where the time goes in v17:
time: 81.7 us; the launch traced here: 80.9 us
  waiting for transfers between devices  45.5 us (56%)
  starting transfers between devices  17.7 us (22%)
  matrix products  8.16 us (10%)
  local copies, waits for them, and re-layouts  4.81 us (6%)
  other arithmetic  2.58 us (3%)
  between operations  2.12 us (3%)
    all_to_all x1, waiting for transfers between devices, body(): lax.all_to_all(both_pencil, 'scan', split_axis=0, concat_axis=1, tiled=True)  21.6 us
    all_to_all x1, waiting for transfers between devices, chunked_forward(): lax.all_to_all(outgoing, 'scan', split_axis=0, concat_axis=0, tiled=True)  21.1 us
    all_to_all x1, starting transfers between devices, body(): lax.all_to_all(both_pencil, 'scan', split_axis=0, concat_axis=1, tiled=True)  6.86 us
    all_to_all x1, starting transfers between devices, chunked_forward(): lax.all_to_all(outgoing, 'scan', split_axis=0, concat_axis=0, tiled=True)  6.32 us
    ppermute x1, starting transfers between devices, chunked_forward(): arrived = lax.ppermute(sent, 'row', [(0, 1), (1, 0)])  3 us
    ppermute x1, waiting for transfers between devices, blur_rows(): arrived = lax.ppermute(sent, axis, [(0, 1), (1, 0)])  2.67 us
    dot_general x2, matrix products, lateral_apply(): return jnp.einsum('rk,pkc->prc', band, padded, precision=highest_mode)  2.28 us
    dot_general x1, matrix products, chunked_forward(): jnp.einsum('karj,pjc->karpc', joint, stacked, precision=highest_mode)  2.21 us
  transfers between devices with their start and end apart: 4, of which 4 were waited for; matrix products, arithmetic and copies ran while one was open for 9% of the time, Pallas kernels for 0%

profile of v17, /device:TPU:0, one launch (start us, length us, event | category | flops | bytes accessed | tf_op | source)
XLA Modules:
  0.0 80.9 jit_solution(225944735529776637)
XLA Ops:
  0.6 0.9 %constant_dynamic-slice_fusion.1 = f32[8,8,512]{2,1,0:T(8,128)S(1)} fusion(f32[8,32,512]{2,1,0:T(8,128)} %param.7, s32[]{:T(128)S(6)} %select_n.44), kind=kLoop, calls=%fused_computation.62 | loop fusion | bytes 262148 | tf_op jit(solution)/shard_map/dynamic_slice | solution.py:32
  1.6 3.0 %collective-permute-start = (f32[8,8,512]{2,1,0:T(8,128)S(1)}, f32[8,8,512]{2,1,0:T(8,128)S(1)}, u32[]{:S(2)}, u32[]{:S(2)}) collective-permute-start(f32[8,8,512]{2,1,0:T(8,128)S(1)} %constant_dynamic-slice_fusion.1), channel_id=1, source_target_pairs={{0,1},{1,0},{2,3},{3,2},{4,5},{5,4},{6,7},{7,6},{8,9},{9,8},{10,11... | collective-permute-start | bytes 393224 | tf_op jit(solution)/shard_map/ppermute | solution.py:33
  4.6 0.8 select_reduce_fusion.1
  5.4 0.1 fusion.31
  5.4 0.1 slice.42
  5.5 0.1 copy.52
  5.6 0.1 pad_convert_fusion
  5.7 2.2 %fusion.4 = f32[16,2,2,8,512]{4,0,3,2,1:T(8,128)S(1)} fusion(f32[8,32,512]{2,1,0:T(8,128)} %param.8, f32[8,32,512]{2,1,0:T(8,128)} %param.7, f32[1,16,2,64]{3,1,2,0:T(8,128)S(1)} %copy.51, f32[1,16,2,64]{3,1,2,0:T(8,128)S(1)} %copy.50), kind=kOutput, calls=%fused_computation.10 | convolution fusion | flops 201592832 | bytes 2113536 | tf_op jit(solution)/shard_map/karj,pjc->karpc/dot_general | solution.py:42
  7.9 0.1 collective-permute-done
  8.1 1.0 %convolution_add_fusion = f32[16,2,2,8,512]{4,0,3,2,1:T(8,128)S(1)} fusion(f32[16,2,2,8,512]{4,0,3,2,1:T(8,128)S(1)} %fusion.4, f32[8,8,512]{2,1,0:T(8,128)S(1)} %collective-permute-done, f32[2,16,2,8]{1,3,2,0:T(8,128)S(1)} %copy.52), kind=kOutput, calls=%fused_computation.2 | convolution fusion | flops 25427968 | bytes 2230272 | tf_op jit(solution)/shard_map/karj,pjc->karpc/dot_general | solution.py:43
  9.1 1.6 %copy.53 = f32[16,2,2,8,512]{4,3,2,1,0:T(8,128)} copy(f32[16,2,2,8,512]{4,0,3,2,1:T(8,128)S(1)} %convolution_add_fusion) | data formatting | bytes 2097152 | tf_op jit(solution)/shard_map/add | solution.py:43
  10.7 0.0 copy-start.1
  10.7 0.0 copy-start.2
  10.7 6.3 %all-to-all-start = ((f32[16,2,2,8,512]{4,3,2,1,0:T(8,128)}), f32[16,2,2,8,512]{4,3,2,1,0:T(8,128)S(1)}, u32[]{:S(2)}, u32[]{:S(2)}) async-start(f32[16,2,2,8,512]{4,3,2,1,0:T(8,128)} %copy.53), calls=%async_computation | async-start | bytes 2097152 | tf_op jit(solution)/shard_map/all_to_all | solution.py:44
  17.0 0.0 copy-done.1
  17.0 0.1 subtract_subtract_fusion.1
  17.1 0.0 copy-done.2
  17.1 1.4 %select_reduce_fusion = f32[128,128]{1,0:T(8,128)S(1)} fusion(f32[64]{0:T(128)S(1)} %copy-done.2, s32[128,128]{1,0:T(8,128)S(1)} %subtract_subtract_fusion.1), kind=kLoop, calls=%fused_computation | loop fusion | flops 3129344 | bytes 131328 | tf_op jit(solution)/shard_map/reduce_sum | solution.py:75
  18.5 0.1 copy.49
  18.6 0.1 bitcast_select_fusion.2
  18.7 0.1 copy.47
  18.8 0.1 fusion.19
  18.9 21.1 %all-to-all-done = f32[16,2,2,8,512]{4,3,2,1,0:T(8,128)S(1)} async-done(((f32[16,2,2,8,512]{4,3,2,1,0:T(8,128)}), f32[16,2,2,8,512]{4,3,2,1,0:T(8,128)S(1)}, u32[]{:S(2)}, u32[]{:S(2)}) %all-to-all-start) | async-done | bytes 1048608 | tf_op jit(solution)/shard_map/all_to_all | solution.py:44
  39.9 0.1 fusion.39
  40.0 0.7 fusion.3
  40.7 0.2 copy.56
  40.9 2.0 %fusion.8 = f32[16,16,1024]{2,1,0:T(8,128)} fusion(f32[128,1024,1]{0,1,2:T(8,128)S(1)} %bitcast.84, f32[16,1,8,128]{3,2,0,1:T(8,128)S(1)} %bitcast.85, f32[16,1,8,128]{3,2,0,1:T(8,128)S(1)} %fusion.19), kind=kOutput, calls=%fused_computation.22 | convolution fusion | flops 402685952 | bytes 1703936 | tf_op jit(solution)/shard_map/dot_general | solution.py:106
  42.9 6.9 %all-to-all-start.1 = ((f32[16,16,1024]{2,1,0:T(8,128)}), f32[16,16,1024]{2,1,0:T(8,128)S(1)}, u32[]{:S(2)}, u32[]{:S(2)}) async-start(f32[16,16,1024]{2,1,0:T(8,128)} %fusion.8), calls=%async_computation.1 | async-start | bytes 2097152 | tf_op jit(solution)/shard_map/all_to_all | solution.py:107
  51.0 21.6 %all-to-all-done.1 = f32[16,16,1024]{2,1,0:T(8,128)S(1)} async-done(((f32[16,16,1024]{2,1,0:T(8,128)}), f32[16,16,1024]{2,1,0:T(8,128)S(1)}, u32[]{:S(2)}, u32[]{:S(2)}) %all-to-all-start.1) | async-done | bytes 1048608 | tf_op jit(solution)/shard_map/all_to_all | solution.py:107
  72.7 0.1 fusion.38
  72.8 0.3 copy.58
  73.1 0.1 reshape.131
  73.2 1.6 %collective-permute-start.1 = (f32[8,8,512]{2,1,0:T(8,128)S(1)}, f32[8,8,512]{2,1,0:T(8,128)S(1)}, u32[]{:S(2)}, u32[]{:S(2)}) collective-permute-start(f32[8,8,512]{2,1,0:T(8,128)S(1)} %constant_dynamic-slice_fusion), channel_id=1, source_target_pairs={{0,1},{1,0},{2,3},{3,2},{4,5},{5,4},{6,7},{7,6},{8,9},{9,8},{10,11... | collective-permute-start | bytes 393224 | tf_op jit(solution)/shard_map/ppermute | solution.py:16
  74.8 0.3 copy.60
  75.1 0.0 copy-start
  75.1 0.9 %reshape.132 = f32[8,32,512]{2,1,0:T(8,128)} reshape(f32[8,16,1024]{2,1,0:T(8,128)S(1)} %copy.60) | data formatting | bytes 1048576 | tf_op jit(solution)/shard_map/reshape | solution.py:114
  76.0 0.6 fusion.30
  76.6 2.7 %collective-permute-done.1 = f32[8,8,512]{2,1,0:T(8,128)S(1)} collective-permute-done((f32[8,8,512]{2,1,0:T(8,128)S(1)}, f32[8,8,512]{2,1,0:T(8,128)S(1)}, u32[]{:S(2)}, u32[]{:S(2)}) %collective-permute-start.1) | collective-permute-done | bytes 131104 | tf_op jit(solution)/shard_map/ppermute | solution.py:16
  79.3 0.0 copy-done
  79.3 1.6 %maximum_multiply_fusion = f32[8,32,512]{2,1,0:T(8,128)} fusion(f32[8,32,512]{2,1,0:T(8,128)S(1)} %copy-done, f32[8,512,32]{1,2,0:T(8,128)S(1)} %fusion.30, f32[8,8,512]{2,1,0:T(8,128)S(1)} %collective-permute-done.1, f32[]{:T(128)S(6)} %mul.18, f32[]{:T(128)} %bitcast.80, f32[32,48]{1,0:T(8,128)S(1)} %get-tuple-element.2, pred[]{:T(512)S(6)} %eq.64), kind=kOutput, calls=%fused_computation.15 | convolution fusion | flops 13631744 | bytes 1736713 | tf_op jit(solution)/shard_map/rk,pkc->prc/dot_general | solution.py:64
  (8 shorter events, 0.1 us)
Async XLA Ops:
  1.6 6.5 %collective-permute-start = (f32[8,8,512]{2,1,0:T(8,128)S(1)}, f32[8,8,512]{2,1,0:T(8,128)S(1)}, u32[]{:S(2)}, u32[]{:S(2)}) collective-permute-start(f32[8,8,512]{2,1,0:T(8,128)S(1)} %constant_dynamic-slice_fusion.1), channel_id=1, source_target_pairs={{0,1},{1,0},{2,3},{3,2},{4,5},{5,4},{6,7},{7,6},{8,9},{9,8},{10,11... | collective-permute-start | bytes 393224 | tf_op jit(solution)/shard_map/ppermute | solution.py:33
  10.7 6.3 %copy-start.1 = (s32[128]{0:T(128)S(1)}, s32[128]{0:T(128)}, u32[]{:S(2)}) copy-start(s32[128]{0:T(128)} %param.9) | copy-start | bytes 1540
  10.7 6.4 %copy-start.2 = (f32[64]{0:T(128)S(1)}, f32[64]{0:T(128)}, u32[]{:S(2)}) copy-start(f32[64]{0:T(128)} %param.10) | copy-start | bytes 772
  10.7 29.3 %all-to-all-start = ((f32[16,2,2,8,512]{4,3,2,1,0:T(8,128)}), f32[16,2,2,8,512]{4,3,2,1,0:T(8,128)S(1)}, u32[]{:S(2)}, u32[]{:S(2)}) async-start(f32[16,2,2,8,512]{4,3,2,1,0:T(8,128)} %copy.53), calls=%async_computation | async-start | bytes 2097152 | tf_op jit(solution)/shard_map/all_to_all | solution.py:44
  42.9 29.8 %all-to-all-start.1 = ((f32[16,16,1024]{2,1,0:T(8,128)}), f32[16,16,1024]{2,1,0:T(8,128)S(1)}, u32[]{:S(2)}, u32[]{:S(2)}) async-start(f32[16,16,1024]{2,1,0:T(8,128)} %fusion.8), calls=%async_computation.1 | async-start | bytes 2097152 | tf_op jit(solution)/shard_map/all_to_all | solution.py:107
  73.2 6.1 %collective-permute-start.1 = (f32[8,8,512]{2,1,0:T(8,128)S(1)}, f32[8,8,512]{2,1,0:T(8,128)S(1)}, u32[]{:S(2)}, u32[]{:S(2)}) collective-permute-start(f32[8,8,512]{2,1,0:T(8,128)S(1)} %constant_dynamic-slice_fusion), channel_id=1, source_target_pairs={{0,1},{1,0},{2,3},{3,2},{4,5},{5,4},{6,7},{7,6},{8,9},{9,8},{10,11... | collective-permute-start | bytes 393224 | tf_op jit(solution)/shard_map/ppermute | solution.py:16
  75.1 4.2 %copy-start = (f32[8,32,512]{2,1,0:T(8,128)S(1)}, f32[8,32,512]{2,1,0:T(8,128)}, u32[]{:S(2)}) copy-start(f32[8,32,512]{2,1,0:T(8,128)} %param.7) | copy-start | bytes 1572868

commit v18 on v16

--- a/solution.py
+++ b/solution.py
@@ -24,6 +24,19 @@
     below = lax.ppermute(head, axis, [((i + 1) % count, i) for i in range(ends)])
     summed = summed + lateral_apply(band[:, :width], above, precision)
     return summed + lateral_apply(band[:, width + rows :], below, precision)
+
+
+def chunked_gradient(band, chunks, width):
+    chunk_count, plane_count, per_chunk, columns = chunks.shape
+    rows = chunk_count * per_chunk
+    halo_chunks = width // per_chunk
+    first = lax.axis_index("row") == 0
+    own = band[:, width : width + rows].reshape(rows, chunk_count, per_chunk)
+    summed = jnp.einsum("rkj,kpjc->prc", own, chunks, precision=high_mode)
+    sent = lax.dynamic_slice_in_dim(chunks, jnp.where(first, chunk_count - halo_chunks, 0), halo_chunks, axis=0)
+    arrived = lax.ppermute(sent, "row", [(0, 1), (1, 0)])
+    edge = jnp.where(first, band[:, width + rows :], band[:, :width]).reshape(rows, halo_chunks, per_chunk)
+    return summed + jnp.einsum("rkj,kpjc->prc", edge, arrived, precision=high_mode)
 
 
 def band_matrix(kernel_taps, row_count, flip):
@@ -77,10 +90,17 @@
     spread = sheet_psf.T.reshape(scan_count, 1, plane_count, all_planes)
     joint = jnp.concatenate([keep, spread], axis=1).reshape(2 * all_planes, all_planes)
     both_pencil = jnp.dot(joint, misfit_pencil, precision=high_mode)
-    both_out = lax.all_to_all(both_pencil, "scan", split_axis=0, concat_axis=1, tiled=True)
-    misfit = both_out[:plane_count]
-    back_volume = both_out[plane_count:].reshape(plane_count, row_count, width_count)
-    gradient = blur_rows(back_band, back_volume, "row", halo_rows, high_mode)
+    if row_count % scan_count == 0 and lax.axis_size("row") == 2:
+        per_chunk = row_count // scan_count
+        incoming = lax.all_to_all(both_pencil.reshape(scan_count, 2 * plane_count, -1), "scan", split_axis=0, concat_axis=0, tiled=True)
+        misfit = incoming[:, :plane_count].transpose(1, 0, 2).reshape(plane_count, flat_count)
+        back_chunks = incoming[:, plane_count:].reshape(scan_count, plane_count, per_chunk, width_count)
+        gradient = chunked_gradient(back_band, back_chunks, halo_rows)
+    else:
+        both_out = lax.all_to_all(both_pencil, "scan", split_axis=0, concat_axis=1, tiled=True)
+        misfit = both_out[:plane_count]
+        back_volume = both_out[plane_count:].reshape(plane_count, row_count, width_count)
+        gradient = blur_rows(back_band, back_volume, "row", halo_rows, high_mode)
     stepped = estimate - step_size[0] * gradient
     shrink_level = step_size[0] * threshold[0]
     new_estimate = jnp.sign(stepped) * jnp.maximum(jnp.abs(stepped) - shrink_level, 0.0)

time: 80.8 us -> 80.7 us (level)
    ppermute x2 -> x1, waiting for transfers between devices: 4.38 us -> 1.48 us  [blur_rows(): arrived = lax.ppermute(sent, axis, [(0, 1), (1, 0)])]
    ppermute x0 -> x1, waiting for transfers between devices: none -> 2.67 us  [chunked_gradient(): arrived = lax.ppermute(sent, 'row', [(0, 1), (1, 0)])]
    dot_general x0 -> x2, matrix products: none -> 2.09 us  [the longest x1 1.44 us: chunked_gradient(): jnp.einsum('rkj,kpjc->prc', edge, arrived, precision=high_mode)]
    dot_general x4 -> x2, matrix products: 3.1 us -> 1.26 us  [lateral_apply(): return jnp.einsum('rk,pkc->prc', band, padded, precision=precision)]
    ppermute x0 -> x1, starting transfers between devices: none -> 1.56 us  [chunked_gradient(): arrived = lax.ppermute(sent, 'row', [(0, 1), (1, 0)])]
    ppermute x2 -> x1, starting transfers between devices: 4.56 us -> 3 us  [blur_rows(): arrived = lax.ppermute(sent, axis, [(0, 1), (1, 0)])]
    another operation x0 -> x1, local copies, waits for them, and re-layouts: none -> 0.87 us  [body(): return (new_estimate, misfit.reshape(plane_count, row_count, width_count))]
where the time goes in v18:
time: 80.7 us; the launch traced here: 79.9 us
  waiting for transfers between devices  46.7 us (58%)
  starting transfers between devices  17.8 us (22%)
  local copies, waits for them, and re-layouts  5.86 us (7%)
  matrix products  5.52 us (7%)
  between operations  2.15 us (3%)
  other arithmetic  1.87 us (2%)
    all_to_all x1, waiting for transfers between devices, body(): lax.all_to_all(both_pencil.reshape(scan_count, 2 * plane_count, -1), 'sca...  21.3 us
    all_to_all x1, waiting for transfers between devices, body(): lax.all_to_all(both_flat, 'scan', split_axis=1, concat_axis=0, tiled=True)  21.2 us
    all_to_all x1, starting transfers between devices, body(): lax.all_to_all(both_pencil.reshape(scan_count, 2 * plane_count, -1), 'sca...  6.87 us
    all_to_all x1, starting transfers between devices, body(): lax.all_to_all(both_flat, 'scan', split_axis=1, concat_axis=0, tiled=True)  6.33 us
    ppermute x1, starting transfers between devices, blur_rows(): arrived = lax.ppermute(sent, axis, [(0, 1), (1, 0)])  3 us
    concatenate x3, local copies, waits for them, and re-layouts, body(): jnp.concatenate([blurred, raw.reshape(plane_count, flat_count)], axis=0)  2.96 us
    ppermute x1, waiting for transfers between devices, chunked_gradient(): arrived = lax.ppermute(sent, 'row', [(0, 1), (1, 0)])  2.67 us
  transfers between devices with their start and end apart: 4, of which 4 were waited for; matrix products, arithmetic and copies ran while one was open for 7% of the time, Pallas kernels for 0%

profile of v18, /device:TPU:0, one launch (start us, length us, event | category | flops | bytes accessed | tf_op | source)
XLA Modules:
  0.0 79.9 jit_solution(2492155858614120982)
XLA Ops:
  0.6 0.0 copy-start
  0.6 0.0 copy-start.2
  0.7 1.0 %constant_dynamic-slice_fusion.1 = f32[8,8,512]{2,1,0:T(8,128)S(1)} fusion(f32[8,32,512]{2,1,0:T(8,128)} %param.7, s32[]{:T(128)S(6)} %select_n.43), kind=kLoop, calls=%fused_computation.57 | loop fusion | bytes 262148 | tf_op jit(solution)/shard_map/dynamic_slice | solution.py:16
  1.6 3.0 %collective-permute-start = (f32[8,8,512]{2,1,0:T(8,128)S(1)}, f32[8,8,512]{2,1,0:T(8,128)S(1)}, u32[]{:S(2)}, u32[]{:S(2)}) collective-permute-start(f32[8,8,512]{2,1,0:T(8,128)S(1)} %constant_dynamic-slice_fusion.1), channel_id=1, source_target_pairs={{0,1},{1,0},{2,3},{3,2},{4,5},{5,4},{6,7},{7,6},{8,9},{9,8},{10,11... | collective-permute-start | bytes 393224 | tf_op jit(solution)/shard_map/ppermute | solution.py:17
  4.6 1.2 %concatenate.13 = f32[8,16,1024]{2,1,0:T(8,128)S(1)} reshape(f32[8,32,512]{2,1,0:T(8,128)} %param.8) | data formatting | bytes 1048576 | tf_op jit(solution)/shard_map/concatenate | solution.py:80
  5.9 0.0 copy-done.2
  5.9 0.1 select_reduce_fusion.2
  6.0 0.0 copy-done
  6.0 0.6 convolution_bitcast_fusion.3
  6.7 1.5 %collective-permute-done = f32[8,8,512]{2,1,0:T(8,128)S(1)} collective-permute-done((f32[8,8,512]{2,1,0:T(8,128)S(1)}, f32[8,8,512]{2,1,0:T(8,128)S(1)}, u32[]{:S(2)}, u32[]{:S(2)}) %collective-permute-start) | collective-permute-done | bytes 131104 | tf_op jit(solution)/shard_map/ppermute | solution.py:17
  8.1 0.6 fusion
  8.8 0.2 concatenate.12
  9.0 0.1 pad_maximum_fusion
  9.1 1.6 %copy.58 = f32[16,16,1024]{2,0,1:T(8,128)} copy(f32[16,16,1024]{2,1,0:T(8,128)S(1)} %pad_maximum_fusion) | data formatting | bytes 2097152 | tf_op jit(solution)/shard_map/concatenate | solution.py:80
  10.6 0.0 copy-start.1
  10.6 0.0 copy-start.3
  10.7 6.3 %all-to-all-start = ((f32[16,16,1024]{2,0,1:T(8,128)}), f32[16,16,1024]{2,0,1:T(8,128)S(1)}, u32[]{:S(2)}, u32[]{:S(2)}) async-start(f32[16,16,1024]{2,0,1:T(8,128)} %copy.58), calls=%async_computation | async-start | bytes 2097152 | tf_op jit(solution)/shard_map/all_to_all | solution.py:81
  17.0 0.0 copy-done.1
  17.0 0.1 subtract_subtract_fusion
  17.1 0.0 copy-done.3
  17.1 1.4 %select_reduce_fusion = f32[128,128]{1,0:T(8,128)S(1)} fusion(f32[64]{0:T(128)S(1)} %copy-done.3, s32[128,128]{1,0:T(8,128)S(1)} %subtract_subtract_fusion), kind=kLoop, calls=%fused_computation | loop fusion | flops 3129344 | bytes 131328 | tf_op jit(solution)/shard_map/reduce_sum | solution.py:65
  18.5 0.1 copy.55
  18.6 0.1 fusion.14
  18.7 21.2 %all-to-all-done = f32[16,16,1024]{2,0,1:T(8,128)S(1)} async-done(((f32[16,16,1024]{2,0,1:T(8,128)}), f32[16,16,1024]{2,0,1:T(8,128)S(1)}, u32[]{:S(2)}, u32[]{:S(2)}) %all-to-all-start) | async-done | bytes 1048608 | tf_op jit(solution)/shard_map/all_to_all | solution.py:81
  39.9 0.6 fusion.1
  40.6 1.5 %fusion.6 = f32[16,16,1024]{2,1,0:T(8,128)} fusion(f32[128,1024,1]{1,0,2:T(8,128)S(1)} %fusion.1, f32[16,1,8,128]{3,2,1,0:T(8,128)S(1)} %fusion.9, f32[16,1,8,128]{3,2,1,0:T(8,128)S(1)} %fusion.14), kind=kOutput, calls=%fused_computation.23 | convolution fusion | flops 201359360 | bytes 1703936 | tf_op jit(solution)/shard_map/dot_general | solution.py:92
  42.1 6.9 %all-to-all-start.1 = ((f32[16,16,1024]{2,1,0:T(8,128)}), f32[16,16,1024]{2,1,0:T(8,128)S(1)}, u32[]{:S(2)}, u32[]{:S(2)}) async-start(f32[16,16,1024]{2,1,0:T(8,128)} %fusion.6), calls=%async_computation.1 | async-start | bytes 2097152 | tf_op jit(solution)/shard_map/all_to_all | solution.py:95
  49.0 0.1 slice.46
  49.1 0.1 copy.59
  49.1 0.1 slice_select_fusion
  49.2 0.1 copy.63
  50.6 21.3 %all-to-all-done.1 = f32[16,16,1024]{2,1,0:T(8,128)S(1)} async-done(((f32[16,16,1024]{2,1,0:T(8,128)}), f32[16,16,1024]{2,1,0:T(8,128)S(1)}, u32[]{:S(2)}, u32[]{:S(2)}) %all-to-all-start.1) | async-done | bytes 1048608 | tf_op jit(solution)/shard_map/all_to_all | solution.py:95
  71.9 0.1 slice_bitcast_fusion
  72.0 0.3 copy.60
  72.4 1.6 %collective-permute-start.1 = (f32[4,8,2,512]{3,0,2,1:T(4,128)S(1)}, f32[4,8,2,512]{3,0,2,1:T(4,128)S(1)}, u32[]{:S(2)}, u32[]{:S(2)}) collective-permute-start(f32[4,8,2,512]{3,0,2,1:T(4,128)S(1)} %constant_dynamic-slice_fusion), channel_id=1, source_target_pairs={{0,1},{1,0},{2,3},{3,2},{4,5},{5,4},{6,7},{7,6},{8,9},{9,8},{10,11... | collective-permute-start | bytes 393224 | tf_op jit(solution)/shard_map/ppermute | solution.py:37
  73.9 0.3 copy.65
  74.2 0.9 %reshape_reshape.3 = f32[8,32,512]{2,1,0:T(8,128)} reshape(f32[8,16,1024]{2,1,0:T(8,128)S(1)} %copy.65) | data formatting | bytes 1048576 | tf_op jit(solution)/shard_map/reshape;reshape | solution.py:107
  75.1 0.7 convolution_bitcast_fusion.1
  75.8 2.7 %collective-permute-done.1 = f32[4,8,2,512]{3,0,2,1:T(4,128)S(1)} collective-permute-done((f32[4,8,2,512]{3,0,2,1:T(4,128)S(1)}, f32[4,8,2,512]{3,0,2,1:T(4,128)S(1)}, u32[]{:S(2)}, u32[]{:S(2)}) %collective-permute-start.1) | collective-permute-done | bytes 131104 | tf_op jit(solution)/shard_map/ppermute | solution.py:37
  78.4 1.4 %maximum_multiply_fusion = f32[8,32,512]{2,1,0:T(8,128)} fusion(f32[8,32,512]{2,1,0:T(8,128)S(1)} %copy-done, f32[8,512,32]{1,2,0:T(8,128)S(1)} %convolution_bitcast_fusion.1, f32[4,8,2,512]{3,0,2,1:T(4,128)S(1)} %collective-permute-done.1, f32[]{:T(128)S(6)} %mul.18, f32[]{:T(128)} %bitcast.74, f32[32,4,2]{0,2,1:T(2,128)S(1)} %bitcast.81), kind=kOutput, calls=%fused_computation.17 | convolution fusion | flops 7340032 | bytes 1704968 | tf_op jit(solution)/shard_map/rkj,kpjc->prc/dot_general | solution.py:39
  (4 shorter events, 0.1 us)
Async XLA Ops:
  0.6 5.4 %copy-start = (f32[8,32,512]{2,1,0:T(8,128)S(1)}, f32[8,32,512]{2,1,0:T(8,128)}, u32[]{:S(2)}) copy-start(f32[8,32,512]{2,1,0:T(8,128)} %param.7) | copy-start | bytes 1572868
  0.6 5.2 %copy-start.2 = (f32[17]{0:T(128)S(1)}, f32[17]{0:T(128)}, u32[]{:S(2)}) copy-start(f32[17]{0:T(128)} %param.11) | copy-start | bytes 208
  1.6 6.5 %collective-permute-start = (f32[8,8,512]{2,1,0:T(8,128)S(1)}, f32[8,8,512]{2,1,0:T(8,128)S(1)}, u32[]{:S(2)}, u32[]{:S(2)}) collective-permute-start(f32[8,8,512]{2,1,0:T(8,128)S(1)} %constant_dynamic-slice_fusion.1), channel_id=1, source_target_pairs={{0,1},{1,0},{2,3},{3,2},{4,5},{5,4},{6,7},{7,6},{8,9},{9,8},{10,11... | collective-permute-start | bytes 393224 | tf_op jit(solution)/shard_map/ppermute | solution.py:17
  10.6 6.3 %copy-start.1 = (s32[128]{0:T(128)S(1)}, s32[128]{0:T(128)}, u32[]{:S(2)}) copy-start(s32[128]{0:T(128)} %param.9) | copy-start | bytes 1540
  10.6 6.4 %copy-start.3 = (f32[64]{0:T(128)S(1)}, f32[64]{0:T(128)}, u32[]{:S(2)}) copy-start(f32[64]{0:T(128)} %param.10) | copy-start | bytes 772
  10.7 29.3 %all-to-all-start = ((f32[16,16,1024]{2,0,1:T(8,128)}), f32[16,16,1024]{2,0,1:T(8,128)S(1)}, u32[]{:S(2)}, u32[]{:S(2)}) async-start(f32[16,16,1024]{2,0,1:T(8,128)} %copy.58), calls=%async_computation | async-start | bytes 2097152 | tf_op jit(solution)/shard_map/all_to_all | solution.py:81
  42.1 29.8 %all-to-all-start.1 = ((f32[16,16,1024]{2,1,0:T(8,128)}), f32[16,16,1024]{2,1,0:T(8,128)S(1)}, u32[]{:S(2)}, u32[]{:S(2)}) async-start(f32[16,16,1024]{2,1,0:T(8,128)} %fusion.6), calls=%async_computation.1 | async-start | bytes 2097152 | tf_op jit(solution)/shard_map/all_to_all | solution.py:95
  72.4 6.1 %collective-permute-start.1 = (f32[4,8,2,512]{3,0,2,1:T(4,128)S(1)}, f32[4,8,2,512]{3,0,2,1:T(4,128)S(1)}, u32[]{:S(2)}, u32[]{:S(2)}) collective-permute-start(f32[4,8,2,512]{3,0,2,1:T(4,128)S(1)} %constant_dynamic-slice_fusion), channel_id=1, source_target_pairs={{0,1},{1,0},{2,3},{3,2},{4,5},{5,4},{6,7},{7,6},{8,9},{9,8},{10,11... | collective-permute-start | bytes 393224 | tf_op jit(solution)/shard_map/ppermute | solution.py:37

commit v19 on v16

--- a/solution.py
+++ b/solution.py
@@ -80,10 +80,30 @@
     both_out = lax.all_to_all(both_pencil, "scan", split_axis=0, concat_axis=1, tiled=True)
     misfit = both_out[:plane_count]
     back_volume = both_out[plane_count:].reshape(plane_count, row_count, width_count)
-    gradient = blur_rows(back_band, back_volume, "row", halo_rows, high_mode)
-    stepped = estimate - step_size[0] * gradient
     shrink_level = step_size[0] * threshold[0]
-    new_estimate = jnp.sign(stepped) * jnp.maximum(jnp.abs(stepped) - shrink_level, 0.0)
+
+    def shrink(values):
+        return jnp.sign(values) * jnp.maximum(jnp.abs(values) - shrink_level, 0.0)
+
+    if lax.axis_size("row") == 2:
+        first = lax.axis_index("row") == 0
+        edge_start = jnp.where(first, row_count - halo_rows, 0)
+        sent = lax.dynamic_slice_in_dim(back_volume, edge_start, halo_rows, axis=1)
+        arrived = lax.ppermute(sent, "row", [(0, 1), (1, 0)])
+        own = lateral_apply(back_band[:, halo_rows : halo_rows + row_count], back_volume, high_mode)
+        stepped = estimate - step_size[0] * own
+        finished = shrink(stepped)
+        edge = jnp.where(
+            first,
+            back_band[row_count - halo_rows :, halo_rows + row_count :],
+            back_band[:halo_rows, :halo_rows],
+        )
+        edge_rows = lax.dynamic_slice_in_dim(stepped, edge_start, halo_rows, axis=1)
+        edge_rows = edge_rows - step_size[0] * lateral_apply(edge, arrived, high_mode)
+        new_estimate = lax.dynamic_update_slice_in_dim(finished, shrink(edge_rows), edge_start, axis=1)
+    else:
+        gradient = blur_rows(back_band, back_volume, "row", halo_rows, high_mode)
+        new_estimate = shrink(estimate - step_size[0] * gradient)
     return (new_estimate, misfit.reshape(plane_count, row_count, width_count))
 
 

time: 80.8 us -> 80.5 us (level)
  matrix products: 5.29 us -> 4.38 us
    ppermute x2 -> x1, waiting for transfers between devices: 4.38 us -> 1.48 us  [blur_rows(): arrived = lax.ppermute(sent, axis, [(0, 1), (1, 0)])]
    ppermute x0 -> x1, waiting for transfers between devices: none -> 2.71 us  [body(): arrived = lax.ppermute(sent, 'row', [(0, 1), (1, 0)])]
    ppermute x0 -> x1, starting transfers between devices: none -> 1.56 us  [body(): arrived = lax.ppermute(sent, 'row', [(0, 1), (1, 0)])]
    ppermute x2 -> x1, starting transfers between devices: 4.56 us -> 3 us  [blur_rows(): arrived = lax.ppermute(sent, axis, [(0, 1), (1, 0)])]
    dot_general x4, matrix products: 3.1 us -> 2.18 us  [lateral_apply(): return jnp.einsum('rk,pkc->prc', band, padded, precision=precision)]
where the time goes in v19:
time: 80.5 us; the launch traced here: 79.7 us
  waiting for transfers between devices  47.1 us (59%)
  starting transfers between devices  17.8 us (22%)
  local copies, waits for them, and re-layouts  6.51 us (8%)
  matrix products  4.38 us (5%)
  between operations  2.15 us (3%)
  other arithmetic  1.8 us (2%)
    all_to_all x1, waiting for transfers between devices, body(): lax.all_to_all(both_pencil, 'scan', split_axis=0, concat_axis=1, tiled=True)  21.6 us
    all_to_all x1, waiting for transfers between devices, body(): lax.all_to_all(both_flat, 'scan', split_axis=1, concat_axis=0, tiled=True)  21.2 us
    all_to_all x1, starting transfers between devices, body(): lax.all_to_all(both_pencil, 'scan', split_axis=0, concat_axis=1, tiled=True)  6.86 us
    all_to_all x1, starting transfers between devices, body(): lax.all_to_all(both_flat, 'scan', split_axis=1, concat_axis=0, tiled=True)  6.33 us
    ppermute x1, starting transfers between devices, blur_rows(): arrived = lax.ppermute(sent, axis, [(0, 1), (1, 0)])  3 us
    concatenate x3, local copies, waits for them, and re-layouts, body(): jnp.concatenate([blurred, raw.reshape(plane_count, flat_count)], axis=0)  2.97 us
    ppermute x1, waiting for transfers between devices, body(): arrived = lax.ppermute(sent, 'row', [(0, 1), (1, 0)])  2.71 us
    dot_general x4, matrix products, lateral_apply(): return jnp.einsum('rk,pkc->prc', band, padded, precision=precision)  2.18 us
  transfers between devices with their start and end apart: 4, of which 4 were waited for; matrix products, arithmetic and copies ran while one was open for 7% of the time, Pallas kernels for 0%

profile of v19, /device:TPU:0, one launch (start us, length us, event | category | flops | bytes accessed | tf_op | source)
XLA Modules:
  0.0 79.7 jit_solution(753771658587223566)
XLA Ops:
  0.6 0.0 copy-start
  0.6 0.0 copy-start.3
  0.7 1.0 %constant_dynamic-slice_fusion.1 = f32[8,8,512]{2,1,0:T(8,128)S(1)} fusion(f32[8,32,512]{2,1,0:T(8,128)} %param.7, s32[]{:T(128)S(6)} %select_n.47), kind=kLoop, calls=%fused_computation.57 | loop fusion | bytes 262148 | tf_op jit(solution)/shard_map/dynamic_slice | solution.py:16
  1.6 3.0 %collective-permute-start = (f32[8,8,512]{2,1,0:T(8,128)S(1)}, f32[8,8,512]{2,1,0:T(8,128)S(1)}, u32[]{:S(2)}, u32[]{:S(2)}) collective-permute-start(f32[8,8,512]{2,1,0:T(8,128)S(1)} %constant_dynamic-slice_fusion.1), channel_id=1, source_target_pairs={{0,1},{1,0},{2,3},{3,2},{4,5},{5,4},{6,7},{7,6},{8,9},{9,8},{10,11... | collective-permute-start | bytes 393224 | tf_op jit(solution)/shard_map/ppermute | solution.py:17
  4.6 1.2 %concatenate.13 = f32[8,16,1024]{2,1,0:T(8,128)S(1)} reshape(f32[8,32,512]{2,1,0:T(8,128)} %param.8) | data formatting | bytes 1048576 | tf_op jit(solution)/shard_map/concatenate | solution.py:67
  5.9 0.0 copy-done.3
  5.9 0.1 select_reduce_fusion.1
  6.0 0.0 copy-done
  6.0 0.6 convolution_bitcast_fusion.1
  6.7 1.5 %collective-permute-done = f32[8,8,512]{2,1,0:T(8,128)S(1)} collective-permute-done((f32[8,8,512]{2,1,0:T(8,128)S(1)}, f32[8,8,512]{2,1,0:T(8,128)S(1)}, u32[]{:S(2)}, u32[]{:S(2)}) %collective-permute-start) | collective-permute-done | bytes 131104 | tf_op jit(solution)/shard_map/ppermute | solution.py:17
  8.1 0.6 fusion
  8.8 0.2 concatenate.12
  9.0 0.1 pad_maximum_fusion
  9.1 1.6 %copy.34 = f32[16,16,1024]{2,0,1:T(8,128)} copy(f32[16,16,1024]{2,1,0:T(8,128)S(1)} %pad_maximum_fusion) | data formatting | bytes 2097152 | tf_op jit(solution)/shard_map/concatenate | solution.py:67
  10.7 0.0 copy-start.2
  10.7 0.0 copy-start.4
  10.7 6.3 %all-to-all-start = ((f32[16,16,1024]{2,0,1:T(8,128)}), f32[16,16,1024]{2,0,1:T(8,128)S(1)}, u32[]{:S(2)}, u32[]{:S(2)}) async-start(f32[16,16,1024]{2,0,1:T(8,128)} %copy.34), calls=%async_computation | async-start | bytes 2097152 | tf_op jit(solution)/shard_map/all_to_all | solution.py:68
  17.0 0.0 copy-done.2
  17.0 0.1 subtract_subtract_fusion
  17.1 0.0 copy-done.4
  17.1 1.4 %select_reduce_fusion = f32[128,128]{1,0:T(8,128)S(1)} fusion(f32[64]{0:T(128)S(1)} %copy-done.4, s32[128,128]{1,0:T(8,128)S(1)} %subtract_subtract_fusion), kind=kLoop, calls=%fused_computation | loop fusion | flops 3129344 | bytes 131328 | tf_op jit(solution)/shard_map/reduce_sum | solution.py:52
  18.5 0.1 copy.31
  18.6 0.1 fusion.14
  18.7 21.2 %all-to-all-done = f32[16,16,1024]{2,0,1:T(8,128)S(1)} async-done(((f32[16,16,1024]{2,0,1:T(8,128)}), f32[16,16,1024]{2,0,1:T(8,128)S(1)}, u32[]{:S(2)}, u32[]{:S(2)}) %all-to-all-start) | async-done | bytes 1048608 | tf_op jit(solution)/shard_map/all_to_all | solution.py:68
  39.9 0.6 fusion.3
  40.6 1.6 %fusion.6 = f32[16,16,1024]{2,1,0:T(8,128)} fusion(f32[128,1024,1]{1,0,2:T(8,128)S(1)} %fusion.3, f32[16,1,8,128]{3,2,1,0:T(8,128)S(1)} %fusion.9, f32[16,1,8,128]{3,2,1,0:T(8,128)S(1)} %fusion.14), kind=kOutput, calls=%fused_computation.22 | convolution fusion | flops 201359360 | bytes 1703936 | tf_op jit(solution)/shard_map/dot_general | solution.py:79
  42.1 6.9 %all-to-all-start.1 = ((f32[16,16,1024]{2,1,0:T(8,128)}), f32[16,16,1024]{2,1,0:T(8,128)S(1)}, u32[]{:S(2)}, u32[]{:S(2)}) async-start(f32[16,16,1024]{2,1,0:T(8,128)} %fusion.6), calls=%async_computation.1 | async-start | bytes 2097152 | tf_op jit(solution)/shard_map/all_to_all | solution.py:80
  50.3 21.6 %all-to-all-done.1 = f32[16,16,1024]{2,1,0:T(8,128)S(1)} async-done(((f32[16,16,1024]{2,1,0:T(8,128)}), f32[16,16,1024]{2,1,0:T(8,128)S(1)}, u32[]{:S(2)}, u32[]{:S(2)}) %all-to-all-start.1) | async-done | bytes 1048608 | tf_op jit(solution)/shard_map/all_to_all | solution.py:80
  72.0 0.1 fusion.33
  72.1 0.3 copy.35
  72.4 0.1 reshape.109
  72.5 1.6 %collective-permute-start.1 = (f32[8,8,512]{2,1,0:T(8,128)S(1)}, f32[8,8,512]{2,1,0:T(8,128)S(1)}, u32[]{:S(2)}, u32[]{:S(2)}) collective-permute-start(f32[8,8,512]{2,1,0:T(8,128)S(1)} %constant_dynamic-slice_fusion), channel_id=1, source_target_pairs={{0,1},{1,0},{2,3},{3,2},{4,5},{5,4},{6,7},{7,6},{8,9},{9,8},{10,11... | collective-permute-start | bytes 393224 | tf_op jit(solution)/shard_map/ppermute | solution.py:92
  74.0 0.6 maximum_multiply_fusion
  74.7 0.3 copy.36
  75.0 0.9 %reshape.110 = f32[8,32,512]{2,1,0:T(8,128)} reshape(f32[8,16,1024]{2,1,0:T(8,128)S(1)} %copy.36) | data formatting | bytes 1048576 | tf_op jit(solution)/shard_map/reshape | solution.py:107
  75.8 2.7 %collective-permute-done.1 = f32[8,8,512]{2,1,0:T(8,128)S(1)} collective-permute-done((f32[8,8,512]{2,1,0:T(8,128)S(1)}, f32[8,8,512]{2,1,0:T(8,128)S(1)}, u32[]{:S(2)}, u32[]{:S(2)}) %collective-permute-start.1) | collective-permute-done | bytes 131104 | tf_op jit(solution)/shard_map/ppermute | solution.py:92
  78.6 0.3 multiply_dynamic-update-slice_fusion
  78.9 0.0 copy-start.1
  78.9 0.8 copy-done.1
  (4 shorter events, 0.1 us)
Async XLA Ops:
  0.6 5.4 %copy-start = (f32[8,32,512]{2,1,0:T(8,128)S(1)}, f32[8,32,512]{2,1,0:T(8,128)}, u32[]{:S(2)}) copy-start(f32[8,32,512]{2,1,0:T(8,128)} %param.7) | copy-start | bytes 1572868
  0.6 5.2 %copy-start.3 = (f32[17]{0:T(128)S(1)}, f32[17]{0:T(128)}, u32[]{:S(2)}) copy-start(f32[17]{0:T(128)} %param.11) | copy-start | bytes 208
  1.6 6.5 %collective-permute-start = (f32[8,8,512]{2,1,0:T(8,128)S(1)}, f32[8,8,512]{2,1,0:T(8,128)S(1)}, u32[]{:S(2)}, u32[]{:S(2)}) collective-permute-start(f32[8,8,512]{2,1,0:T(8,128)S(1)} %constant_dynamic-slice_fusion.1), channel_id=1, source_target_pairs={{0,1},{1,0},{2,3},{3,2},{4,5},{5,4},{6,7},{7,6},{8,9},{9,8},{10,11... | collective-permute-start | bytes 393224 | tf_op jit(solution)/shard_map/ppermute | solution.py:17
  10.7 6.3 %copy-start.2 = (s32[128]{0:T(128)S(1)}, s32[128]{0:T(128)}, u32[]{:S(2)}) copy-start(s32[128]{0:T(128)} %param.9) | copy-start | bytes 1540
  10.7 6.4 %copy-start.4 = (f32[64]{0:T(128)S(1)}, f32[64]{0:T(128)}, u32[]{:S(2)}) copy-start(f32[64]{0:T(128)} %param.10) | copy-start | bytes 772
  10.7 29.3 %all-to-all-start = ((f32[16,16,1024]{2,0,1:T(8,128)}), f32[16,16,1024]{2,0,1:T(8,128)S(1)}, u32[]{:S(2)}, u32[]{:S(2)}) async-start(f32[16,16,1024]{2,0,1:T(8,128)} %copy.34), calls=%async_computation | async-start | bytes 2097152 | tf_op jit(solution)/shard_map/all_to_all | solution.py:68
  42.1 29.8 %all-to-all-start.1 = ((f32[16,16,1024]{2,1,0:T(8,128)}), f32[16,16,1024]{2,1,0:T(8,128)S(1)}, u32[]{:S(2)}, u32[]{:S(2)}) async-start(f32[16,16,1024]{2,1,0:T(8,128)} %fusion.6), calls=%async_computation.1 | async-start | bytes 2097152 | tf_op jit(solution)/shard_map/all_to_all | solution.py:80
  72.5 6.1 %collective-permute-start.1 = (f32[8,8,512]{2,1,0:T(8,128)S(1)}, f32[8,8,512]{2,1,0:T(8,128)S(1)}, u32[]{:S(2)}, u32[]{:S(2)}) collective-permute-start(f32[8,8,512]{2,1,0:T(8,128)S(1)} %constant_dynamic-slice_fusion), channel_id=1, source_target_pairs={{0,1},{1,0},{2,3},{3,2},{4,5},{5,4},{6,7},{7,6},{8,9},{9,8},{10,11... | collective-permute-start | bytes 393224 | tf_op jit(solution)/shard_map/ppermute | solution.py:92
  78.9 0.8 copy-start.1

commit v20 on v19

--- a/solution.py
+++ b/solution.py
@@ -98,9 +98,11 @@
             back_band[row_count - halo_rows :, halo_rows + row_count :],
             back_band[:halo_rows, :halo_rows],
         )
-        edge_rows = lax.dynamic_slice_in_dim(stepped, edge_start, halo_rows, axis=1)
-        edge_rows = edge_rows - step_size[0] * lateral_apply(edge, arrived, high_mode)
-        new_estimate = lax.dynamic_update_slice_in_dim(finished, shrink(edge_rows), edge_start, axis=1)
+        edge_part = lateral_apply(edge, arrived, high_mode)
+        edge_full = lax.dynamic_update_slice_in_dim(jnp.zeros_like(stepped), edge_part, edge_start, axis=1)
+        row_ids = jnp.arange(row_count, dtype=jnp.int32)[None, :, None]
+        at_edge = (row_ids >= edge_start) & (row_ids < edge_start + halo_rows)
+        new_estimate = jnp.where(at_edge, shrink(stepped - step_size[0] * edge_full), finished)
     else:
         gradient = blur_rows(back_band, back_volume, "row", halo_rows, high_mode)
         new_estimate = shrink(estimate - step_size[0] * gradient)

time: 80.5 us -> 81.7 us (1.015)
  blocking collectives: 0 us -> 31.5 us
  waiting for transfers between devices: 47.1 us -> 24.9 us
  starting transfers between devices: 17.8 us -> 10.9 us
    all_to_all x0 -> x1, blocking collectives: none -> 31.5 us  [body(): lax.all_to_all(both_pencil, 'scan', split_axis=0, concat_axis=1, tiled=True)]
    all_to_all x1 -> x0, waiting for transfers between devices: 21.6 us -> none  [body(): lax.all_to_all(both_pencil, 'scan', split_axis=0, concat_axis=1, tiled=True)]
    all_to_all x1 -> x0, starting transfers between devices: 6.86 us -> none  [body(): lax.all_to_all(both_pencil, 'scan', split_axis=0, concat_axis=1, tiled=True)]
    dot_general x4, matrix products: 2.18 us -> 3.18 us  [lateral_apply(): return jnp.einsum('rk,pkc->prc', band, padded, precision=precision)]
    dot_general x1, matrix products: 1.56 us -> 0.58 us  [body(): both_pencil = jnp.dot(joint, misfit_pencil, precision=high_mode)]
  transfers between devices with their start and end apart: 4 -> 3, of which waited for: 4 -> 3; matrix products, arithmetic and copies ran while one was open for 7% -> 6% of each run, Pallas kernels for 0% -> 0%
where the time goes in v20:
time: 81.7 us; the launch traced here: 81.4 us
  blocking collectives  31.5 us (39%)
  waiting for transfers between devices  24.9 us (30%)
  starting transfers between devices  10.9 us (13%)
  local copies, waits for them, and re-layouts  5.75 us (7%)
  matrix products  4.4 us (5%)
  between operations  2.15 us (3%)
  other arithmetic  1.8 us (2%)
    all_to_all x1, blocking collectives, body(): lax.all_to_all(both_pencil, 'scan', split_axis=0, concat_axis=1, tiled=True)  31.5 us
    all_to_all x1, waiting for transfers between devices, body(): lax.all_to_all(both_flat, 'scan', split_axis=1, concat_axis=0, tiled=True)  21.2 us
    all_to_all x1, starting transfers between devices, body(): lax.all_to_all(both_flat, 'scan', split_axis=1, concat_axis=0, tiled=True)  6.33 us
    dot_general x4, matrix products, lateral_apply(): return jnp.einsum('rk,pkc->prc', band, padded, precision=precision)  3.18 us
    ppermute x1, starting transfers between devices, blur_rows(): arrived = lax.ppermute(sent, axis, [(0, 1), (1, 0)])  3 us
    concatenate x3, local copies, waits for them, and re-layouts, body(): jnp.concatenate([blurred, raw.reshape(plane_count, flat_count)], axis=0)  2.97 us
    ppermute x1, waiting for transfers between devices, body(): arrived = lax.ppermute(sent, 'row', [(0, 1), (1, 0)])  2.18 us
  transfers between devices with their start and end apart: 3, of which 3 were waited for; matrix products, arithmetic and copies ran while one was open for 6% of the time, Pallas kernels for 0%

profile of v20, /device:TPU:0, one launch (start us, length us, event | category | flops | bytes accessed | tf_op | source)
XLA Modules:
  0.0 81.4 jit_solution(8354195814493086681)
XLA Ops:
  0.6 0.0 copy-start
  0.6 0.0 copy-start.2
  0.7 1.0 %constant_dynamic-slice_fusion.1 = f32[8,8,512]{2,1,0:T(8,128)S(1)} fusion(f32[8,32,512]{2,1,0:T(8,128)} %param.7, s32[]{:T(128)S(6)} %select_n.46), kind=kLoop, calls=%fused_computation.56 | loop fusion | bytes 262148 | tf_op jit(solution)/shard_map/dynamic_slice | solution.py:16
  1.6 3.0 %collective-permute-start = (f32[8,8,512]{2,1,0:T(8,128)S(1)}, f32[8,8,512]{2,1,0:T(8,128)S(1)}, u32[]{:S(2)}, u32[]{:S(2)}) collective-permute-start(f32[8,8,512]{2,1,0:T(8,128)S(1)} %constant_dynamic-slice_fusion.1), channel_id=1, source_target_pairs={{0,1},{1,0},{2,3},{3,2},{4,5},{5,4},{6,7},{7,6},{8,9},{9,8},{10,11... | collective-permute-start | bytes 393224 | tf_op jit(solution)/shard_map/ppermute | solution.py:17
  4.6 1.2 %concatenate.13 = f32[8,16,1024]{2,1,0:T(8,128)S(1)} reshape(f32[8,32,512]{2,1,0:T(8,128)} %param.8) | data formatting | bytes 1048576 | tf_op jit(solution)/shard_map/concatenate | solution.py:67
  5.9 0.0 copy-done.2
  5.9 0.1 select_reduce_fusion.1
  6.0 0.0 copy-done
  6.0 0.6 convolution_bitcast_fusion.1
  6.7 1.5 %collective-permute-done = f32[8,8,512]{2,1,0:T(8,128)S(1)} collective-permute-done((f32[8,8,512]{2,1,0:T(8,128)S(1)}, f32[8,8,512]{2,1,0:T(8,128)S(1)}, u32[]{:S(2)}, u32[]{:S(2)}) %collective-permute-start) | collective-permute-done | bytes 131104 | tf_op jit(solution)/shard_map/ppermute | solution.py:17
  8.1 0.6 fusion
  8.8 0.2 concatenate.12
  9.0 0.1 pad_maximum_fusion
  9.1 1.6 %copy.34 = f32[16,16,1024]{2,0,1:T(8,128)} copy(f32[16,16,1024]{2,1,0:T(8,128)S(1)} %pad_maximum_fusion) | data formatting | bytes 2097152 | tf_op jit(solution)/shard_map/concatenate | solution.py:67
  10.7 0.0 copy-start.1
  10.7 0.0 copy-start.3
  10.7 6.3 %all-to-all-start = ((f32[16,16,1024]{2,0,1:T(8,128)}), f32[16,16,1024]{2,0,1:T(8,128)S(1)}, u32[]{:S(2)}, u32[]{:S(2)}) async-start(f32[16,16,1024]{2,0,1:T(8,128)} %copy.34), calls=%async_computation | async-start | bytes 2097152 | tf_op jit(solution)/shard_map/all_to_all | solution.py:68
  17.0 0.0 copy-done.1
  17.0 0.1 subtract_subtract_fusion
  17.1 0.0 copy-done.3
  17.1 1.4 %select_reduce_fusion = f32[128,128]{1,0:T(8,128)S(1)} fusion(f32[64]{0:T(128)S(1)} %copy-done.3, s32[128,128]{1,0:T(8,128)S(1)} %subtract_subtract_fusion), kind=kLoop, calls=%fused_computation | loop fusion | flops 3129344 | bytes 131328 | tf_op jit(solution)/shard_map/reduce_sum | solution.py:52
  18.5 0.1 copy.31
  18.6 0.1 fusion.13
  18.7 21.2 %all-to-all-done = f32[16,16,1024]{2,0,1:T(8,128)S(1)} async-done(((f32[16,16,1024]{2,0,1:T(8,128)}), f32[16,16,1024]{2,0,1:T(8,128)S(1)}, u32[]{:S(2)}, u32[]{:S(2)}) %all-to-all-start) | async-done | bytes 1048608 | tf_op jit(solution)/shard_map/all_to_all | solution.py:68
  39.9 0.6 fusion.3
  40.6 0.6 fusion.5
  41.2 31.5 %all_to_all.26 = f32[16,16,1024]{2,1,0:T(8,128)S(1)} all-to-all(f32[16,16,1024]{2,1,0:T(8,128)S(1)} %fusion.5), channel_id=1, replica_groups=mesh['scan'=16,'row'=2] {'scan'}, dimensions={0} | all-to-all | bytes 2097152 | tf_op jit(solution)/shard_map/all_to_all | solution.py:80
  72.7 0.1 fusion.32
  72.8 0.3 copy.35
  73.1 0.1 reshape.120
  73.2 1.6 %collective-permute-start.1 = (f32[8,8,512]{2,1,0:T(8,128)S(1)}, f32[8,8,512]{2,1,0:T(8,128)S(1)}, u32[]{:S(2)}, u32[]{:S(2)}) collective-permute-start(f32[8,8,512]{2,1,0:T(8,128)S(1)} %constant_dynamic-slice_fusion), channel_id=1, source_target_pairs={{0,1},{1,0},{2,3},{3,2},{4,5},{5,4},{6,7},{7,6},{8,9},{9,8},{10,11... | collective-permute-start | bytes 393224 | tf_op jit(solution)/shard_map/ppermute | solution.py:92
  76.1 0.3 copy.36
  76.4 0.9 %reshape.121 = f32[8,32,512]{2,1,0:T(8,128)} reshape(f32[8,16,1024]{2,1,0:T(8,128)S(1)} %copy.36) | data formatting | bytes 1048576 | tf_op jit(solution)/shard_map/reshape | solution.py:109
  77.3 2.2 %collective-permute-done.1 = f32[8,8,512]{2,1,0:T(8,128)S(1)} collective-permute-done((f32[8,8,512]{2,1,0:T(8,128)S(1)}, f32[8,8,512]{2,1,0:T(8,128)S(1)}, u32[]{:S(2)}, u32[]{:S(2)}) %collective-permute-start.1) | collective-permute-done | bytes 131104 | tf_op jit(solution)/shard_map/ppermute | solution.py:92
  79.5 0.3 fusion.4
  79.8 1.7 %multiply_select_fusion = f32[8,32,512]{2,1,0:T(8,128)} fusion(f32[8,32,512]{2,1,0:T(8,128)S(1)} %fusion.4, f32[]{:T(128)S(6)} %mul.29, f32[]{:T(128)} %bitcast.60, f32[8,32,512]{2,1,0:T(8,128)S(1)} %copy-done, f32[8,32,512]{2,1,0:T(8,128)S(1)} %reshape.120, pred[32]{0:T(512)(128)(4,1)S(1)} %compare_and_fusion, f32[32,48]{1,0:T(8,128)S(1)} %get-tuple-element.2), kind=kOutput, calls=%fused_computation.15 | convolution fusion | flops 27131904 | bytes 2104356 | tf_op jit(solution)/shard_map/rk,pkc->prc/dot_general | solution.py:41
  (6 shorter events, 0.1 us)
Async XLA Ops:
  0.6 5.4 %copy-start = (f32[8,32,512]{2,1,0:T(8,128)S(1)}, f32[8,32,512]{2,1,0:T(8,128)}, u32[]{:S(2)}) copy-start(f32[8,32,512]{2,1,0:T(8,128)} %param.7) | copy-start | bytes 1572868
  0.6 5.2 %copy-start.2 = (f32[17]{0:T(128)S(1)}, f32[17]{0:T(128)}, u32[]{:S(2)}) copy-start(f32[17]{0:T(128)} %param.11) | copy-start | bytes 208
  1.6 6.5 %collective-permute-start = (f32[8,8,512]{2,1,0:T(8,128)S(1)}, f32[8,8,512]{2,1,0:T(8,128)S(1)}, u32[]{:S(2)}, u32[]{:S(2)}) collective-permute-start(f32[8,8,512]{2,1,0:T(8,128)S(1)} %constant_dynamic-slice_fusion.1), channel_id=1, source_target_pairs={{0,1},{1,0},{2,3},{3,2},{4,5},{5,4},{6,7},{7,6},{8,9},{9,8},{10,11... | collective-permute-start | bytes 393224 | tf_op jit(solution)/shard_map/ppermute | solution.py:17
  10.7 6.3 %copy-start.1 = (s32[128]{0:T(128)S(1)}, s32[128]{0:T(128)}, u32[]{:S(2)}) copy-start(s32[128]{0:T(128)} %param.9) | copy-start | bytes 1540
  10.7 6.4 %copy-start.3 = (f32[64]{0:T(128)S(1)}, f32[64]{0:T(128)}, u32[]{:S(2)}) copy-start(f32[64]{0:T(128)} %param.10) | copy-start | bytes 772
  10.7 29.3 %all-to-all-start = ((f32[16,16,1024]{2,0,1:T(8,128)}), f32[16,16,1024]{2,0,1:T(8,128)S(1)}, u32[]{:S(2)}, u32[]{:S(2)}) async-start(f32[16,16,1024]{2,0,1:T(8,128)} %copy.34), calls=%async_computation | async-start | bytes 2097152 | tf_op jit(solution)/shard_map/all_to_all | solution.py:68
  73.2 6.2 %collective-permute-start.1 = (f32[8,8,512]{2,1,0:T(8,128)S(1)}, f32[8,8,512]{2,1,0:T(8,128)S(1)}, u32[]{:S(2)}, u32[]{:S(2)}) collective-permute-start(f32[8,8,512]{2,1,0:T(8,128)S(1)} %constant_dynamic-slice_fusion), channel_id=1, source_target_pairs={{0,1},{1,0},{2,3},{3,2},{4,5},{5,4},{6,7},{7,6},{8,9},{9,8},{10,11... | collective-permute-start | bytes 393224 | tf_op jit(solution)/shard_map/ppermute | solution.py:92

commit v21 on v20

--- a/solution.py
+++ b/solution.py
@@ -93,6 +93,7 @@
         own = lateral_apply(back_band[:, halo_rows : halo_rows + row_count], back_volume, high_mode)
         stepped = estimate - step_size[0] * own
         finished = shrink(stepped)
+        finished, stepped = lax.optimization_barrier((finished, stepped))
         edge = jnp.where(
             first,
             back_band[row_count - halo_rows :, halo_rows + row_count :],

time: 81.7 us -> 80.7 us (0.988)
  blocking collectives: 31.5 us -> 0 us
  waiting for transfers between devices: 24.9 us -> 47.1 us
  starting transfers between devices: 10.9 us -> 17.8 us
  other arithmetic: 1.8 us -> 2.85 us
    all_to_all x1 -> x0, blocking collectives: 31.5 us -> none  [body(): lax.all_to_all(both_pencil, 'scan', split_axis=0, concat_axis=1, tiled=True)]
    all_to_all x0 -> x1, waiting for transfers between devices: none -> 21.6 us  [body(): lax.all_to_all(both_pencil, 'scan', split_axis=0, concat_axis=1, tiled=True)]
    all_to_all x0 -> x1, starting transfers between devices: none -> 6.86 us  [body(): lax.all_to_all(both_pencil, 'scan', split_axis=0, concat_axis=1, tiled=True)]
    dot_general x4, matrix products: 3.18 us -> 2.13 us  [lateral_apply(): return jnp.einsum('rk,pkc->prc', band, padded, precision=precision)]
    select_n x0 -> x1, other arithmetic: none -> 1.04 us  [body(): jnp.where(at_edge, shrink(stepped - step_size[0] * edge_full), finished)]
    dot_general x1, matrix products: 0.58 us -> 1.56 us  [body(): both_pencil = jnp.dot(joint, misfit_pencil, precision=high_mode)]
  transfers between devices with their start and end apart: 3 -> 4, of which waited for: 3 -> 4; matrix products, arithmetic and copies ran while one was open for 6% -> 7% of each run, Pallas kernels for 0% -> 0%
where the time goes in v21:
time: 80.7 us; the launch traced here: 79.9 us
  waiting for transfers between devices  47.1 us (58%)
  starting transfers between devices  17.8 us (22%)
  local copies, waits for them, and re-layouts  5.77 us (7%)
  matrix products  4.33 us (5%)
  other arithmetic  2.85 us (4%)
  between operations  2.16 us (3%)
    all_to_all x1, waiting for transfers between devices, body(): lax.all_to_all(both_pencil, 'scan', split_axis=0, concat_axis=1, tiled=True)  21.6 us
    all_to_all x1, waiting for transfers between devices, body(): lax.all_to_all(both_flat, 'scan', split_axis=1, concat_axis=0, tiled=True)  21.2 us
    all_to_all x1, starting transfers between devices, body(): lax.all_to_all(both_pencil, 'scan', split_axis=0, concat_axis=1, tiled=True)  6.86 us
    all_to_all x1, starting transfers between devices, body(): lax.all_to_all(both_flat, 'scan', split_axis=1, concat_axis=0, tiled=True)  6.33 us
    ppermute x1, starting transfers between devices, blur_rows(): arrived = lax.ppermute(sent, axis, [(0, 1), (1, 0)])  3 us
    concatenate x3, local copies, waits for them, and re-layouts, body(): jnp.concatenate([blurred, raw.reshape(plane_count, flat_count)], axis=0)  2.97 us
    ppermute x1, waiting for transfers between devices, body(): arrived = lax.ppermute(sent, 'row', [(0, 1), (1, 0)])  2.71 us
    dot_general x4, matrix products, lateral_apply(): return jnp.einsum('rk,pkc->prc', band, padded, precision=precision)  2.13 us
  transfers between devices with their start and end apart: 4, of which 4 were waited for; matrix products, arithmetic and copies ran while one was open for 7% of the time, Pallas kernels for 0%

profile of v21, /device:TPU:0, one launch (start us, length us, event | category | flops | bytes accessed | tf_op | source)
XLA Modules:
  0.0 79.9 jit_solution(10843144951053909990)
XLA Ops:
  0.6 0.0 copy-start
  0.6 0.0 copy-start.2
  0.7 1.0 %constant_dynamic-slice_fusion.1 = f32[8,8,512]{2,1,0:T(8,128)S(1)} fusion(f32[8,32,512]{2,1,0:T(8,128)} %param.7, s32[]{:T(128)S(6)} %select_n.46), kind=kLoop, calls=%fused_computation.57 | loop fusion | bytes 262148 | tf_op jit(solution)/shard_map/dynamic_slice | solution.py:16
  1.6 3.0 %collective-permute-start = (f32[8,8,512]{2,1,0:T(8,128)S(1)}, f32[8,8,512]{2,1,0:T(8,128)S(1)}, u32[]{:S(2)}, u32[]{:S(2)}) collective-permute-start(f32[8,8,512]{2,1,0:T(8,128)S(1)} %constant_dynamic-slice_fusion.1), channel_id=1, source_target_pairs={{0,1},{1,0},{2,3},{3,2},{4,5},{5,4},{6,7},{7,6},{8,9},{9,8},{10,11... | collective-permute-start | bytes 393224 | tf_op jit(solution)/shard_map/ppermute | solution.py:17
  4.6 1.2 %concatenate.13 = f32[8,16,1024]{2,1,0:T(8,128)S(1)} reshape(f32[8,32,512]{2,1,0:T(8,128)} %param.8) | data formatting | bytes 1048576 | tf_op jit(solution)/shard_map/concatenate | solution.py:67
  5.9 0.0 copy-done.2
  5.9 0.1 select_reduce_fusion.1
  6.0 0.0 copy-done
  6.0 0.6 convolution_bitcast_fusion.1
  6.7 1.5 %collective-permute-done = f32[8,8,512]{2,1,0:T(8,128)S(1)} collective-permute-done((f32[8,8,512]{2,1,0:T(8,128)S(1)}, f32[8,8,512]{2,1,0:T(8,128)S(1)}, u32[]{:S(2)}, u32[]{:S(2)}) %collective-permute-start) | collective-permute-done | bytes 131104 | tf_op jit(solution)/shard_map/ppermute | solution.py:17
  8.1 0.6 fusion
  8.8 0.2 concatenate.12
  9.0 0.1 pad_maximum_fusion
  9.1 1.6 %copy.34 = f32[16,16,1024]{2,0,1:T(8,128)} copy(f32[16,16,1024]{2,1,0:T(8,128)S(1)} %pad_maximum_fusion) | data formatting | bytes 2097152 | tf_op jit(solution)/shard_map/concatenate | solution.py:67
  10.7 0.0 copy-start.1
  10.7 0.0 copy-start.3
  10.7 6.3 %all-to-all-start = ((f32[16,16,1024]{2,0,1:T(8,128)}), f32[16,16,1024]{2,0,1:T(8,128)S(1)}, u32[]{:S(2)}, u32[]{:S(2)}) async-start(f32[16,16,1024]{2,0,1:T(8,128)} %copy.34), calls=%async_computation | async-start | bytes 2097152 | tf_op jit(solution)/shard_map/all_to_all | solution.py:68
  17.0 0.0 copy-done.1
  17.0 0.1 subtract_subtract_fusion
  17.1 0.0 copy-done.3
  17.1 1.4 %select_reduce_fusion = f32[128,128]{1,0:T(8,128)S(1)} fusion(f32[64]{0:T(128)S(1)} %copy-done.3, s32[128,128]{1,0:T(8,128)S(1)} %subtract_subtract_fusion), kind=kLoop, calls=%fused_computation | loop fusion | flops 3129344 | bytes 131328 | tf_op jit(solution)/shard_map/reduce_sum | solution.py:52
  18.5 0.1 copy.31
  18.6 0.1 fusion.13
  18.7 21.2 %all-to-all-done = f32[16,16,1024]{2,0,1:T(8,128)S(1)} async-done(((f32[16,16,1024]{2,0,1:T(8,128)}), f32[16,16,1024]{2,0,1:T(8,128)S(1)}, u32[]{:S(2)}, u32[]{:S(2)}) %all-to-all-start) | async-done | bytes 1048608 | tf_op jit(solution)/shard_map/all_to_all | solution.py:68
  39.9 0.6 fusion.3
  40.6 1.6 %fusion.5 = f32[16,16,1024]{2,1,0:T(8,128)} fusion(f32[128,1024,1]{1,0,2:T(8,128)S(1)} %fusion.3, f32[16,1,8,128]{3,2,1,0:T(8,128)S(1)} %fusion.8, f32[16,1,8,128]{3,2,1,0:T(8,128)S(1)} %fusion.13), kind=kOutput, calls=%fused_computation.22 | convolution fusion | flops 201359360 | bytes 1703936 | tf_op jit(solution)/shard_map/dot_general | solution.py:79
  42.2 6.9 %all-to-all-start.1 = ((f32[16,16,1024]{2,1,0:T(8,128)}), f32[16,16,1024]{2,1,0:T(8,128)S(1)}, u32[]{:S(2)}, u32[]{:S(2)}) async-start(f32[16,16,1024]{2,1,0:T(8,128)} %fusion.5), calls=%async_computation.1 | async-start | bytes 2097152 | tf_op jit(solution)/shard_map/all_to_all | solution.py:80
  50.3 21.6 %all-to-all-done.1 = f32[16,16,1024]{2,1,0:T(8,128)S(1)} async-done(((f32[16,16,1024]{2,1,0:T(8,128)}), f32[16,16,1024]{2,1,0:T(8,128)S(1)}, u32[]{:S(2)}, u32[]{:S(2)}) %all-to-all-start.1) | async-done | bytes 1048608 | tf_op jit(solution)/shard_map/all_to_all | solution.py:80
  72.0 0.1 fusion.32
  72.1 0.3 copy.35
  72.4 0.1 reshape.120
  72.5 1.6 %collective-permute-start.1 = (f32[8,8,512]{2,1,0:T(8,128)S(1)}, f32[8,8,512]{2,1,0:T(8,128)S(1)}, u32[]{:S(2)}, u32[]{:S(2)}) collective-permute-start(f32[8,8,512]{2,1,0:T(8,128)S(1)} %constant_dynamic-slice_fusion), channel_id=1, source_target_pairs={{0,1},{1,0},{2,3},{3,2},{4,5},{5,4},{6,7},{7,6},{8,9},{9,8},{10,11... | collective-permute-start | bytes 393224 | tf_op jit(solution)/shard_map/ppermute | solution.py:92
  74.0 0.6 maximum_multiply_fusion
  74.7 0.3 copy.36
  75.0 0.9 %reshape.121 = f32[8,32,512]{2,1,0:T(8,128)} reshape(f32[8,16,1024]{2,1,0:T(8,128)S(1)} %copy.36) | data formatting | bytes 1048576 | tf_op jit(solution)/shard_map/reshape | solution.py:110
  75.9 2.7 %collective-permute-done.1 = f32[8,8,512]{2,1,0:T(8,128)S(1)} collective-permute-done((f32[8,8,512]{2,1,0:T(8,128)S(1)}, f32[8,8,512]{2,1,0:T(8,128)S(1)}, u32[]{:S(2)}, u32[]{:S(2)}) %collective-permute-start.1) | collective-permute-done | bytes 131104 | tf_op jit(solution)/shard_map/ppermute | solution.py:92
  78.6 0.3 fusion.4
  78.9 1.0 %multiply_select_fusion = f32[8,32,512]{2,1,0:T(8,128)} fusion(f32[8,32,512]{2,1,0:T(8,128)S(1)} %get-tuple-element.5, f32[8,32,512]{2,1,0:T(8,128)S(1)} %get-tuple-element.4, f32[8,32,512]{2,1,0:T(8,128)S(1)} %fusion.4, f32[]{:T(128)} %bitcast.61, f32[]{:T(128)S(6)} %mul.27, pred[32]{0:T(512)(128)(4,1)S(1)} %compare_and_fusion), kind=kLoop, calls=%fused_computation.15 | loop fusion | flops 1048576 | bytes 2097192 | tf_op jit(solution)/shard_map/jit(_where)/select_n | solution.py:106
  (6 shorter events, 0.1 us)
Async XLA Ops:
  0.6 5.4 %copy-start = (f32[8,32,512]{2,1,0:T(8,128)S(1)}, f32[8,32,512]{2,1,0:T(8,128)}, u32[]{:S(2)}) copy-start(f32[8,32,512]{2,1,0:T(8,128)} %param.7) | copy-start | bytes 1572868
  0.6 5.2 %copy-start.2 = (f32[17]{0:T(128)S(1)}, f32[17]{0:T(128)}, u32[]{:S(2)}) copy-start(f32[17]{0:T(128)} %param.11) | copy-start | bytes 208
  1.6 6.5 %collective-permute-start = (f32[8,8,512]{2,1,0:T(8,128)S(1)}, f32[8,8,512]{2,1,0:T(8,128)S(1)}, u32[]{:S(2)}, u32[]{:S(2)}) collective-permute-start(f32[8,8,512]{2,1,0:T(8,128)S(1)} %constant_dynamic-slice_fusion.1), channel_id=1, source_target_pairs={{0,1},{1,0},{2,3},{3,2},{4,5},{5,4},{6,7},{7,6},{8,9},{9,8},{10,11... | collective-permute-start | bytes 393224 | tf_op jit(solution)/shard_map/ppermute | solution.py:17
  10.7 6.3 %copy-start.1 = (s32[128]{0:T(128)S(1)}, s32[128]{0:T(128)}, u32[]{:S(2)}) copy-start(s32[128]{0:T(128)} %param.9) | copy-start | bytes 1540
  10.7 6.4 %copy-start.3 = (f32[64]{0:T(128)S(1)}, f32[64]{0:T(128)}, u32[]{:S(2)}) copy-start(f32[64]{0:T(128)} %param.10) | copy-start | bytes 772
  10.7 29.3 %all-to-all-start = ((f32[16,16,1024]{2,0,1:T(8,128)}), f32[16,16,1024]{2,0,1:T(8,128)S(1)}, u32[]{:S(2)}, u32[]{:S(2)}) async-start(f32[16,16,1024]{2,0,1:T(8,128)} %copy.34), calls=%async_computation | async-start | bytes 2097152 | tf_op jit(solution)/shard_map/all_to_all | solution.py:68
  42.2 29.8 %all-to-all-start.1 = ((f32[16,16,1024]{2,1,0:T(8,128)}), f32[16,16,1024]{2,1,0:T(8,128)S(1)}, u32[]{:S(2)}, u32[]{:S(2)}) async-start(f32[16,16,1024]{2,1,0:T(8,128)} %fusion.5), calls=%async_computation.1 | async-start | bytes 2097152 | tf_op jit(solution)/shard_map/all_to_all | solution.py:80
  72.5 6.1 %collective-permute-start.1 = (f32[8,8,512]{2,1,0:T(8,128)S(1)}, f32[8,8,512]{2,1,0:T(8,128)S(1)}, u32[]{:S(2)}, u32[]{:S(2)}) collective-permute-start(f32[8,8,512]{2,1,0:T(8,128)S(1)} %constant_dynamic-slice_fusion), channel_id=1, source_target_pairs={{0,1},{1,0},{2,3},{3,2},{4,5},{5,4},{6,7},{7,6},{8,9},{9,8},{10,11... | collective-permute-start | bytes 393224 | tf_op jit(solution)/shard_map/ppermute | solution.py:92

commit v22 on v19

--- a/solution.py
+++ b/solution.py
@@ -63,7 +63,23 @@
     sheet_psf = sheet_matrix(offsets, depth_psf, offsets.shape[0])
     blur_band = band_matrix(lateral_psf, row_count, False)
     back_band = band_matrix(lateral_psf, row_count, True)
-    blurred = blur_rows(blur_band, estimate, "row", halo_rows).reshape(plane_count, flat_count)
+    if lax.axis_size("row") == 2:
+        first_row = lax.axis_index("row") == 0
+        front_start = jnp.where(first_row, row_count - halo_rows, 0)
+        front_sent = lax.dynamic_slice_in_dim(estimate, front_start, halo_rows, axis=1)
+        front_arrived = lax.ppermute(front_sent, "row", [(0, 1), (1, 0)])
+        own_blur = lateral_apply(blur_band[:, halo_rows : halo_rows + row_count], estimate)
+        front_edge = jnp.where(
+            first_row,
+            blur_band[row_count - halo_rows :, halo_rows + row_count :],
+            blur_band[:halo_rows, :halo_rows],
+        )
+        edge_rows = lax.dynamic_slice_in_dim(own_blur, front_start, halo_rows, axis=1)
+        edge_rows = edge_rows + lateral_apply(front_edge, front_arrived)
+        blurred = lax.dynamic_update_slice_in_dim(own_blur, edge_rows, front_start, axis=1)
+        blurred = blurred.reshape(plane_count, flat_count)
+    else:
+        blurred = blur_rows(blur_band, estimate, "row", halo_rows).reshape(plane_count, flat_count)
     both_flat = jnp.concatenate([blurred, raw.reshape(plane_count, flat_count)], axis=0)
     both_in = lax.all_to_all(both_flat, "scan", split_axis=1, concat_axis=0, tiled=True)
     both_in = both_in.reshape(lax.axis_size("scan"), 2, plane_count, -1)

time: 80.5 us -> 80.1 us (level)
  local copies, waits for them, and re-layouts: 6.51 us -> 5.45 us
    concatenate x3, local copies, waits for them, and re-layouts: 2.97 us -> 1.93 us  [body(): jnp.concatenate([blurred, raw.reshape(plane_count, flat_count)], axis=0)]
  transfers between devices with their start and end apart: 4 -> 4, of which waited for: 4 -> 4; matrix products, arithmetic and copies ran while one was open for 7% -> 8% of each run, Pallas kernels for 0% -> 0%
where the time goes in v22:
time: 80.1 us; the launch traced here: 79.3 us
  waiting for transfers between devices  46.3 us (58%)
  starting transfers between devices  17.7 us (22%)
  local copies, waits for them, and re-layouts  5.45 us (7%)
  matrix products  5.16 us (6%)
  other arithmetic  2.45 us (3%)
  between operations  2.16 us (3%)
    all_to_all x1, waiting for transfers between devices, body(): lax.all_to_all(both_pencil, 'scan', split_axis=0, concat_axis=1, tiled=True)  21.6 us
    all_to_all x1, waiting for transfers between devices, body(): lax.all_to_all(both_flat, 'scan', split_axis=1, concat_axis=0, tiled=True)  21.2 us
    all_to_all x1, starting transfers between devices, body(): lax.all_to_all(both_pencil, 'scan', split_axis=0, concat_axis=1, tiled=True)  6.86 us
    all_to_all x1, starting transfers between devices, body(): lax.all_to_all(both_flat, 'scan', split_axis=1, concat_axis=0, tiled=True)  6.32 us
    ppermute x1, starting transfers between devices, body(): front_arrived = lax.ppermute(front_sent, 'row', [(0, 1), (1, 0)])  3 us
    dot_general x4, matrix products, lateral_apply(): return jnp.einsum('rk,pkc->prc', band, padded, precision=precision)  2.96 us
    ppermute x1, waiting for transfers between devices, body(): arrived = lax.ppermute(sent, 'row', [(0, 1), (1, 0)])  2.7 us
    concatenate x3, local copies, waits for them, and re-layouts, body(): jnp.concatenate([blurred, raw.reshape(plane_count, flat_count)], axis=0)  1.93 us
  transfers between devices with their start and end apart: 4, of which 4 were waited for; matrix products, arithmetic and copies ran while one was open for 8% of the time, Pallas kernels for 0%

profile of v22, /device:TPU:0, one launch (start us, length us, event | category | flops | bytes accessed | tf_op | source)
XLA Modules:
  0.0 79.3 jit_solution(7512564247991283712)
XLA Ops:
  0.6 0.9 %constant_dynamic-slice_fusion = f32[8,8,512]{2,1,0:T(8,128)S(1)} fusion(f32[8,32,512]{2,1,0:T(8,128)} %param.7, s32[]{:T(128)S(6)} %select_n.45), kind=kLoop, calls=%fused_computation.57 | loop fusion | bytes 262148 | tf_op jit(solution)/shard_map/dynamic_slice | solution.py:69
  1.6 3.0 %collective-permute-start = (f32[8,8,512]{2,1,0:T(8,128)S(1)}, f32[8,8,512]{2,1,0:T(8,128)S(1)}, u32[]{:S(2)}, u32[]{:S(2)}) collective-permute-start(f32[8,8,512]{2,1,0:T(8,128)S(1)} %constant_dynamic-slice_fusion), channel_id=1, source_target_pairs={{0,1},{1,0},{2,3},{3,2},{4,5},{5,4},{6,7},{7,6},{8,9},{9,8},{10,11... | collective-permute-start | bytes 393224 | tf_op jit(solution)/shard_map/ppermute | solution.py:70
  4.6 0.8 select_reduce_fusion.1
  5.4 0.0 copy-start.1
  5.4 1.7 %fusion.22 = f32[32,8,512]{2,0,1:T(8,128)S(1)} fusion(f32[8,32,512]{2,1,0:T(8,128)} %param.7, f32[32,48]{1,0:T(8,128)S(1)} %get-tuple-element.3), kind=kOutput, calls=%fused_computation.44 | convolution fusion | flops 50331648 | bytes 1054720 | tf_op jit(solution)/shard_map/rk,pkc->prc/dot_general | solution.py:41
  7.2 0.0 copy-done.1
  7.2 0.2 concatenate.13
  7.3 0.7 collective-permute-done
  8.1 0.3 fusion.5
  8.4 0.2 concatenate.12
  8.6 0.1 pad_maximum_fusion
  8.7 1.6 %copy.28 = f32[16,16,1024]{2,0,1:T(8,128)} copy(f32[16,16,1024]{2,1,0:T(8,128)S(1)} %pad_maximum_fusion) | data formatting | bytes 2097152 | tf_op jit(solution)/shard_map/concatenate | solution.py:83
  10.3 0.0 copy-start.3
  10.3 0.0 copy-start.4
  10.3 6.3 %all-to-all-start = ((f32[16,16,1024]{2,0,1:T(8,128)}), f32[16,16,1024]{2,0,1:T(8,128)S(1)}, u32[]{:S(2)}, u32[]{:S(2)}) async-start(f32[16,16,1024]{2,0,1:T(8,128)} %copy.28), calls=%async_computation | async-start | bytes 2097152 | tf_op jit(solution)/shard_map/all_to_all | solution.py:84
  16.6 0.0 copy-done.3
  16.6 0.1 subtract_subtract_fusion
  16.7 0.0 copy-done.4
  16.7 1.4 %select_reduce_fusion = f32[128,128]{1,0:T(8,128)S(1)} fusion(f32[64]{0:T(128)S(1)} %copy-done.4, s32[128,128]{1,0:T(8,128)S(1)} %subtract_subtract_fusion), kind=kLoop, calls=%fused_computation | loop fusion | flops 3129344 | bytes 131328 | tf_op jit(solution)/shard_map/reduce_sum | solution.py:52
  18.1 0.1 copy.26
  18.2 0.1 fusion.15
  18.3 21.2 %all-to-all-done = f32[16,16,1024]{2,0,1:T(8,128)S(1)} async-done(((f32[16,16,1024]{2,0,1:T(8,128)}), f32[16,16,1024]{2,0,1:T(8,128)S(1)}, u32[]{:S(2)}, u32[]{:S(2)}) %all-to-all-start) | async-done | bytes 1048608 | tf_op jit(solution)/shard_map/all_to_all | solution.py:84
  39.5 0.6 fusion.2
  40.2 1.6 %fusion.7 = f32[16,16,1024]{2,1,0:T(8,128)} fusion(f32[128,1024,1]{1,0,2:T(8,128)S(1)} %fusion.2, f32[16,1,8,128]{3,2,1,0:T(8,128)S(1)} %fusion.10, f32[16,1,8,128]{3,2,1,0:T(8,128)S(1)} %fusion.15), kind=kOutput, calls=%fused_computation.22 | convolution fusion | flops 201359360 | bytes 1703936 | tf_op jit(solution)/shard_map/dot_general | solution.py:95
  41.7 6.9 %all-to-all-start.1 = ((f32[16,16,1024]{2,1,0:T(8,128)}), f32[16,16,1024]{2,1,0:T(8,128)S(1)}, u32[]{:S(2)}, u32[]{:S(2)}) async-start(f32[16,16,1024]{2,1,0:T(8,128)} %fusion.7), calls=%async_computation.1 | async-start | bytes 2097152 | tf_op jit(solution)/shard_map/all_to_all | solution.py:96
  49.9 21.6 %all-to-all-done.1 = f32[16,16,1024]{2,1,0:T(8,128)S(1)} async-done(((f32[16,16,1024]{2,1,0:T(8,128)}), f32[16,16,1024]{2,1,0:T(8,128)S(1)}, u32[]{:S(2)}, u32[]{:S(2)}) %all-to-all-start.1) | async-done | bytes 1048608 | tf_op jit(solution)/shard_map/all_to_all | solution.py:96
  71.6 0.1 fusion.35
  71.6 0.0 copy-start
  71.7 0.3 copy.29
  72.0 0.1 reshape.109
  72.1 1.6 %collective-permute-start.1 = (f32[8,8,512]{2,1,0:T(8,128)S(1)}, f32[8,8,512]{2,1,0:T(8,128)S(1)}, u32[]{:S(2)}, u32[]{:S(2)}) collective-permute-start(f32[8,8,512]{2,1,0:T(8,128)S(1)} %constant_dynamic-slice_fusion.1), channel_id=1, source_target_pairs={{0,1},{1,0},{2,3},{3,2},{4,5},{5,4},{6,7},{7,6},{8,9},{9,8},{10,11... | collective-permute-start | bytes 393224 | tf_op jit(solution)/shard_map/ppermute | solution.py:108
  73.6 0.0 copy-done
  73.7 0.6 maximum_multiply_fusion
  74.3 0.3 copy.30
  74.6 0.9 %reshape.110 = f32[8,32,512]{2,1,0:T(8,128)} reshape(f32[8,16,1024]{2,1,0:T(8,128)S(1)} %copy.30) | data formatting | bytes 1048576 | tf_op jit(solution)/shard_map/reshape | solution.py:123
  75.5 2.7 %collective-permute-done.1 = f32[8,8,512]{2,1,0:T(8,128)S(1)} collective-permute-done((f32[8,8,512]{2,1,0:T(8,128)S(1)}, f32[8,8,512]{2,1,0:T(8,128)S(1)}, u32[]{:S(2)}, u32[]{:S(2)}) %collective-permute-start.1) | collective-permute-done | bytes 131104 | tf_op jit(solution)/shard_map/ppermute | solution.py:108
  78.2 0.3 multiply_dynamic-update-slice_fusion
  78.5 0.0 copy-start.2
  78.5 0.8 copy-done.2
  (5 shorter events, 0.1 us)
Async XLA Ops:
  1.6 6.5 %collective-permute-start = (f32[8,8,512]{2,1,0:T(8,128)S(1)}, f32[8,8,512]{2,1,0:T(8,128)S(1)}, u32[]{:S(2)}, u32[]{:S(2)}) collective-permute-start(f32[8,8,512]{2,1,0:T(8,128)S(1)} %constant_dynamic-slice_fusion), channel_id=1, source_target_pairs={{0,1},{1,0},{2,3},{3,2},{4,5},{5,4},{6,7},{7,6},{8,9},{9,8},{10,11... | collective-permute-start | bytes 393224 | tf_op jit(solution)/shard_map/ppermute | solution.py:70
  5.4 1.8 %copy-start.1 = (f32[8,32,512]{2,1,0:T(8,128)S(1)}, f32[8,32,512]{2,1,0:T(8,128)}, u32[]{:S(2)}) copy-start(f32[8,32,512]{2,1,0:T(8,128)} %param.8) | copy-start | bytes 1572868
  10.3 6.3 %copy-start.3 = (s32[128]{0:T(128)S(1)}, s32[128]{0:T(128)}, u32[]{:S(2)}) copy-start(s32[128]{0:T(128)} %param.9) | copy-start | bytes 1540
  10.3 6.4 %copy-start.4 = (f32[64]{0:T(128)S(1)}, f32[64]{0:T(128)}, u32[]{:S(2)}) copy-start(f32[64]{0:T(128)} %param.10) | copy-start | bytes 772
  10.3 29.3 %all-to-all-start = ((f32[16,16,1024]{2,0,1:T(8,128)}), f32[16,16,1024]{2,0,1:T(8,128)S(1)}, u32[]{:S(2)}, u32[]{:S(2)}) async-start(f32[16,16,1024]{2,0,1:T(8,128)} %copy.28), calls=%async_computation | async-start | bytes 2097152 | tf_op jit(solution)/shard_map/all_to_all | solution.py:84
  41.7 29.8 %all-to-all-start.1 = ((f32[16,16,1024]{2,1,0:T(8,128)}), f32[16,16,1024]{2,1,0:T(8,128)S(1)}, u32[]{:S(2)}, u32[]{:S(2)}) async-start(f32[16,16,1024]{2,1,0:T(8,128)} %fusion.7), calls=%async_computation.1 | async-start | bytes 2097152 | tf_op jit(solution)/shard_map/all_to_all | solution.py:96
  71.6 2.0 %copy-start = (f32[8,32,512]{2,1,0:T(8,128)S(1)}, f32[8,32,512]{2,1,0:T(8,128)}, u32[]{:S(2)}) copy-start(f32[8,32,512]{2,1,0:T(8,128)} %param.7) | copy-start | bytes 1572868
  72.1 6.1 %collective-permute-start.1 = (f32[8,8,512]{2,1,0:T(8,128)S(1)}, f32[8,8,512]{2,1,0:T(8,128)S(1)}, u32[]{:S(2)}, u32[]{:S(2)}) collective-permute-start(f32[8,8,512]{2,1,0:T(8,128)S(1)} %constant_dynamic-slice_fusion.1), channel_id=1, source_target_pairs={{0,1},{1,0},{2,3},{3,2},{4,5},{5,4},{6,7},{7,6},{8,9},{9,8},{10,11... | collective-permute-start | bytes 393224 | tf_op jit(solution)/shard_map/ppermute | solution.py:108
  78.5 0.8 %copy-start.2 = (f32[8,32,512]{2,1,0:T(8,128)}, f32[8,32,512]{2,1,0:T(8,128)S(1)}, u32[]{:S(2)}) copy-start(f32[8,32,512]{2,1,0:T(8,128)S(1)} %multiply_dynamic-update-slice_fusion) | copy-start | bytes 1572868

commit v23 on v22

--- a/solution.py
+++ b/solution.py
@@ -63,7 +63,9 @@
     sheet_psf = sheet_matrix(offsets, depth_psf, offsets.shape[0])
     blur_band = band_matrix(lateral_psf, row_count, False)
     back_band = band_matrix(lateral_psf, row_count, True)
-    if lax.axis_size("row") == 2:
+    scan_count = lax.axis_size("scan")
+    per_chunk = row_count // scan_count if row_count % scan_count == 0 else 0
+    if lax.axis_size("row") == 2 and per_chunk and halo_rows % per_chunk == 0:
         first_row = lax.axis_index("row") == 0
         front_start = jnp.where(first_row, row_count - halo_rows, 0)
         front_sent = lax.dynamic_slice_in_dim(estimate, front_start, halo_rows, axis=1)
@@ -76,13 +78,21 @@
         )
         edge_rows = lax.dynamic_slice_in_dim(own_blur, front_start, halo_rows, axis=1)
         edge_rows = edge_rows + lateral_apply(front_edge, front_arrived)
-        blurred = lax.dynamic_update_slice_in_dim(own_blur, edge_rows, front_start, axis=1)
-        blurred = blurred.reshape(plane_count, flat_count)
+
+        def chunked(volume):
+            return volume.reshape(plane_count, scan_count, flat_count // scan_count).transpose(1, 0, 2)
+
+        both_chunks = jnp.concatenate([chunked(own_blur), chunked(raw)], axis=1)
+        halo_chunks = halo_rows // per_chunk
+        edge_chunks = edge_rows.reshape(plane_count, halo_chunks, flat_count // scan_count).transpose(1, 0, 2)
+        both_chunks = lax.dynamic_update_slice_in_dim(both_chunks, edge_chunks, front_start // per_chunk, axis=0)
+        both_in = lax.all_to_all(both_chunks, "scan", split_axis=0, concat_axis=0, tiled=True)
+        both_in = both_in.reshape(scan_count, 2, plane_count, -1)
     else:
         blurred = blur_rows(blur_band, estimate, "row", halo_rows).reshape(plane_count, flat_count)
-    both_flat = jnp.concatenate([blurred, raw.reshape(plane_count, flat_count)], axis=0)
-    both_in = lax.all_to_all(both_flat, "scan", split_axis=1, concat_axis=0, tiled=True)
-    both_in = both_in.reshape(lax.axis_size("scan"), 2, plane_count, -1)
+        both_flat = jnp.concatenate([blurred, raw.reshape(plane_count, flat_count)], axis=0)
+        both_in = lax.all_to_all(both_flat, "scan", split_axis=1, concat_axis=0, tiled=True)
+        both_in = both_in.reshape(scan_count, 2, plane_count, -1)
     pencil = both_in[:, 0].reshape(offsets.shape[0], -1)
     raw_pencil = both_in[:, 1].reshape(offsets.shape[0], -1)
     predicted_pencil = jnp.dot(sheet_psf, pencil, precision=highest_mode)

time: 80.1 us -> 80.2 us (level)
    concatenate x3 -> x0, local copies, waits for them, and re-layouts: 1.93 us -> none  [body(): jnp.concatenate([blurred, raw.reshape(plane_count, flat_count)], axis=0)]
    dynamic_update_slice x0 -> x2, local copies, waits for them, and re-layouts: none -> 1.92 us  [body(): lax.dynamic_update_slice_in_dim(both_chunks, edge_chunks, front_start //...]
where the time goes in v23:
time: 80.2 us; the launch traced here: 79.4 us
  waiting for transfers between devices  46 us (57%)
  starting transfers between devices  17.8 us (22%)
  local copies, waits for them, and re-layouts  5.82 us (7%)
  matrix products  5.16 us (6%)
  other arithmetic  2.45 us (3%)
  between operations  2.17 us (3%)
    all_to_all x1, waiting for transfers between devices, body(): lax.all_to_all(both_pencil, 'scan', split_axis=0, concat_axis=1, tiled=True)  21.6 us
    all_to_all x1, waiting for transfers between devices, body(): lax.all_to_all(both_chunks, 'scan', split_axis=0, concat_axis=0, tiled=True)  21.2 us
    all_to_all x1, starting transfers between devices, body(): lax.all_to_all(both_pencil, 'scan', split_axis=0, concat_axis=1, tiled=True)  6.86 us
    all_to_all x1, starting transfers between devices, body(): lax.all_to_all(both_chunks, 'scan', split_axis=0, concat_axis=0, tiled=True)  6.32 us
    ppermute x1, starting transfers between devices, body(): front_arrived = lax.ppermute(front_sent, 'row', [(0, 1), (1, 0)])  3 us
    dot_general x4, matrix products, lateral_apply(): return jnp.einsum('rk,pkc->prc', band, padded, precision=precision)  2.96 us
    ppermute x1, waiting for transfers between devices, body(): arrived = lax.ppermute(sent, 'row', [(0, 1), (1, 0)])  2.66 us
    dynamic_update_slice x2, local copies, waits for them, and re-layouts, body(): lax.dynamic_update_slice_in_dim(both_chunks, edge_chunks, front_start //...  1.92 us
  transfers between devices with their start and end apart: 4, of which 4 were waited for; matrix products, arithmetic and copies ran while one was open for 8% of the time, Pallas kernels for 0%

profile of v23, /device:TPU:0, one launch (start us, length us, event | category | flops | bytes accessed | tf_op | source)
XLA Modules:
  0.0 79.4 jit_solution(4107937848279408932)
XLA Ops:
  0.6 0.9 %constant_dynamic-slice_fusion.1 = f32[8,8,512]{2,1,0:T(8,128)S(1)} fusion(f32[8,32,512]{2,1,0:T(8,128)} %param.7, s32[]{:T(128)S(6)} %select_n.52), kind=kLoop, calls=%fused_computation.57 | loop fusion | bytes 262148 | tf_op jit(solution)/shard_map/dynamic_slice | solution.py:71
  1.6 3.0 %collective-permute-start = (f32[8,8,512]{2,1,0:T(8,128)S(1)}, f32[8,8,512]{2,1,0:T(8,128)S(1)}, u32[]{:S(2)}, u32[]{:S(2)}) collective-permute-start(f32[8,8,512]{2,1,0:T(8,128)S(1)} %constant_dynamic-slice_fusion.1), channel_id=1, source_target_pairs={{0,1},{1,0},{2,3},{3,2},{4,5},{5,4},{6,7},{7,6},{8,9},{9,8},{10,11... | collective-permute-start | bytes 393224 | tf_op jit(solution)/shard_map/ppermute | solution.py:72
  4.6 0.8 select_reduce_fusion.1
  5.4 0.0 copy-start.1
  5.4 1.7 %fusion.21 = f32[32,8,512]{2,0,1:T(8,128)S(1)} fusion(f32[8,32,512]{2,1,0:T(8,128)} %param.7, f32[32,48]{1,0:T(8,128)S(1)} %get-tuple-element.3), kind=kOutput, calls=%fused_computation.43 | convolution fusion | flops 50331648 | bytes 1054720 | tf_op jit(solution)/shard_map/rk,pkc->prc/dot_general | solution.py:41
  7.1 0.2 reshape.107
  7.3 0.0 copy-done.1
  7.3 0.2 reshape.108
  7.5 0.1 pad_maximum_fusion
  7.6 0.5 collective-permute-done
  8.1 0.3 fusion.4
  8.4 0.1 reshape.109
  8.5 0.3 dynamic_update_slice.6
  8.8 1.6 %copy.29 = f32[16,16,1024]{2,1,0:T(8,128)} copy(f32[16,16,1024]{2,0,1:T(8,128)S(1)} %dynamic_update_slice.6) | data formatting | bytes 2097152 | tf_op jit(solution)/shard_map/dynamic_update_slice | solution.py:88
  10.4 0.0 copy-start.3
  10.4 0.0 copy-start.4
  10.4 6.3 %all-to-all-start = ((f32[16,16,1024]{2,1,0:T(8,128)}), f32[16,16,1024]{2,1,0:T(8,128)S(1)}, u32[]{:S(2)}, u32[]{:S(2)}) async-start(f32[16,16,1024]{2,1,0:T(8,128)} %copy.29), calls=%async_computation | async-start | bytes 2097152 | tf_op jit(solution)/shard_map/all_to_all | solution.py:89
  16.7 0.0 copy-done.3
  16.7 0.1 subtract_subtract_fusion
  16.8 0.0 copy-done.4
  16.8 1.4 %select_reduce_fusion = f32[128,128]{1,0:T(8,128)S(1)} fusion(f32[64]{0:T(128)S(1)} %copy-done.4, s32[128,128]{1,0:T(8,128)S(1)} %subtract_subtract_fusion), kind=kLoop, calls=%fused_computation | loop fusion | flops 3129344 | bytes 131328 | tf_op jit(solution)/shard_map/reduce_sum | solution.py:52
  18.2 0.1 copy.27
  18.3 0.1 fusion.14
  18.4 21.2 %all-to-all-done = f32[16,16,1024]{2,1,0:T(8,128)S(1)} async-done(((f32[16,16,1024]{2,1,0:T(8,128)}), f32[16,16,1024]{2,1,0:T(8,128)S(1)}, u32[]{:S(2)}, u32[]{:S(2)}) %all-to-all-start) | async-done | bytes 1048608 | tf_op jit(solution)/shard_map/all_to_all | solution.py:89
  39.7 0.6 fusion.2
  40.3 1.6 %fusion.6 = f32[16,16,1024]{2,1,0:T(8,128)} fusion(f32[128,1024,1]{1,0,2:T(8,128)S(1)} %fusion.2, f32[16,1,8,128]{3,2,1,0:T(8,128)S(1)} %fusion.9, f32[16,1,8,128]{3,2,1,0:T(8,128)S(1)} %fusion.14), kind=kOutput, calls=%fused_computation.21 | convolution fusion | flops 201359360 | bytes 1703936 | tf_op jit(solution)/shard_map/dot_general | solution.py:105
  41.9 6.9 %all-to-all-start.1 = ((f32[16,16,1024]{2,1,0:T(8,128)}), f32[16,16,1024]{2,1,0:T(8,128)S(1)}, u32[]{:S(2)}, u32[]{:S(2)}) async-start(f32[16,16,1024]{2,1,0:T(8,128)} %fusion.6), calls=%async_computation.1 | async-start | bytes 2097152 | tf_op jit(solution)/shard_map/all_to_all | solution.py:106
  50.0 21.6 %all-to-all-done.1 = f32[16,16,1024]{2,1,0:T(8,128)S(1)} async-done(((f32[16,16,1024]{2,1,0:T(8,128)}), f32[16,16,1024]{2,1,0:T(8,128)S(1)}, u32[]{:S(2)}, u32[]{:S(2)}) %all-to-all-start.1) | async-done | bytes 1048608 | tf_op jit(solution)/shard_map/all_to_all | solution.py:106
  71.7 0.1 fusion.34
  71.8 0.0 copy-start
  71.8 0.3 copy.30
  72.1 0.1 reshape.111
  72.2 1.6 %collective-permute-start.1 = (f32[8,8,512]{2,1,0:T(8,128)S(1)}, f32[8,8,512]{2,1,0:T(8,128)S(1)}, u32[]{:S(2)}, u32[]{:S(2)}) collective-permute-start(f32[8,8,512]{2,1,0:T(8,128)S(1)} %constant_dynamic-slice_fusion), channel_id=1, source_target_pairs={{0,1},{1,0},{2,3},{3,2},{4,5},{5,4},{6,7},{7,6},{8,9},{9,8},{10,11... | collective-permute-start | bytes 393224 | tf_op jit(solution)/shard_map/ppermute | solution.py:118
  73.8 0.0 copy-done
  73.8 0.6 maximum_multiply_fusion
  74.4 0.3 copy.31
  74.8 0.9 %reshape.112 = f32[8,32,512]{2,1,0:T(8,128)} reshape(f32[8,16,1024]{2,1,0:T(8,128)S(1)} %copy.31) | data formatting | bytes 1048576 | tf_op jit(solution)/shard_map/reshape | solution.py:133
  75.6 2.7 %collective-permute-done.1 = f32[8,8,512]{2,1,0:T(8,128)S(1)} collective-permute-done((f32[8,8,512]{2,1,0:T(8,128)S(1)}, f32[8,8,512]{2,1,0:T(8,128)S(1)}, u32[]{:S(2)}, u32[]{:S(2)}) %collective-permute-start.1) | collective-permute-done | bytes 131104 | tf_op jit(solution)/shard_map/ppermute | solution.py:118
  78.3 0.3 multiply_dynamic-update-slice_fusion
  78.6 0.0 copy-start.2
  78.6 0.8 copy-done.2
  (4 shorter events, 0.1 us)
Async XLA Ops:
  1.6 6.5 %collective-permute-start = (f32[8,8,512]{2,1,0:T(8,128)S(1)}, f32[8,8,512]{2,1,0:T(8,128)S(1)}, u32[]{:S(2)}, u32[]{:S(2)}) collective-permute-start(f32[8,8,512]{2,1,0:T(8,128)S(1)} %constant_dynamic-slice_fusion.1), channel_id=1, source_target_pairs={{0,1},{1,0},{2,3},{3,2},{4,5},{5,4},{6,7},{7,6},{8,9},{9,8},{10,11... | collective-permute-start | bytes 393224 | tf_op jit(solution)/shard_map/ppermute | solution.py:72
  5.4 1.9 %copy-start.1 = (f32[8,32,512]{2,1,0:T(8,128)S(1)}, f32[8,32,512]{2,1,0:T(8,128)}, u32[]{:S(2)}) copy-start(f32[8,32,512]{2,1,0:T(8,128)} %param.8) | copy-start | bytes 1572868
  10.4 6.3 %copy-start.3 = (s32[128]{0:T(128)S(1)}, s32[128]{0:T(128)}, u32[]{:S(2)}) copy-start(s32[128]{0:T(128)} %param.9) | copy-start | bytes 1540
  10.4 6.4 %copy-start.4 = (f32[64]{0:T(128)S(1)}, f32[64]{0:T(128)}, u32[]{:S(2)}) copy-start(f32[64]{0:T(128)} %param.10) | copy-start | bytes 772
  10.4 29.3 %all-to-all-start = ((f32[16,16,1024]{2,1,0:T(8,128)}), f32[16,16,1024]{2,1,0:T(8,128)S(1)}, u32[]{:S(2)}, u32[]{:S(2)}) async-start(f32[16,16,1024]{2,1,0:T(8,128)} %copy.29), calls=%async_computation | async-start | bytes 2097152 | tf_op jit(solution)/shard_map/all_to_all | solution.py:89
  41.9 29.8 %all-to-all-start.1 = ((f32[16,16,1024]{2,1,0:T(8,128)}), f32[16,16,1024]{2,1,0:T(8,128)S(1)}, u32[]{:S(2)}, u32[]{:S(2)}) async-start(f32[16,16,1024]{2,1,0:T(8,128)} %fusion.6), calls=%async_computation.1 | async-start | bytes 2097152 | tf_op jit(solution)/shard_map/all_to_all | solution.py:106
  71.8 2.0 %copy-start = (f32[8,32,512]{2,1,0:T(8,128)S(1)}, f32[8,32,512]{2,1,0:T(8,128)}, u32[]{:S(2)}) copy-start(f32[8,32,512]{2,1,0:T(8,128)} %param.7) | copy-start | bytes 1572868
  72.2 6.1 %collective-permute-start.1 = (f32[8,8,512]{2,1,0:T(8,128)S(1)}, f32[8,8,512]{2,1,0:T(8,128)S(1)}, u32[]{:S(2)}, u32[]{:S(2)}) collective-permute-start(f32[8,8,512]{2,1,0:T(8,128)S(1)} %constant_dynamic-slice_fusion), channel_id=1, source_target_pairs={{0,1},{1,0},{2,3},{3,2},{4,5},{5,4},{6,7},{7,6},{8,9},{9,8},{10,11... | collective-permute-start | bytes 393224 | tf_op jit(solution)/shard_map/ppermute | solution.py:118
  78.6 0.8 %copy-start.2 = (f32[8,32,512]{2,1,0:T(8,128)}, f32[8,32,512]{2,1,0:T(8,128)S(1)}, u32[]{:S(2)}) copy-start(f32[8,32,512]{2,1,0:T(8,128)S(1)} %multiply_dynamic-update-slice_fusion) | copy-start | bytes 1572868

commit v24 on v22

--- a/solution.py
+++ b/solution.py
@@ -80,8 +80,12 @@
         blurred = blurred.reshape(plane_count, flat_count)
     else:
         blurred = blur_rows(blur_band, estimate, "row", halo_rows).reshape(plane_count, flat_count)
-    both_flat = jnp.concatenate([blurred, raw.reshape(plane_count, flat_count)], axis=0)
-    both_in = lax.all_to_all(both_flat, "scan", split_axis=1, concat_axis=0, tiled=True)
+    if row_count % lax.axis_size("scan") == 0:
+        both_rows = jnp.concatenate([blurred.reshape(plane_count, row_count, width_count), raw], axis=0)
+        both_in = lax.all_to_all(both_rows, "scan", split_axis=1, concat_axis=0, tiled=True)
+    else:
+        both_flat = jnp.concatenate([blurred, raw.reshape(plane_count, flat_count)], axis=0)
+        both_in = lax.all_to_all(both_flat, "scan", split_axis=1, concat_axis=0, tiled=True)
     both_in = both_in.reshape(lax.axis_size("scan"), 2, plane_count, -1)
     pencil = both_in[:, 0].reshape(offsets.shape[0], -1)
     raw_pencil = both_in[:, 1].reshape(offsets.shape[0], -1)

time: 80.1 us -> 81.6 us (1.019)
  local copies, waits for them, and re-layouts: 5.45 us -> 6.82 us
    reshape x0 -> x1, local copies, waits for them, and re-layouts: none -> 0.9 us  [body(): both_in = both_in.reshape(lax.axis_size('scan'), 2, plane_count, -1)]
    concatenate x3 -> x1, local copies, waits for them, and re-layouts: 1.93 us -> 1.58 us  [body(): jnp.concatenate([blurred.reshape(plane_count, row_count, width_count), ra...]
  transfers between devices with their start and end apart: 4 -> 4, of which waited for: 4 -> 4; matrix products, arithmetic and copies ran while one was open for 8% -> 7% of each run, Pallas kernels for 0% -> 0%
where the time goes in v24:
time: 81.6 us; the launch traced here: 80.8 us
  waiting for transfers between devices  46.5 us (57%)
  starting transfers between devices  17.7 us (22%)
  local copies, waits for them, and re-layouts  6.82 us (8%)
  matrix products  5.16 us (6%)
  other arithmetic  2.44 us (3%)
  between operations  2.16 us (3%)
    all_to_all x1, waiting for transfers between devices, body(): lax.all_to_all(both_pencil, 'scan', split_axis=0, concat_axis=1, tiled=True)  21.6 us
    all_to_all x1, waiting for transfers between devices, body(): lax.all_to_all(both_rows, 'scan', split_axis=1, concat_axis=0, tiled=True)  21.2 us
    all_to_all x1, starting transfers between devices, body(): lax.all_to_all(both_pencil, 'scan', split_axis=0, concat_axis=1, tiled=True)  6.86 us
    all_to_all x1, starting transfers between devices, body(): lax.all_to_all(both_rows, 'scan', split_axis=1, concat_axis=0, tiled=True)  6.32 us
    ppermute x1, starting transfers between devices, body(): front_arrived = lax.ppermute(front_sent, 'row', [(0, 1), (1, 0)])  3 us
    dot_general x4, matrix products, lateral_apply(): return jnp.einsum('rk,pkc->prc', band, padded, precision=precision)  2.96 us
    ppermute x1, waiting for transfers between devices, body(): arrived = lax.ppermute(sent, 'row', [(0, 1), (1, 0)])  2.7 us
  transfers between devices with their start and end apart: 4, of which 4 were waited for; matrix products, arithmetic and copies ran while one was open for 7% of the time, Pallas kernels for 0%

profile of v24, /device:TPU:0, one launch (start us, length us, event | category | flops | bytes accessed | tf_op | source)
XLA Modules:
  0.0 80.8 jit_solution(5773874524545842043)
XLA Ops:
  0.6 0.9 %constant_dynamic-slice_fusion = f32[8,8,512]{2,1,0:T(8,128)S(1)} fusion(f32[8,32,512]{2,1,0:T(8,128)} %param.7, s32[]{:T(128)S(6)} %select_n.45), kind=kLoop, calls=%fused_computation.58 | loop fusion | bytes 262148 | tf_op jit(solution)/shard_map/dynamic_slice | solution.py:69
  1.6 3.0 %collective-permute-start = (f32[8,8,512]{2,1,0:T(8,128)S(1)}, f32[8,8,512]{2,1,0:T(8,128)S(1)}, u32[]{:S(2)}, u32[]{:S(2)}) collective-permute-start(f32[8,8,512]{2,1,0:T(8,128)S(1)} %constant_dynamic-slice_fusion), channel_id=1, source_target_pairs={{0,1},{1,0},{2,3},{3,2},{4,5},{5,4},{6,7},{7,6},{8,9},{9,8},{10,11... | collective-permute-start | bytes 393224 | tf_op jit(solution)/shard_map/ppermute | solution.py:70
  4.6 0.8 select_reduce_fusion.1
  5.4 0.0 copy-start.1
  5.4 1.7 %fusion.22 = f32[32,8,512]{2,0,1:T(8,128)S(1)} fusion(f32[8,32,512]{2,1,0:T(8,128)} %param.7, f32[32,48]{1,0:T(8,128)S(1)} %get-tuple-element.3), kind=kOutput, calls=%fused_computation.45 | convolution fusion | flops 50331648 | bytes 1054720 | tf_op jit(solution)/shard_map/rk,pkc->prc/dot_general | solution.py:41
  7.2 0.9 %collective-permute-done = f32[8,8,512]{2,1,0:T(8,128)S(1)} collective-permute-done((f32[8,8,512]{2,1,0:T(8,128)S(1)}, f32[8,8,512]{2,1,0:T(8,128)S(1)}, u32[]{:S(2)}, u32[]{:S(2)}) %collective-permute-start) | collective-permute-done | bytes 131104 | tf_op jit(solution)/shard_map/ppermute | solution.py:70
  8.1 0.3 fusion.5
  8.4 0.0 copy-done.1
  8.4 0.1 pad_maximum_fusion
  8.5 1.6 %copy.25 = f32[16,32,512]{2,0,1:T(8,128)} copy(f32[16,32,512]{2,1,0:T(8,128)S(1)} %pad_maximum_fusion) | data formatting | bytes 2097152 | tf_op jit(solution)/shard_map/concatenate | solution.py:84
  10.1 0.0 copy-start.3
  10.1 0.0 copy-start.4
  10.1 6.3 %all-to-all-start = ((f32[16,32,512]{2,0,1:T(8,128)}), f32[16,32,512]{2,0,1:T(8,128)S(1)}, u32[]{:S(2)}, u32[]{:S(2)}) async-start(f32[16,32,512]{2,0,1:T(8,128)} %copy.25), calls=%async_computation | async-start | bytes 2097152 | tf_op jit(solution)/shard_map/all_to_all | solution.py:85
  16.4 0.0 copy-done.3
  16.4 0.1 subtract_subtract_fusion
  16.5 0.0 copy-done.4
  16.5 1.4 %select_reduce_fusion = f32[128,128]{1,0:T(8,128)S(1)} fusion(f32[64]{0:T(128)S(1)} %copy-done.4, s32[128,128]{1,0:T(8,128)S(1)} %subtract_subtract_fusion), kind=kLoop, calls=%fused_computation | loop fusion | flops 3129344 | bytes 131328 | tf_op jit(solution)/shard_map/reduce_sum | solution.py:52
  17.9 0.1 copy.23
  18.0 0.1 fusion.15
  18.1 21.2 %all-to-all-done = f32[16,32,512]{2,0,1:T(8,128)S(1)} async-done(((f32[16,32,512]{2,0,1:T(8,128)}), f32[16,32,512]{2,0,1:T(8,128)S(1)}, u32[]{:S(2)}, u32[]{:S(2)}) %all-to-all-start) | async-done | bytes 1048608 | tf_op jit(solution)/shard_map/all_to_all | solution.py:85
  39.4 0.8 %copy.30 = f32[16,16,2,512]{3,2,0,1:T(2,128)S(1)} copy(f32[16,16,2,512]{3,0,2,1:T(8,128)S(1)} %bitcast.69) | data formatting | bytes 2097152 | tf_op jit(solution)/shard_map/all_to_all | solution.py:85
  40.2 0.9 %reshape.99 = f32[16,2,8,1024]{3,2,1,0:T(8,128)S(1)} reshape(f32[16,16,2,512]{3,2,1,0:T(2,128)S(1)} %bitcast.71) | data formatting | bytes 2097152 | tf_op jit(solution)/shard_map/reshape | solution.py:89
  41.1 0.6 fusion.2
  41.7 1.6 %fusion.7 = f32[16,16,1024]{2,1,0:T(8,128)} fusion(f32[128,1024,1]{1,0,2:T(8,128)S(1)} %fusion.2, f32[16,1,8,128]{3,2,1,0:T(8,128)S(1)} %fusion.10, f32[16,1,8,128]{3,2,1,0:T(8,128)S(1)} %fusion.15), kind=kOutput, calls=%fused_computation.23 | convolution fusion | flops 201359360 | bytes 1703936 | tf_op jit(solution)/shard_map/dot_general | solution.py:99
  43.3 6.9 %all-to-all-start.1 = ((f32[16,16,1024]{2,1,0:T(8,128)}), f32[16,16,1024]{2,1,0:T(8,128)S(1)}, u32[]{:S(2)}, u32[]{:S(2)}) async-start(f32[16,16,1024]{2,1,0:T(8,128)} %fusion.7), calls=%async_computation.1 | async-start | bytes 2097152 | tf_op jit(solution)/shard_map/all_to_all | solution.py:100
  51.5 21.6 %all-to-all-done.1 = f32[16,16,1024]{2,1,0:T(8,128)S(1)} async-done(((f32[16,16,1024]{2,1,0:T(8,128)}), f32[16,16,1024]{2,1,0:T(8,128)S(1)}, u32[]{:S(2)}, u32[]{:S(2)}) %all-to-all-start.1) | async-done | bytes 1048608 | tf_op jit(solution)/shard_map/all_to_all | solution.py:100
  73.1 0.1 fusion.35
  73.2 0.0 copy-start
  73.2 0.3 copy.27
  73.5 0.1 reshape.100
  73.6 1.6 %collective-permute-start.1 = (f32[8,8,512]{2,1,0:T(8,128)S(1)}, f32[8,8,512]{2,1,0:T(8,128)S(1)}, u32[]{:S(2)}, u32[]{:S(2)}) collective-permute-start(f32[8,8,512]{2,1,0:T(8,128)S(1)} %constant_dynamic-slice_fusion.1), channel_id=1, source_target_pairs={{0,1},{1,0},{2,3},{3,2},{4,5},{5,4},{6,7},{7,6},{8,9},{9,8},{10,11... | collective-permute-start | bytes 393224 | tf_op jit(solution)/shard_map/ppermute | solution.py:112
  75.2 0.0 copy-done
  75.2 0.6 maximum_multiply_fusion
  75.8 0.3 copy.28
  76.1 0.9 %reshape.101 = f32[8,32,512]{2,1,0:T(8,128)} reshape(f32[8,16,1024]{2,1,0:T(8,128)S(1)} %copy.28) | data formatting | bytes 1048576 | tf_op jit(solution)/shard_map/reshape | solution.py:127
  77.0 2.7 %collective-permute-done.1 = f32[8,8,512]{2,1,0:T(8,128)S(1)} collective-permute-done((f32[8,8,512]{2,1,0:T(8,128)S(1)}, f32[8,8,512]{2,1,0:T(8,128)S(1)}, u32[]{:S(2)}, u32[]{:S(2)}) %collective-permute-start.1) | collective-permute-done | bytes 131104 | tf_op jit(solution)/shard_map/ppermute | solution.py:112
  79.7 0.3 multiply_dynamic-update-slice_fusion
  80.0 0.0 copy-start.2
  80.0 0.8 copy-done.2
  (5 shorter events, 0.1 us)
Async XLA Ops:
  1.6 6.5 %collective-permute-start = (f32[8,8,512]{2,1,0:T(8,128)S(1)}, f32[8,8,512]{2,1,0:T(8,128)S(1)}, u32[]{:S(2)}, u32[]{:S(2)}) collective-permute-start(f32[8,8,512]{2,1,0:T(8,128)S(1)} %constant_dynamic-slice_fusion), channel_id=1, source_target_pairs={{0,1},{1,0},{2,3},{3,2},{4,5},{5,4},{6,7},{7,6},{8,9},{9,8},{10,11... | collective-permute-start | bytes 393224 | tf_op jit(solution)/shard_map/ppermute | solution.py:70
  5.4 3.0 %copy-start.1 = (f32[8,32,512]{2,1,0:T(8,128)S(1)}, f32[8,32,512]{2,1,0:T(8,128)}, u32[]{:S(2)}) copy-start(f32[8,32,512]{2,1,0:T(8,128)} %param.8) | copy-start | bytes 1572868
  10.1 6.3 %copy-start.3 = (s32[128]{0:T(128)S(1)}, s32[128]{0:T(128)}, u32[]{:S(2)}) copy-start(s32[128]{0:T(128)} %param.9) | copy-start | bytes 1540
  10.1 6.4 %copy-start.4 = (f32[64]{0:T(128)S(1)}, f32[64]{0:T(128)}, u32[]{:S(2)}) copy-start(f32[64]{0:T(128)} %param.10) | copy-start | bytes 772
  10.1 29.3 %all-to-all-start = ((f32[16,32,512]{2,0,1:T(8,128)}), f32[16,32,512]{2,0,1:T(8,128)S(1)}, u32[]{:S(2)}, u32[]{:S(2)}) async-start(f32[16,32,512]{2,0,1:T(8,128)} %copy.25), calls=%async_computation | async-start | bytes 2097152 | tf_op jit(solution)/shard_map/all_to_all | solution.py:85
  43.3 29.8 %all-to-all-start.1 = ((f32[16,16,1024]{2,1,0:T(8,128)}), f32[16,16,1024]{2,1,0:T(8,128)S(1)}, u32[]{:S(2)}, u32[]{:S(2)}) async-start(f32[16,16,1024]{2,1,0:T(8,128)} %fusion.7), calls=%async_computation.1 | async-start | bytes 2097152 | tf_op jit(solution)/shard_map/all_to_all | solution.py:100
  73.2 2.0 %copy-start = (f32[8,32,512]{2,1,0:T(8,128)S(1)}, f32[8,32,512]{2,1,0:T(8,128)}, u32[]{:S(2)}) copy-start(f32[8,32,512]{2,1,0:T(8,128)} %param.7) | copy-start | bytes 1572868
  73.6 6.1 %collective-permute-start.1 = (f32[8,8,512]{2,1,0:T(8,128)S(1)}, f32[8,8,512]{2,1,0:T(8,128)S(1)}, u32[]{:S(2)}, u32[]{:S(2)}) collective-permute-start(f32[8,8,512]{2,1,0:T(8,128)S(1)} %constant_dynamic-slice_fusion.1), channel_id=1, source_target_pairs={{0,1},{1,0},{2,3},{3,2},{4,5},{5,4},{6,7},{7,6},{8,9},{9,8},{10,11... | collective-permute-start | bytes 393224 | tf_op jit(solution)/shard_map/ppermute | solution.py:112
  80.0 0.8 copy-start.2

commit v25 on v22

--- a/solution.py
+++ b/solution.py
@@ -33,8 +33,10 @@
     lag = in_rows - out_rows
     if flip:
         lag = (tap_count - 1) - lag
-    taps = jnp.arange(tap_count, dtype=jnp.int32)
-    return jnp.sum(jnp.where(lag[:, :, None] == taps, kernel_taps, 0.0), axis=-1)
+    band = jnp.zeros(lag.shape, kernel_taps.dtype)
+    for tap in range(tap_count):
+        band = band + jnp.where(lag == tap, kernel_taps[tap], 0.0)
+    return band
 
 
 def lateral_apply(band, padded, precision=highest_mode):

time: 80.1 us -> 91.3 us (1.14)
  other arithmetic: 2.45 us -> 22.9 us
  waiting for transfers between devices: 46.3 us -> 35.9 us
  local copies, waits for them, and re-layouts: 5.45 us -> 7.43 us
  starting transfers between devices: 17.7 us -> 16.5 us
    add x0 -> x2, other arithmetic: none -> 21.3 us  [band_matrix(): band = band + jnp.where(lag == tap, kernel_taps[tap], 0.0)]
    all_to_all x1, waiting for transfers between devices: 21.6 us -> 11 us  [body(): lax.all_to_all(both_pencil, 'scan', split_axis=0, concat_axis=1, tiled=True)]
    slice x0 -> x1, local copies, waits for them, and re-layouts: none -> 1.98 us  [band_matrix(): band = band + jnp.where(lag == tap, kernel_taps[tap], 0.0)]
    ppermute x1, starting transfers between devices: 1.56 us -> 0.6 us  [body(): arrived = lax.ppermute(sent, 'row', [(0, 1), (1, 0)])]
    ppermute x1, waiting for transfers between devices: 2.7 us -> 3.66 us  [body(): arrived = lax.ppermute(sent, 'row', [(0, 1), (1, 0)])]
  transfers between devices with their start and end apart: 4 -> 4, of which waited for: 4 -> 3; matrix products, arithmetic and copies ran while one was open for 8% -> 32% of each run, Pallas kernels for 0% -> 0%
where the time goes in v25:
time: 91.3 us; the launch traced here: 90.1 us
  waiting for transfers between devices  35.9 us (39%)
  other arithmetic  22.9 us (25%)
  starting transfers between devices  16.5 us (18%)
  local copies, waits for them, and re-layouts  7.43 us (8%)
  matrix products  5.16 us (6%)
  between operations  2.17 us (2%)
    add x2, other arithmetic, band_matrix(): band = band + jnp.where(lag == tap, kernel_taps[tap], 0.0)  21.3 us
    all_to_all x1, waiting for transfers between devices, body(): lax.all_to_all(both_flat, 'scan', split_axis=1, concat_axis=0, tiled=True)  21.2 us
    all_to_all x1, waiting for transfers between devices, body(): lax.all_to_all(both_pencil, 'scan', split_axis=0, concat_axis=1, tiled=True)  11 us
    all_to_all x1, starting transfers between devices, body(): lax.all_to_all(both_pencil, 'scan', split_axis=0, concat_axis=1, tiled=True)  6.86 us
    all_to_all x1, starting transfers between devices, body(): lax.all_to_all(both_flat, 'scan', split_axis=1, concat_axis=0, tiled=True)  6.07 us
    ppermute x1, waiting for transfers between devices, body(): arrived = lax.ppermute(sent, 'row', [(0, 1), (1, 0)])  3.66 us
    ppermute x1, starting transfers between devices, body(): front_arrived = lax.ppermute(front_sent, 'row', [(0, 1), (1, 0)])  3 us
    dot_general x4, matrix products, lateral_apply(): return jnp.einsum('rk,pkc->prc', band, padded, precision=precision)  2.97 us
  transfers between devices with their start and end apart: 4, of which 3 were waited for; matrix products, arithmetic and copies ran while one was open for 32% of the time, Pallas kernels for 0%

profile of v25, /device:TPU:0, one launch (start us, length us, event | category | flops | bytes accessed | tf_op | source)
XLA Modules:
  0.0 90.1 jit_solution(16657286580210544716)
XLA Ops:
  0.6 0.9 %constant_dynamic-slice_fusion = f32[8,8,512]{2,1,0:T(8,128)S(1)} fusion(f32[8,32,512]{2,1,0:T(8,128)} %param.7, s32[]{:T(128)S(6)} %select_n.157), kind=kLoop, calls=%fused_computation.89 | loop fusion | bytes 262148 | tf_op jit(solution)/shard_map/dynamic_slice | solution.py:71
  1.6 3.0 %collective-permute-start = (f32[8,8,512]{2,1,0:T(8,128)S(1)}, f32[8,8,512]{2,1,0:T(8,128)S(1)}, u32[]{:S(2)}, u32[]{:S(2)}) collective-permute-start(f32[8,8,512]{2,1,0:T(8,128)S(1)} %constant_dynamic-slice_fusion), channel_id=1, source_target_pairs={{0,1},{1,0},{2,3},{3,2},{4,5},{5,4},{6,7},{7,6},{8,9},{9,8},{10,11... | collective-permute-start | bytes 393224 | tf_op jit(solution)/shard_map/ppermute | solution.py:72
  4.6 2.0 %fusion.71 = (f32[1]{0:T(128)}, f32[1]{0:T(128)}, f32[1]{0:T(128)}, f32[1]{0:T(128)}, f32[1]{0:T(128)}, /*index=5*/f32[1]{0:T(128)}, f32[1]{0:T(128)}, f32[1]{0:...) fusion(f32[17]{0:T(128)} %param.11), kind=kLoop, calls=%fused_computation.95 | loop fusion | bytes 136 | tf_op jit(solution)/shard_map/slice | solution.py:38
  6.5 10.6 %select_add_fusion.1 = f32[32,48]{1,0:T(8,128)S(1)} fusion(f32[]{:T(128)} %bitcast.21, f32[]{:T(128)} %bitcast.20, f32[]{:T(128)} %bitcast.19, f32[]{:T(128)} %bitcast.18, f32[]{:T(128)} %bitcast.17, f32[]{:T(128)} %bitcast.16, f32[]{:T(128)} %bitcast.15, f32[]{:T(128)} %bitcast.14, f32[]{:T(128)} %bitcast.13, f32[]{:T(128)} %bitcast.12, f32[]{:T(128)} %bitcast.11, ...), kind=kLoop, calls=%fused_computation.42 | loop fusion | flops 78336 | bytes 6212 | tf_op jit(solution)/shard_map/add | solution.py:38
  17.2 0.0 copy-start.1
  17.2 1.7 %fusion.22 = f32[32,8,512]{2,0,1:T(8,128)S(1)} fusion(f32[8,32,512]{2,1,0:T(8,128)} %param.7, f32[32,48]{1,0:T(8,128)S(1)} %select_add_fusion.1), kind=kOutput, calls=%fused_computation.40 | convolution fusion | flops 50331648 | bytes 1054720 | tf_op jit(solution)/shard_map/rk,pkc->prc/dot_general | solution.py:43
  19.0 0.0 copy-done.1
  19.0 0.2 concatenate.13
  19.2 0.0 collective-permute-done
  19.2 0.3 fusion.5
  19.5 0.2 concatenate.12
  19.7 0.1 pad_maximum_fusion
  19.8 1.6 %copy.28 = f32[16,16,1024]{2,0,1:T(8,128)} copy(f32[16,16,1024]{2,1,0:T(8,128)S(1)} %pad_maximum_fusion) | data formatting | bytes 2097152 | tf_op jit(solution)/shard_map/concatenate | solution.py:85
  21.4 0.0 copy-start.3
  21.4 0.0 copy-start.4
  21.4 6.1 %all-to-all-start = ((f32[16,16,1024]{2,0,1:T(8,128)}), f32[16,16,1024]{2,0,1:T(8,128)S(1)}, u32[]{:S(2)}, u32[]{:S(2)}) async-start(f32[16,16,1024]{2,0,1:T(8,128)} %copy.28), calls=%async_computation | async-start | bytes 2097152 | tf_op jit(solution)/shard_map/all_to_all | solution.py:86
  27.5 0.0 copy-done.3
  27.5 0.1 subtract_subtract_fusion
  27.6 0.0 copy-done.4
  27.6 1.4 %select_reduce_fusion = f32[128,128]{1,0:T(8,128)S(1)} fusion(f32[64]{0:T(128)S(1)} %copy-done.4, s32[128,128]{1,0:T(8,128)S(1)} %subtract_subtract_fusion), kind=kLoop, calls=%fused_computation | loop fusion | flops 3129344 | bytes 131328 | tf_op jit(solution)/shard_map/reduce_sum | solution.py:54
  28.9 0.1 copy.26
  29.0 0.1 fusion.15
  29.2 21.2 %all-to-all-done = f32[16,16,1024]{2,0,1:T(8,128)S(1)} async-done(((f32[16,16,1024]{2,0,1:T(8,128)}), f32[16,16,1024]{2,0,1:T(8,128)S(1)}, u32[]{:S(2)}, u32[]{:S(2)}) %all-to-all-start) | async-done | bytes 1048608 | tf_op jit(solution)/shard_map/all_to_all | solution.py:86
  50.4 0.6 fusion.2
  51.1 1.6 %fusion.7 = f32[16,16,1024]{2,1,0:T(8,128)} fusion(f32[128,1024,1]{1,0,2:T(8,128)S(1)} %fusion.2, f32[16,1,8,128]{3,2,1,0:T(8,128)S(1)} %fusion.10, f32[16,1,8,128]{3,2,1,0:T(8,128)S(1)} %fusion.15), kind=kOutput, calls=%fused_computation.18 | convolution fusion | flops 201359360 | bytes 1703936 | tf_op jit(solution)/shard_map/dot_general | solution.py:97
  52.6 6.9 %all-to-all-start.1 = ((f32[16,16,1024]{2,1,0:T(8,128)}), f32[16,16,1024]{2,1,0:T(8,128)S(1)}, u32[]{:S(2)}, u32[]{:S(2)}) async-start(f32[16,16,1024]{2,1,0:T(8,128)} %fusion.7), calls=%async_computation.1 | async-start | bytes 2097152 | tf_op jit(solution)/shard_map/all_to_all | solution.py:98
  60.8 10.6 %select_add_fusion = f32[32,48]{1,0:T(8,128)S(1)} fusion(f32[]{:T(128)} %bitcast.21, f32[]{:T(128)} %bitcast.20, f32[]{:T(128)} %bitcast.19, f32[]{:T(128)} %bitcast.18, f32[]{:T(128)} %bitcast.17, f32[]{:T(128)} %bitcast.16, f32[]{:T(128)} %bitcast.15, f32[]{:T(128)} %bitcast.14, f32[]{:T(128)} %bitcast.13, f32[]{:T(128)} %bitcast.12, f32[]{:T(128)} %bitcast.11, ...), kind=kLoop, calls=%fused_computation.41 | loop fusion | flops 79872 | bytes 6212 | tf_op jit(solution)/shard_map/add | solution.py:38
  71.4 11.0 %all-to-all-done.1 = f32[16,16,1024]{2,1,0:T(8,128)S(1)} async-done(((f32[16,16,1024]{2,1,0:T(8,128)}), f32[16,16,1024]{2,1,0:T(8,128)S(1)}, u32[]{:S(2)}, u32[]{:S(2)}) %all-to-all-start.1) | async-done | bytes 1048608 | tf_op jit(solution)/shard_map/all_to_all | solution.py:98
  82.4 0.1 fusion.70
  82.5 0.0 copy-start
  82.5 0.3 copy.29
  82.8 0.1 reshape.87
  83.0 0.6 collective-permute-start.1
  83.6 0.0 copy-done
  83.6 0.6 maximum_multiply_fusion
  84.2 0.3 copy.30
  84.5 0.9 reshape.88
  85.4 3.7 %collective-permute-done.1 = f32[8,8,512]{2,1,0:T(8,128)S(1)} collective-permute-done((f32[8,8,512]{2,1,0:T(8,128)S(1)}, f32[8,8,512]{2,1,0:T(8,128)S(1)}, u32[]{:S(2)}, u32[]{:S(2)}) %collective-permute-start.1) | collective-permute-done | bytes 131104 | tf_op jit(solution)/shard_map/ppermute | solution.py:110
  89.0 0.3 multiply_dynamic-update-slice_fusion
  89.3 0.0 copy-start.2
  89.4 0.8 copy-done.2
  (4 shorter events, 0.1 us)
Async XLA Ops:
  1.6 17.6 %collective-permute-start = (f32[8,8,512]{2,1,0:T(8,128)S(1)}, f32[8,8,512]{2,1,0:T(8,128)S(1)}, u32[]{:S(2)}, u32[]{:S(2)}) collective-permute-start(f32[8,8,512]{2,1,0:T(8,128)S(1)} %constant_dynamic-slice_fusion), channel_id=1, source_target_pairs={{0,1},{1,0},{2,3},{3,2},{4,5},{5,4},{6,7},{7,6},{8,9},{9,8},{10,11... | collective-permute-start | bytes 393224 | tf_op jit(solution)/shard_map/ppermute | solution.py:72
  17.2 1.8 %copy-start.1 = (f32[8,32,512]{2,1,0:T(8,128)S(1)}, f32[8,32,512]{2,1,0:T(8,128)}, u32[]{:S(2)}) copy-start(f32[8,32,512]{2,1,0:T(8,128)} %param.8) | copy-start | bytes 1572868
  21.4 6.1 %copy-start.3 = (s32[128]{0:T(128)S(1)}, s32[128]{0:T(128)}, u32[]{:S(2)}) copy-start(s32[128]{0:T(128)} %param.9) | copy-start | bytes 1540
  21.4 6.2 %copy-start.4 = (f32[64]{0:T(128)S(1)}, f32[64]{0:T(128)}, u32[]{:S(2)}) copy-start(f32[64]{0:T(128)} %param.10) | copy-start | bytes 772
  21.4 29.0 %all-to-all-start = ((f32[16,16,1024]{2,0,1:T(8,128)}), f32[16,16,1024]{2,0,1:T(8,128)S(1)}, u32[]{:S(2)}, u32[]{:S(2)}) async-start(f32[16,16,1024]{2,0,1:T(8,128)} %copy.28), calls=%async_computation | async-start | bytes 2097152 | tf_op jit(solution)/shard_map/all_to_all | solution.py:86
  52.6 29.8 %all-to-all-start.1 = ((f32[16,16,1024]{2,1,0:T(8,128)}), f32[16,16,1024]{2,1,0:T(8,128)S(1)}, u32[]{:S(2)}, u32[]{:S(2)}) async-start(f32[16,16,1024]{2,1,0:T(8,128)} %fusion.7), calls=%async_computation.1 | async-start | bytes 2097152 | tf_op jit(solution)/shard_map/all_to_all | solution.py:98
  82.5 1.0 %copy-start = (f32[8,32,512]{2,1,0:T(8,128)S(1)}, f32[8,32,512]{2,1,0:T(8,128)}, u32[]{:S(2)}) copy-start(f32[8,32,512]{2,1,0:T(8,128)} %param.7) | copy-start | bytes 1572868
  83.0 6.1 %collective-permute-start.1 = (f32[8,8,512]{2,1,0:T(8,128)S(1)}, f32[8,8,512]{2,1,0:T(8,128)S(1)}, u32[]{:S(2)}, u32[]{:S(2)}) collective-permute-start(f32[8,8,512]{2,1,0:T(8,128)S(1)} %constant_dynamic-slice_fusion.1), channel_id=1, source_target_pairs={{0,1},{1,0},{2,3},{3,2},{4,5},{5,4},{6,7},{7,6},{8,9},{9,8},{10,11... | collective-permute-start | bytes 393224 | tf_op jit(solution)/shard_map/ppermute | solution.py:110
  89.3 0.8 copy-start.2

commit v26 on v22

--- a/solution.py
+++ b/solution.py
@@ -61,8 +61,9 @@
     flat_count = row_count * width_count
     halo_rows = lateral_psf.shape[0] // 2
     sheet_psf = sheet_matrix(offsets, depth_psf, offsets.shape[0])
+    late_taps, sheet_psf = lax.optimization_barrier((lateral_psf, sheet_psf))
+    back_band = band_matrix(late_taps, row_count, True)
     blur_band = band_matrix(lateral_psf, row_count, False)
-    back_band = band_matrix(lateral_psf, row_count, True)
     if lax.axis_size("row") == 2:
         first_row = lax.axis_index("row") == 0
         front_start = jnp.where(first_row, row_count - halo_rows, 0)

time: 80.1 us -> 80.1 us (level)
  no operation moved by 1% of the time
where the time goes in v26:
time: 80.1 us; the launch traced here: 79.4 us
  waiting for transfers between devices  46.2 us (58%)
  starting transfers between devices  17.9 us (22%)
  local copies, waits for them, and re-layouts  5.46 us (7%)
  matrix products  5.11 us (6%)
  other arithmetic  2.59 us (3%)
  between operations  2.18 us (3%)
    all_to_all x1, waiting for transfers between devices, body(): lax.all_to_all(both_pencil, 'scan', split_axis=0, concat_axis=1, tiled=True)  21.5 us
    all_to_all x1, waiting for transfers between devices, body(): lax.all_to_all(both_flat, 'scan', split_axis=1, concat_axis=0, tiled=True)  21.2 us
    all_to_all x1, starting transfers between devices, body(): lax.all_to_all(both_pencil, 'scan', split_axis=0, concat_axis=1, tiled=True)  7 us
    all_to_all x1, starting transfers between devices, body(): lax.all_to_all(both_flat, 'scan', split_axis=1, concat_axis=0, tiled=True)  6.32 us
    ppermute x1, starting transfers between devices, body(): front_arrived = lax.ppermute(front_sent, 'row', [(0, 1), (1, 0)])  3 us
    dot_general x4, matrix products, lateral_apply(): return jnp.einsum('rk,pkc->prc', band, padded, precision=precision)  2.96 us
    ppermute x1, waiting for transfers between devices, body(): arrived = lax.ppermute(sent, 'row', [(0, 1), (1, 0)])  2.71 us
    concatenate x3, local copies, waits for them, and re-layouts, body(): jnp.concatenate([blurred, raw.reshape(plane_count, flat_count)], axis=0)  1.93 us
  transfers between devices with their start and end apart: 4, of which 4 were waited for; matrix products, arithmetic and copies ran while one was open for 8% of the time, Pallas kernels for 0%

profile of v26, /device:TPU:0, one launch (start us, length us, event | category | flops | bytes accessed | tf_op | source)
XLA Modules:
  0.0 79.4 jit_solution(15073636026570310163)
XLA Ops:
  0.6 0.9 %constant_dynamic-slice_fusion = f32[8,8,512]{2,1,0:T(8,128)S(1)} fusion(f32[8,32,512]{2,1,0:T(8,128)} %param.7, s32[]{:T(128)S(6)} %select_n.41), kind=kLoop, calls=%fused_computation.44 | loop fusion | bytes 262148 | tf_op jit(solution)/shard_map/dynamic_slice | solution.py:70
  1.6 3.0 %collective-permute-start = (f32[8,8,512]{2,1,0:T(8,128)S(1)}, f32[8,8,512]{2,1,0:T(8,128)S(1)}, u32[]{:S(2)}, u32[]{:S(2)}) collective-permute-start(f32[8,8,512]{2,1,0:T(8,128)S(1)} %constant_dynamic-slice_fusion), channel_id=1, source_target_pairs={{0,1},{1,0},{2,3},{3,2},{4,5},{5,4},{6,7},{7,6},{8,9},{9,8},{10,11... | collective-permute-start | bytes 393224 | tf_op jit(solution)/shard_map/ppermute | solution.py:71
  4.6 0.8 select_reduce_fusion.2
  5.3 0.0 copy-start.1
  5.3 1.7 %fusion.11 = f32[32,8,512]{2,0,1:T(8,128)S(1)} fusion(f32[8,32,512]{2,1,0:T(8,128)} %param.7, f32[32,48]{1,0:T(8,128)S(1)} %select_reduce_fusion.2), kind=kOutput, calls=%fused_computation.32 | convolution fusion | flops 50331648 | bytes 1054720 | tf_op jit(solution)/shard_map/rk,pkc->prc/dot_general | solution.py:41
  7.1 0.0 copy-done.1
  7.1 0.2 concatenate.13
  7.3 0.8 collective-permute-done
  8.1 0.3 fusion.5
  8.4 0.2 concatenate.12
  8.6 0.1 pad_maximum_fusion
  8.7 1.6 %copy.32 = f32[16,16,1024]{2,0,1:T(8,128)} copy(f32[16,16,1024]{2,1,0:T(8,128)S(1)} %pad_maximum_fusion) | data formatting | bytes 2097152 | tf_op jit(solution)/shard_map/concatenate | solution.py:84
  10.3 0.0 copy-start.3
  10.3 0.0 copy-start.5
  10.3 6.3 %all-to-all-start = ((f32[16,16,1024]{2,0,1:T(8,128)}), f32[16,16,1024]{2,0,1:T(8,128)S(1)}, u32[]{:S(2)}, u32[]{:S(2)}) async-start(f32[16,16,1024]{2,0,1:T(8,128)} %copy.32), calls=%async_computation | async-start | bytes 2097152 | tf_op jit(solution)/shard_map/all_to_all | solution.py:85
  16.6 0.0 copy-done.3
  16.6 0.1 subtract_subtract_fusion
  16.7 0.0 copy-done.5
  16.7 1.4 %select_reduce_fusion = f32[128,128]{1,0:T(8,128)S(1)} fusion(f32[64]{0:T(128)S(1)} %copy-done.5, s32[128,128]{1,0:T(8,128)S(1)} %subtract_subtract_fusion), kind=kLoop, calls=%fused_computation | loop fusion | flops 3129344 | bytes 131328 | tf_op jit(solution)/shard_map/reduce_sum | solution.py:52
  18.1 0.1 and_select_fusion
  18.2 0.1 copy.30
  18.3 0.1 fusion.10
  18.4 21.2 %all-to-all-done = f32[16,16,1024]{2,0,1:T(8,128)S(1)} async-done(((f32[16,16,1024]{2,0,1:T(8,128)}), f32[16,16,1024]{2,0,1:T(8,128)S(1)}, u32[]{:S(2)}, u32[]{:S(2)}) %all-to-all-start) | async-done | bytes 1048608 | tf_op jit(solution)/shard_map/all_to_all | solution.py:85
  39.5 0.6 fusion.2
  40.1 1.6 %fusion.7 = f32[16,16,1024]{2,1,0:T(8,128)} fusion(f32[128,1024,1]{1,0,2:T(8,128)S(1)} %fusion.2, f32[16,1,8,128]{3,2,0,1:T(8,128)S(1)} %bitcast.67, f32[16,1,8,128]{3,2,0,1:T(8,128)S(1)} %fusion.10), kind=kOutput, calls=%fused_computation.22 | convolution fusion | flops 201359360 | bytes 1703936 | tf_op jit(solution)/shard_map/dot_general | solution.py:96
  41.7 0.0 copy-start.4
  41.7 7.0 %all-to-all-start.1 = ((f32[16,16,1024]{2,1,0:T(8,128)}), f32[16,16,1024]{2,1,0:T(8,128)S(1)}, u32[]{:S(2)}, u32[]{:S(2)}) async-start(f32[16,16,1024]{2,1,0:T(8,128)} %fusion.7), calls=%async_computation.1 | async-start | bytes 2097152 | tf_op jit(solution)/shard_map/all_to_all | solution.py:97
  50.0 0.0 copy-done.4
  50.0 0.1 select_reduce_fusion.1
  50.1 21.5 %all-to-all-done.1 = f32[16,16,1024]{2,1,0:T(8,128)S(1)} async-done(((f32[16,16,1024]{2,1,0:T(8,128)}), f32[16,16,1024]{2,1,0:T(8,128)S(1)}, u32[]{:S(2)}, u32[]{:S(2)}) %all-to-all-start.1) | async-done | bytes 1048608 | tf_op jit(solution)/shard_map/all_to_all | solution.py:97
  71.6 0.1 fusion.20
  71.7 0.0 copy-start
  71.7 0.3 copy.33
  72.1 0.1 reshape.109
  72.2 1.6 %collective-permute-start.1 = (f32[8,8,512]{2,1,0:T(8,128)S(1)}, f32[8,8,512]{2,1,0:T(8,128)S(1)}, u32[]{:S(2)}, u32[]{:S(2)}) collective-permute-start(f32[8,8,512]{2,1,0:T(8,128)S(1)} %constant_dynamic-slice_fusion.1), channel_id=1, source_target_pairs={{0,1},{1,0},{2,3},{3,2},{4,5},{5,4},{6,7},{7,6},{8,9},{9,8},{10,11... | collective-permute-start | bytes 393224 | tf_op jit(solution)/shard_map/ppermute | solution.py:109
  73.7 0.0 copy-done
  73.7 0.6 maximum_multiply_fusion
  74.4 0.3 copy.34
  74.7 0.9 %reshape.110 = f32[8,32,512]{2,1,0:T(8,128)} reshape(f32[8,16,1024]{2,1,0:T(8,128)S(1)} %copy.34) | data formatting | bytes 1048576 | tf_op jit(solution)/shard_map/reshape | solution.py:124
  75.5 2.7 %collective-permute-done.1 = f32[8,8,512]{2,1,0:T(8,128)S(1)} collective-permute-done((f32[8,8,512]{2,1,0:T(8,128)S(1)}, f32[8,8,512]{2,1,0:T(8,128)S(1)}, u32[]{:S(2)}, u32[]{:S(2)}) %collective-permute-start.1) | collective-permute-done | bytes 131104 | tf_op jit(solution)/shard_map/ppermute | solution.py:109
  78.2 0.3 multiply_dynamic-update-slice_fusion
  78.6 0.0 copy-start.2
  78.6 0.8 copy-done.2
  (5 shorter events, 0.1 us)
Async XLA Ops:
  1.6 6.5 %collective-permute-start = (f32[8,8,512]{2,1,0:T(8,128)S(1)}, f32[8,8,512]{2,1,0:T(8,128)S(1)}, u32[]{:S(2)}, u32[]{:S(2)}) collective-permute-start(f32[8,8,512]{2,1,0:T(8,128)S(1)} %constant_dynamic-slice_fusion), channel_id=1, source_target_pairs={{0,1},{1,0},{2,3},{3,2},{4,5},{5,4},{6,7},{7,6},{8,9},{9,8},{10,11... | collective-permute-start | bytes 393224 | tf_op jit(solution)/shard_map/ppermute | solution.py:71
  5.3 1.8 %copy-start.1 = (f32[8,32,512]{2,1,0:T(8,128)S(1)}, f32[8,32,512]{2,1,0:T(8,128)}, u32[]{:S(2)}) copy-start(f32[8,32,512]{2,1,0:T(8,128)} %param.8) | copy-start | bytes 1572868
  10.3 6.3 %copy-start.3 = (s32[128]{0:T(128)S(1)}, s32[128]{0:T(128)}, u32[]{:S(2)}) copy-start(s32[128]{0:T(128)} %param.9) | copy-start | bytes 1540
  10.3 6.4 %copy-start.5 = (f32[64]{0:T(128)S(1)}, f32[64]{0:T(128)}, u32[]{:S(2)}) copy-start(f32[64]{0:T(128)} %param.10) | copy-start | bytes 772
  10.3 29.3 %all-to-all-start = ((f32[16,16,1024]{2,0,1:T(8,128)}), f32[16,16,1024]{2,0,1:T(8,128)S(1)}, u32[]{:S(2)}, u32[]{:S(2)}) async-start(f32[16,16,1024]{2,0,1:T(8,128)} %copy.32), calls=%async_computation | async-start | bytes 2097152 | tf_op jit(solution)/shard_map/all_to_all | solution.py:85
  41.7 8.3 %copy-start.4 = (f32[17]{0:T(128)S(1)}, f32[17]{0:T(128)}, u32[]{:S(2)}) copy-start(f32[17]{0:T(128)} %param.11) | copy-start | bytes 208
  41.7 29.9 %all-to-all-start.1 = ((f32[16,16,1024]{2,1,0:T(8,128)}), f32[16,16,1024]{2,1,0:T(8,128)S(1)}, u32[]{:S(2)}, u32[]{:S(2)}) async-start(f32[16,16,1024]{2,1,0:T(8,128)} %fusion.7), calls=%async_computation.1 | async-start | bytes 2097152 | tf_op jit(solution)/shard_map/all_to_all | solution.py:97
  71.7 2.0 %copy-start = (f32[8,32,512]{2,1,0:T(8,128)S(1)}, f32[8,32,512]{2,1,0:T(8,128)}, u32[]{:S(2)}) copy-start(f32[8,32,512]{2,1,0:T(8,128)} %param.7) | copy-start | bytes 1572868
  72.2 6.1 %collective-permute-start.1 = (f32[8,8,512]{2,1,0:T(8,128)S(1)}, f32[8,8,512]{2,1,0:T(8,128)S(1)}, u32[]{:S(2)}, u32[]{:S(2)}) collective-permute-start(f32[8,8,512]{2,1,0:T(8,128)S(1)} %constant_dynamic-slice_fusion.1), channel_id=1, source_target_pairs={{0,1},{1,0},{2,3},{3,2},{4,5},{5,4},{6,7},{7,6},{8,9},{9,8},{10,11... | collective-permute-start | bytes 393224 | tf_op jit(solution)/shard_map/ppermute | solution.py:109
  78.6 0.8 %copy-start.2 = (f32[8,32,512]{2,1,0:T(8,128)}, f32[8,32,512]{2,1,0:T(8,128)S(1)}, u32[]{:S(2)}) copy-start(f32[8,32,512]{2,1,0:T(8,128)S(1)} %multiply_dynamic-update-slice_fusion) | copy-start | bytes 1572868
